TPU v7x, 32 devices: a whole 2x2x4 slice. The times are simulated.
32 devices in a mesh: groups: 2 (over x), seq: 8 (over z, y), exp: 2 (over core).
Axes of the slice: x: 2, y: 2, z: 4, core: 2. Of those that a mesh axis runs over, the one named last changes fastest.
Arguments:
- queries: bfloat16 [4096, 2048], P(('groups', 'seq'), 'exp'), parts along dimension 0, may hold values from -400 to 400
- key_rows: bfloat16 [4096, 256], P(('groups', 'seq'), 'exp'), parts along dimension 0, may hold values from -4 to 4
- values: bfloat16 [4096, 256], P(('groups', 'seq'), 'exp'), parts along dimension 0, may hold values from -4 to 4
- cached_rows: bfloat16 [2, 256, 256], P(None, 'groups', 'exp'), parts along dimension 1, may hold values from -4 to 4
- sink_logits: float32 [32], P('exp'), may hold values from 1 to 5
- out_weight: bfloat16 [2048, 1536], P('exp'), may hold values from -0.375 to 0.375
- residual: bfloat16 [4096, 1536], P(('groups', 'seq')), parts along dimension 0, may hold values from -45 to 45
- norm_gain: float32 [1536], replicated, may hold values from 0.5 to 1.5
- expert_in: bfloat16 [8, 2, 1536, 1536], P('seq', None, None, 'exp'), may hold values from -0.15625 to 0.15625
- expert_out: bfloat16 [8, 1536, 1536], P('seq', 'exp'), may hold values from -0.15625 to 0.15625
- routes: int32 [4096, 4], P(('groups', 'seq')), parts along dimension 0, may hold values from 0 to 7, all different within a row; in each aligned block of 256 rows (0 to 255, 256 to 511, ...) at most 192 rows name the same one
- route_gates: float32 [4096, 4], P(('groups', 'seq')), parts along dimension 0, may hold values from 0.1 to 1
Outputs:
- layer_out: bfloat16 [4096, 1536], P(('groups', 'seq')), parts along dimension 0
There are 2 independent parts, one for each index of `groups`. A program takes and returns all parts, laid end to end along the dimension named above; an argument that names none is the same for every part. Nothing has to cross between parts.
Inputs may be any that keep to these rules, and one draw needn't show every extreme that they name: `routes`: within the rows of one index of seq, each expert is named by at most 192 rows, and in every draw some expert is named by exactly 192 rows of some such block.
All inputs are finite; a program needn't handle non-finite values.
Results may differ from a plain program's by a relative error of at most 0.008.
Values may be sent and summed in bfloat16 or wider, within the bound.
No kernel may reach another device: no remote copies, remote signals or barrier semaphores. Data moves between devices by JAX's collectives and lax.ppermute only.
A program may use at most 128 MiB of HBM per device.

v0:
```python
import jax
import jax.numpy as jnp
from jax import lax
from jax.sharding import PartitionSpec as P

HEAD_DIM = 64
WINDOW = 128
TOP = 4


GLU_ALPHA = 1.702
EPSILON = 1e-05


def shifted(shard, axis, by):
    size = lax.axis_size(axis)
    pairs = [(i, i + by) for i in range(size) if 0 <= i + by < size]
    return lax.ppermute(shard, axis, pairs)


def rms_normalize(mixed_rows, norm_gain):
    mean_square = jnp.mean(mixed_rows * mixed_rows, axis=-1, keepdims=True)
    return (mixed_rows * lax.rsqrt(mean_square + EPSILON) * norm_gain).astype(jnp.bfloat16)


def attend_block(queries, keys_all, values_all, sink_logits, block_rows, window_rows):
    kv_count = keys_all.shape[1] // HEAD_DIM
    group = queries.shape[1] // HEAD_DIM // kv_count
    query_block = queries.reshape(block_rows, kv_count, group, HEAD_DIM)
    key_block = keys_all.reshape(block_rows + window_rows, kv_count, HEAD_DIM)
    value_block = values_all.reshape(block_rows + window_rows, kv_count, HEAD_DIM)
    scores = jnp.einsum(
        "qhgd,khd->hgqk", query_block, key_block, preferred_element_type=jnp.float32
    ) * HEAD_DIM ** (-0.5)
    query_pos = jnp.arange(block_rows)[:, None]
    key_pos = jnp.arange(block_rows + window_rows)[None, :]
    allowed = (key_pos > query_pos) & (key_pos <= query_pos + window_rows)
    scores = jnp.where(allowed, scores, -jnp.inf)
    sink_table = sink_logits.reshape(kv_count, group)[:, :, None]
    largest = jnp.maximum(jnp.max(scores, axis=-1), sink_table)
    weights_exp = jnp.exp(scores - largest[..., None])
    denominator = jnp.exp(sink_table - largest) + jnp.sum(weights_exp, axis=-1)
    probs = (weights_exp / denominator[..., None]).astype(jnp.bfloat16)
    heads_out = jnp.einsum("hgqk,khd->qhgd", probs, value_block, preferred_element_type=jnp.float32)
    return heads_out.astype(jnp.bfloat16).reshape(block_rows, queries.shape[1])


def on_device(
    queries,
    key_rows,
    values,
    cached_rows,
    sink_logits,
    out_weight,
    residual,
    norm_gain,
    expert_in,
    expert_out,
    routes,
    route_gates,
):
    tok_rows = queries.shape[0]
    window_rows = WINDOW
    rim_rows = jnp.stack([key_rows[tok_rows - window_rows :], values[tok_rows - window_rows :]])
    received = shifted(rim_rows, "seq", 1)
    prior = jnp.where(lax.axis_index("seq") == 0, cached_rows, received)
    keys_all = jnp.concatenate([prior[0], key_rows], axis=0)
    values_all = jnp.concatenate([prior[1], values], axis=0)
    block_rows = min(tok_rows, 512)
    pieces = attend_block(queries, keys_all, values_all, sink_logits, block_rows, window_rows)
    partial_rows = jnp.dot(pieces, out_weight, preferred_element_type=jnp.float32)
    mixed_rows = residual.astype(jnp.float32) + lax.psum(partial_rows, "exp")
    normed = rms_normalize(mixed_rows, norm_gain)
    experts = lax.axis_size("seq")
    width = normed.shape[1]
    capacity = 3 * tok_rows * TOP // (2 * experts)
    assigned = tok_rows * TOP
    flat_experts = routes.reshape(-1)
    expert_hits = (flat_experts[:, None] == jnp.arange(experts, dtype=jnp.int32)[None, :]).astype(
        jnp.int32
    )
    slot_rank = jnp.sum(expert_hits * (jnp.cumsum(expert_hits, axis=0) - 1), axis=1)
    slot_index = flat_experts * capacity + slot_rank
    source = jnp.arange(assigned, dtype=jnp.int32) // TOP
    outgoing = (
        jnp.zeros((experts * capacity, width), jnp.bfloat16)
        .at[slot_index]
        .set(normed[source])
        .reshape(experts, capacity, width)
    )
    slot_rows = lax.all_to_all(outgoing, "seq", split_axis=0, concat_axis=0, tiled=True)
    row_shape = slot_rows.shape
    flat_rows = slot_rows.reshape(-1, row_shape[-1])
    gate_up = jnp.einsum("rd,kdf->krf", flat_rows, expert_in[0], preferred_element_type=jnp.float32)
    gate_val = gate_up[0]
    up_val = gate_up[1]
    activation = ((up_val + 1.0) * gate_val * jax.nn.sigmoid(GLU_ALPHA * gate_val)).astype(
        jnp.bfloat16
    )
    returned = lax.all_to_all(
        jnp.dot(activation, expert_out[0], preferred_element_type=jnp.float32)
        .astype(jnp.bfloat16)
        .reshape(row_shape),
        "seq",
        split_axis=0,
        concat_axis=0,
        tiled=True,
    )
    picked = returned.reshape(experts * capacity, width)[slot_index]
    weighted = jnp.sum(
        picked.reshape(tok_rows, TOP, width).astype(jnp.float32) * route_gates[:, :, None], axis=1
    )
    summed_moe = lax.psum(weighted.astype(jnp.bfloat16), "exp").astype(jnp.float32)
    return (mixed_rows + summed_moe).astype(jnp.bfloat16)


def solution(mesh):
    placed = (
        P(("groups", "seq"), "exp"),
        P(("groups", "seq"), "exp"),
        P(("groups", "seq"), "exp"),
        P(None, "groups", "exp"),
        P("exp"),
        P("exp", None),
        P(("groups", "seq"), None),
        P(),
        P("seq", None, None, "exp"),
        P("seq", "exp", None),
        P(("groups", "seq"), None),
        P(("groups", "seq"), None),
    )
    return jax.shard_map(
        on_device, mesh=mesh, in_specs=placed, out_specs=P(("groups", "seq"), None), check_vma=False
    )
```

profile of v0, /device:TPU:0, one launch (start us, length us, event | category | flops | bytes accessed | tf_op | source)
XLA Modules:
  0.0 364.5 jit_solution(16868646617035818337)
XLA Ops:
  6.5 0.0 copy-start
  6.5 0.0 all-reduce.3.cloned.1.call-start
  6.5 0.9 slice_bitcast_fusion
  7.5 5.0 %collective-permute-start = (bf16[2,128,128]{2,1,0:T(8,128)(2,1)S(1)}, bf16[2,128,128]{2,1,0:T(8,128)(2,1)S(1)}, u32[]{:S(2)}, u32[]{:S(2)}) collective-permute-start(bf16[2,128,128]{2,1,0:T(8,128)(2,1)S(1)} %pad_maximum_fusion), channel_id=1, source_target_pairs={{0,2},{2,4},{4,6},{6,8},{8,10},{10,12},{12,14},{1,3},{3,5},{5,7},{... | collective-permute-start | bytes 196616 | tf_op jit(solution)/shard_map/ppermute | solution.py:18
  12.5 0.1 fusion.14
  12.6 0.9 copy.23
  13.5 0.9 copy.21
  14.5 2.0 copy.24
  16.5 0.7 max.17
  17.3 0.0 collective-permute-done
  17.3 0.8 broadcast_select_fusion
  18.1 0.1 copy.22
  18.2 2.1 fusion.1
  20.4 0.0 copy-start.1
  20.4 0.1 broadcast_maximum_fusion
  20.4 2.6 copy-done.1
  23.0 1.3 fusion
  24.3 0.1 exponential_add_fusion
  24.4 0.1 copy.20
  24.5 4.6 %fusion.13 = bf16[2,64,8,256]{3,1,2,0:T(8,128)(2,1)S(1)} fusion(f32[2,384,256,8]{2,1,3,0:T(8,128)} %copy-done.1, f32[2,8,256]{2,1,0:T(8,128)S(1)} %exponential_add_fusion, f32[2,8,256]{2,1,0:T(8,128)S(1)} %broadcast_maximum_fusion, pred[256,384]{0,1:T(8,128)(4,1)S(1)} %fusion.14, bf16[256,2,64]{0,2,1:T(8,128)(2,1)S(1)} %bitcast.81, ...), kind=kOutput, calls=%fused_computation.26 | convolution fusion | flops 209649664 | bytes 7045120 | tf_op jit(solution)/shard_map/hgqk,khd->qhgd/dot_general | solution.py:44
  29.1 0.0 copy-start.2
  29.1 0.0 copy-done
  29.1 0.0 copy-start.3
  29.1 2.2 fusion.30
  31.3 0.0 all-reduce.3.cloned.1.call-update
  31.3 0.0 copy-done.2
  31.3 0.1 copy.27
  31.4 0.1 eq.33
  31.6 0.1 eq.29
  31.7 2.5 reduce-window.6
  34.1 0.3 slice_reduce_fusion
  34.4 0.2 reduce-window.9
  34.6 0.1 copy.26
  34.7 0.1 mul.75
  34.9 0.1 add_bitcast_fusion
  35.0 16.3 %all-reduce.3.cloned.1.call-done = f32[256,1536]{1,0:T(8,128)} async-done(((f32[256,1536]{1,0:T(8,128)}), f32[256,1536]{1,0:T(8,128)}) %all-reduce.3.cloned.1.call-update) | async-done | bytes 1572880 | tf_op jit(solution)/shard_map/psum | solution.py:72
  51.3 1.9 multiply_reduce_fusion.1
  53.2 0.0 copy-done.3
  53.2 2.7 multiply_convert_fusion
  56.0 18.8 %scatter_custom_fusion = bf16[1536,1536]{1,0:T(8,128)(2,1)} fusion(s32[1024]{0:T(1024)S(1)} %bitcast.84, bf16[256,1536]{1,0:T(8,128)(2,1)} %multiply_convert_fusion, s32[1024]{0:T(1024)S(1)} %broadcast_clamp_fusion.1, bf16[]{:T(256)} %constant.45.clone.1), kind=kCustom, calls=%fused_computation.16 | custom fusion | bytes 4719104 | tf_op jit(solution)/shard_map/scatter | solution.py:88
  74.8 110.6 %all_to_all.10 = bf16[8,192,1536]{2,1,0:T(8,128)(2,1)S(1)} all-to-all(bf16[8,192,1536]{2,1,0:T(8,128)(2,1)} %bitcast.74), channel_id=1, replica_groups=mesh['groups'=2,'seq'=8,'exp'=2] {'seq'}, dimensions={0} | all-to-all | bytes 9437184 | tf_op jit(solution)/shard_map/all_to_all | solution.py:91
  185.4 0.0 copy-start.5
  185.4 10.9 %convolution_bitcast_fusion = f32[2,1536,768]{2,1,0:T(8,128)S(1)} fusion(bf16[1536,1536,1]{1,0,2:T(8,128)(2,1)S(1)} %bitcast.76, bf16[1,2,1536,768]{3,2,1,0:T(8,128)(2,1)} %param.20), kind=kOutput, calls=%fused_computation.9 | convolution fusion | flops 7247757312 | bytes 18874368 | tf_op jit(solution)/shard_map/rd,kdf->krf/dot_general | solution.py:94
  196.3 0.0 copy-done.5
  196.4 5.6 %convolution_convert_fusion = bf16[1536,1536]{1,0:T(8,128)(2,1)} fusion(bf16[1,768,1536]{2,1,0:T(8,128)(2,1)S(1)} %copy-done.5, f32[2,1536,768]{2,1,0:T(8,128)S(1)} %convolution_bitcast_fusion), kind=kOutput, calls=%fused_computation.3 | convolution fusion | flops 3635675136 | bytes 16515072 | tf_op jit(solution)/shard_map/dot_general | solution.py:101
  202.0 0.0 copy-start.4
  202.0 4.7 %all-to-all-start.1 = ((bf16[8,192,1536]{2,1,0:T(8,128)(2,1)}), bf16[8,192,1536]{2,1,0:T(8,128)(2,1)}, u32[]{:S(2)}, u32[]{:S(2)}) async-start(bf16[8,192,1536]{2,1,0:T(8,128)(2,1)} %bitcast.75), calls=%async_computation.1 | async-start | bytes 9437184 | tf_op jit(solution)/shard_map/all_to_all | solution.py:100
  206.7 0.0 all-reduce.5.cloned.1.call-start
  206.8 0.0 copy-done.4
  206.8 0.1 copy.29
  206.9 103.8 %all-to-all-done.1 = bf16[8,192,1536]{2,1,0:T(8,128)(2,1)} async-done(((bf16[8,192,1536]{2,1,0:T(8,128)(2,1)}), bf16[8,192,1536]{2,1,0:T(8,128)(2,1)}, u32[]{:S(2)}, u32[]{:S(2)}) %all-to-all-start.1) | async-done | bytes 4718624 | tf_op jit(solution)/shard_map/all_to_all | solution.py:100
  310.7 10.5 %gather_fusion = bf16[1024,1536]{1,0:T(8,128)(2,1)} fusion(bf16[1536,1536]{1,0:T(8,128)(2,1)} %bitcast.26, s32[1024]{0:T(1024)S(1)} %broadcast_clamp_fusion), kind=kCustom, calls=%fused_computation.1 | custom fusion | bytes 6295552 | tf_op jit(solution)/shard_map/gather | solution.py:109
  321.3 6.7 %reshape.154 = f32[256,4,1536]{2,1,0:T(4,128)} reshape(bf16[1024,1536]{1,0:T(8,128)(2,1)} %gather_fusion) | data formatting | bytes 9437184 | tf_op jit(solution)/shard_map/convert_element_type | solution.py:111
  328.0 8.3 %multiply_reduce_fusion = bf16[256,1536]{1,0:T(8,128)(2,1)} fusion(f32[256,4,1536]{2,1,0:T(4,128)} %reshape.154, f32[256,4]{1,0:T(8,128)S(1)} %copy.29), kind=kLoop, calls=%fused_computation.5 | loop fusion | flops 2752512 | bytes 7081984 | tf_op jit(solution)/shard_map/reduce_sum | solution.py:110
  336.3 0.0 all-reduce.5.cloned.1.call-update
  336.3 18.4 %all-reduce.5.cloned.1.call-done = bf16[256,1536]{1,0:T(8,128)(2,1)} async-done(((bf16[256,1536]{1,0:T(8,128)(2,1)}), bf16[256,1536]{1,0:T(8,128)(2,1)}) %all-reduce.5.cloned.1.call-update) | async-done | bytes 786448 | tf_op jit(solution)/shard_map/psum | solution.py:113
  354.7 3.0 add_convert_fusion
  (11 shorter events, 0.1 us)
Async XLA Ops:
  6.5 22.6 %copy-start = (bf16[1024,1536]{1,0:T(8,128)(2,1)S(1)}, bf16[1024,1536]{1,0:T(8,128)(2,1)}, u32[]{:S(2)}) copy-start(bf16[1024,1536]{1,0:T(8,128)(2,1)} %param.17) | copy-start | bytes 9437188
  6.5 44.8 %all-reduce.3.cloned.1.call-start = ((), (), s32[]{:S(2)}) async-start(), calls=%async_computation.2 | async-start | bytes 3145728 | tf_op jit(solution)/shard_map/psum | solution.py:72
  7.5 9.8 %collective-permute-start = (bf16[2,128,128]{2,1,0:T(8,128)(2,1)S(1)}, bf16[2,128,128]{2,1,0:T(8,128)(2,1)S(1)}, u32[]{:S(2)}, u32[]{:S(2)}) collective-permute-start(bf16[2,128,128]{2,1,0:T(8,128)(2,1)S(1)} %pad_maximum_fusion), channel_id=1, source_target_pairs={{0,2},{2,4},{4,6},{6,8},{8,10},{10,12},{12,14},{1,3},{3,5},{5,7},{... | collective-permute-start | bytes 196616 | tf_op jit(solution)/shard_map/ppermute | solution.py:18
  20.4 2.7 copy-start.1
  29.1 2.2 copy-start.2
  29.1 24.1 %copy-start.3 = (f32[1536]{0:T(1024)S(1)}, f32[1536]{0:T(1024)}, u32[]{:S(2)}) copy-start(f32[1536]{0:T(1024)} %param.19) | copy-start | bytes 18436
  185.4 11.0 %copy-start.5 = (bf16[1,768,1536]{2,1,0:T(8,128)(2,1)S(1)}, bf16[1,768,1536]{2,1,0:T(8,128)(2,1)}, u32[]{:S(2)}) copy-start(bf16[1,768,1536]{2,1,0:T(8,128)(2,1)} %param.21) | copy-start | bytes 7077892
  202.0 4.8 %copy-start.4 = (f32[256,4]{0,1:T(4,128)S(1)}, f32[256,4]{0,1:T(4,128)}, u32[]{:S(2)}) copy-start(f32[256,4]{0,1:T(4,128)} %param.23) | copy-start | bytes 12292
  202.0 108.7 %all-to-all-start.1 = ((bf16[8,192,1536]{2,1,0:T(8,128)(2,1)}), bf16[8,192,1536]{2,1,0:T(8,128)(2,1)}, u32[]{:S(2)}, u32[]{:S(2)}) async-start(bf16[8,192,1536]{2,1,0:T(8,128)(2,1)} %bitcast.75), calls=%async_computation.1 | async-start | bytes 9437184 | tf_op jit(solution)/shard_map/all_to_all | solution.py:100
  206.7 148.0 %all-reduce.5.cloned.1.call-start = ((), (), s32[]{:S(2)}) async-start(), calls=%async_computation.3 | async-start | bytes 1572864 | tf_op jit(solution)/shard_map/psum | solution.py:113
Sparse Core Ops, SparseCore 0:
  31.4 19.8 all-reduce.2
  336.4 18.2 all-reduce.4
where the time goes:
time: 366 us; the launch traced here: 365 us
  waiting for transfers between devices  139 us (38%)
  blocking collectives  111 us (30%)
  local copies, waits for them, and re-layouts  45.5 us (12%)
  matrix products  25.4 us (7%)
  other arithmetic  21.1 us (6%)
  between operations  13.6 us (4%)
  starting transfers between devices  9.77 us (3%)
    all_to_all x1, blocking collectives, on_device(): lax.all_to_all(outgoing, 'seq', split_axis=0, concat_axis=0, tiled=True)  111 us
    all_to_all x1, waiting for transfers between devices, on_device(): lax.all_to_all(jnp.dot(activation, expert_out[0], preferred_element_type=...  104 us
    scatter x1, local copies, waits for them, and re-layouts, on_device(): outgoing = jnp.zeros((experts * capacity, width), jnp.bfloat16).at[slot_i...  18.8 us
    psum x1, waiting for transfers between devices, on_device(): lax.psum(weighted.astype(jnp.bfloat16), 'exp').astype(jnp.float32)  18.4 us
    psum x1, waiting for transfers between devices, on_device(): mixed_rows = residual.astype(jnp.float32) + lax.psum(partial_rows, 'exp')  16.3 us
    dot_general x1, matrix products, on_device(): jnp.einsum('rd,kdf->krf', flat_rows, expert_in[0], preferred_element_type...  10.9 us
    gather x1, local copies, waits for them, and re-layouts, on_device(): picked = returned.reshape(experts * capacity, width)[slot_index]  10.5 us
    reduce_sum x1, other arithmetic, on_device(): jnp.sum(picked.reshape(tok_rows, TOP, width).astype(jnp.float32) * route_...  8.31 us
  transfers between devices with their start and end apart: 4, of which 3 were waited for; matrix products, arithmetic and copies ran while one was open for 2% of the time, Pallas kernels for 0%

commit v1 on v0

--- a/solution.py
+++ b/solution.py
@@ -16,6 +16,11 @@
     size = lax.axis_size(axis)
     pairs = [(i, i + by) for i in range(size) if 0 <= i + by < size]
     return lax.ppermute(shard, axis, pairs)
+
+
+def swap_exp(x):
+    size = lax.axis_size("exp")
+    return lax.ppermute(x, "exp", [(i, (i + 1) % size) for i in range(size)])
 
 
 def rms_normalize(mixed_rows, norm_gain):
@@ -69,49 +74,53 @@
     block_rows = min(tok_rows, 512)
     pieces = attend_block(queries, keys_all, values_all, sink_logits, block_rows, window_rows)
     partial_rows = jnp.dot(pieces, out_weight, preferred_element_type=jnp.float32)
-    mixed_rows = residual.astype(jnp.float32) + lax.psum(partial_rows, "exp")
+    mixed_rows = residual.astype(jnp.float32) + (partial_rows + swap_exp(partial_rows))
     normed = rms_normalize(mixed_rows, norm_gain)
+
     experts = lax.axis_size("seq")
     width = normed.shape[1]
     capacity = 3 * tok_rows * TOP // (2 * experts)
-    assigned = tok_rows * TOP
+    half = -(-capacity // 2)
+    slots = experts * half
+    core = lax.axis_index("exp")
     flat_experts = routes.reshape(-1)
     expert_hits = (flat_experts[:, None] == jnp.arange(experts, dtype=jnp.int32)[None, :]).astype(
         jnp.int32
     )
     slot_rank = jnp.sum(expert_hits * (jnp.cumsum(expert_hits, axis=0) - 1), axis=1)
-    slot_index = flat_experts * capacity + slot_rank
-    source = jnp.arange(assigned, dtype=jnp.int32) // TOP
+    local_rank = slot_rank - core * half
+    mine = (local_rank >= 0) & (local_rank < half)
+    slot_id = jnp.where(mine, flat_experts * half + local_rank, -1)
+    slot_iota = jnp.arange(slots, dtype=jnp.int32)
+    pick = (slot_id[:, None] == slot_iota[None, :]).astype(jnp.bfloat16)
+    select = jnp.max(pick.reshape(tok_rows, TOP, slots), axis=1).T
     outgoing = (
-        jnp.zeros((experts * capacity, width), jnp.bfloat16)
-        .at[slot_index]
-        .set(normed[source])
-        .reshape(experts, capacity, width)
+        jnp.dot(select, normed, preferred_element_type=jnp.float32)
+        .astype(jnp.bfloat16)
+        .reshape(experts, half, width)
     )
     slot_rows = lax.all_to_all(outgoing, "seq", split_axis=0, concat_axis=0, tiled=True)
-    row_shape = slot_rows.shape
-    flat_rows = slot_rows.reshape(-1, row_shape[-1])
+    both_rows = jnp.concatenate([slot_rows, swap_exp(slot_rows)], axis=1)
+    flat_rows = both_rows.reshape(-1, width)
     gate_up = jnp.einsum("rd,kdf->krf", flat_rows, expert_in[0], preferred_element_type=jnp.float32)
     gate_val = gate_up[0]
     up_val = gate_up[1]
     activation = ((up_val + 1.0) * gate_val * jax.nn.sigmoid(GLU_ALPHA * gate_val)).astype(
         jnp.bfloat16
     )
-    returned = lax.all_to_all(
+    out_part = (
         jnp.dot(activation, expert_out[0], preferred_element_type=jnp.float32)
         .astype(jnp.bfloat16)
-        .reshape(row_shape),
-        "seq",
-        split_axis=0,
-        concat_axis=0,
-        tiled=True,
+        .reshape(experts, 2 * half, width)
     )
-    picked = returned.reshape(experts * capacity, width)[slot_index]
-    weighted = jnp.sum(
-        picked.reshape(tok_rows, TOP, width).astype(jnp.float32) * route_gates[:, :, None], axis=1
-    )
-    summed_moe = lax.psum(weighted.astype(jnp.bfloat16), "exp").astype(jnp.float32)
-    return (mixed_rows + summed_moe).astype(jnp.bfloat16)
+    own_part = out_part[:, :half]
+    their_part = swap_exp(out_part[:, half:])
+    result = (own_part.astype(jnp.float32) + their_part.astype(jnp.float32)).astype(jnp.bfloat16)
+    returned = lax.all_to_all(result, "seq", split_axis=0, concat_axis=0, tiled=True)
+    picked = jnp.dot(pick, returned.reshape(slots, width), preferred_element_type=jnp.float32)
+    weighted = jnp.sum(picked.reshape(tok_rows, TOP, width) * route_gates[:, :, None], axis=1)
+    moe = weighted + swap_exp(weighted)
+    return (mixed_rows + moe).astype(jnp.bfloat16)
 
 
 def solution(mesh):

time: 366 us -> 180 us (0.49)
  waiting for transfers between devices: 139 us -> 12.3 us
  local copies, waits for them, and re-layouts: 45.5 us -> 7.09 us
  between operations: 13.6 us -> 0.29 us
  other arithmetic: 21.1 us -> 10.1 us
  blocking collectives: 111 us -> 116 us
  starting transfers between devices: 9.77 us -> 5.3 us
    all_to_all x1 -> x0, waiting for transfers between devices: 104 us -> none  [on_device(): lax.all_to_all(jnp.dot(activation, expert_out[0], preferred_element_type=...]
    all_to_all x0 -> x1, blocking collectives: none -> 57.6 us  [on_device(): lax.all_to_all(result, 'seq', split_axis=0, concat_axis=0, tiled=True)]
    all_to_all x1, blocking collectives: 111 us -> 58.6 us  [on_device(): lax.all_to_all(outgoing, 'seq', split_axis=0, concat_axis=0, tiled=True)]
    psum x2 -> x0, waiting for transfers between devices: 34.7 us -> none  [the longest x1 18.4 us: on_device(): lax.psum(weighted.astype(jnp.bfloat16), 'exp').astype(jnp.float32)]
    scatter x1 -> x0, local copies, waits for them, and re-layouts: 18.8 us -> none  [on_device(): outgoing = jnp.zeros((experts * capacity, width), jnp.bfloat16).at[slot_i...]
    ppermute x0 -> x4, waiting for transfers between devices: none -> 12.3 us  [swap_exp(): return lax.ppermute(x, 'exp', [(i, (i + 1) % size) for i in range(size)])]
    gather x1 -> x0, local copies, waits for them, and re-layouts: 10.5 us -> none  [on_device(): picked = returned.reshape(experts * capacity, width)[slot_index]]
    reduce_sum x1 -> x0, other arithmetic: 8.31 us -> none  [on_device(): jnp.sum(picked.reshape(tok_rows, TOP, width).astype(jnp.float32) * route_...]
  transfers between devices with their start and end apart: 4 -> 5, of which waited for: 3 -> 3; matrix products, arithmetic and copies ran while one was open for 2% -> 5% of each run, Pallas kernels for 0% -> 0%
where the time goes in v1:
time: 180 us; the launch traced here: 179 us
  blocking collectives  116 us (64%)
  matrix products  28.2 us (16%)
  waiting for transfers between devices  12.3 us (7%)
  other arithmetic  10.1 us (6%)
  local copies, waits for them, and re-layouts  7.09 us (4%)
  starting transfers between devices  5.3 us (3%)
    all_to_all x1, blocking collectives, on_device(): lax.all_to_all(outgoing, 'seq', split_axis=0, concat_axis=0, tiled=True)  58.6 us
    all_to_all x1, blocking collectives, on_device(): lax.all_to_all(result, 'seq', split_axis=0, concat_axis=0, tiled=True)  57.6 us
    ppermute x4, waiting for transfers between devices, swap_exp(): return lax.ppermute(x, 'exp', [(i, (i + 1) % size) for i in range(size)])  12.3 us
    dot_general x1, matrix products, on_device(): jnp.einsum('rd,kdf->krf', flat_rows, expert_in[0], preferred_element_type...  10.3 us
    dot_general x1, matrix products, on_device(): jnp.dot(activation, expert_out[0], preferred_element_type=jnp.float32)  7.89 us
    ppermute x1, starting transfers between devices, shifted(): return lax.ppermute(shard, axis, pairs)  5.01 us
    unnamed x18, local copies, waits for them, and re-layouts  4.09 us
  transfers between devices with their start and end apart: 5, of which 3 were waited for; matrix products, arithmetic and copies ran while one was open for 5% of the time, Pallas kernels for 0%

profile of v1, /device:TPU:0, one launch (start us, length us, event | category | flops | bytes accessed | tf_op | source)
XLA Modules:
  0.0 179.4 jit_solution(9553181542188381729)
XLA Ops:
  0.0 0.0 copy-start
  0.0 0.9 slice_bitcast_fusion
  0.9 5.0 %collective-permute-start = (bf16[2,128,128]{2,1,0:T(8,128)(2,1)S(1)}, bf16[2,128,128]{2,1,0:T(8,128)(2,1)S(1)}, u32[]{:S(2)}, u32[]{:S(2)}) collective-permute-start(bf16[2,128,128]{2,1,0:T(8,128)(2,1)S(1)} %pad_maximum_fusion.1), channel_id=1, source_target_pairs={{0,2},{2,4},{4,6},{6,8},{8,10},{10,12},{12,14},{1,3},{3,5},{5,7},{... | collective-permute-start | bytes 196616 | tf_op jit(solution)/shard_map/ppermute | solution.py:18
  6.0 0.1 fusion.18
  6.0 0.9 copy.34
  7.0 0.9 copy.32
  7.9 0.7 max.17
  8.7 2.0 %copy.35 = bf16[256,1024]{0,1:T(8,128)(2,1)} copy(bf16[256,1024]{1,0:T(8,128)(2,1)} %param.12) | data formatting | bytes 1048576 | tf_op args[0]
  10.7 0.0 collective-permute-done
  10.7 0.9 broadcast_select_fusion
  11.6 0.1 copy.31
  11.7 0.1 copy.33
  11.8 2.1 %fusion.1 = (f32[2,8,256]{2,1,0:T(8,128)S(1)}, f32[2,384,256,8]{2,1,3,0:T(8,128)S(1)}) fusion(pred[256,384]{0,1:T(8,128)(4,1)S(1)} %fusion.18, bf16[256,2,8,64]{0,3,2,1:T(8,128)(2,1)} %bitcast.83, bf16[256,2,64]{0,2,1:T(8,128)(2,1)S(1)} %bitcast.85, bf16[128,2,64]{0,2,1:T(8,128)(2,1)S(1)} %bitcast.86), kind=kOutput, calls=%fused_computation.7 | convolution fusion | flops 206237696 | bytes 7028736 | tf_op jit(solution)/shard_map/qhgd,khd->hgqk/dot_general | solution.py:37
  14.0 0.1 broadcast_maximum_fusion
  14.0 1.3 fusion
  15.3 0.1 exponential_add_fusion
  15.4 1.8 %fusion.15 = bf16[2,64,8,256]{3,1,2,0:T(8,128)(2,1)S(1)} fusion(f32[2,384,256,8]{2,1,3,0:T(8,128)S(1)} %get-tuple-element.10, f32[2,8,256]{2,1,0:T(8,128)S(1)} %exponential_add_fusion, f32[2,8,256]{2,1,0:T(8,128)S(1)} %broadcast_maximum_fusion, pred[256,384]{0,1:T(8,128)(4,1)S(1)} %fusion.18, bf16[256,2,64]{0,2,1:T(8,128)(2,1)S(1)} %bitcast.87, ...), kind=kOutput, calls=%fused_computation.29 | convolution fusion | flops 209649664 | bytes 7045120 | tf_op jit(solution)/shard_map/hgqk,khd->qhgd/dot_general | solution.py:49
  17.2 0.0 copy-start.1
  17.2 0.0 copy-done
  17.2 2.2 %fusion.34 = f32[256,1536]{1,0:T(8,128)} fusion(bf16[256,1024]{0,1:T(8,128)(2,1)S(1)} %bitcast.84, bf16[1024,1536]{1,0:T(8,128)(2,1)S(1)} %copy-done), kind=kOutput, calls=%fused_computation.68 | convolution fusion | flops 805306368 | bytes 5242880 | tf_op jit(solution)/shard_map/dot_general | solution.py:76
  19.4 0.0 copy-start.2
  19.4 0.0 collective-permute-start.1
  19.4 0.0 copy-done.1
  19.4 0.1 copy.37
  19.5 0.1 eq.69
  19.7 0.1 eq.65
  19.8 0.1 copy.40
  19.9 2.3 %reduce-window.6 = s32[8,8,128]{2,1,0:T(8,128)S(1)} reduce-window(s32[8,8,128]{2,1,0:T(8,128)S(1)} %fusion.26, s32[]{:T(128)} %constant.16.clone.1), window={size=1x1x128 pad=0_0x0_0x127_0}, to_apply=%region_2.3 | reduce-window | flops 1040384 | bytes 65540 | tf_op jit(solution)/shard_map/reduce-window
  22.2 0.3 slice_reduce_fusion
  22.5 0.2 reduce-window.9
  22.7 0.1 add_bitcast_fusion
  22.8 0.1 sub.47
  23.0 0.1 copy.41
  23.0 0.4 fusion.13
  23.5 0.0 collective-permute-done.1
  23.5 2.4 %multiply_reduce_fusion.1 = (f32[256]{0:T(256)S(1)}, f32[256,1536]{1,0:T(8,128)S(1)}) fusion(f32[256,1536]{1,0:T(8,128)} %fusion.34, f32[256,1536]{1,0:T(8,128)} %collective-permute-done.1, bf16[256,1536]{1,0:T(8,128)(2,1)} %param.18), kind=kLoop, calls=%fused_computation.26 | loop fusion | flops 1965824 | bytes 5506048 | tf_op jit(solution)/shard_map/reduce_sum | solution.py:27
  25.9 0.0 copy-done.2
  25.9 0.9 convolution_convert_fusion.1
  26.8 0.0 slice-start
  26.9 58.6 %all_to_all.10 = bf16[8,96,1536]{2,1,0:T(8,128)(2,1)S(1)} all-to-all(bf16[8,96,1536]{2,1,0:T(8,128)(2,1)S(1)} %bitcast.78), channel_id=1, replica_groups=mesh['groups'=2,'seq'=8,'exp'=2] {'seq'}, dimensions={0} | all-to-all | bytes 4718592 | tf_op jit(solution)/shard_map/all_to_all | solution.py:102
  85.4 0.0 slice-start.1
  85.4 0.0 collective-permute-start.2
  85.4 4.5 %collective-permute-done.2 = bf16[8,96,1536]{2,1,0:T(8,128)(2,1)S(1)} collective-permute-done((bf16[8,96,1536]{2,1,0:T(8,128)(2,1)S(1)}, bf16[8,96,1536]{2,1,0:T(8,128)(2,1)S(1)}, u32[]{:S(2)}, u32[]{:S(2)}) %collective-permute-start.2) | collective-permute-done | bytes 2359328 | tf_op jit(solution)/shard_map/ppermute | solution.py:23
  90.0 0.3 pad_maximum_fusion
  90.3 0.0 slice-done
  90.3 0.0 slice-done.1
  90.3 0.0 copy-start.3
  90.3 10.3 %convolution_bitcast_fusion = f32[2,1536,768]{2,1,0:T(8,128)} fusion(bf16[1536,1536,1]{1,0,2:T(8,128)(2,1)S(1)} %bitcast.81, bf16[1,2,1536,768]{3,2,1,0:T(8,128)(2,1)S(1)} %bitcast.91), kind=kOutput, calls=%fused_computation.6 | convolution fusion | flops 7247757312 | bytes 18874368 | tf_op jit(solution)/shard_map/rd,kdf->krf/dot_general | solution.py:105
  100.6 0.0 copy-done.3
  100.6 7.9 %convolution_convert_fusion = bf16[1536,1536]{1,0:T(8,128)(2,1)S(1)} fusion(bf16[1,768,1536]{2,1,0:T(8,128)(2,1)S(1)} %copy-done.3, f32[2,1536,768]{2,1,0:T(8,128)} %convolution_bitcast_fusion), kind=kOutput, calls=%fused_computation | convolution fusion | flops 3635675136 | bytes 16515072 | tf_op jit(solution)/shard_map/dot_general | solution.py:112
  108.5 0.2 slice.46
  108.8 0.0 copy-start.4
  108.8 0.2 collective-permute-start.3
  109.0 4.4 %collective-permute-done.3 = bf16[8,96,1536]{2,1,0:T(8,128)(2,1)S(1)} collective-permute-done((bf16[8,96,1536]{2,1,0:T(8,128)(2,1)S(1)}, bf16[8,96,1536]{2,1,0:T(8,128)(2,1)S(1)}, u32[]{:S(2)}, u32[]{:S(2)}) %collective-permute-start.3) | collective-permute-done | bytes 2359328 | tf_op jit(solution)/shard_map/ppermute | solution.py:23
  113.4 0.7 add_convert_fusion
  114.1 57.6 %all_to_all.11 = bf16[8,96,1536]{2,1,0:T(8,128)(2,1)S(1)} all-to-all(bf16[8,96,1536]{2,1,0:T(8,128)(2,1)S(1)} %add_convert_fusion), channel_id=1, replica_groups=mesh['groups'=2,'seq'=8,'exp'=2] {'seq'}, dimensions={0} | all-to-all | bytes 4718592 | tf_op jit(solution)/shard_map/all_to_all | solution.py:119
  171.6 0.0 copy-done.4
  171.6 3.0 %multiply_reduce_fusion = f32[256,1536]{1,0:T(8,128)S(1)} fusion(bf16[768,1536,1]{1,0,2:T(8,128)(2,1)S(1)} %bitcast.82, f32[256,4]{0,1:T(4,128)S(1)} %copy-done.4, s32[256,4]{0,1:T(4,128)S(1)} %copy.41), kind=kOutput, calls=%fused_computation.2 | convolution fusion | flops 2419458048 | bytes 3940352 | tf_op jit(solution)/shard_map/dot_general | solution.py:120
  174.7 0.1 collective-permute-start.4
  174.8 3.4 %collective-permute-done.4 = f32[256,1536]{1,0:T(8,128)S(1)} collective-permute-done((f32[256,1536]{1,0:T(8,128)S(1)}, f32[256,1536]{1,0:T(8,128)S(1)}, u32[]{:S(2)}, u32[]{:S(2)}) %collective-permute-start.4) | collective-permute-done | bytes 1572896 | tf_op jit(solution)/shard_map/ppermute | solution.py:23
  178.2 1.3 add_convert_fusion.1
  (10 shorter events, 0.1 us)
Async XLA Ops:
  0.0 17.2 %copy-start = (bf16[1024,1536]{1,0:T(8,128)(2,1)S(1)}, bf16[1024,1536]{1,0:T(8,128)(2,1)}, u32[]{:S(2)}) copy-start(bf16[1024,1536]{1,0:T(8,128)(2,1)} %param.17) | copy-start | bytes 9437188
  0.9 9.8 %collective-permute-start = (bf16[2,128,128]{2,1,0:T(8,128)(2,1)S(1)}, bf16[2,128,128]{2,1,0:T(8,128)(2,1)S(1)}, u32[]{:S(2)}, u32[]{:S(2)}) collective-permute-start(bf16[2,128,128]{2,1,0:T(8,128)(2,1)S(1)} %pad_maximum_fusion.1), channel_id=1, source_target_pairs={{0,2},{2,4},{4,6},{6,8},{8,10},{10,12},{12,14},{1,3},{3,5},{5,7},{... | collective-permute-start | bytes 196616 | tf_op jit(solution)/shard_map/ppermute | solution.py:18
  17.2 2.2 %copy-start.1 = (s32[256,4]{0,1:T(4,128)S(1)}, s32[256,4]{0,1:T(4,128)}, u32[]{:S(2)}) copy-start(s32[256,4]{0,1:T(4,128)} %param.22) | copy-start | bytes 12292
  19.4 6.5 %copy-start.2 = (f32[1536]{0:T(1024)S(1)}, f32[1536]{0:T(1024)}, u32[]{:S(2)}) copy-start(f32[1536]{0:T(1024)} %param.19) | copy-start | bytes 18436
  19.4 4.1 %collective-permute-start.1 = (f32[256,1536]{1,0:T(8,128)}, f32[256,1536]{1,0:T(8,128)}, u32[]{:S(2)}, u32[]{:S(2)}) collective-permute-start(f32[256,1536]{1,0:T(8,128)} %fusion.34), channel_id=1, source_target_pairs={{0,1},{1,0},{2,3},{3,2},{4,5},{5,4},{6,7},{7,6},{8,9},{9,8},{10,11... | collective-permute-start | bytes 4718600 | tf_op jit(solution)/shard_map/ppermute | solution.py:23
  26.8 63.5 %slice-start = ((s8[4718592]{0:T(1024)(128)(4,1)}), s8[4194304]{0:T(1024)(128)(4,1)S(1)}, s32[]{:S(2)}) async-start(s8[4718592]{0:T(1024)(128)(4,1)} %bitcast.90), calls=%async_computation.2 | async-start | bytes 8388608
  85.4 4.9 %slice-start.1 = ((s8[4718592]{0:T(1024)(128)(4,1)}), s8[524288]{0:T(1024)(128)(4,1)S(1)}, s32[]{:S(2)}) async-start(s8[4718592]{0:T(1024)(128)(4,1)} %bitcast.90), calls=%async_computation.3 | async-start | bytes 1048576
  85.4 4.5 %collective-permute-start.2 = (bf16[8,96,1536]{2,1,0:T(8,128)(2,1)S(1)}, bf16[8,96,1536]{2,1,0:T(8,128)(2,1)S(1)}, u32[]{:S(2)}, u32[]{:S(2)}) collective-permute-start(bf16[8,96,1536]{2,1,0:T(8,128)(2,1)S(1)} %all_to_all.10), channel_id=1, source_target_pairs={{0,1},{1,0},{2,3},{3,2},{4,5},{5,4},{6,7},{7,6},{8,9},{9,8},{10,11... | collective-permute-start | bytes 7077896 | tf_op jit(solution)/shard_map/ppermute | solution.py:23
  90.3 10.3 %copy-start.3 = (bf16[1,768,1536]{2,1,0:T(8,128)(2,1)S(1)}, bf16[1,768,1536]{2,1,0:T(8,128)(2,1)}, u32[]{:S(2)}) copy-start(bf16[1,768,1536]{2,1,0:T(8,128)(2,1)} %param.21) | copy-start | bytes 7077892
  108.8 62.9 %copy-start.4 = (f32[256,4]{0,1:T(4,128)S(1)}, f32[256,4]{0,1:T(4,128)}, u32[]{:S(2)}) copy-start(f32[256,4]{0,1:T(4,128)} %param.23) | copy-start | bytes 12292
  108.8 4.6 %collective-permute-start.3 = (bf16[8,96,1536]{2,1,0:T(8,128)(2,1)S(1)}, bf16[8,96,1536]{2,1,0:T(8,128)(2,1)S(1)}, u32[]{:S(2)}, u32[]{:S(2)}) collective-permute-start(bf16[8,96,1536]{2,1,0:T(8,128)(2,1)S(1)} %slice.46), channel_id=1, source_target_pairs={{0,1},{1,0},{2,3},{3,2},{4,5},{5,4},{6,7},{7,6},{8,9},{9,8},{10,11... | collective-permute-start | bytes 7077896 | tf_op jit(solution)/shard_map/ppermute | solution.py:23
  174.7 3.5 %collective-permute-start.4 = (f32[256,1536]{1,0:T(8,128)S(1)}, f32[256,1536]{1,0:T(8,128)S(1)}, u32[]{:S(2)}, u32[]{:S(2)}) collective-permute-start(f32[256,1536]{1,0:T(8,128)S(1)} %multiply_reduce_fusion), channel_id=1, source_target_pairs={{0,1},{1,0},{2,3},{3,2},{4,5},{5,4},{6,7},{7,6},{8,9},{9,8},{10,11... | collective-permute-start | bytes 4718600 | tf_op jit(solution)/shard_map/ppermute | solution.py:23

commit v2 on v1

--- a/solution.py
+++ b/solution.py
@@ -50,6 +50,25 @@
     return heads_out.astype(jnp.bfloat16).reshape(block_rows, queries.shape[1])
 
 
+def gathered_slots(normed, routes, core, half, experts):
+    tok_rows, width = normed.shape
+    cores = lax.axis_size("exp")
+    share = tok_rows // cores
+    own_rows = lax.dynamic_slice_in_dim(normed, core * share, share, 0)
+    tokens = lax.all_gather(own_rows, ("seq", "exp"), axis=0, tiled=True).reshape(
+        experts, tok_rows, width
+    )
+    all_routes = lax.all_gather(routes, "seq", axis=0, tiled=False)
+    expert = lax.axis_index("seq")
+    has = jnp.any(all_routes == expert, axis=-1)
+    rank = jnp.cumsum(has.astype(jnp.int32), axis=1) - 1
+    rank_order = (jnp.arange(2 * half, dtype=jnp.int32) + core * half) % (2 * half)
+    select = (has[:, None, :] & (rank[:, None, :] == rank_order[None, :, None])).astype(jnp.bfloat16)
+    return jnp.einsum(
+        "bst,btd->bsd", select, tokens, preferred_element_type=jnp.float32
+    ).astype(jnp.bfloat16)
+
+
 def on_device(
     queries,
     key_rows,
@@ -93,14 +112,17 @@
     slot_id = jnp.where(mine, flat_experts * half + local_rank, -1)
     slot_iota = jnp.arange(slots, dtype=jnp.int32)
     pick = (slot_id[:, None] == slot_iota[None, :]).astype(jnp.bfloat16)
-    select = jnp.max(pick.reshape(tok_rows, TOP, slots), axis=1).T
-    outgoing = (
-        jnp.dot(select, normed, preferred_element_type=jnp.float32)
-        .astype(jnp.bfloat16)
-        .reshape(experts, half, width)
-    )
-    slot_rows = lax.all_to_all(outgoing, "seq", split_axis=0, concat_axis=0, tiled=True)
-    both_rows = jnp.concatenate([slot_rows, swap_exp(slot_rows)], axis=1)
+    if tok_rows <= 2 * capacity:
+        both_rows = gathered_slots(normed, routes, core, half, experts)
+    else:
+        select = jnp.max(pick.reshape(tok_rows, TOP, slots), axis=1).T
+        outgoing = (
+            jnp.dot(select, normed, preferred_element_type=jnp.float32)
+            .astype(jnp.bfloat16)
+            .reshape(experts, half, width)
+        )
+        slot_rows = lax.all_to_all(outgoing, "seq", split_axis=0, concat_axis=0, tiled=True)
+        both_rows = jnp.concatenate([slot_rows, swap_exp(slot_rows)], axis=1)
     flat_rows = both_rows.reshape(-1, width)
     gate_up = jnp.einsum("rd,kdf->krf", flat_rows, expert_in[0], preferred_element_type=jnp.float32)
     gate_val = gate_up[0]

time: 180 us -> 203 us (1.13)
  blocking collectives: 116 us -> 30.7 us
  waiting for transfers between devices: 12.3 us -> 92.2 us
  between operations: 0.29 us -> 13.7 us
  starting transfers between devices: 5.3 us -> 9.91 us
  matrix products: 28.2 us -> 32.8 us
  local copies, waits for them, and re-layouts: 7.09 us -> 10.9 us
  other arithmetic: 10.1 us -> 12.2 us
    all_to_all x2 -> x0, blocking collectives: 116 us -> none  [the longest x1 58.6 us: on_device(): lax.all_to_all(outgoing, 'seq', split_axis=0, concat_axis=0, tiled=True)]
    all_to_all x0 -> x1, waiting for transfers between devices: none -> 50.9 us  [on_device(): lax.all_to_all(result, 'seq', split_axis=0, concat_axis=0, tiled=True)]
    all_gather x0 -> x1, blocking collectives: none -> 30.7 us  [gathered_slots(): all_routes = lax.all_gather(routes, 'seq', axis=0, tiled=False)]
    all_gather x0 -> x1, waiting for transfers between devices: none -> 29.8 us  [gathered_slots(): lax.all_gather(own_rows, ('seq', 'exp'), axis=0, tiled=True)]
    all_to_all x0 -> x1, starting transfers between devices: none -> 4.5 us  [on_device(): lax.all_to_all(result, 'seq', split_axis=0, concat_axis=0, tiled=True)]
    dot_general x1, matrix products: 7.89 us -> 4.16 us  [on_device(): jnp.dot(activation, expert_out[0], preferred_element_type=jnp.float32)]
    unnamed x18 -> x20, local copies, waits for them, and re-layouts: 4.09 us -> 7.71 us
    dot_general x1, matrix products: 0.9 us -> 4.22 us  [gathered_slots(): jnp.einsum('bst,btd->bsd', select, tokens, preferred_element_type=jnp.flo...]
  transfers between devices with their start and end apart: 5 -> 6, of which waited for: 3 -> 5; matrix products, arithmetic and copies ran while one was open for 5% -> 5% of each run, Pallas kernels for 0% -> 0%
where the time goes in v2:
time: 203 us; the launch traced here: 202 us
  waiting for transfers between devices  92.2 us (45%)
  matrix products  32.8 us (16%)
  blocking collectives  30.7 us (15%)
  between operations  13.7 us (7%)
  other arithmetic  12.2 us (6%)
  local copies, waits for them, and re-layouts  10.9 us (5%)
  starting transfers between devices  9.91 us (5%)
    all_to_all x1, waiting for transfers between devices, on_device(): lax.all_to_all(result, 'seq', split_axis=0, concat_axis=0, tiled=True)  50.9 us
    all_gather x1, blocking collectives, gathered_slots(): all_routes = lax.all_gather(routes, 'seq', axis=0, tiled=False)  30.7 us
    all_gather x1, waiting for transfers between devices, gathered_slots(): lax.all_gather(own_rows, ('seq', 'exp'), axis=0, tiled=True)  29.8 us
    ppermute x3, waiting for transfers between devices, swap_exp(): return lax.ppermute(x, 'exp', [(i, (i + 1) % size) for i in range(size)])  11.4 us
    dot_general x1, matrix products, on_device(): jnp.einsum('rd,kdf->krf', flat_rows, expert_in[0], preferred_element_type...  10.8 us
    unnamed x20, local copies, waits for them, and re-layouts  7.71 us
    ppermute x1, starting transfers between devices, shifted(): return lax.ppermute(shard, axis, pairs)  5.01 us
    dot_general x1, matrix products, on_device(): jnp.dot(pick, returned.reshape(slots, width), preferred_element_type=jnp....  4.8 us
  transfers between devices with their start and end apart: 6, of which 5 were waited for; matrix products, arithmetic and copies ran while one was open for 5% of the time, Pallas kernels for 0%

profile of v2, /device:TPU:0, one launch (start us, length us, event | category | flops | bytes accessed | tf_op | source)
XLA Modules:
  0.0 202.4 jit_solution(9819337192422974932)
XLA Ops:
  6.5 0.0 copy-start
  6.5 0.0 all-gather.3.cloned.1.call-start
  6.5 0.9 slice_bitcast_fusion
  7.5 5.0 %collective-permute-start = (bf16[2,128,128]{2,1,0:T(8,128)(2,1)S(1)}, bf16[2,128,128]{2,1,0:T(8,128)(2,1)S(1)}, u32[]{:S(2)}, u32[]{:S(2)}) collective-permute-start(bf16[2,128,128]{2,1,0:T(8,128)(2,1)S(1)} %pad_maximum_fusion), channel_id=1, source_target_pairs={{0,2},{2,4},{4,6},{6,8},{8,10},{10,12},{12,14},{1,3},{3,5},{5,7},{... | collective-permute-start | bytes 196616 | tf_op jit(solution)/shard_map/ppermute | solution.py:18
  12.5 0.1 fusion.21
  12.6 0.9 copy.22
  13.5 0.9 copy.20
  14.5 2.0 %copy.23 = bf16[256,1024]{0,1:T(8,128)(2,1)} copy(bf16[256,1024]{1,0:T(8,128)(2,1)} %param.12) | data formatting | bytes 1048576 | tf_op args[0]
  16.5 0.7 max.17
  17.3 0.0 collective-permute-done
  17.3 0.8 broadcast_select_fusion
  18.1 0.1 copy.21
  18.2 2.1 %fusion.1 = (f32[2,8,256]{2,1,0:T(8,128)S(1)}, f32[2,384,256,8]{2,1,3,0:T(8,128)S(1)}) fusion(pred[256,384]{0,1:T(8,128)(4,1)S(1)} %fusion.21, bf16[256,2,8,64]{0,3,2,1:T(8,128)(2,1)} %bitcast.86, bf16[256,2,64]{0,2,1:T(8,128)(2,1)S(1)} %bitcast.88, bf16[128,2,64]{0,2,1:T(8,128)(2,1)S(1)} %bitcast.89), kind=kOutput, calls=%fused_computation.7 | convolution fusion | flops 206237696 | bytes 7028736 | tf_op jit(solution)/shard_map/qhgd,khd->hgqk/dot_general | solution.py:37
  20.4 0.0 copy-start.1
  20.4 0.1 broadcast_maximum_fusion
  20.4 2.6 %copy-done.1 = f32[2,384,256,8]{2,1,3,0:T(8,128)} copy-done((f32[2,384,256,8]{2,1,3,0:T(8,128)}, f32[2,384,256,8]{2,1,3,0:T(8,128)S(1)}, u32[]{:S(2)}) %copy-start.1) | copy-done | bytes 6291480
  23.0 1.3 fusion
  24.3 0.1 exponential_add_fusion
  24.4 0.1 copy.19
  24.5 4.6 %fusion.15 = bf16[2,64,8,256]{3,1,2,0:T(8,128)(2,1)S(1)} fusion(f32[2,384,256,8]{2,1,3,0:T(8,128)} %copy-done.1, f32[2,8,256]{2,1,0:T(8,128)S(1)} %exponential_add_fusion, f32[2,8,256]{2,1,0:T(8,128)S(1)} %broadcast_maximum_fusion, pred[256,384]{0,1:T(8,128)(4,1)S(1)} %fusion.21, bf16[256,2,64]{0,2,1:T(8,128)(2,1)S(1)} %bitcast.90, ...), kind=kOutput, calls=%fused_computation.26 | convolution fusion | flops 209649664 | bytes 7045120 | tf_op jit(solution)/shard_map/hgqk,khd->qhgd/dot_general | solution.py:49
  29.1 0.0 copy-done
  29.1 0.0 copy-start.5
  29.1 2.2 %fusion.37 = f32[256,1536]{1,0:T(8,128)} fusion(bf16[256,1024]{0,1:T(8,128)(2,1)S(1)} %bitcast.87, bf16[1024,1536]{1,0:T(8,128)(2,1)S(1)} %copy-done), kind=kOutput, calls=%fused_computation.74 | convolution fusion | flops 805306368 | bytes 5242880 | tf_op jit(solution)/shard_map/dot_general | solution.py:95
  31.2 0.0 collective-permute-start.1
  31.2 3.7 %collective-permute-done.1 = f32[256,1536]{1,0:T(8,128)} collective-permute-done((f32[256,1536]{1,0:T(8,128)}, f32[256,1536]{1,0:T(8,128)}, u32[]{:S(2)}, u32[]{:S(2)}) %collective-permute-start.1) | collective-permute-done | bytes 1572896 | tf_op jit(solution)/shard_map/ppermute | solution.py:23
  35.0 2.4 %multiply_reduce_fusion.1 = (f32[256]{0:T(256)S(1)}, f32[256,1536]{1,0:T(8,128)S(1)}) fusion(f32[256,1536]{1,0:T(8,128)} %fusion.37, f32[256,1536]{1,0:T(8,128)} %collective-permute-done.1, bf16[256,1536]{1,0:T(8,128)(2,1)} %param.18), kind=kLoop, calls=%fused_computation.21 | loop fusion | flops 1965824 | bytes 5506048 | tf_op jit(solution)/shard_map/reduce_sum | solution.py:27
  37.4 0.1 dynamic-slice
  37.5 1.0 copy-done.2
  38.6 0.0 copy-done.5
  38.6 0.9 fusion.17
  39.4 0.0 all-gather.3.cloned.1.call-update
  39.5 0.0 copy-done.4
  39.5 30.7 %all-gather = s32[2048,4]{0,1:T(4,128)S(1)} all-gather(s32[256,4]{0,1:T(4,128)S(1)} %copy-done.4), channel_id=2, replica_groups=mesh['groups'=2,'seq'=8,'exp'=2] {'seq'}, dimensions={0}, use_global_device_ids=true | all-gather | bytes 36864 | tf_op jit(solution)/shard_map/all_gather | solution.py:61
  70.2 0.6 reduce-window.16
  70.8 0.2 slice_reduce_fusion.1
  71.1 0.1 add_bitcast_fusion.1
  71.1 29.8 %all-gather.3.cloned.1.call-done = bf16[2048,1536]{1,0:T(8,128)(2,1)} async-done(((bf16[128,1536]{1,0:T(8,128)(2,1)}), bf16[2048,1536]{1,0:T(8,128)(2,1)}) %all-gather.3.cloned.1.call-update) | async-done | bytes 6291472 | tf_op jit(solution)/shard_map/all_gather | solution.py:58
  101.0 4.2 %convolution_convert_fusion.1 = bf16[8,192,1536]{2,1,0:T(8,128)(2,1)S(1)} fusion(bf16[8,256,1536]{2,1,0:T(8,128)(2,1)} %bitcast.82, s32[8,256]{1,0:T(8,128)S(1)} %add_bitcast_fusion.1, s32[192]{0:T(256)S(1)} %and_select_fusion, pred[8,256]{1,0:T(8,128)(4,1)S(1)} %reshape.158), kind=kOutput, calls=%fused_computation.14 | convolution fusion | flops 1211105280 | bytes 11021056 | tf_op jit(solution)/shard_map/bst,btd->bsd/dot_general | solution.py:67
  105.2 0.0 copy-start.6
  105.2 10.8 %convolution_bitcast_fusion = f32[2,1536,768]{2,1,0:T(8,128)S(1)} fusion(bf16[1536,1536,1]{1,0,2:T(8,128)(2,1)S(1)} %bitcast.83, bf16[1,2,1536,768]{3,2,1,0:T(8,128)(2,1)} %param.20), kind=kOutput, calls=%fused_computation.6 | convolution fusion | flops 7247757312 | bytes 18874368 | tf_op jit(solution)/shard_map/rd,kdf->krf/dot_general | solution.py:127
  116.0 0.0 copy-done.6
  116.0 4.2 %convolution_convert_fusion = bf16[1536,1536]{1,0:T(8,128)(2,1)S(1)} fusion(bf16[1,768,1536]{2,1,0:T(8,128)(2,1)S(1)} %copy-done.6, f32[2,1536,768]{2,1,0:T(8,128)S(1)} %convolution_bitcast_fusion), kind=kOutput, calls=%fused_computation | convolution fusion | flops 3635675136 | bytes 16515072 | tf_op jit(solution)/shard_map/dot_general | solution.py:134
  120.2 0.2 slice.55
  120.4 0.3 collective-permute-start.2
  120.7 4.3 %collective-permute-done.2 = bf16[8,96,1536]{2,1,0:T(8,128)(2,1)S(1)} collective-permute-done((bf16[8,96,1536]{2,1,0:T(8,128)(2,1)S(1)}, bf16[8,96,1536]{2,1,0:T(8,128)(2,1)S(1)}, u32[]{:S(2)}, u32[]{:S(2)}) %collective-permute-start.2) | collective-permute-done | bytes 2359328 | tf_op jit(solution)/shard_map/ppermute | solution.py:23
  125.0 2.1 %add_convert_fusion = bf16[8,96,1536]{2,1,0:T(8,128)(2,1)} fusion(bf16[8,96,1536]{2,1,0:T(8,128)(2,1)S(1)} %collective-permute-done.2, bf16[8,192,1536]{2,1,0:T(8,128)(2,1)S(1)} %bitcast.85), kind=kLoop, calls=%fused_computation.13 | loop fusion | flops 4718592 | bytes 7077888 | tf_op jit(solution)/shard_map/convert_element_type | solution.py:140
  127.0 4.5 %all-to-all-start = ((bf16[8,96,1536]{2,1,0:T(8,128)(2,1)}), bf16[8,96,1536]{2,1,0:T(8,128)(2,1)}, u32[]{:S(2)}, u32[]{:S(2)}) async-start(bf16[8,96,1536]{2,1,0:T(8,128)(2,1)} %add_convert_fusion), calls=%async_computation | async-start | bytes 4718592 | tf_op jit(solution)/shard_map/all_to_all | solution.py:141
  131.5 0.1 copy.25
  131.7 0.1 eq.83
  131.8 0.1 eq.79
  131.9 2.3 %reduce-window.14 = s32[8,8,128]{2,1,0:T(8,128)S(1)} reduce-window(s32[8,8,128]{2,1,0:T(8,128)S(1)} %fusion.29, s32[]{:T(128)} %constant.19.clone.1), window={size=1x1x128 pad=0_0x0_0x127_0}, to_apply=%region_2.3 | reduce-window | flops 1040384 | bytes 65540 | tf_op jit(solution)/shard_map/reduce-window
  134.2 0.3 slice_reduce_fusion
  134.5 0.2 reduce-window.15
  134.6 0.1 add_bitcast_fusion
  134.8 0.1 sub.53
  134.9 0.1 copy.28
  135.1 0.1 copy.29
  135.2 50.9 %all-to-all-done = bf16[8,96,1536]{2,1,0:T(8,128)(2,1)} async-done(((bf16[8,96,1536]{2,1,0:T(8,128)(2,1)}), bf16[8,96,1536]{2,1,0:T(8,128)(2,1)}, u32[]{:S(2)}, u32[]{:S(2)}) %all-to-all-start) | async-done | bytes 2359328 | tf_op jit(solution)/shard_map/all_to_all | solution.py:141
  186.1 0.0 copy-done.7
  186.1 4.8 %multiply_reduce_fusion = f32[256,1536]{1,0:T(8,128)S(1)} fusion(bf16[768,1536,1]{1,0,2:T(8,128)(2,1)} %bitcast.27, f32[256,4]{0,1:T(4,128)S(1)} %copy-done.7, s32[256,4]{0,1:T(4,128)S(1)} %copy.29), kind=kOutput, calls=%fused_computation.2 | convolution fusion | flops 2419458048 | bytes 3940352 | tf_op jit(solution)/shard_map/dot_general | solution.py:142
  190.9 0.1 collective-permute-start.3
  191.0 3.4 %collective-permute-done.3 = f32[256,1536]{1,0:T(8,128)S(1)} collective-permute-done((f32[256,1536]{1,0:T(8,128)S(1)}, f32[256,1536]{1,0:T(8,128)S(1)}, u32[]{:S(2)}, u32[]{:S(2)}) %collective-permute-start.3) | collective-permute-done | bytes 1572896 | tf_op jit(solution)/shard_map/ppermute | solution.py:23
  194.4 0.0 copy-done.3
  194.4 1.2 add_convert_fusion.1
  (19 shorter events, 0.2 us)
Async XLA Ops:
  6.5 22.5 %copy-start = (bf16[1024,1536]{1,0:T(8,128)(2,1)S(1)}, bf16[1024,1536]{1,0:T(8,128)(2,1)}, u32[]{:S(2)}) copy-start(bf16[1024,1536]{1,0:T(8,128)(2,1)} %param.17) | copy-start | bytes 9437188
  6.5 94.4 %all-gather.3.cloned.1.call-start = ((), (), s32[]{:S(2)}) async-start(), calls=%async_computation.1 | async-start | bytes 6684672 | tf_op jit(solution)/shard_map/all_gather | solution.py:58
  7.5 9.8 %collective-permute-start = (bf16[2,128,128]{2,1,0:T(8,128)(2,1)S(1)}, bf16[2,128,128]{2,1,0:T(8,128)(2,1)S(1)}, u32[]{:S(2)}, u32[]{:S(2)}) collective-permute-start(bf16[2,128,128]{2,1,0:T(8,128)(2,1)S(1)} %pad_maximum_fusion), channel_id=1, source_target_pairs={{0,2},{2,4},{4,6},{6,8},{8,10},{10,12},{12,14},{1,3},{3,5},{5,7},{... | collective-permute-start | bytes 196616 | tf_op jit(solution)/shard_map/ppermute | solution.py:18
  20.4 2.7 %copy-start.1 = (f32[2,384,256,8]{2,1,3,0:T(8,128)}, f32[2,384,256,8]{2,1,3,0:T(8,128)S(1)}, u32[]{:S(2)}) copy-start(f32[2,384,256,8]{2,1,3,0:T(8,128)S(1)} %get-tuple-element.10) | copy-start | bytes 18874372
  29.1 9.5 %copy-start.5 = (f32[1536]{0:T(1024)S(1)}, f32[1536]{0:T(1024)}, u32[]{:S(2)}) copy-start(f32[1536]{0:T(1024)} %param.19) | copy-start | bytes 18436
  31.2 8.2 %copy-start.4 = (s32[256,4]{0,1:T(4,128)S(1)}, s32[256,4]{0,1:T(4,128)}, u32[]{:S(2)}) copy-start(s32[256,4]{0,1:T(4,128)} %param.22) | copy-start | bytes 12292
  31.2 3.8 %collective-permute-start.1 = (f32[256,1536]{1,0:T(8,128)}, f32[256,1536]{1,0:T(8,128)}, u32[]{:S(2)}, u32[]{:S(2)}) collective-permute-start(f32[256,1536]{1,0:T(8,128)} %fusion.37), channel_id=1, source_target_pairs={{0,1},{1,0},{2,3},{3,2},{4,5},{5,4},{6,7},{7,6},{8,9},{9,8},{10,11... | collective-permute-start | bytes 4718600 | tf_op jit(solution)/shard_map/ppermute | solution.py:23
  37.4 1.1 copy-start.2
  105.2 10.8 %copy-start.6 = (bf16[1,768,1536]{2,1,0:T(8,128)(2,1)S(1)}, bf16[1,768,1536]{2,1,0:T(8,128)(2,1)}, u32[]{:S(2)}) copy-start(bf16[1,768,1536]{2,1,0:T(8,128)(2,1)} %param.21) | copy-start | bytes 7077892
  120.4 4.6 %collective-permute-start.2 = (bf16[8,96,1536]{2,1,0:T(8,128)(2,1)S(1)}, bf16[8,96,1536]{2,1,0:T(8,128)(2,1)S(1)}, u32[]{:S(2)}, u32[]{:S(2)}) collective-permute-start(bf16[8,96,1536]{2,1,0:T(8,128)(2,1)S(1)} %slice.55), channel_id=1, source_target_pairs={{0,1},{1,0},{2,3},{3,2},{4,5},{5,4},{6,7},{7,6},{8,9},{9,8},{10,11... | collective-permute-start | bytes 7077896 | tf_op jit(solution)/shard_map/ppermute | solution.py:23
  127.0 59.1 %copy-start.7 = (f32[256,4]{0,1:T(4,128)S(1)}, f32[256,4]{0,1:T(4,128)}, u32[]{:S(2)}) copy-start(f32[256,4]{0,1:T(4,128)} %param.23) | copy-start | bytes 12292
  127.0 59.1 %all-to-all-start = ((bf16[8,96,1536]{2,1,0:T(8,128)(2,1)}), bf16[8,96,1536]{2,1,0:T(8,128)(2,1)}, u32[]{:S(2)}, u32[]{:S(2)}) async-start(bf16[8,96,1536]{2,1,0:T(8,128)(2,1)} %add_convert_fusion), calls=%async_computation | async-start | bytes 4718592 | tf_op jit(solution)/shard_map/all_to_all | solution.py:141
  186.1 8.3 %copy-start.3 = (f32[256,1536]{1,0:T(8,128)S(1)}, f32[256,1536]{1,0:T(8,128)}, u32[]{:S(2)}) copy-start(f32[256,1536]{1,0:T(8,128)} %copy-done.2) | copy-start | bytes 4718596
  190.9 3.5 %collective-permute-start.3 = (f32[256,1536]{1,0:T(8,128)S(1)}, f32[256,1536]{1,0:T(8,128)S(1)}, u32[]{:S(2)}, u32[]{:S(2)}) collective-permute-start(f32[256,1536]{1,0:T(8,128)S(1)} %multiply_reduce_fusion), channel_id=1, source_target_pairs={{0,1},{1,0},{2,3},{3,2},{4,5},{5,4},{6,7},{7,6},{8,9},{9,8},{10,11... | collective-permute-start | bytes 4718600 | tf_op jit(solution)/shard_map/ppermute | solution.py:23
Sparse Core Ops, SparseCore 0:
  39.6 61.3 all-gather.2

commit v3 on v1

--- a/solution.py
+++ b/solution.py
@@ -50,6 +50,13 @@
     return heads_out.astype(jnp.bfloat16).reshape(block_rows, queries.shape[1])
 
 
+def expert_hidden(rows, expert_in):
+    gate_up = jnp.einsum("rd,kdf->krf", rows, expert_in, preferred_element_type=jnp.float32)
+    gate_val = gate_up[0]
+    up_val = gate_up[1]
+    return ((up_val + 1.0) * gate_val * jax.nn.sigmoid(GLU_ALPHA * gate_val)).astype(jnp.bfloat16)
+
+
 def on_device(
     queries,
     key_rows,
@@ -100,21 +107,20 @@
         .reshape(experts, half, width)
     )
     slot_rows = lax.all_to_all(outgoing, "seq", split_axis=0, concat_axis=0, tiled=True)
-    both_rows = jnp.concatenate([slot_rows, swap_exp(slot_rows)], axis=1)
-    flat_rows = both_rows.reshape(-1, width)
-    gate_up = jnp.einsum("rd,kdf->krf", flat_rows, expert_in[0], preferred_element_type=jnp.float32)
-    gate_val = gate_up[0]
-    up_val = gate_up[1]
-    activation = ((up_val + 1.0) * gate_val * jax.nn.sigmoid(GLU_ALPHA * gate_val)).astype(
-        jnp.bfloat16
+    other_rows = swap_exp(slot_rows)
+    own_hidden = expert_hidden(slot_rows.reshape(-1, width), expert_in[0])
+    own_hidden, other_rows = lax.optimization_barrier((own_hidden, other_rows))
+    other_hidden = expert_hidden(other_rows.reshape(-1, width), expert_in[0])
+    their_part = swap_exp(
+        jnp.dot(other_hidden, expert_out[0], preferred_element_type=jnp.float32)
+        .astype(jnp.bfloat16)
+        .reshape(experts, half, width)
     )
-    out_part = (
-        jnp.dot(activation, expert_out[0], preferred_element_type=jnp.float32)
+    own_part = (
+        jnp.dot(own_hidden, expert_out[0], preferred_element_type=jnp.float32)
         .astype(jnp.bfloat16)
-        .reshape(experts, 2 * half, width)
+        .reshape(experts, half, width)
     )
-    own_part = out_part[:, :half]
-    their_part = swap_exp(out_part[:, half:])
     result = (own_part.astype(jnp.float32) + their_part.astype(jnp.float32)).astype(jnp.bfloat16)
     returned = lax.all_to_all(result, "seq", split_axis=0, concat_axis=0, tiled=True)
     picked = jnp.dot(pick, returned.reshape(slots, width), preferred_element_type=jnp.float32)

time: 180 us -> 171 us (0.950)
  waiting for transfers between devices: 12.3 us -> 5.61 us
  matrix products: 28.2 us -> 24.4 us
    ppermute x4, waiting for transfers between devices: 12.3 us -> 5.61 us  [swap_exp(): return lax.ppermute(x, 'exp', [(i, (i + 1) % size) for i in range(size)])]
    dot_general x2 -> x4, matrix products: 18.2 us -> 11.7 us  [the longest x2 7.62 us: expert_hidden(): jnp.einsum('rd,kdf->krf', rows, expert_in, preferred_element_type=jnp.flo...]
    dot_general x1, matrix products: 1.82 us -> 4.57 us  [attend_block(): jnp.einsum('hgqk,khd->qhgd', probs, value_block, preferred_element_type=j...]
    unnamed x18 -> x20, local copies, waits for them, and re-layouts: 4.09 us -> 5.39 us
  transfers between devices with their start and end apart: 5 -> 5, of which waited for: 3 -> 2; matrix products, arithmetic and copies ran while one was open for 5% -> 9% of each run, Pallas kernels for 0% -> 0%
where the time goes in v3:
time: 171 us
  blocking collectives  116 us (68%)
  matrix products  24.4 us (14%)
  other arithmetic  10.5 us (6%)
  local copies, waits for them, and re-layouts  8.14 us (5%)
  starting transfers between devices  5.63 us (3%)
  waiting for transfers between devices  5.61 us (3%)
    all_to_all x1, blocking collectives, on_device(): lax.all_to_all(outgoing, 'seq', split_axis=0, concat_axis=0, tiled=True)  58.3 us
    all_to_all x1, blocking collectives, on_device(): lax.all_to_all(result, 'seq', split_axis=0, concat_axis=0, tiled=True)  57.8 us
    dot_general x2, matrix products, expert_hidden(): jnp.einsum('rd,kdf->krf', rows, expert_in, preferred_element_type=jnp.flo...  7.62 us
    ppermute x4, waiting for transfers between devices, swap_exp(): return lax.ppermute(x, 'exp', [(i, (i + 1) % size) for i in range(size)])  5.61 us
    unnamed x20, local copies, waits for them, and re-layouts  5.39 us
    ppermute x1, starting transfers between devices, shifted(): return lax.ppermute(shard, axis, pairs)  5.01 us
    dot_general x1, matrix products, attend_block(): jnp.einsum('hgqk,khd->qhgd', probs, value_block, preferred_element_type=j...  4.57 us
  transfers between devices with their start and end apart: 5, of which 2 were waited for; matrix products, arithmetic and copies ran while one was open for 9% of the time, Pallas kernels for 0%

profile of v3, /device:TPU:0, one launch (start us, length us, event | category | flops | bytes accessed | tf_op | source)
XLA Modules:
  0.0 170.7 jit_solution(15773404157289949328)
XLA Ops:
  0.0 0.0 copy-start
  0.0 0.9 slice_bitcast_fusion
  0.9 5.0 %collective-permute-start = (bf16[2,128,128]{2,1,0:T(8,128)(2,1)S(1)}, bf16[2,128,128]{2,1,0:T(8,128)(2,1)S(1)}, u32[]{:S(2)}, u32[]{:S(2)}) collective-permute-start(bf16[2,128,128]{2,1,0:T(8,128)(2,1)S(1)} %pad_maximum_fusion), channel_id=1, source_target_pairs={{0,2},{2,4},{4,6},{6,8},{8,10},{10,12},{12,14},{1,3},{3,5},{5,7},{... | collective-permute-start | bytes 196616 | tf_op jit(solution)/shard_map/ppermute | solution.py:18
  6.0 0.1 fusion.34
  6.0 0.9 copy.34
  7.0 0.9 copy.32
  7.9 2.0 %copy.35 = bf16[256,1024]{0,1:T(8,128)(2,1)} copy(bf16[256,1024]{1,0:T(8,128)(2,1)} %param.12) | data formatting | bytes 1048576 | tf_op args[0]
  10.0 0.7 max.17
  10.7 0.0 collective-permute-done
  10.7 0.8 broadcast_select_fusion
  11.6 0.1 copy.33
  11.7 2.1 %fusion.1 = (f32[2,8,256]{2,1,0:T(8,128)S(1)}, f32[2,384,256,8]{2,1,3,0:T(8,128)S(1)}) fusion(pred[256,384]{0,1:T(8,128)(4,1)S(1)} %fusion.34, bf16[256,2,8,64]{0,3,2,1:T(8,128)(2,1)} %bitcast.101, bf16[256,2,64]{0,2,1:T(8,128)(2,1)S(1)} %bitcast.103, bf16[128,2,64]{0,2,1:T(8,128)(2,1)S(1)} %bitcast.104), kind=kOutput, calls=%fused_computation.5 | convolution fusion | flops 206237696 | bytes 7028736 | tf_op jit(solution)/shard_map/qhgd,khd->hgqk/dot_general | solution.py:37
  13.8 0.0 copy-start.1
  13.8 0.1 broadcast_maximum_fusion
  13.9 1.3 fusion
  15.2 1.3 copy-done.1
  16.5 0.1 exponential_add_fusion
  16.6 0.1 copy.31
  16.7 4.6 %fusion.27 = bf16[2,64,8,256]{3,1,2,0:T(8,128)(2,1)S(1)} fusion(f32[2,384,256,8]{2,1,3,0:T(8,128)} %copy-done.1, f32[2,8,256]{2,1,0:T(8,128)S(1)} %exponential_add_fusion, f32[2,8,256]{2,1,0:T(8,128)S(1)} %broadcast_maximum_fusion, pred[256,384]{0,1:T(8,128)(4,1)S(1)} %fusion.34, bf16[256,2,64]{0,2,1:T(8,128)(2,1)S(1)} %bitcast.105, ...), kind=kOutput, calls=%fused_computation.38 | convolution fusion | flops 209649664 | bytes 7045120 | tf_op jit(solution)/shard_map/hgqk,khd->qhgd/dot_general | solution.py:49
  21.3 0.0 copy-done
  21.3 0.0 copy-start.2
  21.3 2.2 %fusion.50 = f32[256,1536]{1,0:T(8,128)} fusion(bf16[256,1024]{0,1:T(8,128)(2,1)S(1)} %bitcast.102, bf16[1024,1536]{1,0:T(8,128)(2,1)S(1)} %copy-done), kind=kOutput, calls=%fused_computation.80 | convolution fusion | flops 805306368 | bytes 5242880 | tf_op jit(solution)/shard_map/dot_general | solution.py:83
  23.4 0.0 collective-permute-start.1
  23.4 0.0 copy-done.2
  23.4 0.1 copy.37
  23.6 0.1 eq.69
  23.7 0.1 eq.65
  23.8 2.3 %reduce-window.6 = s32[8,8,128]{2,1,0:T(8,128)S(1)} reduce-window(s32[8,8,128]{2,1,0:T(8,128)S(1)} %fusion.42, s32[]{:T(128)} %constant.16.clone.1), window={size=1x1x128 pad=0_0x0_0x127_0}, to_apply=%region_2.3 | reduce-window | flops 1040384 | bytes 65540 | tf_op jit(solution)/shard_map/reduce-window
  26.1 0.3 slice_reduce_fusion
  26.4 0.2 reduce-window.9
  26.5 0.1 add_bitcast_fusion
  26.7 0.1 sub.47
  26.8 0.1 copy.40
  27.0 0.1 copy.41
  27.1 0.4 fusion.25
  27.5 0.0 copy-start.3
  27.5 0.0 collective-permute-done.1
  27.5 0.0 slice-start
  27.6 2.6 %multiply_reduce_fusion.1 = (f32[256]{0:T(256)S(1)}, f32[256,1536]{1,0:T(8,128)S(1)}) fusion(f32[256,1536]{1,0:T(8,128)} %fusion.50, f32[256,1536]{1,0:T(8,128)} %collective-permute-done.1, bf16[256,1536]{1,0:T(8,128)(2,1)} %param.18), kind=kLoop, calls=%fused_computation.35 | loop fusion | flops 1965824 | bytes 5506048 | tf_op jit(solution)/shard_map/reduce_sum | solution.py:27
  30.1 0.0 copy-done.3
  30.1 0.0 slice-start.1
  30.2 0.9 convolution_convert_fusion.2
  31.1 58.3 %all_to_all.10 = bf16[8,96,1536]{2,1,0:T(8,128)(2,1)S(1)} all-to-all(bf16[8,96,1536]{2,1,0:T(8,128)(2,1)S(1)} %bitcast.97), channel_id=1, replica_groups=mesh['groups'=2,'seq'=8,'exp'=2] {'seq'}, dimensions={0} | all-to-all | bytes 4718592 | tf_op jit(solution)/shard_map/all_to_all | solution.py:109
  89.4 0.0 collective-permute-start.2
  89.4 0.0 slice-done
  89.4 0.0 slice-done.1
  89.4 3.8 %fusion.19 = f32[2,768,768]{2,1,0:T(8,128)S(1)} fusion(bf16[768,1536,1]{1,0,2:T(8,128)(2,1)S(1)} %bitcast.99, bf16[1,2,1536,768]{3,2,1,0:T(8,128)(2,1)S(1)} %bitcast.109), kind=kOutput, calls=%fused_computation.30 | convolution fusion | flops 3623878656 | bytes 11796480 | tf_op jit(solution)/shard_map/rd,kdf->krf/dot_general | solution.py:54
  93.2 0.7 fusion.31
  93.9 0.0 collective-permute-done.2
  93.9 0.0 copy-start.4
  93.9 3.8 %fusion.22 = f32[2,768,768]{2,1,0:T(8,128)S(1)} fusion(bf16[768,1536,1]{1,0,2:T(8,128)(2,1)S(1)} %bitcast.110, bf16[1,2,1536,768]{3,2,1,0:T(8,128)(2,1)S(1)} %bitcast.109), kind=kOutput, calls=%fused_computation.31 | convolution fusion | flops 3623878656 | bytes 11796480 | tf_op jit(solution)/shard_map/rd,kdf->krf/dot_general | solution.py:54
  97.7 0.0 copy-done.4
  97.7 2.1 %convolution_convert_fusion = bf16[768,1536]{1,0:T(8,128)(2,1)S(1)} fusion(bf16[1,768,1536]{2,1,0:T(8,128)(2,1)S(1)} %copy-done.4, f32[2,768,768]{2,1,0:T(8,128)S(1)} %fusion.22), kind=kOutput, calls=%fused_computation.12 | convolution fusion | flops 1817837568 | bytes 9437184 | tf_op jit(solution)/shard_map/dot_general | solution.py:115
  99.8 0.5 collective-permute-start.3
  100.4 2.0 %convolution_convert_fusion.1 = bf16[768,1536]{1,0:T(8,128)(2,1)S(1)} fusion(bf16[768,768]{1,0:T(8,128)(2,1)S(1)} %fusion.31, bf16[1,768,1536]{2,1,0:T(8,128)(2,1)S(1)} %copy-done.4), kind=kOutput, calls=%fused_computation.13 | convolution fusion | flops 1813118976 | bytes 5898240 | tf_op jit(solution)/shard_map/dot_general | solution.py:120
  102.3 2.2 %collective-permute-done.3 = bf16[8,96,1536]{2,1,0:T(8,128)(2,1)S(1)} collective-permute-done((bf16[8,96,1536]{2,1,0:T(8,128)(2,1)S(1)}, bf16[8,96,1536]{2,1,0:T(8,128)(2,1)S(1)}, u32[]{:S(2)}, u32[]{:S(2)}) %collective-permute-start.3) | collective-permute-done | bytes 2359328 | tf_op jit(solution)/shard_map/ppermute | solution.py:23
  104.5 0.7 fusion.2
  105.2 0.0 copy-start.5
  105.2 57.8 %all_to_all.11 = bf16[8,96,1536]{2,1,0:T(8,128)(2,1)S(1)} all-to-all(bf16[8,96,1536]{2,1,0:T(8,128)(2,1)S(1)} %fusion.2), channel_id=1, replica_groups=mesh['groups'=2,'seq'=8,'exp'=2] {'seq'}, dimensions={0} | all-to-all | bytes 4718592 | tf_op jit(solution)/shard_map/all_to_all | solution.py:125
  163.0 0.0 copy-done.5
  163.0 3.0 %multiply_reduce_fusion = f32[256,1536]{1,0:T(8,128)S(1)} fusion(bf16[768,1536,1]{1,0,2:T(8,128)(2,1)S(1)} %bitcast.100, f32[256,4]{0,1:T(4,128)S(1)} %copy-done.5, s32[256,4]{0,1:T(4,128)S(1)} %copy.41), kind=kOutput, calls=%fused_computation.1 | convolution fusion | flops 2419458048 | bytes 3940352 | tf_op jit(solution)/shard_map/dot_general | solution.py:126
  166.0 0.1 collective-permute-start.4
  166.1 3.4 %collective-permute-done.4 = f32[256,1536]{1,0:T(8,128)S(1)} collective-permute-done((f32[256,1536]{1,0:T(8,128)S(1)}, f32[256,1536]{1,0:T(8,128)S(1)}, u32[]{:S(2)}, u32[]{:S(2)}) %collective-permute-start.4) | collective-permute-done | bytes 1572896 | tf_op jit(solution)/shard_map/ppermute | solution.py:23
  169.5 1.2 add_convert_fusion
  (10 shorter events, 0.1 us)
Async XLA Ops:
  0.0 21.3 %copy-start = (bf16[1024,1536]{1,0:T(8,128)(2,1)S(1)}, bf16[1024,1536]{1,0:T(8,128)(2,1)}, u32[]{:S(2)}) copy-start(bf16[1024,1536]{1,0:T(8,128)(2,1)} %param.17) | copy-start | bytes 9437188
  0.9 9.8 %collective-permute-start = (bf16[2,128,128]{2,1,0:T(8,128)(2,1)S(1)}, bf16[2,128,128]{2,1,0:T(8,128)(2,1)S(1)}, u32[]{:S(2)}, u32[]{:S(2)}) collective-permute-start(bf16[2,128,128]{2,1,0:T(8,128)(2,1)S(1)} %pad_maximum_fusion), channel_id=1, source_target_pairs={{0,2},{2,4},{4,6},{6,8},{8,10},{10,12},{12,14},{1,3},{3,5},{5,7},{... | collective-permute-start | bytes 196616 | tf_op jit(solution)/shard_map/ppermute | solution.py:18
  13.8 2.7 %copy-start.1 = (f32[2,384,256,8]{2,1,3,0:T(8,128)}, f32[2,384,256,8]{2,1,3,0:T(8,128)S(1)}, u32[]{:S(2)}) copy-start(f32[2,384,256,8]{2,1,3,0:T(8,128)S(1)} %get-tuple-element.14) | copy-start | bytes 18874372
  21.3 2.2 %copy-start.2 = (s32[256,4]{0,1:T(4,128)S(1)}, s32[256,4]{0,1:T(4,128)}, u32[]{:S(2)}) copy-start(s32[256,4]{0,1:T(4,128)} %param.22) | copy-start | bytes 12292
  23.4 4.1 %collective-permute-start.1 = (f32[256,1536]{1,0:T(8,128)}, f32[256,1536]{1,0:T(8,128)}, u32[]{:S(2)}, u32[]{:S(2)}) collective-permute-start(f32[256,1536]{1,0:T(8,128)} %fusion.50), channel_id=1, source_target_pairs={{0,1},{1,0},{2,3},{3,2},{4,5},{5,4},{6,7},{7,6},{8,9},{9,8},{10,11... | collective-permute-start | bytes 4718600 | tf_op jit(solution)/shard_map/ppermute | solution.py:23
  27.5 2.6 %copy-start.3 = (f32[1536]{0:T(1024)S(1)}, f32[1536]{0:T(1024)}, u32[]{:S(2)}) copy-start(f32[1536]{0:T(1024)} %param.19) | copy-start | bytes 18436
  27.5 61.8 %slice-start = ((s8[4718592]{0:T(1024)(128)(4,1)}), s8[4194304]{0:T(1024)(128)(4,1)S(1)}, s32[]{:S(2)}) async-start(s8[4718592]{0:T(1024)(128)(4,1)} %bitcast.108), calls=%async_computation.2 | async-start | bytes 8388608
  30.1 59.2 %slice-start.1 = ((s8[4718592]{0:T(1024)(128)(4,1)}), s8[524288]{0:T(1024)(128)(4,1)S(1)}, s32[]{:S(2)}) async-start(s8[4718592]{0:T(1024)(128)(4,1)} %bitcast.108), calls=%async_computation.3 | async-start | bytes 1048576
  89.4 4.5 %collective-permute-start.2 = (bf16[8,96,1536]{2,1,0:T(8,128)(2,1)S(1)}, bf16[8,96,1536]{2,1,0:T(8,128)(2,1)S(1)}, u32[]{:S(2)}, u32[]{:S(2)}) collective-permute-start(bf16[8,96,1536]{2,1,0:T(8,128)(2,1)S(1)} %all_to_all.10), channel_id=1, source_target_pairs={{0,1},{1,0},{2,3},{3,2},{4,5},{5,4},{6,7},{7,6},{8,9},{9,8},{10,11... | collective-permute-start | bytes 7077896 | tf_op jit(solution)/shard_map/ppermute | solution.py:23
  93.9 3.8 %copy-start.4 = (bf16[1,768,1536]{2,1,0:T(8,128)(2,1)S(1)}, bf16[1,768,1536]{2,1,0:T(8,128)(2,1)}, u32[]{:S(2)}) copy-start(bf16[1,768,1536]{2,1,0:T(8,128)(2,1)} %param.21) | copy-start | bytes 7077892
  99.8 4.7 %collective-permute-start.3 = (bf16[8,96,1536]{2,1,0:T(8,128)(2,1)S(1)}, bf16[8,96,1536]{2,1,0:T(8,128)(2,1)S(1)}, u32[]{:S(2)}, u32[]{:S(2)}) collective-permute-start(bf16[8,96,1536]{2,1,0:T(8,128)(2,1)S(1)} %bitcast.111), channel_id=1, source_target_pairs={{0,1},{1,0},{2,3},{3,2},{4,5},{5,4},{6,7},{7,6},{8,9},{9,8},{10,11... | collective-permute-start | bytes 7077896 | tf_op jit(solution)/shard_map/ppermute | solution.py:23
  105.2 57.8 %copy-start.5 = (f32[256,4]{0,1:T(4,128)S(1)}, f32[256,4]{0,1:T(4,128)}, u32[]{:S(2)}) copy-start(f32[256,4]{0,1:T(4,128)} %param.23) | copy-start | bytes 12292
  166.0 3.5 %collective-permute-start.4 = (f32[256,1536]{1,0:T(8,128)S(1)}, f32[256,1536]{1,0:T(8,128)S(1)}, u32[]{:S(2)}, u32[]{:S(2)}) collective-permute-start(f32[256,1536]{1,0:T(8,128)S(1)} %multiply_reduce_fusion), channel_id=1, source_target_pairs={{0,1},{1,0},{2,3},{3,2},{4,5},{5,4},{6,7},{7,6},{8,9},{9,8},{10,11... | collective-permute-start | bytes 4718600 | tf_op jit(solution)/shard_map/ppermute | solution.py:23

commit v4 on v3

--- a/solution.py
+++ b/solution.py
@@ -6,6 +6,7 @@
 HEAD_DIM = 64
 WINDOW = 128
 TOP = 4
+CHUNKS = 2
 
 
 GLU_ALPHA = 1.702
@@ -57,6 +58,25 @@
     return ((up_val + 1.0) * gate_val * jax.nn.sigmoid(GLU_ALPHA * gate_val)).astype(jnp.bfloat16)
 
 
+def serve_rows(slot_rows, expert_in, expert_out):
+    blocks, piece, width = slot_rows.shape
+    other_rows = swap_exp(slot_rows)
+    own_hidden = expert_hidden(slot_rows.reshape(-1, width), expert_in)
+    own_hidden, other_rows = lax.optimization_barrier((own_hidden, other_rows))
+    other_hidden = expert_hidden(other_rows.reshape(-1, width), expert_in)
+    their_part = swap_exp(
+        jnp.dot(other_hidden, expert_out, preferred_element_type=jnp.float32)
+        .astype(jnp.bfloat16)
+        .reshape(blocks, piece, width)
+    )
+    own_part = (
+        jnp.dot(own_hidden, expert_out, preferred_element_type=jnp.float32)
+        .astype(jnp.bfloat16)
+        .reshape(blocks, piece, width)
+    )
+    return (own_part.astype(jnp.float32) + their_part.astype(jnp.float32)).astype(jnp.bfloat16)
+
+
 def on_device(
     queries,
     key_rows,
@@ -106,23 +126,23 @@
         .astype(jnp.bfloat16)
         .reshape(experts, half, width)
     )
-    slot_rows = lax.all_to_all(outgoing, "seq", split_axis=0, concat_axis=0, tiled=True)
-    other_rows = swap_exp(slot_rows)
-    own_hidden = expert_hidden(slot_rows.reshape(-1, width), expert_in[0])
-    own_hidden, other_rows = lax.optimization_barrier((own_hidden, other_rows))
-    other_hidden = expert_hidden(other_rows.reshape(-1, width), expert_in[0])
-    their_part = swap_exp(
-        jnp.dot(other_hidden, expert_out[0], preferred_element_type=jnp.float32)
-        .astype(jnp.bfloat16)
-        .reshape(experts, half, width)
-    )
-    own_part = (
-        jnp.dot(own_hidden, expert_out[0], preferred_element_type=jnp.float32)
-        .astype(jnp.bfloat16)
-        .reshape(experts, half, width)
-    )
-    result = (own_part.astype(jnp.float32) + their_part.astype(jnp.float32)).astype(jnp.bfloat16)
-    returned = lax.all_to_all(result, "seq", split_axis=0, concat_axis=0, tiled=True)
+    chunks = CHUNKS if half % CHUNKS == 0 else 1
+    piece = half // CHUNKS if chunks == CHUNKS else half
+    arrived = [
+        lax.all_to_all(
+            outgoing[:, q * piece : (q + 1) * piece], "seq", split_axis=0, concat_axis=0, tiled=True
+        )
+        for q in range(chunks)
+    ]
+    results = []
+    served = None
+    for q in range(chunks):
+        slot_rows = arrived[q]
+        if served is not None:
+            slot_rows, served = lax.optimization_barrier((slot_rows, served))
+        served = serve_rows(slot_rows, expert_in[0], expert_out[0])
+        results.append(lax.all_to_all(served, "seq", split_axis=0, concat_axis=0, tiled=True))
+    returned = jnp.concatenate(results, axis=1)
     picked = jnp.dot(pick, returned.reshape(slots, width), preferred_element_type=jnp.float32)
     weighted = jnp.sum(picked.reshape(tok_rows, TOP, width) * route_gates[:, :, None], axis=1)
     moe = weighted + swap_exp(weighted)

time: 171 us -> 176 us (1.029)
  blocking collectives: 116 us -> 67.1 us
  waiting for transfers between devices: 5.61 us -> 34.3 us
  matrix products: 24.4 us -> 36.1 us
  starting transfers between devices: 5.63 us -> 14.8 us
  other arithmetic: 10.5 us -> 13.6 us
    all_to_all x2, blocking collectives: 116 us -> 67.1 us  [the longest x1 34.3 us: on_device(): lax.all_to_all(outgoing[:, q * piece:(q + 1) * piece], 'seq', split_axis=...]
    all_to_all x0 -> x2, waiting for transfers between devices: none -> 28.1 us  [the longest x1 14.1 us: on_device(): lax.all_to_all(served, 'seq', split_axis=0, concat_axis=0, tiled=True)]
    dot_general x2 -> x4, matrix products: 7.62 us -> 19 us  [expert_hidden(): jnp.einsum('rd,kdf->krf', rows, expert_in, preferred_element_type=jnp.flo...]
    all_to_all x0 -> x2, starting transfers between devices: none -> 8.7 us  [the longest x1 4.44 us: on_device(): lax.all_to_all(outgoing[:, q * piece:(q + 1) * piece], 'seq', split_axis=...]
    convert_element_type x1 -> x2, other arithmetic: 0.67 us -> 2.7 us  [serve_rows(): (own_part.astype(jnp.float32) + their_part.astype(jnp.float32)).astype(jn...]
    ppermute x4 -> x6, waiting for transfers between devices: 5.61 us -> 6.19 us  [swap_exp(): return lax.ppermute(x, 'exp', [(i, (i + 1) % size) for i in range(size)])]
    dot_general x2 -> x4, matrix products: 4.04 us -> 4.34 us  [the longest x2 2.19 us: serve_rows(): jnp.dot(other_hidden, expert_out, preferred_element_type=jnp.float32)]
    unnamed x20 -> x26, local copies, waits for them, and re-layouts: 5.39 us -> 5.63 us
  transfers between devices with their start and end apart: 5 -> 9, of which waited for: 2 -> 5; matrix products, arithmetic and copies ran while one was open for 9% -> 20% of each run, Pallas kernels for 0% -> 0%
where the time goes in v4:
time: 176 us; the launch traced here: 175 us
  blocking collectives  67.1 us (38%)
  matrix products  36.1 us (21%)
  waiting for transfers between devices  34.3 us (19%)
  starting transfers between devices  14.8 us (8%)
  other arithmetic  13.6 us (8%)
  local copies, waits for them, and re-layouts  8.93 us (5%)
    all_to_all x1, blocking collectives, on_device(): lax.all_to_all(outgoing[:, q * piece:(q + 1) * piece], 'seq', split_axis=...  34.3 us
    all_to_all x1, blocking collectives, on_device(): lax.all_to_all(served, 'seq', split_axis=0, concat_axis=0, tiled=True)  32.8 us
    dot_general x4, matrix products, expert_hidden(): jnp.einsum('rd,kdf->krf', rows, expert_in, preferred_element_type=jnp.flo...  19 us
    all_to_all x1, waiting for transfers between devices, on_device(): lax.all_to_all(served, 'seq', split_axis=0, concat_axis=0, tiled=True)  14.1 us
    all_to_all x1, waiting for transfers between devices, on_device(): lax.all_to_all(outgoing[:, q * piece:(q + 1) * piece], 'seq', split_axis=...  13.9 us
    ppermute x6, waiting for transfers between devices, swap_exp(): return lax.ppermute(x, 'exp', [(i, (i + 1) % size) for i in range(size)])  6.19 us
    unnamed x26, local copies, waits for them, and re-layouts  5.63 us
    ppermute x1, starting transfers between devices, shifted(): return lax.ppermute(shard, axis, pairs)  4.87 us
  transfers between devices with their start and end apart: 9, of which 5 were waited for; matrix products, arithmetic and copies ran while one was open for 20% of the time, Pallas kernels for 0%

profile of v4, /device:TPU:0, one launch (start us, length us, event | category | flops | bytes accessed | tf_op | source)
XLA Modules:
  0.0 175.3 jit_solution(17801960278995483247)
XLA Ops:
  0.0 0.9 slice_bitcast_fusion
  0.9 0.6 pad_maximum_fusion.1
  1.6 4.9 %collective-permute-start = (bf16[2,128,128]{2,1,0:T(8,128)(2,1)}, bf16[2,128,128]{2,1,0:T(8,128)(2,1)S(1)}, u32[]{:S(2)}, u32[]{:S(2)}) collective-permute-start(bf16[2,128,128]{2,1,0:T(8,128)(2,1)} %pad_maximum_fusion.1), channel_id=1, source_target_pairs={{0,2},{2,4},{4,6},{6,8},{8,10},{10,12},{12,14},{1,3},{3,5},{5,7},{... | collective-permute-start | bytes 196616 | tf_op jit(solution)/shard_map/ppermute | solution.py:19
  6.5 0.1 fusion.57
  6.5 0.9 copy.34
  7.5 0.9 copy.32
  8.4 2.0 %copy.35 = bf16[256,1024]{0,1:T(8,128)(2,1)} copy(bf16[256,1024]{1,0:T(8,128)(2,1)} %param.12) | data formatting | bytes 1048576 | tf_op args[0]
  10.5 0.1 max.17
  10.6 0.0 collective-permute-done
  10.6 0.1 copy.33
  10.7 2.1 %fusion.1 = (f32[2,8,256]{2,1,0:T(8,128)S(1)}, f32[2,384,256,8]{2,1,3,0:T(8,128)S(1)}) fusion(pred[256,384]{0,1:T(8,128)(4,1)S(1)} %fusion.57, bf16[256,2,8,64]{0,3,2,1:T(8,128)(2,1)} %bitcast.132, bf16[256,2,64]{0,2,1:T(8,128)(2,1)S(1)} %bitcast.136, bf16[128,2,64]{0,2,1:T(8,128)(2,1)S(1)} %bitcast.137), kind=kOutput, calls=%fused_computation.5 | convolution fusion | flops 206237696 | bytes 7028736 | tf_op jit(solution)/shard_map/qhgd,khd->hgqk/dot_general | solution.py:38
  12.8 0.1 broadcast_maximum_fusion
  12.9 1.3 fusion
  14.2 1.3 copy-done.1
  15.5 0.1 exponential_add_fusion
  15.6 0.1 copy.31
  15.7 4.6 %fusion.34 = bf16[2,64,8,256]{3,1,2,0:T(8,128)(2,1)S(1)} fusion(f32[2,384,256,8]{2,1,3,0:T(8,128)} %copy-done.1, f32[2,8,256]{2,1,0:T(8,128)S(1)} %exponential_add_fusion, f32[2,8,256]{2,1,0:T(8,128)S(1)} %broadcast_maximum_fusion, pred[256,384]{0,1:T(8,128)(4,1)S(1)} %fusion.57, bf16[256,2,64]{0,2,1:T(8,128)(2,1)S(1)} %bitcast.138, ...), kind=kOutput, calls=%fused_computation.43 | convolution fusion | flops 209649664 | bytes 7045120 | tf_op jit(solution)/shard_map/hgqk,khd->qhgd/dot_general | solution.py:50
  20.3 0.0 copy-start.5
  20.3 2.2 %fusion.76 = f32[256,1536]{1,0:T(8,128)} fusion(bf16[256,1024]{0,1:T(8,128)(2,1)S(1)} %bitcast.135, bf16[1024,1536]{1,0:T(8,128)(2,1)S(1)} %copy-done), kind=kOutput, calls=%fused_computation.107 | convolution fusion | flops 805306368 | bytes 5242880 | tf_op jit(solution)/shard_map/dot_general | solution.py:103
  22.4 0.1 copy.37
  22.6 0.1 eq.69
  22.7 0.1 eq.65
  22.8 2.3 %reduce-window.6 = s32[8,8,128]{2,1,0:T(8,128)S(1)} reduce-window(s32[8,8,128]{2,1,0:T(8,128)S(1)} %fusion.65, s32[]{:T(128)} %constant.16.clone.1), window={size=1x1x128 pad=0_0x0_0x127_0}, to_apply=%region_2.3 | reduce-window | flops 1040384 | bytes 65540 | tf_op jit(solution)/shard_map/reduce-window
  25.1 0.3 slice_reduce_fusion
  25.4 0.2 reduce-window.9
  25.6 0.1 add_bitcast_fusion
  25.7 0.1 sub.47
  25.8 0.1 copy.40
  26.0 0.1 copy.41
  26.1 0.4 fusion.32
  26.5 0.0 copy-start.6
  26.6 2.4 %multiply_reduce_fusion.1 = (f32[256]{0:T(256)S(1)}, f32[256,1536]{1,0:T(8,128)S(1)}) fusion(f32[256,1536]{1,0:T(8,128)} %fusion.76, f32[256,1536]{1,0:T(8,128)} %collective-permute-done.1, bf16[256,1536]{1,0:T(8,128)(2,1)} %param.18), kind=kLoop, calls=%fused_computation.40 | loop fusion | flops 1965824 | bytes 5506048 | tf_op jit(solution)/shard_map/reduce_sum | solution.py:28
  29.0 0.9 convolution_convert_fusion
  29.9 0.2 copy-done.2
  30.1 1.2 fusion.74
  31.3 34.3 %all_to_all.20 = bf16[8,48,1536]{2,1,0:T(8,128)(2,1)} all-to-all(bf16[8,48,1536]{2,1,0:T(8,128)(2,1)S(1)} %get-tuple-element.17), channel_id=1, replica_groups=mesh['groups'=2,'seq'=8,'exp'=2] {'seq'}, dimensions={0} | all-to-all | bytes 2359296 | tf_op jit(solution)/shard_map/all_to_all | solution.py:132
  65.7 4.4 %all-to-all-start.2 = ((bf16[8,48,1536]{2,1,0:T(8,128)(2,1)}), bf16[8,48,1536]{2,1,0:T(8,128)(2,1)}, u32[]{:S(2)}, u32[]{:S(2)}) async-start(bf16[8,48,1536]{2,1,0:T(8,128)(2,1)} %get-tuple-element.18), calls=%async_computation.2 | async-start | bytes 2359296 | tf_op jit(solution)/shard_map/all_to_all | solution.py:132
  70.1 4.7 %fusion.20 = f32[2,384,768]{2,1,0:T(8,128)S(1)} fusion(bf16[384,1536,1]{1,0,2:T(8,128)(2,1)} %bitcast.18, bf16[1,2,1536,768]{3,2,1,0:T(8,128)(2,1)} %param.20), kind=kOutput, calls=%fused_computation.33 | convolution fusion | flops 1811939328 | bytes 8257536 | tf_op jit(solution)/shard_map/rd,kdf->krf/dot_general | solution.py:55
  74.8 0.3 fusion.55
  75.2 0.0 copy-start.7
  75.2 4.8 %fusion.23 = f32[2,384,768]{2,1,0:T(8,128)S(1)} fusion(bf16[384,1536,1]{1,0,2:T(8,128)(2,1)} %bitcast.25, bf16[1,2,1536,768]{3,2,1,0:T(8,128)(2,1)} %param.20), kind=kOutput, calls=%fused_computation.34 | convolution fusion | flops 1811939328 | bytes 8257536 | tf_op jit(solution)/shard_map/rd,kdf->krf/dot_general | solution.py:55
  80.0 1.1 convolution_convert_fusion.3
  81.1 0.6 collective-permute-start.3
  81.7 1.1 convolution_convert_fusion.4
  82.8 1.4 collective-permute-done.3
  84.2 1.4 fusion.15
  85.5 13.9 %all-to-all-done.2 = bf16[8,48,1536]{2,1,0:T(8,128)(2,1)} async-done(((bf16[8,48,1536]{2,1,0:T(8,128)(2,1)}), bf16[8,48,1536]{2,1,0:T(8,128)(2,1)}, u32[]{:S(2)}, u32[]{:S(2)}) %all-to-all-start.2) | async-done | bytes 1179680 | tf_op jit(solution)/shard_map/all_to_all | solution.py:132
  99.5 4.3 %all-to-all-start.1 = ((bf16[8,48,1536]{2,1,0:T(8,128)(2,1)}), bf16[8,48,1536]{2,1,0:T(8,128)(2,1)}, u32[]{:S(2)}, u32[]{:S(2)}) async-start(bf16[8,48,1536]{2,1,0:T(8,128)(2,1)} %fusion.15), calls=%async_computation.1 | async-start | bytes 2359296 | tf_op jit(solution)/shard_map/all_to_all | solution.py:144
  103.7 4.7 %fusion.26 = f32[2,384,768]{2,1,0:T(8,128)S(1)} fusion(bf16[384,1536,1]{1,0,2:T(8,128)(2,1)} %bitcast.30, bf16[1,2,1536,768]{3,2,1,0:T(8,128)(2,1)} %param.20), kind=kOutput, calls=%fused_computation.35 | convolution fusion | flops 1811939328 | bytes 8257536 | tf_op jit(solution)/shard_map/rd,kdf->krf/dot_general | solution.py:55
  108.4 0.3 fusion.56
  108.8 0.0 copy-start.8
  108.8 4.8 %fusion.29 = f32[2,384,768]{2,1,0:T(8,128)S(1)} fusion(bf16[384,1536,1]{1,0,2:T(8,128)(2,1)} %bitcast.35, bf16[1,2,1536,768]{3,2,1,0:T(8,128)(2,1)} %param.20), kind=kOutput, calls=%fused_computation.36 | convolution fusion | flops 1811939328 | bytes 8257536 | tf_op jit(solution)/shard_map/rd,kdf->krf/dot_general | solution.py:55
  113.7 1.1 convolution_convert_fusion.1
  114.8 0.6 collective-permute-start.5
  115.3 1.1 convolution_convert_fusion.2
  116.4 1.4 collective-permute-done.5
  117.8 1.3 fusion.14
  119.1 14.1 %all-to-all-done.1 = bf16[8,48,1536]{2,1,0:T(8,128)(2,1)} async-done(((bf16[8,48,1536]{2,1,0:T(8,128)(2,1)}), bf16[8,48,1536]{2,1,0:T(8,128)(2,1)}, u32[]{:S(2)}, u32[]{:S(2)}) %all-to-all-start.1) | async-done | bytes 1179680 | tf_op jit(solution)/shard_map/all_to_all | solution.py:144
  133.3 32.8 %all_to_all.21 = bf16[8,48,1536]{2,1,0:T(8,128)(2,1)S(1)} all-to-all(bf16[8,48,1536]{2,1,0:T(8,128)(2,1)} %fusion.14), channel_id=1, replica_groups=mesh['groups'=2,'seq'=8,'exp'=2] {'seq'}, dimensions={0} | all-to-all | bytes 2359296 | tf_op jit(solution)/shard_map/all_to_all | solution.py:144
  166.0 1.5 pad_maximum_fusion
  167.5 3.0 %multiply_reduce_fusion = f32[256,1536]{1,0:T(8,128)S(1)} fusion(bf16[768,1536,1]{1,0,2:T(8,128)(2,1)S(1)} %bitcast.131, f32[256,4]{0,1:T(4,128)S(1)} %copy-done.9, s32[256,4]{0,1:T(4,128)S(1)} %copy.41), kind=kOutput, calls=%fused_computation.1 | convolution fusion | flops 2419458048 | bytes 3940352 | tf_op jit(solution)/shard_map/dot_general | solution.py:146
  170.6 0.1 collective-permute-start.6
  170.7 3.4 %collective-permute-done.6 = f32[256,1536]{1,0:T(8,128)S(1)} collective-permute-done((f32[256,1536]{1,0:T(8,128)S(1)}, f32[256,1536]{1,0:T(8,128)S(1)}, u32[]{:S(2)}, u32[]{:S(2)}) %collective-permute-start.6) | collective-permute-done | bytes 1572896 | tf_op jit(solution)/shard_map/ppermute | solution.py:24
  174.1 1.2 add_convert_fusion
  (31 shorter events, 0.1 us)
Async XLA Ops:
  0.0 20.3 %copy-start = (bf16[1024,1536]{1,0:T(8,128)(2,1)S(1)}, bf16[1024,1536]{1,0:T(8,128)(2,1)}, u32[]{:S(2)}) copy-start(bf16[1024,1536]{1,0:T(8,128)(2,1)} %param.17) | copy-start | bytes 9437188
  0.0 10.5 %copy-start.10 = (f32[16]{0:T(128)S(1)}, f32[16]{0:T(128)}, u32[]{:S(2)}) copy-start(f32[16]{0:T(128)} %param.16) | copy-start | bytes 196
  0.0 10.6 %copy-start.4 = (bf16[2,128,128]{2,1,0:T(8,128)(2,1)S(1)}, bf16[2,128,128]{2,1,0:T(8,128)(2,1)}, u32[]{:S(2)}) copy-start(bf16[2,128,128]{2,1,0:T(8,128)(2,1)} %param.15) | copy-start | bytes 196612
  1.6 9.0 %collective-permute-start = (bf16[2,128,128]{2,1,0:T(8,128)(2,1)}, bf16[2,128,128]{2,1,0:T(8,128)(2,1)S(1)}, u32[]{:S(2)}, u32[]{:S(2)}) collective-permute-start(bf16[2,128,128]{2,1,0:T(8,128)(2,1)} %pad_maximum_fusion.1), channel_id=1, source_target_pairs={{0,2},{2,4},{4,6},{6,8},{8,10},{10,12},{12,14},{1,3},{3,5},{5,7},{... | collective-permute-start | bytes 196616 | tf_op jit(solution)/shard_map/ppermute | solution.py:19
  12.8 2.7 %copy-start.1 = (f32[2,384,256,8]{2,1,3,0:T(8,128)}, f32[2,384,256,8]{2,1,3,0:T(8,128)S(1)}, u32[]{:S(2)}) copy-start(f32[2,384,256,8]{2,1,3,0:T(8,128)S(1)} %get-tuple-element.22) | copy-start | bytes 18874372
  20.3 2.2 %copy-start.5 = (s32[256,4]{0,1:T(4,128)S(1)}, s32[256,4]{0,1:T(4,128)}, u32[]{:S(2)}) copy-start(s32[256,4]{0,1:T(4,128)} %param.22) | copy-start | bytes 12292
  22.4 4.1 %collective-permute-start.1 = (f32[256,1536]{1,0:T(8,128)}, f32[256,1536]{1,0:T(8,128)}, u32[]{:S(2)}, u32[]{:S(2)}) collective-permute-start(f32[256,1536]{1,0:T(8,128)} %fusion.76), channel_id=1, source_target_pairs={{0,1},{1,0},{2,3},{3,2},{4,5},{5,4},{6,7},{7,6},{8,9},{9,8},{10,11... | collective-permute-start | bytes 4718600 | tf_op jit(solution)/shard_map/ppermute | solution.py:24
  26.5 2.5 %copy-start.6 = (f32[1536]{0:T(1024)S(1)}, f32[1536]{0:T(1024)}, u32[]{:S(2)}) copy-start(f32[1536]{0:T(1024)} %param.19) | copy-start | bytes 18436
  29.0 1.2 copy-start.2
  65.7 9.5 %collective-permute-start.2 = (bf16[8,48,1536]{2,1,0:T(8,128)(2,1)}, bf16[8,48,1536]{2,1,0:T(8,128)(2,1)}, u32[]{:S(2)}, u32[]{:S(2)}) collective-permute-start(bf16[8,48,1536]{2,1,0:T(8,128)(2,1)} %all_to_all.20), channel_id=1, source_target_pairs={{0,1},{1,0},{2,3},{3,2},{4,5},{5,4},{6,7},{7,6},{8,9},{9,8},{10,11... | collective-permute-start | bytes 3538952 | tf_op jit(solution)/shard_map/ppermute | solution.py:24
  65.7 33.8 %all-to-all-start.2 = ((bf16[8,48,1536]{2,1,0:T(8,128)(2,1)}), bf16[8,48,1536]{2,1,0:T(8,128)(2,1)}, u32[]{:S(2)}, u32[]{:S(2)}) async-start(bf16[8,48,1536]{2,1,0:T(8,128)(2,1)} %get-tuple-element.18), calls=%async_computation.2 | async-start | bytes 2359296 | tf_op jit(solution)/shard_map/all_to_all | solution.py:132
  75.2 4.8 %copy-start.7 = (bf16[1,768,1536]{2,1,0:T(8,128)(2,1)S(1)}, bf16[1,768,1536]{2,1,0:T(8,128)(2,1)}, u32[]{:S(2)}) copy-start(bf16[1,768,1536]{2,1,0:T(8,128)(2,1)} %param.21) | copy-start | bytes 7077892
  81.1 3.0 %collective-permute-start.3 = (bf16[8,48,1536]{2,1,0:T(8,128)(2,1)S(1)}, bf16[8,48,1536]{2,1,0:T(8,128)(2,1)S(1)}, u32[]{:S(2)}, u32[]{:S(2)}) collective-permute-start(bf16[8,48,1536]{2,1,0:T(8,128)(2,1)S(1)} %bitcast.141), channel_id=1, source_target_pairs={{0,1},{1,0},{2,3},{3,2},{4,5},{5,4},{6,7},{7,6},{8,9},{9,8},{10,11... | collective-permute-start | bytes 3538952 | tf_op jit(solution)/shard_map/ppermute | solution.py:24
  99.5 9.3 %collective-permute-start.4 = (bf16[8,48,1536]{2,1,0:T(8,128)(2,1)}, bf16[8,48,1536]{2,1,0:T(8,128)(2,1)}, u32[]{:S(2)}, u32[]{:S(2)}) collective-permute-start(bf16[8,48,1536]{2,1,0:T(8,128)(2,1)} %all-to-all-done.2), channel_id=1, source_target_pairs={{0,1},{1,0},{2,3},{3,2},{4,5},{5,4},{6,7},{7,6},{8,9},{9,8},{10,11... | collective-permute-start | bytes 3538952 | tf_op jit(solution)/shard_map/ppermute | solution.py:24
  99.5 33.8 %all-to-all-start.1 = ((bf16[8,48,1536]{2,1,0:T(8,128)(2,1)}), bf16[8,48,1536]{2,1,0:T(8,128)(2,1)}, u32[]{:S(2)}, u32[]{:S(2)}) async-start(bf16[8,48,1536]{2,1,0:T(8,128)(2,1)} %fusion.15), calls=%async_computation.1 | async-start | bytes 2359296 | tf_op jit(solution)/shard_map/all_to_all | solution.py:144
  108.8 4.8 %copy-start.8 = (bf16[1,768,1536]{2,1,0:T(8,128)(2,1)S(1)}, bf16[1,768,1536]{2,1,0:T(8,128)(2,1)}, u32[]{:S(2)}) copy-start(bf16[1,768,1536]{2,1,0:T(8,128)(2,1)} %param.21) | copy-start | bytes 7077892
  114.8 3.0 %collective-permute-start.5 = (bf16[8,48,1536]{2,1,0:T(8,128)(2,1)S(1)}, bf16[8,48,1536]{2,1,0:T(8,128)(2,1)S(1)}, u32[]{:S(2)}, u32[]{:S(2)}) collective-permute-start(bf16[8,48,1536]{2,1,0:T(8,128)(2,1)S(1)} %bitcast.142), channel_id=1, source_target_pairs={{0,1},{1,0},{2,3},{3,2},{4,5},{5,4},{6,7},{7,6},{8,9},{9,8},{10,11... | collective-permute-start | bytes 3538952 | tf_op jit(solution)/shard_map/ppermute | solution.py:24
  166.0 1.5 copy-start.9
  167.5 6.5 %copy-start.3 = (f32[256,1536]{1,0:T(8,128)S(1)}, f32[256,1536]{1,0:T(8,128)}, u32[]{:S(2)}) copy-start(f32[256,1536]{1,0:T(8,128)} %copy-done.2) | copy-start | bytes 4718596
  170.6 3.5 %collective-permute-start.6 = (f32[256,1536]{1,0:T(8,128)S(1)}, f32[256,1536]{1,0:T(8,128)S(1)}, u32[]{:S(2)}, u32[]{:S(2)}) collective-permute-start(f32[256,1536]{1,0:T(8,128)S(1)} %multiply_reduce_fusion), channel_id=1, source_target_pairs={{0,1},{1,0},{2,3},{3,2},{4,5},{5,4},{6,7},{7,6},{8,9},{9,8},{10,11... | collective-permute-start | bytes 4718600 | tf_op jit(solution)/shard_map/ppermute | solution.py:24

commit v5 on v3

--- a/solution.py
+++ b/solution.py
@@ -1,6 +1,8 @@
 import jax
 import jax.numpy as jnp
 from jax import lax
+from jax.experimental import pallas as pl
+from jax.experimental.pallas import tpu as pltpu
 from jax.sharding import PartitionSpec as P
 
 HEAD_DIM = 64
@@ -55,6 +57,68 @@
     gate_val = gate_up[0]
     up_val = gate_up[1]
     return ((up_val + 1.0) * gate_val * jax.nn.sigmoid(GLU_ALPHA * gate_val)).astype(jnp.bfloat16)
+
+
+def attention_kernel(sink_ref, q_ref, k_ref, v_ref, o_ref):
+    rows = q_ref.shape[0]
+    keys = k_ref.shape[2]
+    pair_cols = 2 * HEAD_DIM
+    pairs = q_ref.shape[1] // pair_cols
+    per_kv = pairs // k_ref.shape[0]
+    q_pos = lax.broadcasted_iota(jnp.int32, (rows, keys), 0)
+    k_pos = lax.broadcasted_iota(jnp.int32, (rows, keys), 1)
+    allowed = (k_pos > q_pos) & (k_pos <= q_pos + WINDOW)
+    for j in range(pairs):
+        kv = j // per_kv
+        q_pair = q_ref[:, j * pair_cols : (j + 1) * pair_cols]
+        total = None
+        for a in range(2):
+            scores = lax.dot_general(
+                q_pair, k_ref[kv, a], (((1,), (1,)), ((), ())), preferred_element_type=jnp.float32
+            ) * HEAD_DIM ** (-0.5)
+            scores = jnp.where(allowed, scores, -jnp.inf)
+            sink = sink_ref[2 * j + a]
+            largest = jnp.maximum(jnp.max(scores, axis=-1, keepdims=True), sink)
+            weights_exp = jnp.exp(scores - largest)
+            denominator = jnp.exp(sink - largest) + jnp.sum(weights_exp, axis=-1, keepdims=True)
+            probs = (weights_exp / denominator).astype(jnp.bfloat16)
+            out = jnp.dot(probs, v_ref[kv, a], preferred_element_type=jnp.float32)
+            total = out if total is None else total + out
+        o_ref[:, j * pair_cols : (j + 1) * pair_cols] = total.astype(o_ref.dtype)
+
+
+def placed_heads(rows_all):
+    keys, cols = rows_all.shape
+    kv_count = cols // HEAD_DIM
+    zeros = jnp.zeros((keys, HEAD_DIM), rows_all.dtype)
+    out = []
+    for kv in range(kv_count):
+        head = rows_all[:, kv * HEAD_DIM : (kv + 1) * HEAD_DIM]
+        out.append(jnp.stack([jnp.concatenate([head, zeros], 1), jnp.concatenate([zeros, head], 1)]))
+    return jnp.stack(out)
+
+
+def attend_kernel(queries, keys_all, values_all, sink_logits):
+    rows, cols = queries.shape
+    keys = keys_all.shape[0]
+    heads = cols // HEAD_DIM
+    cost = pl.CostEstimate(
+        flops=4 * 2 * rows * keys * 2 * HEAD_DIM * heads,
+        transcendentals=rows * keys * heads,
+        bytes_accessed=2 * rows * cols * 2 + 2 * 2 * keys_all.size * 2 * 2,
+    )
+    return pl.pallas_call(
+        attention_kernel,
+        out_shape=jax.ShapeDtypeStruct((rows, cols), jnp.bfloat16),
+        in_specs=[
+            pl.BlockSpec(memory_space=pltpu.SMEM),
+            pl.BlockSpec(memory_space=pltpu.VMEM),
+            pl.BlockSpec(memory_space=pltpu.VMEM),
+            pl.BlockSpec(memory_space=pltpu.VMEM),
+        ],
+        out_specs=pl.BlockSpec(memory_space=pltpu.VMEM),
+        cost_estimate=cost,
+    )(sink_logits, queries, placed_heads(keys_all), placed_heads(values_all))
 
 
 def on_device(
@@ -78,8 +142,7 @@
     prior = jnp.where(lax.axis_index("seq") == 0, cached_rows, received)
     keys_all = jnp.concatenate([prior[0], key_rows], axis=0)
     values_all = jnp.concatenate([prior[1], values], axis=0)
-    block_rows = min(tok_rows, 512)
-    pieces = attend_block(queries, keys_all, values_all, sink_logits, block_rows, window_rows)
+    pieces = attend_kernel(queries, keys_all, values_all, sink_logits)
     partial_rows = jnp.dot(pieces, out_weight, preferred_element_type=jnp.float32)
     mixed_rows = residual.astype(jnp.float32) + (partial_rows + swap_exp(partial_rows))
     normed = rms_normalize(mixed_rows, norm_gain)

time: 171 us -> 173 us (1.012)
  Pallas kernels: 0 us -> 6.58 us
  local copies, waits for them, and re-layouts: 8.14 us -> 2.37 us
  matrix products: 24.4 us -> 18.8 us
  other arithmetic: 10.5 us -> 13.6 us
  blocking collectives: 116 us -> 118 us
  waiting for transfers between devices: 5.61 us -> 7.49 us
    dot_general x2 -> x0, matrix products: 6.69 us -> none  [the longest x1 4.57 us: attend_block(): jnp.einsum('hgqk,khd->qhgd', probs, value_block, preferred_element_type=j...]
    pallas_call x0 -> x1, Pallas kernels: none -> 6.58 us  [attend_kernel(): pl.pallas_call(attention_kernel, out_shape=jax.ShapeDtypeStruct((rows, co...]
    unnamed x20 -> x15, local copies, waits for them, and re-layouts: 5.39 us -> 0.17 us
    concatenate x0 -> x3, other arithmetic: none -> 2.95 us  [the longest x1 1.01 us: on_device(): values_all = jnp.concatenate([prior[1], values], axis=0)]
    ppermute x1, waiting for transfers between devices: 0.01 us -> 1.88 us  [shifted(): return lax.ppermute(shard, axis, pairs)]
    all_to_all x1, blocking collectives: 58.3 us -> 60.1 us  [on_device(): lax.all_to_all(outgoing, 'seq', split_axis=0, concat_axis=0, tiled=True)]
    another operation x2 -> x8, other arithmetic: 2.43 us -> 4.07 us
  transfers between devices with their start and end apart: 5 -> 5, of which waited for: 2 -> 3; matrix products, arithmetic and copies ran while one was open for 9% -> 6% of each run, Pallas kernels for 0% -> 0%
where the time goes in v5:
time: 173 us
  blocking collectives  118 us (68%)
  matrix products  18.8 us (11%)
  other arithmetic  13.6 us (8%)
  waiting for transfers between devices  7.49 us (4%)
  Pallas kernels  6.58 us (4%)
  starting transfers between devices  5.63 us (3%)
  local copies, waits for them, and re-layouts  2.37 us (1%)
    all_to_all x1, blocking collectives, on_device(): lax.all_to_all(outgoing, 'seq', split_axis=0, concat_axis=0, tiled=True)  60.1 us
    all_to_all x1, blocking collectives, on_device(): lax.all_to_all(result, 'seq', split_axis=0, concat_axis=0, tiled=True)  57.8 us
    dot_general x2, matrix products, expert_hidden(): jnp.einsum('rd,kdf->krf', rows, expert_in, preferred_element_type=jnp.flo...  7.62 us
    pallas_call x1, Pallas kernels, attend_kernel(): pl.pallas_call(attention_kernel, out_shape=jax.ShapeDtypeStruct((rows, co...  6.58 us
    ppermute x4, waiting for transfers between devices, swap_exp(): return lax.ppermute(x, 'exp', [(i, (i + 1) % size) for i in range(size)])  5.61 us
    ppermute x1, starting transfers between devices, shifted(): return lax.ppermute(shard, axis, pairs)  5.01 us
  transfers between devices with their start and end apart: 5, of which 3 were waited for; matrix products, arithmetic and copies ran while one was open for 6% of the time, Pallas kernels for 0%

profile of v5, /device:TPU:0, one launch (start us, length us, event | category | flops | bytes accessed | tf_op | source)
XLA Modules:
  0.0 172.6 jit_solution(4048064551301535374)
XLA Ops:
  0.0 0.0 copy-start
  0.0 0.9 slice_bitcast_fusion
  0.9 5.0 %collective-permute-start = (bf16[2,128,128]{2,1,0:T(8,128)(2,1)S(1)}, bf16[2,128,128]{2,1,0:T(8,128)(2,1)S(1)}, u32[]{:S(2)}, u32[]{:S(2)}) collective-permute-start(bf16[2,128,128]{2,1,0:T(8,128)(2,1)S(1)} %pad_maximum_fusion.4), channel_id=1, source_target_pairs={{0,2},{2,4},{4,6},{6,8},{8,10},{10,12},{12,14},{1,3},{3,5},{5,7},{... | collective-permute-start | bytes 196616 | tf_op jit(solution)/shard_map/ppermute | solution.py:20
  6.0 1.9 %collective-permute-done = bf16[2,128,128]{2,1,0:T(8,128)(2,1)S(1)} collective-permute-done((bf16[2,128,128]{2,1,0:T(8,128)(2,1)S(1)}, bf16[2,128,128]{2,1,0:T(8,128)(2,1)S(1)}, u32[]{:S(2)}, u32[]{:S(2)}) %collective-permute-start) | collective-permute-done | bytes 65568 | tf_op jit(solution)/shard_map/ppermute | solution.py:20
  7.8 0.8 broadcast_select_fusion
  8.7 1.0 slice_maximum_fusion
  9.7 0.1 pad_bitcast_fusion.2
  9.8 0.1 pad_bitcast_fusion.1
  9.9 1.0 slice_maximum_fusion.1
  11.0 0.1 pad_bitcast_fusion.5
  11.1 0.1 pad_bitcast_fusion.4
  11.2 0.9 maximum_select_fusion.1
  12.2 0.8 pad_maximum_fusion.1.v_ref
  13.0 0.8 pad_maximum_fusion.k_ref
  13.8 6.6 %shard_map.118 = bf16[256,1024]{1,0:T(8,128)(2,1)} custom-call(f32[16]{0:T(128)} %sink_ref.1, bf16[256,1024]{1,0:T(8,128)(2,1)} %q_ref.1, bf16[2,2,384,128]{3,2,1,0:T(8,128)(2,1)} %pad_maximum_fusion.k_ref, bf16[2,2,384,128]{3,2,1,0:T(8,128)(2,1)} %pad_maximum_fusion.1.v_ref), custom_call_target="tpu_custom_call" | custom-call | flops 1610612736 | bytes 1835008 | tf_op jit(solution)/shard_map/pallas_call | solution.py:110
  20.3 0.0 copy-done
  20.3 0.0 copy-start.1
  20.3 3.2 %fusion.36 = f32[256,1536]{1,0:T(8,128)} fusion(bf16[256,1024]{1,0:T(8,128)(2,1)} %shard_map.118, bf16[1024,1536]{1,0:T(8,128)(2,1)S(1)} %copy-done), kind=kOutput, calls=%fused_computation.76 | convolution fusion | flops 805306368 | bytes 5242880 | tf_op jit(solution)/shard_map/dot_general | solution.py:146
  23.5 0.0 collective-permute-start.1
  23.5 0.0 copy-done.1
  23.5 0.1 copy.19
  23.7 0.1 eq.69
  23.8 0.1 eq.65
  23.9 2.3 %reduce-window.6 = s32[8,8,128]{2,1,0:T(8,128)S(1)} reduce-window(s32[8,8,128]{2,1,0:T(8,128)S(1)} %fusion.32, s32[]{:T(128)} %constant.16.clone.1), window={size=1x1x128 pad=0_0x0_0x127_0}, to_apply=%region_0.1 | reduce-window | flops 1040384 | bytes 65540 | tf_op jit(solution)/shard_map/reduce-window
  26.2 0.3 slice_reduce_fusion
  26.5 0.2 reduce-window.9
  26.6 0.1 add_bitcast_fusion
  26.8 0.1 sub.26
  26.9 0.1 copy.22
  27.1 0.1 copy.23
  27.2 0.4 fusion.22
  27.6 0.0 copy-start.2
  27.6 0.0 collective-permute-done.1
  27.7 0.0 slice-start
  27.7 2.6 %multiply_reduce_fusion.1 = (f32[256]{0:T(256)S(1)}, f32[256,1536]{1,0:T(8,128)S(1)}) fusion(f32[256,1536]{1,0:T(8,128)} %fusion.36, f32[256,1536]{1,0:T(8,128)} %collective-permute-done.1, bf16[256,1536]{1,0:T(8,128)(2,1)} %param.18), kind=kLoop, calls=%fused_computation.29 | loop fusion | flops 1965824 | bytes 5506048 | tf_op jit(solution)/shard_map/reduce_sum | solution.py:29
  30.2 0.0 copy-done.2
  30.3 0.0 slice-start.1
  30.3 0.9 convolution_convert_fusion.2
  31.2 60.1 %all_to_all.10 = bf16[8,96,1536]{2,1,0:T(8,128)(2,1)S(1)} all-to-all(bf16[8,96,1536]{2,1,0:T(8,128)(2,1)S(1)} %bitcast.91), channel_id=1, replica_groups=mesh['groups'=2,'seq'=8,'exp'=2] {'seq'}, dimensions={0} | all-to-all | bytes 4718592 | tf_op jit(solution)/shard_map/all_to_all | solution.py:172
  91.3 0.0 collective-permute-start.2
  91.3 0.0 slice-done
  91.3 0.0 slice-done.1
  91.3 3.8 %fusion.16 = f32[2,768,768]{2,1,0:T(8,128)S(1)} fusion(bf16[768,1536,1]{1,0,2:T(8,128)(2,1)S(1)} %bitcast.93, bf16[1,2,1536,768]{3,2,1,0:T(8,128)(2,1)S(1)} %bitcast.99), kind=kOutput, calls=%fused_computation.24 | convolution fusion | flops 3623878656 | bytes 11796480 | tf_op jit(solution)/shard_map/rd,kdf->krf/dot_general | solution.py:56
  95.1 0.7 fusion.27
  95.8 0.0 collective-permute-done.2
  95.8 0.0 copy-start.3
  95.8 3.8 %fusion.19 = f32[2,768,768]{2,1,0:T(8,128)S(1)} fusion(bf16[768,1536,1]{1,0,2:T(8,128)(2,1)S(1)} %bitcast.100, bf16[1,2,1536,768]{3,2,1,0:T(8,128)(2,1)S(1)} %bitcast.99), kind=kOutput, calls=%fused_computation.25 | convolution fusion | flops 3623878656 | bytes 11796480 | tf_op jit(solution)/shard_map/rd,kdf->krf/dot_general | solution.py:56
  99.6 0.0 copy-done.3
  99.6 2.1 %convolution_convert_fusion = bf16[768,1536]{1,0:T(8,128)(2,1)S(1)} fusion(bf16[1,768,1536]{2,1,0:T(8,128)(2,1)S(1)} %copy-done.3, f32[2,768,768]{2,1,0:T(8,128)S(1)} %fusion.19), kind=kOutput, calls=%fused_computation.7 | convolution fusion | flops 1817837568 | bytes 9437184 | tf_op jit(solution)/shard_map/dot_general | solution.py:178
  101.7 0.5 collective-permute-start.3
  102.3 2.0 %convolution_convert_fusion.1 = bf16[768,1536]{1,0:T(8,128)(2,1)S(1)} fusion(bf16[768,768]{1,0:T(8,128)(2,1)S(1)} %fusion.27, bf16[1,768,1536]{2,1,0:T(8,128)(2,1)S(1)} %copy-done.3), kind=kOutput, calls=%fused_computation.8 | convolution fusion | flops 1813118976 | bytes 5898240 | tf_op jit(solution)/shard_map/dot_general | solution.py:183
  104.2 2.2 %collective-permute-done.3 = bf16[8,96,1536]{2,1,0:T(8,128)(2,1)S(1)} collective-permute-done((bf16[8,96,1536]{2,1,0:T(8,128)(2,1)S(1)}, bf16[8,96,1536]{2,1,0:T(8,128)(2,1)S(1)}, u32[]{:S(2)}, u32[]{:S(2)}) %collective-permute-start.3) | collective-permute-done | bytes 2359328 | tf_op jit(solution)/shard_map/ppermute | solution.py:25
  106.4 0.7 fusion
  107.1 0.0 copy-start.4
  107.1 57.8 %all_to_all.11 = bf16[8,96,1536]{2,1,0:T(8,128)(2,1)S(1)} all-to-all(bf16[8,96,1536]{2,1,0:T(8,128)(2,1)S(1)} %fusion), channel_id=1, replica_groups=mesh['groups'=2,'seq'=8,'exp'=2] {'seq'}, dimensions={0} | all-to-all | bytes 4718592 | tf_op jit(solution)/shard_map/all_to_all | solution.py:188
  164.9 0.0 copy-done.4
  164.9 3.0 %multiply_reduce_fusion = f32[256,1536]{1,0:T(8,128)S(1)} fusion(bf16[768,1536,1]{1,0,2:T(8,128)(2,1)S(1)} %bitcast.94, f32[256,4]{0,1:T(4,128)S(1)} %copy-done.4, s32[256,4]{0,1:T(4,128)S(1)} %copy.23), kind=kOutput, calls=%fused_computation | convolution fusion | flops 2419458048 | bytes 3940352 | tf_op jit(solution)/shard_map/dot_general | solution.py:189
  167.9 0.1 collective-permute-start.4
  168.0 3.4 %collective-permute-done.4 = f32[256,1536]{1,0:T(8,128)S(1)} collective-permute-done((f32[256,1536]{1,0:T(8,128)S(1)}, f32[256,1536]{1,0:T(8,128)S(1)}, u32[]{:S(2)}, u32[]{:S(2)}) %collective-permute-start.4) | collective-permute-done | bytes 1572896 | tf_op jit(solution)/shard_map/ppermute | solution.py:25
  171.4 1.2 add_convert_fusion
  (13 shorter events, 0.2 us)
Async XLA Ops:
  0.0 20.3 %copy-start = (bf16[1024,1536]{1,0:T(8,128)(2,1)S(1)}, bf16[1024,1536]{1,0:T(8,128)(2,1)}, u32[]{:S(2)}) copy-start(bf16[1024,1536]{1,0:T(8,128)(2,1)} %param.17) | copy-start | bytes 9437188
  0.9 6.9 %collective-permute-start = (bf16[2,128,128]{2,1,0:T(8,128)(2,1)S(1)}, bf16[2,128,128]{2,1,0:T(8,128)(2,1)S(1)}, u32[]{:S(2)}, u32[]{:S(2)}) collective-permute-start(bf16[2,128,128]{2,1,0:T(8,128)(2,1)S(1)} %pad_maximum_fusion.4), channel_id=1, source_target_pairs={{0,2},{2,4},{4,6},{6,8},{8,10},{10,12},{12,14},{1,3},{3,5},{5,7},{... | collective-permute-start | bytes 196616 | tf_op jit(solution)/shard_map/ppermute | solution.py:20
  20.3 3.2 %copy-start.1 = (s32[256,4]{0,1:T(4,128)S(1)}, s32[256,4]{0,1:T(4,128)}, u32[]{:S(2)}) copy-start(s32[256,4]{0,1:T(4,128)} %param.22) | copy-start | bytes 12292
  23.5 4.1 %collective-permute-start.1 = (f32[256,1536]{1,0:T(8,128)}, f32[256,1536]{1,0:T(8,128)}, u32[]{:S(2)}, u32[]{:S(2)}) collective-permute-start(f32[256,1536]{1,0:T(8,128)} %fusion.36), channel_id=1, source_target_pairs={{0,1},{1,0},{2,3},{3,2},{4,5},{5,4},{6,7},{7,6},{8,9},{9,8},{10,11... | collective-permute-start | bytes 4718600 | tf_op jit(solution)/shard_map/ppermute | solution.py:25
  27.6 2.6 %copy-start.2 = (f32[1536]{0:T(1024)S(1)}, f32[1536]{0:T(1024)}, u32[]{:S(2)}) copy-start(f32[1536]{0:T(1024)} %param.19) | copy-start | bytes 18436
  27.7 63.6 %slice-start = ((s8[4718592]{0:T(1024)(128)(4,1)}), s8[4194304]{0:T(1024)(128)(4,1)S(1)}, s32[]{:S(2)}) async-start(s8[4718592]{0:T(1024)(128)(4,1)} %bitcast.98), calls=%async_computation.2 | async-start | bytes 8388608
  30.3 61.0 %slice-start.1 = ((s8[4718592]{0:T(1024)(128)(4,1)}), s8[524288]{0:T(1024)(128)(4,1)S(1)}, s32[]{:S(2)}) async-start(s8[4718592]{0:T(1024)(128)(4,1)} %bitcast.98), calls=%async_computation.3 | async-start | bytes 1048576
  91.3 4.5 %collective-permute-start.2 = (bf16[8,96,1536]{2,1,0:T(8,128)(2,1)S(1)}, bf16[8,96,1536]{2,1,0:T(8,128)(2,1)S(1)}, u32[]{:S(2)}, u32[]{:S(2)}) collective-permute-start(bf16[8,96,1536]{2,1,0:T(8,128)(2,1)S(1)} %all_to_all.10), channel_id=1, source_target_pairs={{0,1},{1,0},{2,3},{3,2},{4,5},{5,4},{6,7},{7,6},{8,9},{9,8},{10,11... | collective-permute-start | bytes 7077896 | tf_op jit(solution)/shard_map/ppermute | solution.py:25
  95.8 3.8 %copy-start.3 = (bf16[1,768,1536]{2,1,0:T(8,128)(2,1)S(1)}, bf16[1,768,1536]{2,1,0:T(8,128)(2,1)}, u32[]{:S(2)}) copy-start(bf16[1,768,1536]{2,1,0:T(8,128)(2,1)} %param.21) | copy-start | bytes 7077892
  101.7 4.7 %collective-permute-start.3 = (bf16[8,96,1536]{2,1,0:T(8,128)(2,1)S(1)}, bf16[8,96,1536]{2,1,0:T(8,128)(2,1)S(1)}, u32[]{:S(2)}, u32[]{:S(2)}) collective-permute-start(bf16[8,96,1536]{2,1,0:T(8,128)(2,1)S(1)} %bitcast.101), channel_id=1, source_target_pairs={{0,1},{1,0},{2,3},{3,2},{4,5},{5,4},{6,7},{7,6},{8,9},{9,8},{10,11... | collective-permute-start | bytes 7077896 | tf_op jit(solution)/shard_map/ppermute | solution.py:25
  107.1 57.8 %copy-start.4 = (f32[256,4]{0,1:T(4,128)S(1)}, f32[256,4]{0,1:T(4,128)}, u32[]{:S(2)}) copy-start(f32[256,4]{0,1:T(4,128)} %param.23) | copy-start | bytes 12292
  167.9 3.5 %collective-permute-start.4 = (f32[256,1536]{1,0:T(8,128)S(1)}, f32[256,1536]{1,0:T(8,128)S(1)}, u32[]{:S(2)}, u32[]{:S(2)}) collective-permute-start(f32[256,1536]{1,0:T(8,128)S(1)} %multiply_reduce_fusion), channel_id=1, source_target_pairs={{0,1},{1,0},{2,3},{3,2},{4,5},{5,4},{6,7},{7,6},{8,9},{9,8},{10,11... | collective-permute-start | bytes 4718600 | tf_op jit(solution)/shard_map/ppermute | solution.py:25

commit v6 on v3

--- a/solution.py
+++ b/solution.py
@@ -1,6 +1,8 @@
 import jax
 import jax.numpy as jnp
 from jax import lax
+from jax.experimental import pallas as pl
+from jax.experimental.pallas import tpu as pltpu
 from jax.sharding import PartitionSpec as P
 
 HEAD_DIM = 64
@@ -57,6 +59,76 @@
     return ((up_val + 1.0) * gate_val * jax.nn.sigmoid(GLU_ALPHA * gate_val)).astype(jnp.bfloat16)
 
 
+def attention_kernel(sink_ref, q_ref, pk_ref, k_ref, pv_ref, v_ref, o_ref):
+    rows = q_ref.shape[0]
+    prior = pk_ref.shape[0]
+    span = 2 * WINDOW
+    pair_cols = 2 * HEAD_DIM
+    pairs = q_ref.shape[1] // pair_cols
+    kv_count = k_ref.shape[1] // HEAD_DIM
+    per_kv = pairs // kv_count
+    keys_all = jnp.concatenate([pk_ref[...], k_ref[...]], axis=0)
+    values_all = jnp.concatenate([pv_ref[...], v_ref[...]], axis=0)
+    q_pos = lax.broadcasted_iota(jnp.int32, (WINDOW, span), 0)
+    k_pos = lax.broadcasted_iota(jnp.int32, (WINDOW, span), 1)
+    allowed = (k_pos > q_pos) & (k_pos <= q_pos + WINDOW)
+    lane_half = lax.broadcasted_iota(jnp.int32, (span, pair_cols), 1) // HEAD_DIM
+    for b in range(rows // WINDOW):
+        first = b * WINDOW + prior - WINDOW
+        key_win = keys_all[first : first + span]
+        value_win = values_all[first : first + span]
+        swapped_k = pltpu.roll(key_win, HEAD_DIM, 1)
+        swapped_v = pltpu.roll(value_win, HEAD_DIM, 1)
+        placed = {}
+        for kv in range(kv_count):
+            for a in range(2):
+                src_k = key_win if (kv % 2) == a else swapped_k
+                src_v = value_win if (kv % 2) == a else swapped_v
+                placed[kv, a] = (
+                    jnp.where(lane_half == a, src_k, jnp.zeros_like(src_k)),
+                    jnp.where(lane_half == a, src_v, jnp.zeros_like(src_v)),
+                )
+        for j in range(pairs):
+            kv = j // per_kv
+            q_pair = q_ref[b * WINDOW : (b + 1) * WINDOW, j * pair_cols : (j + 1) * pair_cols]
+            total = None
+            for a in range(2):
+                k_placed, v_placed = placed[kv, a]
+                scores = lax.dot_general(
+                    q_pair, k_placed, (((1,), (1,)), ((), ())), preferred_element_type=jnp.float32
+                ) * HEAD_DIM ** (-0.5)
+                scores = jnp.where(allowed, scores, -jnp.inf)
+                sink = sink_ref[2 * j + a]
+                largest = jnp.maximum(jnp.max(scores, axis=-1, keepdims=True), sink)
+                weights_exp = jnp.exp(scores - largest)
+                denominator = jnp.exp(sink - largest) + jnp.sum(weights_exp, axis=-1, keepdims=True)
+                probs = (weights_exp * (1.0 / denominator)).astype(jnp.bfloat16)
+                out = jnp.dot(probs, v_placed, preferred_element_type=jnp.float32)
+                total = out if total is None else total + out
+            o_ref[b * WINDOW : (b + 1) * WINDOW, j * pair_cols : (j + 1) * pair_cols] = total.astype(
+                o_ref.dtype
+            )
+
+
+def attend_kernel(queries, prior_keys, key_rows, prior_values, values, sink_logits):
+    rows, cols = queries.shape
+    heads = cols // HEAD_DIM
+    span = 2 * WINDOW
+    cost = pl.CostEstimate(
+        flops=2 * 2 * rows * span * 2 * HEAD_DIM * heads,
+        transcendentals=rows * span * heads,
+        bytes_accessed=2 * rows * cols * 2 + 2 * (rows + WINDOW) * key_rows.shape[1] * 2,
+    )
+    vmem = pl.BlockSpec(memory_space=pltpu.VMEM)
+    return pl.pallas_call(
+        attention_kernel,
+        out_shape=jax.ShapeDtypeStruct((rows, cols), jnp.bfloat16),
+        in_specs=[pl.BlockSpec(memory_space=pltpu.SMEM)] + [vmem] * 5,
+        out_specs=vmem,
+        cost_estimate=cost,
+    )(sink_logits, queries, prior_keys, key_rows, prior_values, values)
+
+
 def on_device(
     queries,
     key_rows,
@@ -76,10 +148,7 @@
     rim_rows = jnp.stack([key_rows[tok_rows - window_rows :], values[tok_rows - window_rows :]])
     received = shifted(rim_rows, "seq", 1)
     prior = jnp.where(lax.axis_index("seq") == 0, cached_rows, received)
-    keys_all = jnp.concatenate([prior[0], key_rows], axis=0)
-    values_all = jnp.concatenate([prior[1], values], axis=0)
-    block_rows = min(tok_rows, 512)
-    pieces = attend_block(queries, keys_all, values_all, sink_logits, block_rows, window_rows)
+    pieces = attend_kernel(queries, prior[0], key_rows, prior[1], values, sink_logits)
     partial_rows = jnp.dot(pieces, out_weight, preferred_element_type=jnp.float32)
     mixed_rows = residual.astype(jnp.float32) + (partial_rows + swap_exp(partial_rows))
     normed = rms_normalize(mixed_rows, norm_gain)

time: 171 us -> 170 us (level)
  Pallas kernels: 0 us -> 7.73 us
  matrix products: 24.4 us -> 18.8 us
  local copies, waits for them, and re-layouts: 8.14 us -> 2.58 us
  blocking collectives: 116 us -> 118 us
  waiting for transfers between devices: 5.61 us -> 7.49 us
    pallas_call x0 -> x1, Pallas kernels: none -> 7.73 us  [attend_kernel(): pl.pallas_call(attention_kernel, out_shape=jax.ShapeDtypeStruct((rows, co...]
    dot_general x2 -> x0, matrix products: 6.69 us -> none  [the longest x1 4.57 us: attend_block(): jnp.einsum('hgqk,khd->qhgd', probs, value_block, preferred_element_type=j...]
    unnamed x20 -> x15, local copies, waits for them, and re-layouts: 5.39 us -> 0.17 us
    ppermute x1, waiting for transfers between devices: 0.01 us -> 1.88 us  [shifted(): return lax.ppermute(shard, axis, pairs)]
    all_to_all x1, blocking collectives: 58.3 us -> 60.1 us  [on_device(): lax.all_to_all(outgoing, 'seq', split_axis=0, concat_axis=0, tiled=True)]
  transfers between devices with their start and end apart: 5 -> 5, of which waited for: 2 -> 3; matrix products, arithmetic and copies ran while one was open for 9% -> 6% of each run, Pallas kernels for 0% -> 0%
where the time goes in v6:
time: 170 us; the launch traced here: 169 us
  blocking collectives  118 us (69%)
  matrix products  18.8 us (11%)
  other arithmetic  8.98 us (5%)
  Pallas kernels  7.73 us (5%)
  waiting for transfers between devices  7.49 us (4%)
  starting transfers between devices  5.64 us (3%)
  local copies, waits for them, and re-layouts  2.58 us (2%)
    all_to_all x1, blocking collectives, on_device(): lax.all_to_all(outgoing, 'seq', split_axis=0, concat_axis=0, tiled=True)  60.1 us
    all_to_all x1, blocking collectives, on_device(): lax.all_to_all(result, 'seq', split_axis=0, concat_axis=0, tiled=True)  57.8 us
    pallas_call x1, Pallas kernels, attend_kernel(): pl.pallas_call(attention_kernel, out_shape=jax.ShapeDtypeStruct((rows, co...  7.73 us
    dot_general x2, matrix products, expert_hidden(): jnp.einsum('rd,kdf->krf', rows, expert_in, preferred_element_type=jnp.flo...  7.62 us
    ppermute x4, waiting for transfers between devices, swap_exp(): return lax.ppermute(x, 'exp', [(i, (i + 1) % size) for i in range(size)])  5.61 us
    ppermute x1, starting transfers between devices, shifted(): return lax.ppermute(shard, axis, pairs)  5.01 us
  transfers between devices with their start and end apart: 5, of which 3 were waited for; matrix products, arithmetic and copies ran while one was open for 6% of the time, Pallas kernels for 0%

profile of v6, /device:TPU:0, one launch (start us, length us, event | category | flops | bytes accessed | tf_op | source)
XLA Modules:
  0.0 169.3 jit_solution(14435600301128317466)
XLA Ops:
  0.0 0.0 copy-start
  0.0 0.9 slice_bitcast_fusion.2
  0.9 5.0 %collective-permute-start = (bf16[2,128,128]{2,1,0:T(8,128)(2,1)S(1)}, bf16[2,128,128]{2,1,0:T(8,128)(2,1)S(1)}, u32[]{:S(2)}, u32[]{:S(2)}) collective-permute-start(bf16[2,128,128]{2,1,0:T(8,128)(2,1)S(1)} %pad_maximum_fusion), channel_id=1, source_target_pairs={{0,2},{2,4},{4,6},{6,8},{8,10},{10,12},{12,14},{1,3},{3,5},{5,7},{... | collective-permute-start | bytes 196616 | tf_op jit(solution)/shard_map/ppermute | solution.py:20
  6.0 1.9 %collective-permute-done = bf16[2,128,128]{2,1,0:T(8,128)(2,1)S(1)} collective-permute-done((bf16[2,128,128]{2,1,0:T(8,128)(2,1)S(1)}, bf16[2,128,128]{2,1,0:T(8,128)(2,1)S(1)}, u32[]{:S(2)}, u32[]{:S(2)}) %collective-permute-start) | collective-permute-done | bytes 65568 | tf_op jit(solution)/shard_map/ppermute | solution.py:20
  7.8 0.8 broadcast_select_fusion
  8.7 0.6 slice_bitcast_fusion
  9.3 7.7 %shard_map.118 = bf16[256,1024]{1,0:T(8,128)(2,1)} custom-call(f32[16]{0:T(128)} %sink_ref.1, bf16[256,1024]{1,0:T(8,128)(2,1)} %q_ref.1, bf16[128,128]{1,0:T(8,128)(2,1)} %get-tuple-element.12.pk_ref, bf16[256,128]{1,0:T(8,128)(2,1)} %k_ref.1, bf16[128,128]{1,0:T(8,128)(2,1)} %get-tuple-element.11.pv_ref, bf16[256,128]{1,0:T(8,128)(2,1)} %v_ref.1), custom_call_target="tpu_custom_call" | custom-call | flops 536870912 | bytes 1245184 | tf_op jit(solution)/shard_map/pallas_call | solution.py:123
  17.0 0.0 copy-done
  17.0 0.0 copy-start.1
  17.1 3.2 %fusion.35 = f32[256,1536]{1,0:T(8,128)} fusion(bf16[256,1024]{1,0:T(8,128)(2,1)} %shard_map.118, bf16[1024,1536]{1,0:T(8,128)(2,1)S(1)} %copy-done), kind=kOutput, calls=%fused_computation.57 | convolution fusion | flops 805306368 | bytes 5242880 | tf_op jit(solution)/shard_map/dot_general | solution.py:152
  20.2 0.0 collective-permute-start.1
  20.2 0.0 copy-done.1
  20.2 0.1 copy.19
  20.4 0.1 eq.69
  20.5 0.1 eq.65
  20.6 2.3 %reduce-window.6 = s32[8,8,128]{2,1,0:T(8,128)S(1)} reduce-window(s32[8,8,128]{2,1,0:T(8,128)S(1)} %fusion.32, s32[]{:T(128)} %constant.13.clone.1), window={size=1x1x128 pad=0_0x0_0x127_0}, to_apply=%region_0.1 | reduce-window | flops 1040384 | bytes 65540 | tf_op jit(solution)/shard_map/reduce-window
  22.9 0.3 slice_reduce_fusion
  23.2 0.2 reduce-window.9
  23.4 0.1 add_bitcast_fusion
  23.5 0.1 sub.26
  23.6 0.1 copy.22
  23.8 0.1 copy.23
  23.9 0.4 fusion.22
  24.3 0.0 copy-start.2
  24.3 0.0 collective-permute-done.1
  24.4 0.0 slice-start
  24.4 2.6 %multiply_reduce_fusion.1 = (f32[256]{0:T(256)S(1)}, f32[256,1536]{1,0:T(8,128)S(1)}) fusion(f32[256,1536]{1,0:T(8,128)} %fusion.35, f32[256,1536]{1,0:T(8,128)} %collective-permute-done.1, bf16[256,1536]{1,0:T(8,128)(2,1)} %param.18), kind=kLoop, calls=%fused_computation.29 | loop fusion | flops 1965824 | bytes 5506048 | tf_op jit(solution)/shard_map/reduce_sum | solution.py:29
  26.9 0.0 copy-done.2
  27.0 0.0 slice-start.1
  27.0 0.9 convolution_convert_fusion.2
  27.9 60.1 %all_to_all.10 = bf16[8,96,1536]{2,1,0:T(8,128)(2,1)S(1)} all-to-all(bf16[8,96,1536]{2,1,0:T(8,128)(2,1)S(1)} %bitcast.69), channel_id=1, replica_groups=mesh['groups'=2,'seq'=8,'exp'=2] {'seq'}, dimensions={0} | all-to-all | bytes 4718592 | tf_op jit(solution)/shard_map/all_to_all | solution.py:178
  88.0 0.0 collective-permute-start.2
  88.0 0.0 slice-done
  88.0 0.0 slice-done.1
  88.0 3.8 %fusion.16 = f32[2,768,768]{2,1,0:T(8,128)S(1)} fusion(bf16[768,1536,1]{1,0,2:T(8,128)(2,1)S(1)} %bitcast.71, bf16[1,2,1536,768]{3,2,1,0:T(8,128)(2,1)S(1)} %bitcast.75), kind=kOutput, calls=%fused_computation.24 | convolution fusion | flops 3623878656 | bytes 11796480 | tf_op jit(solution)/shard_map/rd,kdf->krf/dot_general | solution.py:56
  91.8 0.7 fusion.27
  92.5 0.0 collective-permute-done.2
  92.5 0.0 copy-start.3
  92.5 3.8 %fusion.19 = f32[2,768,768]{2,1,0:T(8,128)S(1)} fusion(bf16[768,1536,1]{1,0,2:T(8,128)(2,1)S(1)} %bitcast.76, bf16[1,2,1536,768]{3,2,1,0:T(8,128)(2,1)S(1)} %bitcast.75), kind=kOutput, calls=%fused_computation.25 | convolution fusion | flops 3623878656 | bytes 11796480 | tf_op jit(solution)/shard_map/rd,kdf->krf/dot_general | solution.py:56
  96.4 0.0 copy-done.3
  96.4 2.1 %convolution_convert_fusion = bf16[768,1536]{1,0:T(8,128)(2,1)S(1)} fusion(bf16[1,768,1536]{2,1,0:T(8,128)(2,1)S(1)} %copy-done.3, f32[2,768,768]{2,1,0:T(8,128)S(1)} %fusion.19), kind=kOutput, calls=%fused_computation.7 | convolution fusion | flops 1817837568 | bytes 9437184 | tf_op jit(solution)/shard_map/dot_general | solution.py:184
  98.4 0.6 collective-permute-start.3
  99.0 2.0 %convolution_convert_fusion.1 = bf16[768,1536]{1,0:T(8,128)(2,1)S(1)} fusion(bf16[768,768]{1,0:T(8,128)(2,1)S(1)} %fusion.27, bf16[1,768,1536]{2,1,0:T(8,128)(2,1)S(1)} %copy-done.3), kind=kOutput, calls=%fused_computation.8 | convolution fusion | flops 1813118976 | bytes 5898240 | tf_op jit(solution)/shard_map/dot_general | solution.py:189
  101.0 2.2 %collective-permute-done.3 = bf16[8,96,1536]{2,1,0:T(8,128)(2,1)S(1)} collective-permute-done((bf16[8,96,1536]{2,1,0:T(8,128)(2,1)S(1)}, bf16[8,96,1536]{2,1,0:T(8,128)(2,1)S(1)}, u32[]{:S(2)}, u32[]{:S(2)}) %collective-permute-start.3) | collective-permute-done | bytes 2359328 | tf_op jit(solution)/shard_map/ppermute | solution.py:25
  103.2 0.7 fusion
  103.8 0.0 copy-start.4
  103.8 57.8 %all_to_all.11 = bf16[8,96,1536]{2,1,0:T(8,128)(2,1)S(1)} all-to-all(bf16[8,96,1536]{2,1,0:T(8,128)(2,1)S(1)} %fusion), channel_id=1, replica_groups=mesh['groups'=2,'seq'=8,'exp'=2] {'seq'}, dimensions={0} | all-to-all | bytes 4718592 | tf_op jit(solution)/shard_map/all_to_all | solution.py:194
  161.6 0.0 copy-done.4
  161.6 3.0 %multiply_reduce_fusion = f32[256,1536]{1,0:T(8,128)S(1)} fusion(bf16[768,1536,1]{1,0,2:T(8,128)(2,1)S(1)} %bitcast.72, f32[256,4]{0,1:T(4,128)S(1)} %copy-done.4, s32[256,4]{0,1:T(4,128)S(1)} %copy.23), kind=kOutput, calls=%fused_computation | convolution fusion | flops 2419458048 | bytes 3940352 | tf_op jit(solution)/shard_map/dot_general | solution.py:195
  164.6 0.1 collective-permute-start.4
  164.7 3.4 %collective-permute-done.4 = f32[256,1536]{1,0:T(8,128)S(1)} collective-permute-done((f32[256,1536]{1,0:T(8,128)S(1)}, f32[256,1536]{1,0:T(8,128)S(1)}, u32[]{:S(2)}, u32[]{:S(2)}) %collective-permute-start.4) | collective-permute-done | bytes 1572896 | tf_op jit(solution)/shard_map/ppermute | solution.py:25
  168.1 1.2 add_convert_fusion
  (8 shorter events, 0.1 us)
Async XLA Ops:
  0.0 17.0 %copy-start = (bf16[1024,1536]{1,0:T(8,128)(2,1)S(1)}, bf16[1024,1536]{1,0:T(8,128)(2,1)}, u32[]{:S(2)}) copy-start(bf16[1024,1536]{1,0:T(8,128)(2,1)} %param.17) | copy-start | bytes 9437188
  0.9 6.9 %collective-permute-start = (bf16[2,128,128]{2,1,0:T(8,128)(2,1)S(1)}, bf16[2,128,128]{2,1,0:T(8,128)(2,1)S(1)}, u32[]{:S(2)}, u32[]{:S(2)}) collective-permute-start(bf16[2,128,128]{2,1,0:T(8,128)(2,1)S(1)} %pad_maximum_fusion), channel_id=1, source_target_pairs={{0,2},{2,4},{4,6},{6,8},{8,10},{10,12},{12,14},{1,3},{3,5},{5,7},{... | collective-permute-start | bytes 196616 | tf_op jit(solution)/shard_map/ppermute | solution.py:20
  17.0 3.2 %copy-start.1 = (s32[256,4]{0,1:T(4,128)S(1)}, s32[256,4]{0,1:T(4,128)}, u32[]{:S(2)}) copy-start(s32[256,4]{0,1:T(4,128)} %param.22) | copy-start | bytes 12292
  20.2 4.1 %collective-permute-start.1 = (f32[256,1536]{1,0:T(8,128)}, f32[256,1536]{1,0:T(8,128)}, u32[]{:S(2)}, u32[]{:S(2)}) collective-permute-start(f32[256,1536]{1,0:T(8,128)} %fusion.35), channel_id=1, source_target_pairs={{0,1},{1,0},{2,3},{3,2},{4,5},{5,4},{6,7},{7,6},{8,9},{9,8},{10,11... | collective-permute-start | bytes 4718600 | tf_op jit(solution)/shard_map/ppermute | solution.py:25
  24.3 2.6 %copy-start.2 = (f32[1536]{0:T(1024)S(1)}, f32[1536]{0:T(1024)}, u32[]{:S(2)}) copy-start(f32[1536]{0:T(1024)} %param.19) | copy-start | bytes 18436
  24.4 63.7 %slice-start = ((s8[4718592]{0:T(1024)(128)(4,1)}), s8[4194304]{0:T(1024)(128)(4,1)S(1)}, s32[]{:S(2)}) async-start(s8[4718592]{0:T(1024)(128)(4,1)} %bitcast.74), calls=%async_computation.2 | async-start | bytes 8388608
  27.0 61.1 %slice-start.1 = ((s8[4718592]{0:T(1024)(128)(4,1)}), s8[524288]{0:T(1024)(128)(4,1)S(1)}, s32[]{:S(2)}) async-start(s8[4718592]{0:T(1024)(128)(4,1)} %bitcast.74), calls=%async_computation.3 | async-start | bytes 1048576
  88.0 4.5 %collective-permute-start.2 = (bf16[8,96,1536]{2,1,0:T(8,128)(2,1)S(1)}, bf16[8,96,1536]{2,1,0:T(8,128)(2,1)S(1)}, u32[]{:S(2)}, u32[]{:S(2)}) collective-permute-start(bf16[8,96,1536]{2,1,0:T(8,128)(2,1)S(1)} %all_to_all.10), channel_id=1, source_target_pairs={{0,1},{1,0},{2,3},{3,2},{4,5},{5,4},{6,7},{7,6},{8,9},{9,8},{10,11... | collective-permute-start | bytes 7077896 | tf_op jit(solution)/shard_map/ppermute | solution.py:25
  92.5 3.8 %copy-start.3 = (bf16[1,768,1536]{2,1,0:T(8,128)(2,1)S(1)}, bf16[1,768,1536]{2,1,0:T(8,128)(2,1)}, u32[]{:S(2)}) copy-start(bf16[1,768,1536]{2,1,0:T(8,128)(2,1)} %param.21) | copy-start | bytes 7077892
  98.4 4.7 %collective-permute-start.3 = (bf16[8,96,1536]{2,1,0:T(8,128)(2,1)S(1)}, bf16[8,96,1536]{2,1,0:T(8,128)(2,1)S(1)}, u32[]{:S(2)}, u32[]{:S(2)}) collective-permute-start(bf16[8,96,1536]{2,1,0:T(8,128)(2,1)S(1)} %bitcast.77), channel_id=1, source_target_pairs={{0,1},{1,0},{2,3},{3,2},{4,5},{5,4},{6,7},{7,6},{8,9},{9,8},{10,11... | collective-permute-start | bytes 7077896 | tf_op jit(solution)/shard_map/ppermute | solution.py:25
  103.8 57.8 %copy-start.4 = (f32[256,4]{0,1:T(4,128)S(1)}, f32[256,4]{0,1:T(4,128)}, u32[]{:S(2)}) copy-start(f32[256,4]{0,1:T(4,128)} %param.23) | copy-start | bytes 12292
  164.6 3.5 %collective-permute-start.4 = (f32[256,1536]{1,0:T(8,128)S(1)}, f32[256,1536]{1,0:T(8,128)S(1)}, u32[]{:S(2)}, u32[]{:S(2)}) collective-permute-start(f32[256,1536]{1,0:T(8,128)S(1)} %multiply_reduce_fusion), channel_id=1, source_target_pairs={{0,1},{1,0},{2,3},{3,2},{4,5},{5,4},{6,7},{7,6},{8,9},{9,8},{10,11... | collective-permute-start | bytes 4718600 | tf_op jit(solution)/shard_map/ppermute | solution.py:25

commit v7 on v6

--- a/solution.py
+++ b/solution.py
@@ -129,6 +129,67 @@
     )(sink_logits, queries, prior_keys, key_rows, prior_values, values)
 
 
+def serve_rows(slot_rows, expert_in, expert_out):
+    blocks, piece, width = slot_rows.shape
+    other_rows = swap_exp(slot_rows)
+    own_hidden = expert_hidden(slot_rows.reshape(-1, width), expert_in)
+    own_hidden, other_rows = lax.optimization_barrier((own_hidden, other_rows))
+    other_hidden = expert_hidden(other_rows.reshape(-1, width), expert_in)
+    their_part = swap_exp(
+        jnp.dot(other_hidden, expert_out, preferred_element_type=jnp.float32)
+        .astype(jnp.bfloat16)
+        .reshape(blocks, piece, width)
+    )
+    own_part = (
+        jnp.dot(own_hidden, expert_out, preferred_element_type=jnp.float32)
+        .astype(jnp.bfloat16)
+        .reshape(blocks, piece, width)
+    )
+    return (own_part.astype(jnp.float32) + their_part.astype(jnp.float32)).astype(jnp.bfloat16)
+
+
+def swap_half(x):
+    return lax.ppermute(x, "half", [(0, 1), (1, 0)])
+
+
+def core_rows(x, core, share):
+    return lax.dynamic_slice_in_dim(x, core * share, share, 0)
+
+
+def join_rows(mine, theirs, core):
+    return jnp.where(core == 0, jnp.concatenate([mine, theirs], 0), jnp.concatenate([theirs, mine], 0))
+
+
+def slot_ids(routes, core, half, first_expert, quads):
+    experts = lax.axis_size("half") * quads
+    flat = routes.reshape(-1)
+    hits = (flat[:, None] == jnp.arange(experts, dtype=jnp.int32)[None, :]).astype(jnp.int32)
+    rank = jnp.sum(hits * (jnp.cumsum(hits, axis=0) - 1), axis=1)
+    local_rank = rank - core * half
+    local_expert = flat - first_expert
+    mine = (local_rank >= 0) & (local_rank < half) & (local_expert >= 0) & (local_expert < quads)
+    return jnp.where(mine, local_expert * half + local_rank, -1)
+
+
+def dispatch(normed, ids, slots, quads, half):
+    tok_rows, width = normed.shape
+    pick = (ids[:, None] == jnp.arange(slots, dtype=jnp.int32)[None, :]).astype(jnp.bfloat16)
+    select = jnp.max(pick.reshape(tok_rows, TOP, slots), axis=1).T
+    outgoing = (
+        jnp.dot(select, normed, preferred_element_type=jnp.float32)
+        .astype(jnp.bfloat16)
+        .reshape(quads, half, width)
+    )
+    return pick, lax.all_to_all(outgoing, "quad", split_axis=0, concat_axis=0, tiled=True)
+
+
+def combine(pick, returned, gates):
+    tok_rows = gates.shape[0]
+    slots, width = pick.shape[1], returned.shape[-1]
+    picked = jnp.dot(pick, returned.reshape(slots, width), preferred_element_type=jnp.float32)
+    return jnp.sum(picked.reshape(tok_rows, TOP, width) * gates[:, :, None], axis=1)
+
+
 def on_device(
     queries,
     key_rows,
@@ -145,74 +206,73 @@
 ):
     tok_rows = queries.shape[0]
     window_rows = WINDOW
+    quads = lax.axis_size("quad")
+    side = lax.axis_index("half")
+    seq_index = side * quads + lax.axis_index("quad")
+    core = lax.axis_index("exp")
     rim_rows = jnp.stack([key_rows[tok_rows - window_rows :], values[tok_rows - window_rows :]])
-    received = shifted(rim_rows, "seq", 1)
-    prior = jnp.where(lax.axis_index("seq") == 0, cached_rows, received)
+    received = shifted(rim_rows, ("half", "quad"), 1)
+    prior = jnp.where(seq_index == 0, cached_rows, received)
     pieces = attend_kernel(queries, prior[0], key_rows, prior[1], values, sink_logits)
     partial_rows = jnp.dot(pieces, out_weight, preferred_element_type=jnp.float32)
     mixed_rows = residual.astype(jnp.float32) + (partial_rows + swap_exp(partial_rows))
     normed = rms_normalize(mixed_rows, norm_gain)
 
-    experts = lax.axis_size("seq")
+    experts = lax.axis_size("half") * quads
     width = normed.shape[1]
+    share = tok_rows // lax.axis_size("exp")
     capacity = 3 * tok_rows * TOP // (2 * experts)
     half = -(-capacity // 2)
-    slots = experts * half
-    core = lax.axis_index("exp")
-    flat_experts = routes.reshape(-1)
-    expert_hits = (flat_experts[:, None] == jnp.arange(experts, dtype=jnp.int32)[None, :]).astype(
-        jnp.int32
-    )
-    slot_rank = jnp.sum(expert_hits * (jnp.cumsum(expert_hits, axis=0) - 1), axis=1)
-    local_rank = slot_rank - core * half
-    mine = (local_rank >= 0) & (local_rank < half)
-    slot_id = jnp.where(mine, flat_experts * half + local_rank, -1)
-    slot_iota = jnp.arange(slots, dtype=jnp.int32)
-    pick = (slot_id[:, None] == slot_iota[None, :]).astype(jnp.bfloat16)
-    select = jnp.max(pick.reshape(tok_rows, TOP, slots), axis=1).T
-    outgoing = (
-        jnp.dot(select, normed, preferred_element_type=jnp.float32)
-        .astype(jnp.bfloat16)
-        .reshape(experts, half, width)
-    )
-    slot_rows = lax.all_to_all(outgoing, "seq", split_axis=0, concat_axis=0, tiled=True)
-    other_rows = swap_exp(slot_rows)
-    own_hidden = expert_hidden(slot_rows.reshape(-1, width), expert_in[0])
-    own_hidden, other_rows = lax.optimization_barrier((own_hidden, other_rows))
-    other_hidden = expert_hidden(other_rows.reshape(-1, width), expert_in[0])
-    their_part = swap_exp(
-        jnp.dot(other_hidden, expert_out[0], preferred_element_type=jnp.float32)
-        .astype(jnp.bfloat16)
-        .reshape(experts, half, width)
-    )
-    own_part = (
-        jnp.dot(own_hidden, expert_out[0], preferred_element_type=jnp.float32)
-        .astype(jnp.bfloat16)
-        .reshape(experts, half, width)
-    )
-    result = (own_part.astype(jnp.float32) + their_part.astype(jnp.float32)).astype(jnp.bfloat16)
-    returned = lax.all_to_all(result, "seq", split_axis=0, concat_axis=0, tiled=True)
-    picked = jnp.dot(pick, returned.reshape(slots, width), preferred_element_type=jnp.float32)
-    weighted = jnp.sum(picked.reshape(tok_rows, TOP, width) * route_gates[:, :, None], axis=1)
-    moe = weighted + swap_exp(weighted)
-    return (mixed_rows + moe).astype(jnp.bfloat16)
+    slots = quads * half
+    first_expert = side * quads
+
+    partner_part = swap_half(core_rows(normed, core, share))
+    partner_routes = swap_half(routes)
+    partner_gates = swap_half(route_gates)
+    own_ids = slot_ids(routes, core, half, first_expert, quads)
+    own_pick, own_arrived = dispatch(normed, own_ids, slots, quads, half)
+    partner_normed = join_rows(partner_part, swap_exp(partner_part), core)
+    partner_ids = slot_ids(partner_routes, core, half, first_expert, quads)
+    partner_pick, partner_arrived = dispatch(partner_normed, partner_ids, slots, quads, half)
+
+    served = serve_rows(
+        jnp.concatenate([own_arrived, partner_arrived], axis=0), expert_in[0], expert_out[0]
+    )
+    own_back = lax.all_to_all(served[:quads], "quad", split_axis=0, concat_axis=0, tiled=True)
+    partner_back = lax.all_to_all(served[quads:], "quad", split_axis=0, concat_axis=0, tiled=True)
+
+    partner_sum = combine(partner_pick, partner_back, partner_gates)
+    other_core = 1 - core
+    partner_rows = core_rows(partner_sum, core, share) + swap_exp(
+        core_rows(partner_sum, other_core, share)
+    )
+    from_partner = swap_half(partner_rows.astype(jnp.bfloat16))
+    own_sum = combine(own_pick, own_back, route_gates)
+    own_rows = core_rows(own_sum, core, share) + swap_exp(core_rows(own_sum, other_core, share))
+    moe_rows = own_rows + from_partner.astype(jnp.float32)
+    out_rows = (core_rows(mixed_rows, core, share) + moe_rows).astype(jnp.bfloat16)
+    return join_rows(out_rows, swap_exp(out_rows), core)
 
 
 def solution(mesh):
+    groups, seq, exp = mesh.devices.shape
+    fine = jax.sharding.Mesh(
+        mesh.devices.reshape(groups, 2, seq // 2, exp), ("groups", "half", "quad", "exp")
+    )
+    rows = ("groups", "half", "quad")
+    experts = ("half", "quad")
     placed = (
-        P(("groups", "seq"), "exp"),
-        P(("groups", "seq"), "exp"),
-        P(("groups", "seq"), "exp"),
+        P(rows, "exp"),
+        P(rows, "exp"),
+        P(rows, "exp"),
         P(None, "groups", "exp"),
         P("exp"),
         P("exp", None),
-        P(("groups", "seq"), None),
+        P(rows, None),
         P(),
-        P("seq", None, None, "exp"),
-        P("seq", "exp", None),
-        P(("groups", "seq"), None),
-        P(("groups", "seq"), None),
-    )
-    return jax.shard_map(
-        on_device, mesh=mesh, in_specs=placed, out_specs=P(("groups", "seq"), None), check_vma=False
-    )
+        P(experts, None, None, "exp"),
+        P(experts, "exp", None),
+        P(rows, None),
+        P(rows, None),
+    )
+    return jax.shard_map(on_device, mesh=fine, in_specs=placed, out_specs=P(rows, None), check_vma=False)

time: 170 us -> 193 us (1.14)
  blocking collectives: 118 us -> 19.6 us
  waiting for transfers between devices: 7.49 us -> 75.5 us
  starting transfers between devices: 5.64 us -> 32.1 us
  local copies, waits for them, and re-layouts: 2.58 us -> 15.4 us
  matrix products: 18.8 us -> 29.2 us
  other arithmetic: 8.98 us -> 12.9 us
    all_to_all x2 -> x1, blocking collectives: 118 us -> 19.6 us  [on_device(): lax.all_to_all(served[quads:], 'quad', split_axis=0, concat_axis=0, tiled...]
    ppermute x0 -> x4, waiting for transfers between devices: none -> 55 us  [swap_half(): return lax.ppermute(x, 'half', [(0, 1), (1, 0)])]
    all_to_all x0 -> x3, waiting for transfers between devices: none -> 13.2 us  [the longest x2 13.2 us: dispatch(): lax.all_to_all(outgoing, 'quad', split_axis=0, concat_axis=0, tiled=True)]
    all_to_all x0 -> x3, starting transfers between devices: none -> 13 us  [the longest x2 8.73 us: dispatch(): lax.all_to_all(outgoing, 'quad', split_axis=0, concat_axis=0, tiled=True)]
    ppermute x0 -> x4, starting transfers between devices: none -> 12.8 us  [swap_half(): return lax.ppermute(x, 'half', [(0, 1), (1, 0)])]
    dot_general x4 -> x6, matrix products: 7.96 us -> 15.6 us  [the longest x2 7.11 us: combine(): jnp.dot(pick, returned.reshape(slots, width), preferred_element_type=jnp....]
    unnamed x15 -> x26, local copies, waits for them, and re-layouts: 0.17 us -> 5.69 us
    dot_general x2, matrix products: 7.62 us -> 10.4 us  [expert_hidden(): jnp.einsum('rd,kdf->krf', rows, expert_in, preferred_element_type=jnp.flo...]
  transfers between devices with their start and end apart: 5 -> 15, of which waited for: 3 -> 9; matrix products, arithmetic and copies ran while one was open for 6% -> 17% of each run, Pallas kernels for 0% -> 0%
where the time goes in v7:
time: 193 us
  waiting for transfers between devices  75.5 us (39%)
  starting transfers between devices  32.1 us (17%)
  matrix products  29.2 us (15%)
  blocking collectives  19.6 us (10%)
  local copies, waits for them, and re-layouts  15.4 us (8%)
  other arithmetic  12.9 us (7%)
  Pallas kernels  7.73 us (4%)
    ppermute x4, waiting for transfers between devices, swap_half(): return lax.ppermute(x, 'half', [(0, 1), (1, 0)])  55 us
    all_to_all x1, blocking collectives, on_device(): lax.all_to_all(served[quads:], 'quad', split_axis=0, concat_axis=0, tiled...  19.6 us
    all_to_all x2, waiting for transfers between devices, dispatch(): lax.all_to_all(outgoing, 'quad', split_axis=0, concat_axis=0, tiled=True)  13.2 us
    ppermute x4, starting transfers between devices, swap_half(): return lax.ppermute(x, 'half', [(0, 1), (1, 0)])  12.8 us
    dot_general x2, matrix products, expert_hidden(): jnp.einsum('rd,kdf->krf', rows, expert_in, preferred_element_type=jnp.flo...  10.4 us
    all_to_all x2, starting transfers between devices, dispatch(): lax.all_to_all(outgoing, 'quad', split_axis=0, concat_axis=0, tiled=True)  8.73 us
    pallas_call x1, Pallas kernels, attend_kernel(): pl.pallas_call(attention_kernel, out_shape=jax.ShapeDtypeStruct((rows, co...  7.73 us
    dot_general x2, matrix products, combine(): jnp.dot(pick, returned.reshape(slots, width), preferred_element_type=jnp....  7.11 us
  transfers between devices with their start and end apart: 15, of which 9 were waited for; matrix products, arithmetic and copies ran while one was open for 17% of the time, Pallas kernels for 0%

profile of v7, /device:TPU:0, one launch (start us, length us, event | category | flops | bytes accessed | tf_op | source)
XLA Modules:
  0.0 192.8 jit_solution(11009997778089243111)
XLA Ops:
  0.0 0.9 slice_bitcast_fusion.2
  0.9 5.0 %collective-permute-start = (bf16[2,128,128]{2,1,0:T(8,128)(2,1)S(1)}, bf16[2,128,128]{2,1,0:T(8,128)(2,1)S(1)}, u32[]{:S(2)}, u32[]{:S(2)}) collective-permute-start(bf16[2,128,128]{2,1,0:T(8,128)(2,1)S(1)} %pad_maximum_fusion), channel_id=1, source_target_pairs={{0,2},{2,4},{4,6},{6,8},{8,10},{10,12},{12,14},{1,3},{3,5},{5,7},{... | collective-permute-start | bytes 196616 | tf_op jit(solution)/shard_map/ppermute | solution.py:20
  6.0 1.9 collective-permute-done
  7.8 0.8 broadcast_select_fusion
  8.7 0.6 slice_bitcast_fusion
  9.3 7.7 %shard_map.118 = bf16[256,1024]{1,0:T(8,128)(2,1)} custom-call(f32[16]{0:T(128)} %sink_ref.1, bf16[256,1024]{1,0:T(8,128)(2,1)} %q_ref.1, bf16[128,128]{1,0:T(8,128)(2,1)} %get-tuple-element.14.pk_ref, bf16[256,128]{1,0:T(8,128)(2,1)} %k_ref.1, bf16[128,128]{1,0:T(8,128)(2,1)} %get-tuple-element.13.pv_ref, bf16[256,128]{1,0:T(8,128)(2,1)} %v_ref.1), custom_call_target="tpu_custom_call" | custom-call | flops 536870912 | bytes 1245184 | tf_op jit(solution)/shard_map/pallas_call | solution.py:123
  17.1 3.2 %fusion.52 = f32[256,1536]{1,0:T(8,128)} fusion(bf16[256,1024]{1,0:T(8,128)(2,1)} %shard_map.118, bf16[1024,1536]{1,0:T(8,128)(2,1)S(1)} %copy-done), kind=kOutput, calls=%fused_computation.89 | convolution fusion | flops 805306368 | bytes 5242880 | tf_op jit(solution)/shard_map/dot_general | solution.py:217
  20.2 0.1 copy.41
  20.4 0.1 eq.135
  20.5 0.1 eq.131
  20.6 2.3 %reduce-window.14 = s32[8,8,128]{2,1,0:T(8,128)S(1)} reduce-window(s32[8,8,128]{2,1,0:T(8,128)S(1)} %fusion.46, s32[]{:T(128)} %constant.16.clone.1), window={size=1x1x128 pad=0_0x0_0x127_0}, to_apply=%region_0.1 | reduce-window | flops 1040384 | bytes 65540 | tf_op jit(solution)/shard_map/reduce-window
  22.9 0.3 slice_reduce_fusion.1
  23.2 0.2 reduce-window.15
  23.5 0.1 sub.64
  23.7 0.2 fusion.33
  24.0 2.4 %multiply_reduce_fusion.2 = (f32[256]{0:T(256)S(1)}, f32[256,1536]{1,0:T(8,128)S(1)}) fusion(f32[256,1536]{1,0:T(8,128)} %fusion.52, f32[256,1536]{1,0:T(8,128)} %collective-permute-done.1, bf16[256,1536]{1,0:T(8,128)(2,1)} %param.18), kind=kLoop, calls=%fused_computation.27 | loop fusion | flops 1965824 | bytes 5506048 | tf_op jit(solution)/shard_map/reduce_sum | solution.py:29
  26.4 1.1 copy-done.1
  27.6 0.2 multiply_convert_fusion
  27.8 0.9 copy-done.3
  28.7 1.5 convolution_convert_fusion.3
  30.2 4.3 %all-to-all-start = ((bf16[4,96,1536]{2,1,0:T(8,128)(2,1)}), bf16[4,96,1536]{2,1,0:T(8,128)(2,1)}, u32[]{:S(2)}, u32[]{:S(2)}) async-start(bf16[4,96,1536]{2,1,0:T(8,128)(2,1)} %bitcast.96), calls=%async_computation | async-start | bytes 2359296 | tf_op jit(solution)/shard_map/all_to_all | solution.py:183
  34.4 3.6 %collective-permute-start.2 = (s32[256,4]{0,1:T(4,128)S(1)}, s32[256,4]{0,1:T(4,128)S(1)}, u32[]{:S(2)}, u32[]{:S(2)}) collective-permute-start(s32[256,4]{0,1:T(4,128)S(1)} %copy-done.6), channel_id=1, source_target_pairs={{0,8},{8,0},{1,9},{9,1},{2,10},{10,2},{3,11},{11,3},{4,12},{12,4},... | collective-permute-start | bytes 12296 | tf_op jit(solution)/shard_map/ppermute | solution.py:152
  38.0 10.3 %collective-permute-done.2 = s32[256,4]{0,1:T(4,128)S(1)} collective-permute-done((s32[256,4]{0,1:T(4,128)S(1)}, s32[256,4]{0,1:T(4,128)S(1)}, u32[]{:S(2)}, u32[]{:S(2)}) %collective-permute-start.2) | collective-permute-done | bytes 4128 | tf_op jit(solution)/shard_map/ppermute | solution.py:152
  48.3 0.1 copy.46
  48.5 0.1 eq.150
  48.6 2.3 %reduce-window.16 = s32[8,8,128]{2,1,0:T(8,128)S(1)} reduce-window(s32[8,8,128]{2,1,0:T(8,128)S(1)} %fusion.47, s32[]{:T(128)} %constant.16.clone.1), window={size=1x1x128 pad=0_0x0_0x127_0}, to_apply=%region_5.6 | reduce-window | flops 1040384 | bytes 65540 | tf_op jit(solution)/shard_map/reduce-window.2
  50.9 1.8 constant_dynamic-slice_fusion.2
  52.7 3.3 %collective-permute-start.3 = (bf16[128,1536]{1,0:T(8,128)(2,1)}, bf16[128,1536]{1,0:T(8,128)(2,1)}, u32[]{:S(2)}, u32[]{:S(2)}) collective-permute-start(bf16[128,1536]{1,0:T(8,128)(2,1)} %constant_dynamic-slice_fusion.2), channel_id=1, source_target_pairs={{0,8},{8,0},{1,9},{9,1},{2,10},{10,2},{3,11},{11,3},{4,12},{12,4},... | collective-permute-start | bytes 1179656 | tf_op jit(solution)/shard_map/ppermute | solution.py:152
  56.0 0.3 slice_reduce_fusion
  56.3 0.1 eq.146
  56.4 0.2 reduce-window.19
  56.6 17.0 %collective-permute-done.3 = bf16[128,1536]{1,0:T(8,128)(2,1)} collective-permute-done((bf16[128,1536]{1,0:T(8,128)(2,1)}, bf16[128,1536]{1,0:T(8,128)(2,1)}, u32[]{:S(2)}, u32[]{:S(2)}) %collective-permute-start.3) | collective-permute-done | bytes 393248 | tf_op jit(solution)/shard_map/ppermute | solution.py:152
  73.6 0.1 sub.71
  73.8 0.2 fusion.32
  74.1 1.6 collective-permute-done.4
  75.7 3.0 %convolution_convert_fusion.2 = bf16[384,1536]{1,0:T(8,128)(2,1)} fusion(bf16[256,384]{1,0:T(8,128)(2,1)S(1)} %fusion.32, bf16[128,1536]{1,0:T(8,128)(2,1)} %collective-permute-done.4, bf16[128,1536]{1,0:T(8,128)(2,1)} %collective-permute-done.3, pred[]{:T(512)S(6)} %eq.129), kind=kOutput, calls=%fused_computation.10 | convolution fusion | flops 306118656 | bytes 2162689 | tf_op jit(solution)/shard_map/dot_general | solution.py:179
  78.7 4.5 %all-to-all-start.1 = ((bf16[4,96,1536]{2,1,0:T(8,128)(2,1)}), bf16[4,96,1536]{2,1,0:T(8,128)(2,1)}, u32[]{:S(2)}, u32[]{:S(2)}) async-start(bf16[4,96,1536]{2,1,0:T(8,128)(2,1)} %bitcast.99), calls=%async_computation.1 | async-start | bytes 2359296 | tf_op jit(solution)/shard_map/all_to_all | solution.py:183
  83.1 2.4 %constant_dynamic-update-slice_fusion.1 = bf16[8,96,1536]{2,1,0:T(8,128)(2,1)} fusion(bf16[4,96,1536]{2,1,0:T(8,128)(2,1)} %all-to-all-done), kind=kLoop, calls=%fused_computation.76 | loop fusion | bytes 2359296
  85.5 13.2 %all-to-all-done.1 = bf16[4,96,1536]{2,1,0:T(8,128)(2,1)} async-done(((bf16[4,96,1536]{2,1,0:T(8,128)(2,1)}), bf16[4,96,1536]{2,1,0:T(8,128)(2,1)}, u32[]{:S(2)}, u32[]{:S(2)}) %all-to-all-start.1) | async-done | bytes 1179680 | tf_op jit(solution)/shard_map/all_to_all | solution.py:183
  98.6 2.5 %constant_dynamic-update-slice_fusion = bf16[8,96,1536]{2,1,0:T(8,128)(2,1)} fusion(bf16[8,96,1536]{2,1,0:T(8,128)(2,1)} %constant_dynamic-update-slice_fusion.1, bf16[4,96,1536]{2,1,0:T(8,128)(2,1)} %all-to-all-done.1), kind=kLoop, calls=%fused_computation.75 | loop fusion | bytes 2359296 | tf_op jit(solution)/shard_map/concatenate | solution.py:239
  101.2 6.6 %fusion.13 = f32[2,768,768]{2,1,0:T(8,128)S(1)} fusion(bf16[768,1536,1]{1,0,2:T(8,128)(2,1)} %bitcast.100, bf16[1,2,1536,768]{3,2,1,0:T(8,128)(2,1)} %param.20), kind=kOutput, calls=%fused_computation.22 | convolution fusion | flops 3623878656 | bytes 11796480 | tf_op jit(solution)/shard_map/rd,kdf->krf/dot_general | solution.py:56
  107.8 0.7 fusion.31
  108.5 3.8 %fusion.16 = f32[2,768,768]{2,1,0:T(8,128)S(1)} fusion(bf16[768,1536,1]{1,0,2:T(8,128)(2,1)S(1)} %bitcast.105, bf16[1,2,1536,768]{3,2,1,0:T(8,128)(2,1)S(1)} %bitcast.104), kind=kOutput, calls=%fused_computation.23 | convolution fusion | flops 3623878656 | bytes 11796480 | tf_op jit(solution)/shard_map/rd,kdf->krf/dot_general | solution.py:56
  112.3 2.1 %convolution_convert_fusion = bf16[768,1536]{1,0:T(8,128)(2,1)S(1)} fusion(bf16[1,768,1536]{2,1,0:T(8,128)(2,1)S(1)} %copy-done.8, f32[2,768,768]{2,1,0:T(8,128)S(1)} %fusion.16), kind=kOutput, calls=%fused_computation.8 | convolution fusion | flops 1817837568 | bytes 9437184 | tf_op jit(solution)/shard_map/dot_general | solution.py:139
  114.4 0.6 collective-permute-start.6
  115.0 2.0 %convolution_convert_fusion.1 = bf16[768,1536]{1,0:T(8,128)(2,1)S(1)} fusion(bf16[768,768]{1,0:T(8,128)(2,1)S(1)} %fusion.31, bf16[1,768,1536]{2,1,0:T(8,128)(2,1)S(1)} %copy-done.8), kind=kOutput, calls=%fused_computation.9 | convolution fusion | flops 1813118976 | bytes 5898240 | tf_op jit(solution)/shard_map/dot_general | solution.py:144
  117.0 2.2 %collective-permute-done.6 = bf16[8,96,1536]{2,1,0:T(8,128)(2,1)S(1)} collective-permute-done((bf16[8,96,1536]{2,1,0:T(8,128)(2,1)S(1)}, bf16[8,96,1536]{2,1,0:T(8,128)(2,1)S(1)}, u32[]{:S(2)}, u32[]{:S(2)}) %collective-permute-start.6) | collective-permute-done | bytes 2359328 | tf_op jit(solution)/shard_map/ppermute | solution.py:25
  119.2 0.7 fusion
  119.8 1.2 fusion.51
  121.1 19.6 %all_to_all.20 = bf16[4,96,1536]{2,1,0:T(8,128)(2,1)} all-to-all(bf16[4,96,1536]{2,1,0:T(8,128)(2,1)S(1)} %get-tuple-element.12), channel_id=1, replica_groups=mesh['groups'=2,'half'=2,'quad'=4,'exp'=2] {'quad'}, dimensions={0} | all-to-all | bytes 2359296 | tf_op jit(solution)/shard_map/all_to_all | solution.py:242
  140.7 4.3 %all-to-all-start.2 = ((bf16[4,96,1536]{2,1,0:T(8,128)(2,1)}), bf16[4,96,1536]{2,1,0:T(8,128)(2,1)}, u32[]{:S(2)}, u32[]{:S(2)}) async-start(bf16[4,96,1536]{2,1,0:T(8,128)(2,1)} %get-tuple-element.11), calls=%async_computation.2 | async-start | bytes 2359296 | tf_op jit(solution)/shard_map/all_to_all | solution.py:241
  145.0 2.6 %collective-permute-start.8 = (f32[256,4]{0,1:T(4,128)S(1)}, f32[256,4]{0,1:T(4,128)S(1)}, u32[]{:S(2)}, u32[]{:S(2)}) collective-permute-start(f32[256,4]{0,1:T(4,128)S(1)} %copy-done.9), channel_id=1, source_target_pairs={{0,8},{8,0},{1,9},{9,1},{2,10},{10,2},{3,11},{11,3},{4,12},{12,4},... | collective-permute-start | bytes 12296 | tf_op jit(solution)/shard_map/ppermute | solution.py:152
  147.6 9.8 %collective-permute-done.8 = f32[256,4]{0,1:T(4,128)S(1)} collective-permute-done((f32[256,4]{0,1:T(4,128)S(1)}, f32[256,4]{0,1:T(4,128)S(1)}, u32[]{:S(2)}, u32[]{:S(2)}) %collective-permute-start.8) | collective-permute-done | bytes 4128 | tf_op jit(solution)/shard_map/ppermute | solution.py:152
  157.4 3.5 %multiply_reduce_fusion = f32[256,1536]{1,0:T(8,128)S(1)} fusion(f32[256,4]{0,1:T(4,128)S(1)} %collective-permute-done.8, bf16[384,1536,1]{1,0,2:T(8,128)(2,1)} %bitcast.98, s32[256,4]{0,1:T(4,128)S(1)} %add_select_fusion), kind=kOutput, calls=%fused_computation | convolution fusion | flops 1211105280 | bytes 2760704 | tf_op jit(solution)/shard_map/dot_general | solution.py:189
  160.9 1.1 copy-done.4
  162.1 0.9 constant_dynamic-slice_fusion
  163.0 3.6 %multiply_reduce_fusion.1 = f32[256,1536]{1,0:T(8,128)S(1)} fusion(bf16[384,1536,1]{1,0,2:T(8,128)(2,1)} %bitcast.22, f32[256,4]{0,1:T(4,128)S(1)} %copy-done.9, s32[256,4]{0,1:T(4,128)S(1)} %add_select_fusion.1), kind=kOutput, calls=%fused_computation.1 | convolution fusion | flops 1211105280 | bytes 2760704 | tf_op jit(solution)/shard_map/dot_general | solution.py:189
  166.7 0.6 collective-permute-start.7
  167.3 1.3 add_convert_fusion.1
  168.5 3.4 %collective-permute-start.10 = (bf16[128,1536]{1,0:T(8,128)(2,1)S(1)}, bf16[128,1536]{1,0:T(8,128)(2,1)S(1)}, u32[]{:S(2)}, u32[]{:S(2)}) collective-permute-start(bf16[128,1536]{1,0:T(8,128)(2,1)S(1)} %add_convert_fusion.1), channel_id=1, source_target_pairs={{0,8},{8,0},{1,9},{9,1},{2,10},{10,2},{3,11},{11,3},{4,12},{12,4},... | collective-permute-start | bytes 1179656 | tf_op jit(solution)/shard_map/ppermute | solution.py:152
  171.9 17.8 %collective-permute-done.10 = bf16[128,1536]{1,0:T(8,128)(2,1)S(1)} collective-permute-done((bf16[128,1536]{1,0:T(8,128)(2,1)S(1)}, bf16[128,1536]{1,0:T(8,128)(2,1)S(1)}, u32[]{:S(2)}, u32[]{:S(2)}) %collective-permute-start.10) | collective-permute-done | bytes 393248 | tf_op jit(solution)/shard_map/ppermute | solution.py:152
  189.7 0.2 add_convert_fusion
  190.0 1.7 collective-permute-done.11
  191.7 1.0 maximum_select_fusion.2
  (48 shorter events, 0.6 us)
Async XLA Ops:
  0.0 17.0 %copy-start = (bf16[1024,1536]{1,0:T(8,128)(2,1)S(1)}, bf16[1024,1536]{1,0:T(8,128)(2,1)}, u32[]{:S(2)}) copy-start(bf16[1024,1536]{1,0:T(8,128)(2,1)} %param.17) | copy-start | bytes 9437188
  0.9 6.9 %collective-permute-start = (bf16[2,128,128]{2,1,0:T(8,128)(2,1)S(1)}, bf16[2,128,128]{2,1,0:T(8,128)(2,1)S(1)}, u32[]{:S(2)}, u32[]{:S(2)}) collective-permute-start(bf16[2,128,128]{2,1,0:T(8,128)(2,1)S(1)} %pad_maximum_fusion), channel_id=1, source_target_pairs={{0,2},{2,4},{4,6},{6,8},{8,10},{10,12},{12,14},{1,3},{3,5},{5,7},{... | collective-permute-start | bytes 196616 | tf_op jit(solution)/shard_map/ppermute | solution.py:20
  17.0 3.2 %copy-start.6 = (s32[256,4]{0,1:T(4,128)S(1)}, s32[256,4]{0,1:T(4,128)}, u32[]{:S(2)}) copy-start(s32[256,4]{0,1:T(4,128)} %param.22) | copy-start | bytes 12292
  20.2 3.8 %collective-permute-start.1 = (f32[256,1536]{1,0:T(8,128)}, f32[256,1536]{1,0:T(8,128)}, u32[]{:S(2)}, u32[]{:S(2)}) collective-permute-start(f32[256,1536]{1,0:T(8,128)} %fusion.52), channel_id=1, source_target_pairs={{0,1},{1,0},{2,3},{3,2},{4,5},{5,4},{6,7},{7,6},{8,9},{9,8},{10,11... | collective-permute-start | bytes 4718600 | tf_op jit(solution)/shard_map/ppermute | solution.py:25
  23.9 3.6 %copy-start.7 = (f32[1536]{0:T(1024)S(1)}, f32[1536]{0:T(1024)}, u32[]{:S(2)}) copy-start(f32[1536]{0:T(1024)} %param.19) | copy-start | bytes 18436
  26.4 1.2 copy-start.1
  27.8 0.9 copy-start.3
  30.2 48.5 %all-to-all-start = ((bf16[4,96,1536]{2,1,0:T(8,128)(2,1)}), bf16[4,96,1536]{2,1,0:T(8,128)(2,1)}, u32[]{:S(2)}, u32[]{:S(2)}) async-start(bf16[4,96,1536]{2,1,0:T(8,128)(2,1)} %bitcast.96), calls=%async_computation | async-start | bytes 2359296 | tf_op jit(solution)/shard_map/all_to_all | solution.py:183
  34.4 13.9 %collective-permute-start.2 = (s32[256,4]{0,1:T(4,128)S(1)}, s32[256,4]{0,1:T(4,128)S(1)}, u32[]{:S(2)}, u32[]{:S(2)}) collective-permute-start(s32[256,4]{0,1:T(4,128)S(1)} %copy-done.6), channel_id=1, source_target_pairs={{0,8},{8,0},{1,9},{9,1},{2,10},{10,2},{3,11},{11,3},{4,12},{12,4},... | collective-permute-start | bytes 12296 | tf_op jit(solution)/shard_map/ppermute | solution.py:152
  52.7 21.0 %collective-permute-start.3 = (bf16[128,1536]{1,0:T(8,128)(2,1)}, bf16[128,1536]{1,0:T(8,128)(2,1)}, u32[]{:S(2)}, u32[]{:S(2)}) collective-permute-start(bf16[128,1536]{1,0:T(8,128)(2,1)} %constant_dynamic-slice_fusion.2), channel_id=1, source_target_pairs={{0,8},{8,0},{1,9},{9,1},{2,10},{10,2},{3,11},{11,3},{4,12},{12,4},... | collective-permute-start | bytes 1179656 | tf_op jit(solution)/shard_map/ppermute | solution.py:152
  73.6 2.1 %collective-permute-start.4 = (bf16[128,1536]{1,0:T(8,128)(2,1)}, bf16[128,1536]{1,0:T(8,128)(2,1)}, u32[]{:S(2)}, u32[]{:S(2)}) collective-permute-start(bf16[128,1536]{1,0:T(8,128)(2,1)} %collective-permute-done.3), channel_id=1, source_target_pairs={{0,1},{1,0},{2,3},{3,2},{4,5},{5,4},{6,7},{7,6},{8,9},{9,8},{10,11... | collective-permute-start | bytes 1179656 | tf_op jit(solution)/shard_map/ppermute | solution.py:25
  78.7 20.0 %all-to-all-start.1 = ((bf16[4,96,1536]{2,1,0:T(8,128)(2,1)}), bf16[4,96,1536]{2,1,0:T(8,128)(2,1)}, u32[]{:S(2)}, u32[]{:S(2)}) async-start(bf16[4,96,1536]{2,1,0:T(8,128)(2,1)} %bitcast.99), calls=%async_computation.1 | async-start | bytes 2359296 | tf_op jit(solution)/shard_map/all_to_all | solution.py:183
  98.6 9.8 %slice-start = ((s8[4718592]{0:T(1024)(128)(4,1)}), s8[4194304]{0:T(1024)(128)(4,1)S(1)}, s32[]{:S(2)}) async-start(s8[4718592]{0:T(1024)(128)(4,1)} %bitcast.103), calls=%async_computation.4 | async-start | bytes 8388608
  101.2 7.3 %collective-permute-start.5 = (bf16[8,96,1536]{2,1,0:T(8,128)(2,1)}, bf16[8,96,1536]{2,1,0:T(8,128)(2,1)S(1)}, u32[]{:S(2)}, u32[]{:S(2)}) collective-permute-start(bf16[8,96,1536]{2,1,0:T(8,128)(2,1)} %constant_dynamic-update-slice_fusion), channel_id=1, source_target_pairs={{0,1},{1,0},{2,3},{3,2},{4,5},{5,4},{6,7},{7,6},{8,9},{9,8},{10,11... | collective-permute-start | bytes 7077896 | tf_op jit(solution)/shard_map/ppermute | solution.py:25
  101.2 7.3 %slice-start.1 = ((s8[4718592]{0:T(1024)(128)(4,1)}), s8[524288]{0:T(1024)(128)(4,1)S(1)}, s32[]{:S(2)}) async-start(s8[4718592]{0:T(1024)(128)(4,1)} %bitcast.103), calls=%async_computation.5 | async-start | bytes 1048576
  108.5 3.8 %copy-start.8 = (bf16[1,768,1536]{2,1,0:T(8,128)(2,1)S(1)}, bf16[1,768,1536]{2,1,0:T(8,128)(2,1)}, u32[]{:S(2)}) copy-start(bf16[1,768,1536]{2,1,0:T(8,128)(2,1)} %param.21) | copy-start | bytes 7077892
  114.4 4.8 %collective-permute-start.6 = (bf16[8,96,1536]{2,1,0:T(8,128)(2,1)S(1)}, bf16[8,96,1536]{2,1,0:T(8,128)(2,1)S(1)}, u32[]{:S(2)}, u32[]{:S(2)}) collective-permute-start(bf16[8,96,1536]{2,1,0:T(8,128)(2,1)S(1)} %bitcast.106), channel_id=1, source_target_pairs={{0,1},{1,0},{2,3},{3,2},{4,5},{5,4},{6,7},{7,6},{8,9},{9,8},{10,11... | collective-permute-start | bytes 7077896 | tf_op jit(solution)/shard_map/ppermute | solution.py:25
  121.1 23.9 %copy-start.9 = (f32[256,4]{0,1:T(4,128)S(1)}, f32[256,4]{0,1:T(4,128)}, u32[]{:S(2)}) copy-start(f32[256,4]{0,1:T(4,128)} %param.23) | copy-start | bytes 12292
  140.7 22.3 %all-to-all-start.2 = ((bf16[4,96,1536]{2,1,0:T(8,128)(2,1)}), bf16[4,96,1536]{2,1,0:T(8,128)(2,1)}, u32[]{:S(2)}, u32[]{:S(2)}) async-start(bf16[4,96,1536]{2,1,0:T(8,128)(2,1)} %get-tuple-element.11), calls=%async_computation.2 | async-start | bytes 2359296 | tf_op jit(solution)/shard_map/all_to_all | solution.py:241
  145.0 12.4 %collective-permute-start.8 = (f32[256,4]{0,1:T(4,128)S(1)}, f32[256,4]{0,1:T(4,128)S(1)}, u32[]{:S(2)}, u32[]{:S(2)}) collective-permute-start(f32[256,4]{0,1:T(4,128)S(1)} %copy-done.9), channel_id=1, source_target_pairs={{0,8},{8,0},{1,9},{9,1},{2,10},{10,2},{3,11},{11,3},{4,12},{12,4},... | collective-permute-start | bytes 12296 | tf_op jit(solution)/shard_map/ppermute | solution.py:152
  160.9 1.2 copy-start.4
  163.0 4.3 %collective-permute-start.9 = (f32[128,1536]{1,0:T(8,128)}, f32[128,1536]{1,0:T(8,128)}, u32[]{:S(2)}, u32[]{:S(2)}) collective-permute-start(f32[128,1536]{1,0:T(8,128)} %constant_dynamic-slice_fusion), channel_id=1, source_target_pairs={{0,1},{1,0},{2,3},{3,2},{4,5},{5,4},{6,7},{7,6},{8,9},{9,8},{10,11... | collective-permute-start | bytes 2359304 | tf_op jit(solution)/shard_map/ppermute | solution.py:25
  163.0 4.3 %copy-start.5 = (f32[256,1536]{1,0:T(8,128)S(1)}, f32[256,1536]{1,0:T(8,128)}, u32[]{:S(2)}) copy-start(f32[256,1536]{1,0:T(8,128)} %copy-done.4) | copy-start | bytes 4718596
  166.6 23.1 %copy-start.2 = (f32[256,1536]{1,0:T(8,128)S(1)}, f32[256,1536]{1,0:T(8,128)}, u32[]{:S(2)}) copy-start(f32[256,1536]{1,0:T(8,128)} %copy-done.1) | copy-start | bytes 4718596
  166.7 5.2 %collective-permute-start.7 = (f32[128,1536]{1,0:T(8,128)S(1)}, f32[128,1536]{1,0:T(8,128)S(1)}, u32[]{:S(2)}, u32[]{:S(2)}) collective-permute-start(f32[128,1536]{1,0:T(8,128)S(1)} %constant_dynamic-slice_fusion.1), channel_id=1, source_target_pairs={{0,1},{1,0},{2,3},{3,2},{4,5},{5,4},{6,7},{7,6},{8,9},{9,8},{10,11... | collective-permute-start | bytes 2359304 | tf_op jit(solution)/shard_map/ppermute | solution.py:25
  168.5 21.2 %collective-permute-start.10 = (bf16[128,1536]{1,0:T(8,128)(2,1)S(1)}, bf16[128,1536]{1,0:T(8,128)(2,1)S(1)}, u32[]{:S(2)}, u32[]{:S(2)}) collective-permute-start(bf16[128,1536]{1,0:T(8,128)(2,1)S(1)} %add_convert_fusion.1), channel_id=1, source_target_pairs={{0,8},{8,0},{1,9},{9,1},{2,10},{10,2},{3,11},{11,3},{4,12},{12,4},... | collective-permute-start | bytes 1179656 | tf_op jit(solution)/shard_map/ppermute | solution.py:152
  189.9 1.8 collective-permute-start.11

commit v8 on v6

--- a/solution.py
+++ b/solution.py
@@ -160,10 +160,15 @@
     slots = experts * half
     core = lax.axis_index("exp")
     flat_experts = routes.reshape(-1)
-    expert_hits = (flat_experts[:, None] == jnp.arange(experts, dtype=jnp.int32)[None, :]).astype(
-        jnp.int32
-    )
-    slot_rank = jnp.sum(expert_hits * (jnp.cumsum(expert_hits, axis=0) - 1), axis=1)
+    route_hits = (routes[:, :, None] == jnp.arange(experts, dtype=jnp.int32)[None, None, :]).astype(
+        jnp.float32
+    )
+    token_hits = jnp.sum(route_hits, axis=1)
+    earlier = (
+        jnp.arange(tok_rows, dtype=jnp.int32)[None, :] < jnp.arange(tok_rows, dtype=jnp.int32)[:, None]
+    ).astype(jnp.bfloat16)
+    before = jnp.dot(earlier, token_hits.astype(jnp.bfloat16), preferred_element_type=jnp.float32)
+    slot_rank = jnp.sum(route_hits * before[:, None, :], axis=2).astype(jnp.int32).reshape(-1)
     local_rank = slot_rank - core * half
     mine = (local_rank >= 0) & (local_rank < half)
     slot_id = jnp.where(mine, flat_experts * half + local_rank, -1)
@@ -192,9 +197,15 @@
     )
     result = (own_part.astype(jnp.float32) + their_part.astype(jnp.float32)).astype(jnp.bfloat16)
     returned = lax.all_to_all(result, "seq", split_axis=0, concat_axis=0, tiled=True)
-    picked = jnp.dot(pick, returned.reshape(slots, width), preferred_element_type=jnp.float32)
-    weighted = jnp.sum(picked.reshape(tok_rows, TOP, width) * route_gates[:, :, None], axis=1)
-    moe = weighted + swap_exp(weighted)
+    flat_returned = returned.reshape(slots, width)
+    outs = []
+    for rows in (slice(0, tok_rows // 2), slice(tok_rows // 2, tok_rows)):
+        picked = jnp.dot(
+            pick[rows.start * TOP : rows.stop * TOP], flat_returned, preferred_element_type=jnp.float32
+        )
+        weighted = jnp.sum(picked.reshape(-1, TOP, width) * route_gates[rows][:, :, None], axis=1)
+        outs.append((weighted, swap_exp(weighted)))
+    moe = jnp.concatenate([mine + theirs for mine, theirs in outs], axis=0)
     return (mixed_rows + moe).astype(jnp.bfloat16)
 
 

time: 170 us -> 174 us (1.024)
  blocking collectives: 118 us -> 59.8 us
  waiting for transfers between devices: 7.49 us -> 58.6 us
  starting transfers between devices: 5.64 us -> 10.8 us
  matrix products: 18.8 us -> 22.3 us
  local copies, waits for them, and re-layouts: 2.58 us -> 5.89 us
    all_to_all x1 -> x0, blocking collectives: 57.8 us -> none  [on_device(): lax.all_to_all(result, 'seq', split_axis=0, concat_axis=0, tiled=True)]
    all_to_all x0 -> x1, waiting for transfers between devices: none -> 49.6 us  [on_device(): lax.all_to_all(result, 'seq', split_axis=0, concat_axis=0, tiled=True)]
    all_to_all x0 -> x1, starting transfers between devices: none -> 4.59 us  [on_device(): lax.all_to_all(result, 'seq', split_axis=0, concat_axis=0, tiled=True)]
    dot_general x1 -> x3, matrix products: 3.03 us -> 6.57 us  [the longest x2 6.42 us: on_device(): jnp.dot(pick[rows.start * TOP:rows.stop * TOP], flat_returned, preferred_...]
    dot_general x0 -> x2, local copies, waits for them, and re-layouts: none -> 3.21 us  [on_device(): jnp.dot(pick[rows.start * TOP:rows.stop * TOP], flat_returned, preferred_...]
    another operation x2 -> x0, other arithmetic: 2.43 us -> none
    ppermute x4 -> x5, waiting for transfers between devices: 5.61 us -> 7.07 us  [swap_exp(): return lax.ppermute(x, 'exp', [(i, (i + 1) % size) for i in range(size)])]
  transfers between devices with their start and end apart: 5 -> 7, of which waited for: 3 -> 5; matrix products, arithmetic and copies ran while one was open for 6% -> 9% of each run, Pallas kernels for 0% -> 0%
where the time goes in v8:
time: 174 us
  blocking collectives  59.8 us (34%)
  waiting for transfers between devices  58.6 us (34%)
  matrix products  22.3 us (13%)
  starting transfers between devices  10.8 us (6%)
  other arithmetic  8.44 us (5%)
  Pallas kernels  7.73 us (4%)
  local copies, waits for them, and re-layouts  5.89 us (3%)
    all_to_all x1, blocking collectives, on_device(): lax.all_to_all(outgoing, 'seq', split_axis=0, concat_axis=0, tiled=True)  59.8 us
    all_to_all x1, waiting for transfers between devices, on_device(): lax.all_to_all(result, 'seq', split_axis=0, concat_axis=0, tiled=True)  49.6 us
    pallas_call x1, Pallas kernels, attend_kernel(): pl.pallas_call(attention_kernel, out_shape=jax.ShapeDtypeStruct((rows, co...  7.73 us
    dot_general x2, matrix products, expert_hidden(): jnp.einsum('rd,kdf->krf', rows, expert_in, preferred_element_type=jnp.flo...  7.62 us
    ppermute x5, waiting for transfers between devices, swap_exp(): return lax.ppermute(x, 'exp', [(i, (i + 1) % size) for i in range(size)])  7.07 us
    dot_general x2, matrix products, on_device(): jnp.dot(pick[rows.start * TOP:rows.stop * TOP], flat_returned, preferred_...  6.42 us
    ppermute x1, starting transfers between devices, shifted(): return lax.ppermute(shard, axis, pairs)  5.01 us
    all_to_all x1, starting transfers between devices, on_device(): lax.all_to_all(result, 'seq', split_axis=0, concat_axis=0, tiled=True)  4.59 us
  transfers between devices with their start and end apart: 7, of which 5 were waited for; matrix products, arithmetic and copies ran while one was open for 9% of the time, Pallas kernels for 0%

profile of v8, /device:TPU:0, one launch (start us, length us, event | category | flops | bytes accessed | tf_op | source)
XLA Modules:
  0.0 173.7 jit_solution(1675415414698829962)
XLA Ops:
  0.0 0.0 copy-start
  0.0 0.9 slice_bitcast_fusion.2
  0.9 5.0 %collective-permute-start = (bf16[2,128,128]{2,1,0:T(8,128)(2,1)S(1)}, bf16[2,128,128]{2,1,0:T(8,128)(2,1)S(1)}, u32[]{:S(2)}, u32[]{:S(2)}) collective-permute-start(bf16[2,128,128]{2,1,0:T(8,128)(2,1)S(1)} %pad_maximum_fusion), channel_id=1, source_target_pairs={{0,2},{2,4},{4,6},{6,8},{8,10},{10,12},{12,14},{1,3},{3,5},{5,7},{... | collective-permute-start | bytes 196616 | tf_op jit(solution)/shard_map/ppermute | solution.py:20
  6.0 1.9 %collective-permute-done = bf16[2,128,128]{2,1,0:T(8,128)(2,1)S(1)} collective-permute-done((bf16[2,128,128]{2,1,0:T(8,128)(2,1)S(1)}, bf16[2,128,128]{2,1,0:T(8,128)(2,1)S(1)}, u32[]{:S(2)}, u32[]{:S(2)}) %collective-permute-start) | collective-permute-done | bytes 65568 | tf_op jit(solution)/shard_map/ppermute | solution.py:20
  7.8 0.8 broadcast_select_fusion
  8.7 0.6 slice_bitcast_fusion
  9.3 7.7 %shard_map.118 = bf16[256,1024]{1,0:T(8,128)(2,1)} custom-call(f32[16]{0:T(128)} %sink_ref.1, bf16[256,1024]{1,0:T(8,128)(2,1)} %q_ref.1, bf16[128,128]{1,0:T(8,128)(2,1)} %get-tuple-element.14.pk_ref, bf16[256,128]{1,0:T(8,128)(2,1)} %k_ref.1, bf16[128,128]{1,0:T(8,128)(2,1)} %get-tuple-element.13.pv_ref, bf16[256,128]{1,0:T(8,128)(2,1)} %v_ref.1), custom_call_target="tpu_custom_call" | custom-call | flops 536870912 | bytes 1245184 | tf_op jit(solution)/shard_map/pallas_call | solution.py:123
  17.0 0.0 copy-done
  17.0 0.0 copy-start.4
  17.1 3.2 %fusion.38 = f32[256,1536]{1,0:T(8,128)} fusion(bf16[256,1024]{1,0:T(8,128)(2,1)} %shard_map.118, bf16[1024,1536]{1,0:T(8,128)(2,1)S(1)} %copy-done), kind=kOutput, calls=%fused_computation.60 | convolution fusion | flops 805306368 | bytes 5242880 | tf_op jit(solution)/shard_map/dot_general | solution.py:152
  20.2 0.0 collective-permute-start.1
  20.2 0.0 copy-done.4
  20.2 0.2 fusion.32
  20.4 0.1 select_reduce_fusion
  20.5 0.4 fusion.22
  20.9 0.0 copy-start.5
  20.9 3.1 %collective-permute-done.1 = f32[256,1536]{1,0:T(8,128)} collective-permute-done((f32[256,1536]{1,0:T(8,128)}, f32[256,1536]{1,0:T(8,128)}, u32[]{:S(2)}, u32[]{:S(2)}) %collective-permute-start.1) | collective-permute-done | bytes 1572896 | tf_op jit(solution)/shard_map/ppermute | solution.py:25
  24.0 0.0 slice-start
  24.0 2.6 %multiply_reduce_fusion = (f32[256]{0:T(256)S(1)}, f32[256,1536]{1,0:T(8,128)S(1)}) fusion(f32[256,1536]{1,0:T(8,128)} %fusion.38, f32[256,1536]{1,0:T(8,128)} %collective-permute-done.1, bf16[256,1536]{1,0:T(8,128)(2,1)} %param.18), kind=kLoop, calls=%fused_computation.32 | loop fusion | flops 1965824 | bytes 5506048 | tf_op jit(solution)/shard_map/reduce_sum | solution.py:29
  26.5 0.0 copy-start.1
  26.6 0.0 copy-done.5
  26.6 0.0 slice-start.1
  26.6 0.9 convolution_convert_fusion.2
  27.5 59.8 %all_to_all.10 = bf16[8,96,1536]{2,1,0:T(8,128)(2,1)S(1)} all-to-all(bf16[8,96,1536]{2,1,0:T(8,128)(2,1)S(1)} %bitcast.53), channel_id=1, replica_groups=mesh['groups'=2,'seq'=8,'exp'=2] {'seq'}, dimensions={0} | all-to-all | bytes 4718592 | tf_op jit(solution)/shard_map/all_to_all | solution.py:183
  87.3 0.0 copy-done.1
  87.3 0.0 collective-permute-start.2
  87.3 0.0 slice-done
  87.3 0.0 slice-done.1
  87.3 3.8 %fusion.14 = f32[2,768,768]{2,1,0:T(8,128)S(1)} fusion(bf16[768,1536,1]{1,0,2:T(8,128)(2,1)S(1)} %bitcast.55, bf16[1,2,1536,768]{3,2,1,0:T(8,128)(2,1)S(1)} %bitcast.57), kind=kOutput, calls=%fused_computation.24 | convolution fusion | flops 3623878656 | bytes 11796480 | tf_op jit(solution)/shard_map/rd,kdf->krf/dot_general | solution.py:56
  91.1 0.7 fusion.29
  91.8 0.0 collective-permute-done.2
  91.8 0.0 copy-start.7
  91.8 3.8 %fusion.17 = f32[2,768,768]{2,1,0:T(8,128)S(1)} fusion(bf16[768,1536,1]{1,0,2:T(8,128)(2,1)S(1)} %bitcast.58, bf16[1,2,1536,768]{3,2,1,0:T(8,128)(2,1)S(1)} %bitcast.57), kind=kOutput, calls=%fused_computation.25 | convolution fusion | flops 3623878656 | bytes 11796480 | tf_op jit(solution)/shard_map/rd,kdf->krf/dot_general | solution.py:56
  95.6 0.0 copy-done.7
  95.6 2.1 %convolution_convert_fusion = bf16[768,1536]{1,0:T(8,128)(2,1)S(1)} fusion(bf16[1,768,1536]{2,1,0:T(8,128)(2,1)S(1)} %copy-done.7, f32[2,768,768]{2,1,0:T(8,128)S(1)} %fusion.17), kind=kOutput, calls=%fused_computation.6 | convolution fusion | flops 1817837568 | bytes 9437184 | tf_op jit(solution)/shard_map/dot_general | solution.py:189
  97.7 0.5 collective-permute-start.3
  98.2 2.0 %convolution_convert_fusion.1 = bf16[768,1536]{1,0:T(8,128)(2,1)S(1)} fusion(bf16[768,768]{1,0:T(8,128)(2,1)S(1)} %fusion.29, bf16[1,768,1536]{2,1,0:T(8,128)(2,1)S(1)} %copy-done.7), kind=kOutput, calls=%fused_computation.7 | convolution fusion | flops 1813118976 | bytes 5898240 | tf_op jit(solution)/shard_map/dot_general | solution.py:194
  100.2 2.2 %collective-permute-done.3 = bf16[8,96,1536]{2,1,0:T(8,128)(2,1)S(1)} collective-permute-done((bf16[8,96,1536]{2,1,0:T(8,128)(2,1)S(1)}, bf16[8,96,1536]{2,1,0:T(8,128)(2,1)S(1)}, u32[]{:S(2)}, u32[]{:S(2)}) %collective-permute-start.3) | collective-permute-done | bytes 2359328 | tf_op jit(solution)/shard_map/ppermute | solution.py:25
  102.4 2.1 %fusion = bf16[8,96,1536]{2,1,0:T(8,128)(2,1)} fusion(bf16[8,96,1536]{2,1,0:T(8,128)(2,1)S(1)} %bitcast.54, bf16[8,96,1536]{2,1,0:T(8,128)(2,1)S(1)} %collective-permute-done.3), kind=kLoop, calls=%fused_computation.1 | loop fusion | flops 4718592 | bytes 7077888 | tf_op jit(solution)/shard_map/convert_element_type | solution.py:198
  104.5 4.6 %all-to-all-start.1 = ((bf16[8,96,1536]{2,1,0:T(8,128)(2,1)}), bf16[8,96,1536]{2,1,0:T(8,128)(2,1)}, u32[]{:S(2)}, u32[]{:S(2)}) async-start(bf16[8,96,1536]{2,1,0:T(8,128)(2,1)} %fusion), calls=%async_computation.1 | async-start | bytes 4718592 | tf_op jit(solution)/shard_map/all_to_all | solution.py:199
  109.1 0.0 copy-start.6
  109.1 0.1 copy.22
  109.2 0.1 reshape.88
  109.3 0.5 iota_compare_fusion.1
  109.9 0.8 fusion.36
  110.7 2.2 %dot_general.33 = pred[128,4,768]{2,1,0:T(4,128)(4,1)} reshape(pred[512,768]{1,0:T(8,128)(4,1)} %get-tuple-element.11) | data formatting | bytes 786432 | tf_op jit(solution)/shard_map/dot_general | solution.py:203
  112.9 1.0 dot_general.40
  113.9 0.0 copy-done.6
  113.9 49.6 %all-to-all-done.1 = bf16[8,96,1536]{2,1,0:T(8,128)(2,1)} async-done(((bf16[8,96,1536]{2,1,0:T(8,128)(2,1)}), bf16[8,96,1536]{2,1,0:T(8,128)(2,1)}, u32[]{:S(2)}, u32[]{:S(2)}) %all-to-all-start.1) | async-done | bytes 2359328 | tf_op jit(solution)/shard_map/all_to_all | solution.py:199
  163.5 0.0 copy-start.3
  163.5 3.3 %fusion.20 = f32[128,1536]{1,0:T(8,128)S(1)} fusion(bf16[768,1536,1]{1,0,2:T(8,128)(2,1)} %bitcast.18, f32[128,4]{0,1:T(4,128)S(1)} %get-tuple-element.15, pred[128,4,768]{2,1,0:T(4,128)(4,1)} %dot_general.33), kind=kOutput, calls=%fused_computation.26 | convolution fusion | flops 1209335808 | bytes 3540992 | tf_op jit(solution)/shard_map/dot_general | solution.py:203
  166.8 0.1 collective-permute-start.4
  166.9 0.0 copy-done.3
  166.9 3.1 %fusion.21 = f32[128,1536]{1,0:T(8,128)S(1)} fusion(bf16[768,1536,1]{1,0,2:T(8,128)(2,1)} %bitcast.18, f32[128,4]{0,1:T(4,128)S(1)} %get-tuple-element.16, pred[128,4,768]{2,1,0:T(4,128)(4,1)S(1)} %copy-done.3), kind=kOutput, calls=%fused_computation.27 | convolution fusion | flops 1209335808 | bytes 3540992 | tf_op jit(solution)/shard_map/dot_general | solution.py:203
  170.0 0.0 copy-start.2
  170.1 0.6 collective-permute-start.5
  170.6 0.0 collective-permute-done.4
  170.6 0.1 add.66
  170.7 1.8 %collective-permute-done.5 = f32[128,1536]{1,0:T(8,128)S(1)} collective-permute-done((f32[128,1536]{1,0:T(8,128)S(1)}, f32[128,1536]{1,0:T(8,128)S(1)}, u32[]{:S(2)}, u32[]{:S(2)}) %collective-permute-start.5) | collective-permute-done | bytes 786464 | tf_op jit(solution)/shard_map/ppermute | solution.py:25
  172.5 0.1 add.67
  172.6 0.0 copy-done.2
  172.6 1.1 fusion.23
  (6 shorter events, 0.0 us)
Async XLA Ops:
  0.0 17.0 %copy-start = (bf16[1024,1536]{1,0:T(8,128)(2,1)S(1)}, bf16[1024,1536]{1,0:T(8,128)(2,1)}, u32[]{:S(2)}) copy-start(bf16[1024,1536]{1,0:T(8,128)(2,1)} %param.17) | copy-start | bytes 9437188
  0.9 6.9 %collective-permute-start = (bf16[2,128,128]{2,1,0:T(8,128)(2,1)S(1)}, bf16[2,128,128]{2,1,0:T(8,128)(2,1)S(1)}, u32[]{:S(2)}, u32[]{:S(2)}) collective-permute-start(bf16[2,128,128]{2,1,0:T(8,128)(2,1)S(1)} %pad_maximum_fusion), channel_id=1, source_target_pairs={{0,2},{2,4},{4,6},{6,8},{8,10},{10,12},{12,14},{1,3},{3,5},{5,7},{... | collective-permute-start | bytes 196616 | tf_op jit(solution)/shard_map/ppermute | solution.py:20
  17.0 3.2 %copy-start.4 = (s32[256,4]{0,1:T(4,128)S(1)}, s32[256,4]{0,1:T(4,128)}, u32[]{:S(2)}) copy-start(s32[256,4]{0,1:T(4,128)} %param.22) | copy-start | bytes 12292
  20.2 3.8 %collective-permute-start.1 = (f32[256,1536]{1,0:T(8,128)}, f32[256,1536]{1,0:T(8,128)}, u32[]{:S(2)}, u32[]{:S(2)}) collective-permute-start(f32[256,1536]{1,0:T(8,128)} %fusion.38), channel_id=1, source_target_pairs={{0,1},{1,0},{2,3},{3,2},{4,5},{5,4},{6,7},{7,6},{8,9},{9,8},{10,11... | collective-permute-start | bytes 4718600 | tf_op jit(solution)/shard_map/ppermute | solution.py:25
  20.9 5.7 %copy-start.5 = (f32[1536]{0:T(1024)S(1)}, f32[1536]{0:T(1024)}, u32[]{:S(2)}) copy-start(f32[1536]{0:T(1024)} %param.19) | copy-start | bytes 18436
  24.0 63.3 %slice-start = ((s8[4718592]{0:T(1024)(128)(4,1)}), s8[4194304]{0:T(1024)(128)(4,1)S(1)}, s32[]{:S(2)}) async-start(s8[4718592]{0:T(1024)(128)(4,1)} %bitcast.56), calls=%async_computation.2 | async-start | bytes 8388608
  26.5 60.7 %copy-start.1 = (f32[256,1536]{1,0:T(8,128)}, f32[256,1536]{1,0:T(8,128)S(1)}, u32[]{:S(2)}) copy-start(f32[256,1536]{1,0:T(8,128)S(1)} %get-tuple-element.10) | copy-start | bytes 4718596
  26.6 60.7 %slice-start.1 = ((s8[4718592]{0:T(1024)(128)(4,1)}), s8[524288]{0:T(1024)(128)(4,1)S(1)}, s32[]{:S(2)}) async-start(s8[4718592]{0:T(1024)(128)(4,1)} %bitcast.56), calls=%async_computation.3 | async-start | bytes 1048576
  87.3 4.5 %collective-permute-start.2 = (bf16[8,96,1536]{2,1,0:T(8,128)(2,1)S(1)}, bf16[8,96,1536]{2,1,0:T(8,128)(2,1)S(1)}, u32[]{:S(2)}, u32[]{:S(2)}) collective-permute-start(bf16[8,96,1536]{2,1,0:T(8,128)(2,1)S(1)} %all_to_all.10), channel_id=1, source_target_pairs={{0,1},{1,0},{2,3},{3,2},{4,5},{5,4},{6,7},{7,6},{8,9},{9,8},{10,11... | collective-permute-start | bytes 7077896 | tf_op jit(solution)/shard_map/ppermute | solution.py:25
  91.8 3.8 %copy-start.7 = (bf16[1,768,1536]{2,1,0:T(8,128)(2,1)S(1)}, bf16[1,768,1536]{2,1,0:T(8,128)(2,1)}, u32[]{:S(2)}) copy-start(bf16[1,768,1536]{2,1,0:T(8,128)(2,1)} %param.21) | copy-start | bytes 7077892
  97.7 4.7 %collective-permute-start.3 = (bf16[8,96,1536]{2,1,0:T(8,128)(2,1)S(1)}, bf16[8,96,1536]{2,1,0:T(8,128)(2,1)S(1)}, u32[]{:S(2)}, u32[]{:S(2)}) collective-permute-start(bf16[8,96,1536]{2,1,0:T(8,128)(2,1)S(1)} %bitcast.59), channel_id=1, source_target_pairs={{0,1},{1,0},{2,3},{3,2},{4,5},{5,4},{6,7},{7,6},{8,9},{9,8},{10,11... | collective-permute-start | bytes 7077896 | tf_op jit(solution)/shard_map/ppermute | solution.py:25
  104.5 59.0 %all-to-all-start.1 = ((bf16[8,96,1536]{2,1,0:T(8,128)(2,1)}), bf16[8,96,1536]{2,1,0:T(8,128)(2,1)}, u32[]{:S(2)}, u32[]{:S(2)}) async-start(bf16[8,96,1536]{2,1,0:T(8,128)(2,1)} %fusion), calls=%async_computation.1 | async-start | bytes 4718592 | tf_op jit(solution)/shard_map/all_to_all | solution.py:199
  109.1 4.8 %copy-start.6 = (f32[256,4]{0,1:T(4,128)S(1)}, f32[256,4]{0,1:T(4,128)}, u32[]{:S(2)}) copy-start(f32[256,4]{0,1:T(4,128)} %param.23) | copy-start | bytes 12292
  163.5 3.4 %copy-start.3 = (pred[128,4,768]{2,1,0:T(4,128)(4,1)S(1)}, pred[128,4,768]{2,1,0:T(4,128)(4,1)}, u32[]{:S(2)}) copy-start(pred[128,4,768]{2,1,0:T(4,128)(4,1)} %dot_general.40) | copy-start | bytes 1179652
  166.8 3.8 %collective-permute-start.4 = (f32[128,1536]{1,0:T(8,128)S(1)}, f32[128,1536]{1,0:T(8,128)S(1)}, u32[]{:S(2)}, u32[]{:S(2)}) collective-permute-start(f32[128,1536]{1,0:T(8,128)S(1)} %fusion.20), channel_id=1, source_target_pairs={{0,1},{1,0},{2,3},{3,2},{4,5},{5,4},{6,7},{7,6},{8,9},{9,8},{10,11... | collective-permute-start | bytes 2359304 | tf_op jit(solution)/shard_map/ppermute | solution.py:25
  170.0 2.6 %copy-start.2 = (f32[256,1536]{1,0:T(8,128)S(1)}, f32[256,1536]{1,0:T(8,128)}, u32[]{:S(2)}) copy-start(f32[256,1536]{1,0:T(8,128)} %copy-done.1) | copy-start | bytes 4718596
  170.1 2.5 %collective-permute-start.5 = (f32[128,1536]{1,0:T(8,128)S(1)}, f32[128,1536]{1,0:T(8,128)S(1)}, u32[]{:S(2)}, u32[]{:S(2)}) collective-permute-start(f32[128,1536]{1,0:T(8,128)S(1)} %fusion.21), channel_id=1, source_target_pairs={{0,1},{1,0},{2,3},{3,2},{4,5},{5,4},{6,7},{7,6},{8,9},{9,8},{10,11... | collective-permute-start | bytes 2359304 | tf_op jit(solution)/shard_map/ppermute | solution.py:25

commit v9 on v6

--- a/solution.py
+++ b/solution.py
@@ -192,9 +192,19 @@
     )
     result = (own_part.astype(jnp.float32) + their_part.astype(jnp.float32)).astype(jnp.bfloat16)
     returned = lax.all_to_all(result, "seq", split_axis=0, concat_axis=0, tiled=True)
-    picked = jnp.dot(pick, returned.reshape(slots, width), preferred_element_type=jnp.float32)
-    weighted = jnp.sum(picked.reshape(tok_rows, TOP, width) * route_gates[:, :, None], axis=1)
-    moe = weighted + swap_exp(weighted)
+    gate_table = jnp.sum(
+        pick.reshape(tok_rows, TOP, slots).astype(jnp.float32) * route_gates[:, :, None], axis=1
+    )
+    gate_high = gate_table.astype(jnp.bfloat16)
+    gate_low = (gate_table - gate_high.astype(jnp.float32)).astype(jnp.bfloat16)
+    flat_returned = returned.reshape(slots, width)
+    parts = []
+    for rows in (slice(0, tok_rows // 2), slice(tok_rows // 2, tok_rows)):
+        weighted = jnp.dot(
+            gate_high[rows], flat_returned, preferred_element_type=jnp.float32
+        ) + jnp.dot(gate_low[rows], flat_returned, preferred_element_type=jnp.float32)
+        parts.append(weighted + swap_exp(weighted))
+    moe = jnp.concatenate(parts, axis=0)
     return (mixed_rows + moe).astype(jnp.bfloat16)
 
 

time: 170 us -> 177 us (1.041)
  blocking collectives: 118 us -> 60.1 us
  waiting for transfers between devices: 7.49 us -> 59.2 us
  matrix products: 18.8 us -> 24.5 us
  starting transfers between devices: 5.64 us -> 10.7 us
  other arithmetic: 8.98 us -> 11.8 us
    all_to_all x1 -> x0, blocking collectives: 57.8 us -> none  [on_device(): lax.all_to_all(result, 'seq', split_axis=0, concat_axis=0, tiled=True)]
    all_to_all x0 -> x1, waiting for transfers between devices: none -> 53.3 us  [on_device(): lax.all_to_all(result, 'seq', split_axis=0, concat_axis=0, tiled=True)]
    dot_general x1 -> x4, matrix products: 3.03 us -> 8.73 us  [the longest x2 4.43 us: on_device(): jnp.dot(gate_low[rows], flat_returned, preferred_element_type=jnp.float32)]
    all_to_all x0 -> x1, starting transfers between devices: none -> 4.5 us  [on_device(): lax.all_to_all(result, 'seq', split_axis=0, concat_axis=0, tiled=True)]
    ppermute x4 -> x5, waiting for transfers between devices: 5.61 us -> 4.02 us  [swap_exp(): return lax.ppermute(x, 'exp', [(i, (i + 1) % size) for i in range(size)])]
  transfers between devices with their start and end apart: 5 -> 7, of which waited for: 3 -> 4; matrix products, arithmetic and copies ran while one was open for 6% -> 8% of each run, Pallas kernels for 0% -> 0%
where the time goes in v9:
time: 177 us
  blocking collectives  60.1 us (34%)
  waiting for transfers between devices  59.2 us (33%)
  matrix products  24.5 us (14%)
  other arithmetic  11.8 us (7%)
  starting transfers between devices  10.7 us (6%)
  Pallas kernels  7.74 us (4%)
  local copies, waits for them, and re-layouts  2.59 us (1%)
    all_to_all x1, blocking collectives, on_device(): lax.all_to_all(outgoing, 'seq', split_axis=0, concat_axis=0, tiled=True)  60.1 us
    all_to_all x1, waiting for transfers between devices, on_device(): lax.all_to_all(result, 'seq', split_axis=0, concat_axis=0, tiled=True)  53.3 us
    pallas_call x1, Pallas kernels, attend_kernel(): pl.pallas_call(attention_kernel, out_shape=jax.ShapeDtypeStruct((rows, co...  7.74 us
    dot_general x2, matrix products, expert_hidden(): jnp.einsum('rd,kdf->krf', rows, expert_in, preferred_element_type=jnp.flo...  7.62 us
    ppermute x1, starting transfers between devices, shifted(): return lax.ppermute(shard, axis, pairs)  5.01 us
    all_to_all x1, starting transfers between devices, on_device(): lax.all_to_all(result, 'seq', split_axis=0, concat_axis=0, tiled=True)  4.5 us
    dot_general x2, matrix products, on_device(): jnp.dot(gate_low[rows], flat_returned, preferred_element_type=jnp.float32)  4.43 us
    dot_general x2, matrix products, on_device(): jnp.dot(gate_high[rows], flat_returned, preferred_element_type=jnp.float32)  4.29 us
  transfers between devices with their start and end apart: 7, of which 4 were waited for; matrix products, arithmetic and copies ran while one was open for 8% of the time, Pallas kernels for 0%

profile of v9, /device:TPU:0, one launch (start us, length us, event | category | flops | bytes accessed | tf_op | source)
XLA Modules:
  0.0 176.9 jit_solution(8100440221521021256)
XLA Ops:
  0.0 0.0 copy-start
  0.0 0.9 slice_bitcast_fusion.2
  0.9 5.0 %collective-permute-start = (bf16[2,128,128]{2,1,0:T(8,128)(2,1)S(1)}, bf16[2,128,128]{2,1,0:T(8,128)(2,1)S(1)}, u32[]{:S(2)}, u32[]{:S(2)}) collective-permute-start(bf16[2,128,128]{2,1,0:T(8,128)(2,1)S(1)} %pad_maximum_fusion), channel_id=1, source_target_pairs={{0,2},{2,4},{4,6},{6,8},{8,10},{10,12},{12,14},{1,3},{3,5},{5,7},{... | collective-permute-start | bytes 196616 | tf_op jit(solution)/shard_map/ppermute | solution.py:20
  6.0 1.9 %collective-permute-done = bf16[2,128,128]{2,1,0:T(8,128)(2,1)S(1)} collective-permute-done((bf16[2,128,128]{2,1,0:T(8,128)(2,1)S(1)}, bf16[2,128,128]{2,1,0:T(8,128)(2,1)S(1)}, u32[]{:S(2)}, u32[]{:S(2)}) %collective-permute-start) | collective-permute-done | bytes 65568 | tf_op jit(solution)/shard_map/ppermute | solution.py:20
  7.8 0.8 broadcast_select_fusion
  8.7 0.6 slice_bitcast_fusion
  9.3 7.7 %shard_map.118 = bf16[256,1024]{1,0:T(8,128)(2,1)} custom-call(f32[16]{0:T(128)} %sink_ref.1, bf16[256,1024]{1,0:T(8,128)(2,1)} %q_ref.1, bf16[128,128]{1,0:T(8,128)(2,1)} %get-tuple-element.14.pk_ref, bf16[256,128]{1,0:T(8,128)(2,1)} %k_ref.1, bf16[128,128]{1,0:T(8,128)(2,1)} %get-tuple-element.13.pv_ref, bf16[256,128]{1,0:T(8,128)(2,1)} %v_ref.1), custom_call_target="tpu_custom_call" | custom-call | flops 536870912 | bytes 1245184 | tf_op jit(solution)/shard_map/pallas_call | solution.py:123
  17.1 0.0 copy-done
  17.1 0.0 copy-start.4
  17.1 3.2 %fusion.39 = f32[256,1536]{1,0:T(8,128)} fusion(bf16[256,1024]{1,0:T(8,128)(2,1)} %shard_map.118, bf16[1024,1536]{1,0:T(8,128)(2,1)S(1)} %copy-done), kind=kOutput, calls=%fused_computation.64 | convolution fusion | flops 805306368 | bytes 5242880 | tf_op jit(solution)/shard_map/dot_general | solution.py:152
  20.3 0.0 collective-permute-start.1
  20.3 0.0 copy-done.4
  20.3 0.1 copy.20
  20.4 0.1 eq.47
  20.5 0.1 eq.43
  20.7 2.3 %reduce-window.6 = s32[8,8,128]{2,1,0:T(8,128)S(1)} reduce-window(s32[8,8,128]{2,1,0:T(8,128)S(1)} %fusion.36, s32[]{:T(128)} %constant.13.clone.1), window={size=1x1x128 pad=0_0x0_0x127_0}, to_apply=%region_0.1 | reduce-window | flops 1040384 | bytes 65540 | tf_op jit(solution)/shard_map/reduce-window
  22.9 0.3 slice_reduce_fusion
  23.2 0.2 reduce-window.9
  23.4 0.1 add_bitcast_fusion
  23.5 0.1 sub.29
  23.6 0.1 copy.23
  23.8 0.1 copy.24
  23.9 0.4 fusion.20
  24.4 0.0 copy-start.5
  24.4 0.0 collective-permute-done.1
  24.4 0.0 slice-start
  24.4 2.6 %multiply_reduce_fusion.1 = (f32[256]{0:T(256)S(1)}, f32[256,1536]{1,0:T(8,128)S(1)}) fusion(f32[256,1536]{1,0:T(8,128)} %fusion.39, f32[256,1536]{1,0:T(8,128)} %collective-permute-done.1, bf16[256,1536]{1,0:T(8,128)(2,1)} %param.18), kind=kLoop, calls=%fused_computation.30 | loop fusion | flops 1965824 | bytes 5506048 | tf_op jit(solution)/shard_map/reduce_sum | solution.py:29
  27.0 0.0 copy-done.5
  27.0 0.0 slice-start.1
  27.0 0.9 convolution_convert_fusion.2
  27.9 60.1 %all_to_all.10 = bf16[8,96,1536]{2,1,0:T(8,128)(2,1)S(1)} all-to-all(bf16[8,96,1536]{2,1,0:T(8,128)(2,1)S(1)} %bitcast.67), channel_id=1, replica_groups=mesh['groups'=2,'seq'=8,'exp'=2] {'seq'}, dimensions={0} | all-to-all | bytes 4718592 | tf_op jit(solution)/shard_map/all_to_all | solution.py:178
  88.0 0.0 copy-done.1
  88.0 0.0 collective-permute-start.2
  88.0 0.0 slice-done
  88.0 0.0 slice-done.1
  88.0 3.8 %fusion.14 = f32[2,768,768]{2,1,0:T(8,128)S(1)} fusion(bf16[768,1536,1]{1,0,2:T(8,128)(2,1)S(1)} %bitcast.69, bf16[1,2,1536,768]{3,2,1,0:T(8,128)(2,1)S(1)} %bitcast.72), kind=kOutput, calls=%fused_computation.24 | convolution fusion | flops 3623878656 | bytes 11796480 | tf_op jit(solution)/shard_map/rd,kdf->krf/dot_general | solution.py:56
  91.9 0.7 fusion.25
  92.5 0.0 collective-permute-done.2
  92.5 3.8 %fusion.17 = f32[2,768,768]{2,1,0:T(8,128)S(1)} fusion(bf16[768,1536,1]{1,0,2:T(8,128)(2,1)S(1)} %bitcast.73, bf16[1,2,1536,768]{3,2,1,0:T(8,128)(2,1)S(1)} %bitcast.72), kind=kOutput, calls=%fused_computation.25 | convolution fusion | flops 3623878656 | bytes 11796480 | tf_op jit(solution)/shard_map/rd,kdf->krf/dot_general | solution.py:56
  96.4 0.0 copy-done.7
  96.4 2.1 %convolution_convert_fusion = bf16[768,1536]{1,0:T(8,128)(2,1)S(1)} fusion(bf16[1,768,1536]{2,1,0:T(8,128)(2,1)S(1)} %copy-done.7, f32[2,768,768]{2,1,0:T(8,128)S(1)} %fusion.17), kind=kOutput, calls=%fused_computation.6 | convolution fusion | flops 1817837568 | bytes 9437184 | tf_op jit(solution)/shard_map/dot_general | solution.py:184
  98.4 0.6 collective-permute-start.3
  99.0 2.0 %convolution_convert_fusion.1 = bf16[768,1536]{1,0:T(8,128)(2,1)S(1)} fusion(bf16[768,768]{1,0:T(8,128)(2,1)S(1)} %fusion.25, bf16[1,768,1536]{2,1,0:T(8,128)(2,1)S(1)} %copy-done.7), kind=kOutput, calls=%fused_computation.7 | convolution fusion | flops 1813118976 | bytes 5898240 | tf_op jit(solution)/shard_map/dot_general | solution.py:189
  101.0 2.2 %collective-permute-done.3 = bf16[8,96,1536]{2,1,0:T(8,128)(2,1)S(1)} collective-permute-done((bf16[8,96,1536]{2,1,0:T(8,128)(2,1)S(1)}, bf16[8,96,1536]{2,1,0:T(8,128)(2,1)S(1)}, u32[]{:S(2)}, u32[]{:S(2)}) %collective-permute-start.3) | collective-permute-done | bytes 2359328 | tf_op jit(solution)/shard_map/ppermute | solution.py:25
  103.2 2.1 %fusion = bf16[8,96,1536]{2,1,0:T(8,128)(2,1)} fusion(bf16[8,96,1536]{2,1,0:T(8,128)(2,1)S(1)} %bitcast.68, bf16[8,96,1536]{2,1,0:T(8,128)(2,1)S(1)} %collective-permute-done.3), kind=kLoop, calls=%fused_computation.1 | loop fusion | flops 4718592 | bytes 7077888 | tf_op jit(solution)/shard_map/convert_element_type | solution.py:193
  105.2 4.5 %all-to-all-start.1 = ((bf16[8,96,1536]{2,1,0:T(8,128)(2,1)}), bf16[8,96,1536]{2,1,0:T(8,128)(2,1)}, u32[]{:S(2)}, u32[]{:S(2)}) async-start(bf16[8,96,1536]{2,1,0:T(8,128)(2,1)} %fusion), calls=%async_computation.1 | async-start | bytes 4718592 | tf_op jit(solution)/shard_map/all_to_all | solution.py:194
  109.7 0.0 copy-done.6
  109.8 0.5 multiply_reduce_fusion
  110.3 0.8 subtract_convert_fusion
  111.1 53.3 %all-to-all-done.1 = bf16[8,96,1536]{2,1,0:T(8,128)(2,1)} async-done(((bf16[8,96,1536]{2,1,0:T(8,128)(2,1)}), bf16[8,96,1536]{2,1,0:T(8,128)(2,1)}, u32[]{:S(2)}, u32[]{:S(2)}) %all-to-all-start.1) | async-done | bytes 2359328 | tf_op jit(solution)/shard_map/all_to_all | solution.py:194
  164.4 2.3 %fusion.31 = f32[128,1536]{1,0:T(8,128)S(1)} fusion(bf16[768,1536]{1,0:T(8,128)(2,1)} %bitcast.18, bf16[256,768]{1,0:T(8,128)(2,1)} %get-tuple-element.9), kind=kOutput, calls=%fused_computation.41 | convolution fusion | flops 301989888 | bytes 3342336 | tf_op jit(solution)/shard_map/dot_general | solution.py:205
  166.7 0.0 copy-done.3
  166.7 2.1 %fusion.28 = f32[128,1536]{1,0:T(8,128)S(1)} fusion(bf16[768,1536]{1,0:T(8,128)(2,1)} %bitcast.18, bf16[256,768]{1,0:T(8,128)(2,1)S(1)} %copy-done.3), kind=kOutput, calls=%fused_computation.38 | convolution fusion | flops 301989888 | bytes 3342336 | tf_op jit(solution)/shard_map/dot_general | solution.py:205
  168.9 2.1 %convolution_add_fusion.1 = f32[128,1536]{1,0:T(8,128)S(1)} fusion(f32[128,1536]{1,0:T(8,128)S(1)} %fusion.31, bf16[768,1536]{1,0:T(8,128)(2,1)} %bitcast.18, bf16[256,768]{1,0:T(8,128)(2,1)S(1)} %get-tuple-element.10), kind=kOutput, calls=%fused_computation.13 | convolution fusion | flops 302186496 | bytes 4128768 | tf_op jit(solution)/shard_map/dot_general | solution.py:203
  171.0 0.1 collective-permute-start.4
  171.1 2.1 %convolution_add_fusion = f32[128,1536]{1,0:T(8,128)S(1)} fusion(f32[128,1536]{1,0:T(8,128)S(1)} %fusion.28, bf16[768,1536]{1,0:T(8,128)(2,1)} %bitcast.18, bf16[256,768]{1,0:T(8,128)(2,1)S(1)} %get-tuple-element.10), kind=kOutput, calls=%fused_computation.12 | convolution fusion | flops 302186496 | bytes 4128768 | tf_op jit(solution)/shard_map/dot_general | solution.py:203
  173.3 0.0 copy-start.2
  173.3 0.6 collective-permute-start.5
  173.8 0.0 collective-permute-done.4
  173.8 0.1 add.71
  173.9 1.8 %collective-permute-done.5 = f32[128,1536]{1,0:T(8,128)S(1)} collective-permute-done((f32[128,1536]{1,0:T(8,128)S(1)}, f32[128,1536]{1,0:T(8,128)S(1)}, u32[]{:S(2)}, u32[]{:S(2)}) %collective-permute-start.5) | collective-permute-done | bytes 786464 | tf_op jit(solution)/shard_map/ppermute | solution.py:25
  175.8 0.1 add.73
  175.8 0.0 copy-done.2
  175.9 1.1 fusion.21
  (12 shorter events, 0.1 us)
Async XLA Ops:
  0.0 17.1 %copy-start = (bf16[1024,1536]{1,0:T(8,128)(2,1)S(1)}, bf16[1024,1536]{1,0:T(8,128)(2,1)}, u32[]{:S(2)}) copy-start(bf16[1024,1536]{1,0:T(8,128)(2,1)} %param.17) | copy-start | bytes 9437188
  0.9 6.9 %collective-permute-start = (bf16[2,128,128]{2,1,0:T(8,128)(2,1)S(1)}, bf16[2,128,128]{2,1,0:T(8,128)(2,1)S(1)}, u32[]{:S(2)}, u32[]{:S(2)}) collective-permute-start(bf16[2,128,128]{2,1,0:T(8,128)(2,1)S(1)} %pad_maximum_fusion), channel_id=1, source_target_pairs={{0,2},{2,4},{4,6},{6,8},{8,10},{10,12},{12,14},{1,3},{3,5},{5,7},{... | collective-permute-start | bytes 196616 | tf_op jit(solution)/shard_map/ppermute | solution.py:20
  17.1 3.2 %copy-start.4 = (s32[256,4]{0,1:T(4,128)S(1)}, s32[256,4]{0,1:T(4,128)}, u32[]{:S(2)}) copy-start(s32[256,4]{0,1:T(4,128)} %param.22) | copy-start | bytes 12292
  20.3 4.1 %collective-permute-start.1 = (f32[256,1536]{1,0:T(8,128)}, f32[256,1536]{1,0:T(8,128)}, u32[]{:S(2)}, u32[]{:S(2)}) collective-permute-start(f32[256,1536]{1,0:T(8,128)} %fusion.39), channel_id=1, source_target_pairs={{0,1},{1,0},{2,3},{3,2},{4,5},{5,4},{6,7},{7,6},{8,9},{9,8},{10,11... | collective-permute-start | bytes 4718600 | tf_op jit(solution)/shard_map/ppermute | solution.py:25
  24.4 2.6 %copy-start.5 = (f32[1536]{0:T(1024)S(1)}, f32[1536]{0:T(1024)}, u32[]{:S(2)}) copy-start(f32[1536]{0:T(1024)} %param.19) | copy-start | bytes 18436
  24.4 63.6 %slice-start = ((s8[4718592]{0:T(1024)(128)(4,1)}), s8[4194304]{0:T(1024)(128)(4,1)S(1)}, s32[]{:S(2)}) async-start(s8[4718592]{0:T(1024)(128)(4,1)} %bitcast.71), calls=%async_computation.2 | async-start | bytes 8388608
  27.0 61.1 %copy-start.1 = (f32[256,1536]{1,0:T(8,128)}, f32[256,1536]{1,0:T(8,128)S(1)}, u32[]{:S(2)}) copy-start(f32[256,1536]{1,0:T(8,128)S(1)} %get-tuple-element.12) | copy-start | bytes 4718596
  27.0 61.0 %slice-start.1 = ((s8[4718592]{0:T(1024)(128)(4,1)}), s8[524288]{0:T(1024)(128)(4,1)S(1)}, s32[]{:S(2)}) async-start(s8[4718592]{0:T(1024)(128)(4,1)} %bitcast.71), calls=%async_computation.3 | async-start | bytes 1048576
  88.0 4.5 %collective-permute-start.2 = (bf16[8,96,1536]{2,1,0:T(8,128)(2,1)S(1)}, bf16[8,96,1536]{2,1,0:T(8,128)(2,1)S(1)}, u32[]{:S(2)}, u32[]{:S(2)}) collective-permute-start(bf16[8,96,1536]{2,1,0:T(8,128)(2,1)S(1)} %all_to_all.10), channel_id=1, source_target_pairs={{0,1},{1,0},{2,3},{3,2},{4,5},{5,4},{6,7},{7,6},{8,9},{9,8},{10,11... | collective-permute-start | bytes 7077896 | tf_op jit(solution)/shard_map/ppermute | solution.py:25
  92.5 3.8 %copy-start.7 = (bf16[1,768,1536]{2,1,0:T(8,128)(2,1)S(1)}, bf16[1,768,1536]{2,1,0:T(8,128)(2,1)}, u32[]{:S(2)}) copy-start(bf16[1,768,1536]{2,1,0:T(8,128)(2,1)} %param.21) | copy-start | bytes 7077892
  98.4 4.7 %collective-permute-start.3 = (bf16[8,96,1536]{2,1,0:T(8,128)(2,1)S(1)}, bf16[8,96,1536]{2,1,0:T(8,128)(2,1)S(1)}, u32[]{:S(2)}, u32[]{:S(2)}) collective-permute-start(bf16[8,96,1536]{2,1,0:T(8,128)(2,1)S(1)} %bitcast.74), channel_id=1, source_target_pairs={{0,1},{1,0},{2,3},{3,2},{4,5},{5,4},{6,7},{7,6},{8,9},{9,8},{10,11... | collective-permute-start | bytes 7077896 | tf_op jit(solution)/shard_map/ppermute | solution.py:25
  105.2 4.5 %copy-start.6 = (f32[256,4]{0,1:T(4,128)S(1)}, f32[256,4]{0,1:T(4,128)}, u32[]{:S(2)}) copy-start(f32[256,4]{0,1:T(4,128)} %param.23) | copy-start | bytes 12292
  105.2 59.2 %all-to-all-start.1 = ((bf16[8,96,1536]{2,1,0:T(8,128)(2,1)}), bf16[8,96,1536]{2,1,0:T(8,128)(2,1)}, u32[]{:S(2)}, u32[]{:S(2)}) async-start(bf16[8,96,1536]{2,1,0:T(8,128)(2,1)} %fusion), calls=%async_computation.1 | async-start | bytes 4718592 | tf_op jit(solution)/shard_map/all_to_all | solution.py:194
  164.4 2.3 %copy-start.3 = (bf16[256,768]{1,0:T(8,128)(2,1)S(1)}, bf16[256,768]{1,0:T(8,128)(2,1)}, u32[]{:S(2)}) copy-start(bf16[256,768]{1,0:T(8,128)(2,1)} %get-tuple-element.9) | copy-start | bytes 1179652
  171.0 2.8 %collective-permute-start.4 = (f32[128,1536]{1,0:T(8,128)S(1)}, f32[128,1536]{1,0:T(8,128)S(1)}, u32[]{:S(2)}, u32[]{:S(2)}) collective-permute-start(f32[128,1536]{1,0:T(8,128)S(1)} %convolution_add_fusion.1), channel_id=1, source_target_pairs={{0,1},{1,0},{2,3},{3,2},{4,5},{5,4},{6,7},{7,6},{8,9},{9,8},{10,11... | collective-permute-start | bytes 2359304 | tf_op jit(solution)/shard_map/ppermute | solution.py:25
  173.3 2.6 %copy-start.2 = (f32[256,1536]{1,0:T(8,128)S(1)}, f32[256,1536]{1,0:T(8,128)}, u32[]{:S(2)}) copy-start(f32[256,1536]{1,0:T(8,128)} %copy-done.1) | copy-start | bytes 4718596
  173.3 2.5 %collective-permute-start.5 = (f32[128,1536]{1,0:T(8,128)S(1)}, f32[128,1536]{1,0:T(8,128)S(1)}, u32[]{:S(2)}, u32[]{:S(2)}) collective-permute-start(f32[128,1536]{1,0:T(8,128)S(1)} %convolution_add_fusion), channel_id=1, source_target_pairs={{0,1},{1,0},{2,3},{3,2},{4,5},{5,4},{6,7},{7,6},{8,9},{9,8},{10,11... | collective-permute-start | bytes 2359304 | tf_op jit(solution)/shard_map/ppermute | solution.py:25

commit v10 on v7

--- a/solution.py
+++ b/solution.py
@@ -180,7 +180,7 @@
         .astype(jnp.bfloat16)
         .reshape(quads, half, width)
     )
-    return pick, lax.all_to_all(outgoing, "quad", split_axis=0, concat_axis=0, tiled=True)
+    return pick, outgoing
 
 
 def combine(pick, returned, gates):
@@ -229,17 +229,18 @@
     partner_part = swap_half(core_rows(normed, core, share))
     partner_routes = swap_half(routes)
     partner_gates = swap_half(route_gates)
-    own_ids = slot_ids(routes, core, half, first_expert, quads)
-    own_pick, own_arrived = dispatch(normed, own_ids, slots, quads, half)
     partner_normed = join_rows(partner_part, swap_exp(partner_part), core)
     partner_ids = slot_ids(partner_routes, core, half, first_expert, quads)
-    partner_pick, partner_arrived = dispatch(partner_normed, partner_ids, slots, quads, half)
-
-    served = serve_rows(
-        jnp.concatenate([own_arrived, partner_arrived], axis=0), expert_in[0], expert_out[0]
-    )
-    own_back = lax.all_to_all(served[:quads], "quad", split_axis=0, concat_axis=0, tiled=True)
-    partner_back = lax.all_to_all(served[quads:], "quad", split_axis=0, concat_axis=0, tiled=True)
+    partner_pick, partner_out = dispatch(partner_normed, partner_ids, slots, quads, half)
+    own_ids = slot_ids(routes, core, half, first_expert, quads)
+    own_pick, own_out = dispatch(normed, own_ids, slots, quads, half)
+    arrived = lax.all_to_all(
+        jnp.concatenate([own_out, partner_out], axis=1), "quad", split_axis=0, concat_axis=0, tiled=True
+    )
+    served = serve_rows(arrived, expert_in[0], expert_out[0])
+    back = lax.all_to_all(served, "quad", split_axis=0, concat_axis=0, tiled=True)
+    own_back = back[:, :half]
+    partner_back = back[:, half:]
 
     partner_sum = combine(partner_pick, partner_back, partner_gates)
     other_core = 1 - core

time: 193 us -> 172 us (0.89)
  starting transfers between devices: 32.1 us -> 18.1 us
  blocking collectives: 19.6 us -> 31.6 us
  local copies, waits for them, and re-layouts: 15.4 us -> 8.78 us
  matrix products: 29.2 us -> 22.7 us
  waiting for transfers between devices: 75.5 us -> 69.1 us
    ppermute x4, waiting for transfers between devices: 55 us -> 37.7 us  [swap_half(): return lax.ppermute(x, 'half', [(0, 1), (1, 0)])]
    all_to_all x3 -> x1, waiting for transfers between devices: 13.2 us -> 27.1 us  [on_device(): lax.all_to_all(served, 'quad', split_axis=0, concat_axis=0, tiled=True)]
    all_to_all x1, blocking collectives: 19.6 us -> 31.6 us  [on_device(): lax.all_to_all(jnp.concatenate([own_out, partner_out], axis=1), 'quad', s...]
    all_to_all x3 -> x1, starting transfers between devices: 13 us -> 4.62 us  [on_device(): lax.all_to_all(served, 'quad', split_axis=0, concat_axis=0, tiled=True)]
    ppermute x4, starting transfers between devices: 12.8 us -> 7.26 us  [swap_half(): return lax.ppermute(x, 'half', [(0, 1), (1, 0)])]
    unnamed x26 -> x21, local copies, waits for them, and re-layouts: 5.69 us -> 2.9 us
    dot_general x2, matrix products: 10.4 us -> 7.62 us  [expert_hidden(): jnp.einsum('rd,kdf->krf', rows, expert_in, preferred_element_type=jnp.flo...]
    dot_general x2, matrix products: 7.11 us -> 4.47 us  [combine(): jnp.dot(pick, returned.reshape(slots, width), preferred_element_type=jnp....]
  transfers between devices with their start and end apart: 15 -> 13, of which waited for: 9 -> 7; matrix products, arithmetic and copies ran while one was open for 17% -> 15% of each run, Pallas kernels for 0% -> 5%
where the time goes in v10:
time: 172 us
  waiting for transfers between devices  69.1 us (40%)
  blocking collectives  31.6 us (18%)
  matrix products  22.7 us (13%)
  starting transfers between devices  18.1 us (11%)
  other arithmetic  13.2 us (8%)
  local copies, waits for them, and re-layouts  8.78 us (5%)
  Pallas kernels  7.75 us (5%)
    ppermute x4, waiting for transfers between devices, swap_half(): return lax.ppermute(x, 'half', [(0, 1), (1, 0)])  37.7 us
    all_to_all x1, blocking collectives, on_device(): lax.all_to_all(jnp.concatenate([own_out, partner_out], axis=1), 'quad', s...  31.6 us
    all_to_all x1, waiting for transfers between devices, on_device(): lax.all_to_all(served, 'quad', split_axis=0, concat_axis=0, tiled=True)  27.1 us
    pallas_call x1, Pallas kernels, attend_kernel(): pl.pallas_call(attention_kernel, out_shape=jax.ShapeDtypeStruct((rows, co...  7.75 us
    dot_general x2, matrix products, expert_hidden(): jnp.einsum('rd,kdf->krf', rows, expert_in, preferred_element_type=jnp.flo...  7.62 us
    ppermute x4, starting transfers between devices, swap_half(): return lax.ppermute(x, 'half', [(0, 1), (1, 0)])  7.26 us
    ppermute x1, starting transfers between devices, shifted(): return lax.ppermute(shard, axis, pairs)  5.01 us
    another operation x4, other arithmetic  4.86 us
  transfers between devices with their start and end apart: 13, of which 7 were waited for; matrix products, arithmetic and copies ran while one was open for 15% of the time, Pallas kernels for 5%

profile of v10, /device:TPU:0, one launch (start us, length us, event | category | flops | bytes accessed | tf_op | source)
XLA Modules:
  0.0 171.7 jit_solution(7689867747471561459)
XLA Ops:
  0.0 0.9 slice_bitcast_fusion.2
  0.9 5.0 %collective-permute-start = (bf16[2,128,128]{2,1,0:T(8,128)(2,1)S(1)}, bf16[2,128,128]{2,1,0:T(8,128)(2,1)S(1)}, u32[]{:S(2)}, u32[]{:S(2)}) collective-permute-start(bf16[2,128,128]{2,1,0:T(8,128)(2,1)S(1)} %pad_maximum_fusion.1), channel_id=1, source_target_pairs={{0,2},{2,4},{4,6},{6,8},{8,10},{10,12},{12,14},{1,3},{3,5},{5,7},{... | collective-permute-start | bytes 196616 | tf_op jit(solution)/shard_map/ppermute | solution.py:20
  6.0 2.7 %collective-permute-start.2 = (s32[256,4]{0,1:T(4,128)}, s32[256,4]{0,1:T(4,128)S(1)}, u32[]{:S(2)}, u32[]{:S(2)}) collective-permute-start(s32[256,4]{0,1:T(4,128)} %param.22), channel_id=1, source_target_pairs={{0,8},{8,0},{1,9},{9,1},{2,10},{10,2},{3,11},{11,3},{4,12},{12,4},... | collective-permute-start | bytes 12296 | tf_op jit(solution)/shard_map/ppermute | solution.py:152
  8.6 0.8 copy.41
  9.5 0.1 eq.135
  9.6 0.1 eq.131
  9.7 0.9 broadcast_select_fusion
  10.6 0.6 slice_bitcast_fusion
  11.2 7.7 %shard_map.118 = bf16[256,1024]{1,0:T(8,128)(2,1)} custom-call(f32[16]{0:T(128)} %sink_ref.1, bf16[256,1024]{1,0:T(8,128)(2,1)} %q_ref.1, bf16[128,128]{1,0:T(8,128)(2,1)} %get-tuple-element.14.pk_ref, bf16[256,128]{1,0:T(8,128)(2,1)} %k_ref.1, bf16[128,128]{1,0:T(8,128)(2,1)} %get-tuple-element.13.pv_ref, bf16[256,128]{1,0:T(8,128)(2,1)} %v_ref.1), custom_call_target="tpu_custom_call" | custom-call | flops 536870912 | bytes 1245184 | tf_op jit(solution)/shard_map/pallas_call | solution.py:123
  19.0 3.2 %fusion.52 = f32[256,1536]{1,0:T(8,128)} fusion(bf16[256,1024]{1,0:T(8,128)(2,1)} %shard_map.118, bf16[1024,1536]{1,0:T(8,128)(2,1)S(1)} %copy-done), kind=kOutput, calls=%fused_computation.88 | convolution fusion | flops 805306368 | bytes 5242880 | tf_op jit(solution)/shard_map/dot_general | solution.py:217
  22.1 2.3 %reduce-window.14 = s32[8,8,128]{2,1,0:T(8,128)S(1)} reduce-window(s32[8,8,128]{2,1,0:T(8,128)S(1)} %fusion.46, s32[]{:T(128)} %constant.16.clone.1), window={size=1x1x128 pad=0_0x0_0x127_0}, to_apply=%region_0.1 | reduce-window | flops 1040384 | bytes 65540 | tf_op jit(solution)/shard_map/reduce-window
  24.4 0.3 slice_reduce_fusion.1
  24.7 0.2 reduce-window.15
  24.9 0.1 add_bitcast_fusion.1
  25.0 0.1 copy.46
  25.1 0.1 eq.150
  25.3 0.1 eq.146
  25.4 2.3 %reduce-window.16 = s32[8,8,128]{2,1,0:T(8,128)S(1)} reduce-window(s32[8,8,128]{2,1,0:T(8,128)S(1)} %fusion.47, s32[]{:T(128)} %constant.16.clone.1), window={size=1x1x128 pad=0_0x0_0x127_0}, to_apply=%region_5.6 | reduce-window | flops 1040384 | bytes 65540 | tf_op jit(solution)/shard_map/reduce-window.2
  27.7 0.3 slice_reduce_fusion
  27.9 0.2 reduce-window.19
  28.1 0.1 add_bitcast_fusion
  28.2 0.1 sub.71
  28.4 0.1 copy.48
  28.4 2.4 %multiply_reduce_fusion.2 = (f32[256]{0:T(256)S(1)}, f32[256,1536]{1,0:T(8,128)S(1)}) fusion(f32[256,1536]{1,0:T(8,128)} %fusion.52, f32[256,1536]{1,0:T(8,128)} %collective-permute-done.1, bf16[256,1536]{1,0:T(8,128)(2,1)} %param.18), kind=kLoop, calls=%fused_computation.28 | loop fusion | flops 1965824 | bytes 5506048 | tf_op jit(solution)/shard_map/reduce_sum | solution.py:29
  30.9 1.1 copy-done.1
  32.1 0.2 multiply_convert_fusion
  32.3 0.9 copy-done.3
  33.1 0.8 constant_dynamic-slice_fusion.2
  33.9 1.6 collective-permute-start.3
  35.5 0.1 sub.64
  35.6 0.1 copy.43
  35.7 0.2 fusion.32
  36.0 19.1 %collective-permute-done.3 = bf16[128,1536]{1,0:T(8,128)(2,1)} collective-permute-done((bf16[128,1536]{1,0:T(8,128)(2,1)}, bf16[128,1536]{1,0:T(8,128)(2,1)}, u32[]{:S(2)}, u32[]{:S(2)}) %collective-permute-start.3) | collective-permute-done | bytes 393248 | tf_op jit(solution)/shard_map/ppermute | solution.py:152
  55.1 0.2 fusion.33
  55.3 1.6 convolution_convert_fusion.3
  56.9 0.1 collective-permute-done.4
  57.0 1.8 %convolution_convert_fusion.2 = bf16[384,1536]{1,0:T(8,128)(2,1)S(1)} fusion(bf16[256,384]{1,0:T(8,128)(2,1)S(1)} %fusion.32, bf16[128,1536]{1,0:T(8,128)(2,1)S(1)} %collective-permute-done.4, bf16[128,1536]{1,0:T(8,128)(2,1)} %collective-permute-done.3, pred[]{:T(512)S(6)} %eq.129), kind=kOutput, calls=%fused_computation.10 | convolution fusion | flops 306118656 | bytes 2162689 | tf_op jit(solution)/shard_map/dot_general | solution.py:179
  58.8 0.2 pad_maximum_fusion
  59.0 31.6 %all_to_all.10 = bf16[4,192,1536]{2,1,0:T(8,128)(2,1)S(1)} all-to-all(bf16[4,192,1536]{2,1,0:T(8,128)(2,1)S(1)} %pad_maximum_fusion), channel_id=1, replica_groups=mesh['groups'=2,'half'=2,'quad'=4,'exp'=2] {'quad'}, dimensions={0} | all-to-all | bytes 4718592 | tf_op jit(solution)/shard_map/all_to_all | solution.py:237
  90.5 3.8 %fusion.13 = f32[2,768,768]{2,1,0:T(8,128)S(1)} fusion(bf16[768,1536,1]{1,0,2:T(8,128)(2,1)S(1)} %bitcast.98, bf16[1,2,1536,768]{3,2,1,0:T(8,128)(2,1)S(1)} %bitcast.105), kind=kOutput, calls=%fused_computation.23 | convolution fusion | flops 3623878656 | bytes 11796480 | tf_op jit(solution)/shard_map/rd,kdf->krf/dot_general | solution.py:56
  94.4 0.7 fusion.31
  95.1 3.8 %fusion.16 = f32[2,768,768]{2,1,0:T(8,128)S(1)} fusion(bf16[768,1536,1]{1,0,2:T(8,128)(2,1)S(1)} %bitcast.106, bf16[1,2,1536,768]{3,2,1,0:T(8,128)(2,1)S(1)} %bitcast.105), kind=kOutput, calls=%fused_computation.24 | convolution fusion | flops 3623878656 | bytes 11796480 | tf_op jit(solution)/shard_map/rd,kdf->krf/dot_general | solution.py:56
  98.9 2.1 %convolution_convert_fusion = bf16[768,1536]{1,0:T(8,128)(2,1)S(1)} fusion(bf16[1,768,1536]{2,1,0:T(8,128)(2,1)S(1)} %copy-done.6, f32[2,768,768]{2,1,0:T(8,128)S(1)} %fusion.16), kind=kOutput, calls=%fused_computation.8 | convolution fusion | flops 1817837568 | bytes 9437184 | tf_op jit(solution)/shard_map/dot_general | solution.py:139
  101.0 0.5 collective-permute-start.6
  101.5 2.0 %convolution_convert_fusion.1 = bf16[768,1536]{1,0:T(8,128)(2,1)S(1)} fusion(bf16[768,768]{1,0:T(8,128)(2,1)S(1)} %fusion.31, bf16[1,768,1536]{2,1,0:T(8,128)(2,1)S(1)} %copy-done.6), kind=kOutput, calls=%fused_computation.9 | convolution fusion | flops 1813118976 | bytes 5898240 | tf_op jit(solution)/shard_map/dot_general | solution.py:144
  103.5 2.2 %collective-permute-done.6 = bf16[4,192,1536]{2,1,0:T(8,128)(2,1)S(1)} collective-permute-done((bf16[4,192,1536]{2,1,0:T(8,128)(2,1)S(1)}, bf16[4,192,1536]{2,1,0:T(8,128)(2,1)S(1)}, u32[]{:S(2)}, u32[]{:S(2)}) %collective-permute-start.6) | collective-permute-done | bytes 2359328 | tf_op jit(solution)/shard_map/ppermute | solution.py:25
  105.7 2.0 %fusion = bf16[4,192,1536]{2,1,0:T(8,128)(2,1)} fusion(bf16[4,192,1536]{2,1,0:T(8,128)(2,1)S(1)} %bitcast.97, bf16[4,192,1536]{2,1,0:T(8,128)(2,1)S(1)} %collective-permute-done.6), kind=kLoop, calls=%fused_computation.3 | loop fusion | flops 4718592 | bytes 7077888 | tf_op jit(solution)/shard_map/convert_element_type | solution.py:148
  107.7 4.6 %all-to-all-start.1 = ((bf16[4,192,1536]{2,1,0:T(8,128)(2,1)}), bf16[4,192,1536]{2,1,0:T(8,128)(2,1)}, u32[]{:S(2)}, u32[]{:S(2)}) async-start(bf16[4,192,1536]{2,1,0:T(8,128)(2,1)} %fusion), calls=%async_computation.1 | async-start | bytes 4718592 | tf_op jit(solution)/shard_map/all_to_all | solution.py:241
  112.3 1.5 collective-permute-start.8
  113.8 27.1 %all-to-all-done.1 = bf16[4,192,1536]{2,1,0:T(8,128)(2,1)} async-done(((bf16[4,192,1536]{2,1,0:T(8,128)(2,1)}), bf16[4,192,1536]{2,1,0:T(8,128)(2,1)}, u32[]{:S(2)}, u32[]{:S(2)}) %all-to-all-start.1) | async-done | bytes 2359328 | tf_op jit(solution)/shard_map/all_to_all | solution.py:241
  140.9 1.9 %fusion.51 = (bf16[4,96,1536]{2,1,0:T(8,128)(2,1)S(1)}, bf16[4,96,1536]{2,1,0:T(8,128)(2,1)S(1)}) fusion(bf16[4,192,1536]{2,1,0:T(8,128)(2,1)} %all-to-all-done.1), kind=kLoop, calls=%fused_computation.87 | loop fusion | bytes 4718592 | tf_op jit(solution)/shard_map/slice | solution.py:242
  142.8 2.2 %multiply_reduce_fusion = f32[256,1536]{1,0:T(8,128)S(1)} fusion(f32[256,4]{0,1:T(4,128)S(1)} %collective-permute-done.8, bf16[384,1536,1]{1,0,2:T(8,128)(2,1)S(1)} %bitcast.100, s32[256,4]{0,1:T(4,128)S(1)} %add_select_fusion), kind=kOutput, calls=%fused_computation | convolution fusion | flops 1211105280 | bytes 2760704 | tf_op jit(solution)/shard_map/dot_general | solution.py:189
  145.0 0.1 constant_dynamic-slice_fusion
  145.1 0.1 collective-permute-start.9
  145.2 2.2 %multiply_reduce_fusion.1 = f32[256,1536]{1,0:T(8,128)S(1)} fusion(bf16[384,1536,1]{1,0,2:T(8,128)(2,1)S(1)} %bitcast.99, f32[256,4]{0,1:T(4,128)S(1)} %copy-done.7, s32[256,4]{0,1:T(4,128)S(1)} %add_select_fusion.1), kind=kOutput, calls=%fused_computation.1 | convolution fusion | flops 1211105280 | bytes 2760704 | tf_op jit(solution)/shard_map/dot_general | solution.py:189
  147.5 0.6 collective-permute-start.7
  148.1 0.1 add_convert_fusion.1
  148.2 1.5 collective-permute-start.10
  149.7 0.3 collective-permute-done.7
  150.0 18.6 %collective-permute-done.10 = bf16[128,1536]{1,0:T(8,128)(2,1)S(1)} collective-permute-done((bf16[128,1536]{1,0:T(8,128)(2,1)S(1)}, bf16[128,1536]{1,0:T(8,128)(2,1)S(1)}, u32[]{:S(2)}, u32[]{:S(2)}) %collective-permute-start.10) | collective-permute-done | bytes 393248 | tf_op jit(solution)/shard_map/ppermute | solution.py:152
  168.6 0.2 add_convert_fusion
  168.8 0.1 collective-permute-start.11
  168.9 1.7 collective-permute-done.11
  170.6 1.0 maximum_select_fusion.2
  (38 shorter events, 0.3 us)
Async XLA Ops:
  0.0 19.0 %copy-start = (bf16[1024,1536]{1,0:T(8,128)(2,1)S(1)}, bf16[1024,1536]{1,0:T(8,128)(2,1)}, u32[]{:S(2)}) copy-start(bf16[1024,1536]{1,0:T(8,128)(2,1)} %param.17) | copy-start | bytes 9437188
  0.9 8.8 %collective-permute-start = (bf16[2,128,128]{2,1,0:T(8,128)(2,1)S(1)}, bf16[2,128,128]{2,1,0:T(8,128)(2,1)S(1)}, u32[]{:S(2)}, u32[]{:S(2)}) collective-permute-start(bf16[2,128,128]{2,1,0:T(8,128)(2,1)S(1)} %pad_maximum_fusion.1), channel_id=1, source_target_pairs={{0,2},{2,4},{4,6},{6,8},{8,10},{10,12},{12,14},{1,3},{3,5},{5,7},{... | collective-permute-start | bytes 196616 | tf_op jit(solution)/shard_map/ppermute | solution.py:20
  6.0 19.0 %collective-permute-start.2 = (s32[256,4]{0,1:T(4,128)}, s32[256,4]{0,1:T(4,128)S(1)}, u32[]{:S(2)}, u32[]{:S(2)}) collective-permute-start(s32[256,4]{0,1:T(4,128)} %param.22), channel_id=1, source_target_pairs={{0,8},{8,0},{1,9},{9,1},{2,10},{10,2},{3,11},{11,3},{4,12},{12,4},... | collective-permute-start | bytes 12296 | tf_op jit(solution)/shard_map/ppermute | solution.py:152
  22.1 6.3 %collective-permute-start.1 = (f32[256,1536]{1,0:T(8,128)}, f32[256,1536]{1,0:T(8,128)}, u32[]{:S(2)}, u32[]{:S(2)}) collective-permute-start(f32[256,1536]{1,0:T(8,128)} %fusion.52), channel_id=1, source_target_pairs={{0,1},{1,0},{2,3},{3,2},{4,5},{5,4},{6,7},{7,6},{8,9},{9,8},{10,11... | collective-permute-start | bytes 4718600 | tf_op jit(solution)/shard_map/ppermute | solution.py:25
  28.4 3.6 %copy-start.5 = (f32[1536]{0:T(1024)S(1)}, f32[1536]{0:T(1024)}, u32[]{:S(2)}) copy-start(f32[1536]{0:T(1024)} %param.19) | copy-start | bytes 18436
  30.9 1.2 copy-start.1
  30.9 5.1 %copy-start.4 = (s32[256,4]{0,1:T(4,128)S(1)}, s32[256,4]{0,1:T(4,128)}, u32[]{:S(2)}) copy-start(s32[256,4]{0,1:T(4,128)} %param.22) | copy-start | bytes 12292
  32.3 0.9 copy-start.3
  33.9 21.1 %collective-permute-start.3 = (bf16[128,1536]{1,0:T(8,128)(2,1)}, bf16[128,1536]{1,0:T(8,128)(2,1)}, u32[]{:S(2)}, u32[]{:S(2)}) collective-permute-start(bf16[128,1536]{1,0:T(8,128)(2,1)} %constant_dynamic-slice_fusion.2), channel_id=1, source_target_pairs={{0,8},{8,0},{1,9},{9,1},{2,10},{10,2},{3,11},{11,3},{4,12},{12,4},... | collective-permute-start | bytes 1179656 | tf_op jit(solution)/shard_map/ppermute | solution.py:152
  55.1 1.9 %collective-permute-start.4 = (bf16[128,1536]{1,0:T(8,128)(2,1)}, bf16[128,1536]{1,0:T(8,128)(2,1)S(1)}, u32[]{:S(2)}, u32[]{:S(2)}) collective-permute-start(bf16[128,1536]{1,0:T(8,128)(2,1)} %collective-permute-done.3), channel_id=1, source_target_pairs={{0,1},{1,0},{2,3},{3,2},{4,5},{5,4},{6,7},{7,6},{8,9},{9,8},{10,11... | collective-permute-start | bytes 1179656 | tf_op jit(solution)/shard_map/ppermute | solution.py:25
  57.0 33.5 %slice-start = ((s8[4718592]{0:T(1024)(128)(4,1)}), s8[4194304]{0:T(1024)(128)(4,1)S(1)}, s32[]{:S(2)}) async-start(s8[4718592]{0:T(1024)(128)(4,1)} %bitcast.104), calls=%async_computation.2 | async-start | bytes 8388608
  58.8 31.8 %slice-start.1 = ((s8[4718592]{0:T(1024)(128)(4,1)}), s8[524288]{0:T(1024)(128)(4,1)S(1)}, s32[]{:S(2)}) async-start(s8[4718592]{0:T(1024)(128)(4,1)} %bitcast.104), calls=%async_computation.3 | async-start | bytes 1048576
  90.5 4.5 %collective-permute-start.5 = (bf16[4,192,1536]{2,1,0:T(8,128)(2,1)S(1)}, bf16[4,192,1536]{2,1,0:T(8,128)(2,1)S(1)}, u32[]{:S(2)}, u32[]{:S(2)}) collective-permute-start(bf16[4,192,1536]{2,1,0:T(8,128)(2,1)S(1)} %all_to_all.10), channel_id=1, source_target_pairs={{0,1},{1,0},{2,3},{3,2},{4,5},{5,4},{6,7},{7,6},{8,9},{9,8},{10,11... | collective-permute-start | bytes 7077896 | tf_op jit(solution)/shard_map/ppermute | solution.py:25
  95.1 3.8 %copy-start.6 = (bf16[1,768,1536]{2,1,0:T(8,128)(2,1)S(1)}, bf16[1,768,1536]{2,1,0:T(8,128)(2,1)}, u32[]{:S(2)}) copy-start(bf16[1,768,1536]{2,1,0:T(8,128)(2,1)} %param.21) | copy-start | bytes 7077892
  101.0 4.7 %collective-permute-start.6 = (bf16[4,192,1536]{2,1,0:T(8,128)(2,1)S(1)}, bf16[4,192,1536]{2,1,0:T(8,128)(2,1)S(1)}, u32[]{:S(2)}, u32[]{:S(2)}) collective-permute-start(bf16[4,192,1536]{2,1,0:T(8,128)(2,1)S(1)} %bitcast.107), channel_id=1, source_target_pairs={{0,1},{1,0},{2,3},{3,2},{4,5},{5,4},{6,7},{7,6},{8,9},{9,8},{10,11... | collective-permute-start | bytes 7077896 | tf_op jit(solution)/shard_map/ppermute | solution.py:25
  107.7 4.6 %copy-start.7 = (f32[256,4]{0,1:T(4,128)S(1)}, f32[256,4]{0,1:T(4,128)}, u32[]{:S(2)}) copy-start(f32[256,4]{0,1:T(4,128)} %param.23) | copy-start | bytes 12292
  107.7 33.2 %all-to-all-start.1 = ((bf16[4,192,1536]{2,1,0:T(8,128)(2,1)}), bf16[4,192,1536]{2,1,0:T(8,128)(2,1)}, u32[]{:S(2)}, u32[]{:S(2)}) async-start(bf16[4,192,1536]{2,1,0:T(8,128)(2,1)} %fusion), calls=%async_computation.1 | async-start | bytes 4718592 | tf_op jit(solution)/shard_map/all_to_all | solution.py:241
  112.3 30.5 %collective-permute-start.8 = (f32[256,4]{0,1:T(4,128)S(1)}, f32[256,4]{0,1:T(4,128)S(1)}, u32[]{:S(2)}, u32[]{:S(2)}) collective-permute-start(f32[256,4]{0,1:T(4,128)S(1)} %copy-done.7), channel_id=1, source_target_pairs={{0,8},{8,0},{1,9},{9,1},{2,10},{10,2},{3,11},{11,3},{4,12},{12,4},... | collective-permute-start | bytes 12296 | tf_op jit(solution)/shard_map/ppermute | solution.py:152
  145.1 3.0 %collective-permute-start.9 = (f32[128,1536]{1,0:T(8,128)S(1)}, f32[128,1536]{1,0:T(8,128)S(1)}, u32[]{:S(2)}, u32[]{:S(2)}) collective-permute-start(f32[128,1536]{1,0:T(8,128)S(1)} %constant_dynamic-slice_fusion), channel_id=1, source_target_pairs={{0,1},{1,0},{2,3},{3,2},{4,5},{5,4},{6,7},{7,6},{8,9},{9,8},{10,11... | collective-permute-start | bytes 2359304 | tf_op jit(solution)/shard_map/ppermute | solution.py:25
  147.4 21.2 %copy-start.2 = (f32[256,1536]{1,0:T(8,128)S(1)}, f32[256,1536]{1,0:T(8,128)}, u32[]{:S(2)}) copy-start(f32[256,1536]{1,0:T(8,128)} %copy-done.1) | copy-start | bytes 4718596
  147.5 2.5 %collective-permute-start.7 = (f32[128,1536]{1,0:T(8,128)S(1)}, f32[128,1536]{1,0:T(8,128)S(1)}, u32[]{:S(2)}, u32[]{:S(2)}) collective-permute-start(f32[128,1536]{1,0:T(8,128)S(1)} %constant_dynamic-slice_fusion.1), channel_id=1, source_target_pairs={{0,1},{1,0},{2,3},{3,2},{4,5},{5,4},{6,7},{7,6},{8,9},{9,8},{10,11... | collective-permute-start | bytes 2359304 | tf_op jit(solution)/shard_map/ppermute | solution.py:25
  148.2 20.4 %collective-permute-start.10 = (bf16[128,1536]{1,0:T(8,128)(2,1)S(1)}, bf16[128,1536]{1,0:T(8,128)(2,1)S(1)}, u32[]{:S(2)}, u32[]{:S(2)}) collective-permute-start(bf16[128,1536]{1,0:T(8,128)(2,1)S(1)} %add_convert_fusion.1), channel_id=1, source_target_pairs={{0,8},{8,0},{1,9},{9,1},{2,10},{10,2},{3,11},{11,3},{4,12},{12,4},... | collective-permute-start | bytes 1179656 | tf_op jit(solution)/shard_map/ppermute | solution.py:152
  168.8 1.8 %collective-permute-start.11 = (bf16[128,1536]{1,0:T(8,128)(2,1)S(1)}, bf16[128,1536]{1,0:T(8,128)(2,1)S(1)}, u32[]{:S(2)}, u32[]{:S(2)}) collective-permute-start(bf16[128,1536]{1,0:T(8,128)(2,1)S(1)} %add_convert_fusion), channel_id=1, source_target_pairs={{0,1},{1,0},{2,3},{3,2},{4,5},{5,4},{6,7},{7,6},{8,9},{9,8},{10,11... | collective-permute-start | bytes 1179656 | tf_op jit(solution)/shard_map/ppermute | solution.py:25

commit v11 on v7

--- a/solution.py
+++ b/solution.py
@@ -171,6 +171,21 @@
     return jnp.where(mine, local_expert * half + local_rank, -1)
 
 
+def half_slot_ids(routes, core, share, first_expert, quads):
+    tok_rows = routes.shape[0]
+    experts = lax.axis_size("half") * quads
+    flat = routes.reshape(-1)
+    token = jnp.arange(tok_rows * TOP, dtype=jnp.int32) // TOP
+    in_half = (token // share) == core
+    hits = ((flat[:, None] == jnp.arange(experts, dtype=jnp.int32)[None, :]) & in_half[:, None]).astype(
+        jnp.int32
+    )
+    rank = jnp.sum(hits * (jnp.cumsum(hits, axis=0) - 1), axis=1)
+    local_expert = flat - first_expert
+    mine = in_half & (local_expert >= 0) & (local_expert < quads)
+    return jnp.where(mine, local_expert * share + rank, -1)
+
+
 def dispatch(normed, ids, slots, quads, half):
     tok_rows, width = normed.shape
     pick = (ids[:, None] == jnp.arange(slots, dtype=jnp.int32)[None, :]).astype(jnp.bfloat16)
@@ -180,7 +195,7 @@
         .astype(jnp.bfloat16)
         .reshape(quads, half, width)
     )
-    return pick, lax.all_to_all(outgoing, "quad", split_axis=0, concat_axis=0, tiled=True)
+    return pick, outgoing
 
 
 def combine(pick, returned, gates):
@@ -226,28 +241,33 @@
     slots = quads * half
     first_expert = side * quads
 
-    partner_part = swap_half(core_rows(normed, core, share))
+    own_rows_in = core_rows(normed, core, share)
+    own_ids = slot_ids(routes, core, half, first_expert, quads)
+    own_pick, own_out = dispatch(normed, own_ids, slots, quads, half)
+    own_out, own_rows_in = lax.optimization_barrier((own_out, own_rows_in))
+    partner_part = swap_half(own_rows_in)
     partner_routes = swap_half(routes)
     partner_gates = swap_half(route_gates)
-    own_ids = slot_ids(routes, core, half, first_expert, quads)
-    own_pick, own_arrived = dispatch(normed, own_ids, slots, quads, half)
-    partner_normed = join_rows(partner_part, swap_exp(partner_part), core)
-    partner_ids = slot_ids(partner_routes, core, half, first_expert, quads)
-    partner_pick, partner_arrived = dispatch(partner_normed, partner_ids, slots, quads, half)
-
+    own_arrived = lax.all_to_all(own_out, "quad", split_axis=0, concat_axis=0, tiled=True)
+    partner_ids = core_rows(
+        half_slot_ids(partner_routes, core, share, first_expert, quads).reshape(tok_rows, TOP),
+        core,
+        share,
+    ).reshape(-1)
+    partner_pick, partner_out = dispatch(partner_part, partner_ids, quads * share, quads, share)
+    partner_arrived = lax.all_to_all(partner_out, "quad", split_axis=0, concat_axis=0, tiled=True)
     served = serve_rows(
-        jnp.concatenate([own_arrived, partner_arrived], axis=0), expert_in[0], expert_out[0]
-    )
-    own_back = lax.all_to_all(served[:quads], "quad", split_axis=0, concat_axis=0, tiled=True)
-    partner_back = lax.all_to_all(served[quads:], "quad", split_axis=0, concat_axis=0, tiled=True)
-
-    partner_sum = combine(partner_pick, partner_back, partner_gates)
+        jnp.concatenate([own_arrived, partner_arrived], axis=1), expert_in[0], expert_out[0]
+    )
+    partner_back = lax.all_to_all(served[:, half:], "quad", split_axis=0, concat_axis=0, tiled=True)
+    partner_rows = combine(partner_pick, partner_back, core_rows(partner_gates, core, share))
+    own_served, partner_msg = lax.optimization_barrier(
+        (served[:, :half], partner_rows.astype(jnp.bfloat16))
+    )
+    from_partner = swap_half(partner_msg)
+    own_back = lax.all_to_all(own_served, "quad", split_axis=0, concat_axis=0, tiled=True)
+    own_sum = combine(own_pick, own_back, route_gates)
     other_core = 1 - core
-    partner_rows = core_rows(partner_sum, core, share) + swap_exp(
-        core_rows(partner_sum, other_core, share)
-    )
-    from_partner = swap_half(partner_rows.astype(jnp.bfloat16))
-    own_sum = combine(own_pick, own_back, route_gates)
     own_rows = core_rows(own_sum, core, share) + swap_exp(core_rows(own_sum, other_core, share))
     moe_rows = own_rows + from_partner.astype(jnp.float32)
     out_rows = (core_rows(mixed_rows, core, share) + moe_rows).astype(jnp.bfloat16)

time: 193 us -> 212 us (1.098)
  waiting for transfers between devices: 75.5 us -> 99.6 us
  blocking collectives: 19.6 us -> 0 us
  starting transfers between devices: 32.1 us -> 36.6 us
  local copies, waits for them, and re-layouts: 15.4 us -> 19.6 us
  other arithmetic: 12.9 us -> 16.8 us
    all_to_all x1 -> x0, blocking collectives: 19.6 us -> none  [on_device(): lax.all_to_all(served[quads:], 'quad', split_axis=0, concat_axis=0, tiled...]
    all_to_all x3 -> x4, waiting for transfers between devices: 13.2 us -> 31.8 us  [the longest x1 16.6 us: on_device(): lax.all_to_all(partner_out, 'quad', split_axis=0, concat_axis=0, tiled=True)]
    ppermute x4, waiting for transfers between devices: 55 us -> 62.7 us  [swap_half(): return lax.ppermute(x, 'half', [(0, 1), (1, 0)])]
    all_to_all x3 -> x4, starting transfers between devices: 13 us -> 20.6 us  [the longest x1 7.47 us: on_device(): lax.all_to_all(own_served, 'quad', split_axis=0, concat_axis=0, tiled=True)]
    ppermute x4, starting transfers between devices: 12.8 us -> 10.3 us  [swap_half(): return lax.ppermute(x, 'half', [(0, 1), (1, 0)])]
    slice x2 -> x3, local copies, waits for them, and re-layouts: 1.53 us -> 3.96 us  [the longest x1 2.4 us: on_device(): served[:, :half]]
    ppermute x7 -> x5, waiting for transfers between devices: 5.51 us -> 4.27 us  [swap_exp(): return lax.ppermute(x, 'exp', [(i, (i + 1) % size) for i in range(size)])]
    unnamed x26 -> x24, local copies, waits for them, and re-layouts: 5.69 us -> 5.91 us
  transfers between devices with their start and end apart: 15 -> 14, of which waited for: 9 -> 9; matrix products, arithmetic and copies ran while one was open for 17% -> 16% of each run, Pallas kernels for 0% -> 0%
where the time goes in v11:
time: 212 us
  waiting for transfers between devices  99.6 us (47%)
  starting transfers between devices  36.6 us (17%)
  matrix products  30.8 us (15%)
  local copies, waits for them, and re-layouts  19.6 us (9%)
  other arithmetic  16.8 us (8%)
  Pallas kernels  7.73 us (4%)
    ppermute x4, waiting for transfers between devices, swap_half(): return lax.ppermute(x, 'half', [(0, 1), (1, 0)])  62.7 us
    all_to_all x1, waiting for transfers between devices, on_device(): lax.all_to_all(partner_out, 'quad', split_axis=0, concat_axis=0, tiled=True)  16.6 us
    all_to_all x1, waiting for transfers between devices, on_device(): lax.all_to_all(own_served, 'quad', split_axis=0, concat_axis=0, tiled=True)  15.2 us
    dot_general x2, matrix products, expert_hidden(): jnp.einsum('rd,kdf->krf', rows, expert_in, preferred_element_type=jnp.flo...  11.7 us
    ppermute x4, starting transfers between devices, swap_half(): return lax.ppermute(x, 'half', [(0, 1), (1, 0)])  10.3 us
    pallas_call x1, Pallas kernels, attend_kernel(): pl.pallas_call(attention_kernel, out_shape=jax.ShapeDtypeStruct((rows, co...  7.73 us
    all_to_all x1, starting transfers between devices, on_device(): lax.all_to_all(own_served, 'quad', split_axis=0, concat_axis=0, tiled=True)  7.47 us
    dot_general x2, matrix products, combine(): jnp.dot(pick, returned.reshape(slots, width), preferred_element_type=jnp....  6.9 us
  transfers between devices with their start and end apart: 14, of which 9 were waited for; matrix products, arithmetic and copies ran while one was open for 16% of the time, Pallas kernels for 0%

profile of v11, /device:TPU:0, one launch (start us, length us, event | category | flops | bytes accessed | tf_op | source)
XLA Modules:
  0.0 211.5 jit_solution(6147438087813037438)
XLA Ops:
  0.0 0.9 slice_bitcast_fusion.2
  0.9 5.0 %collective-permute-start = (bf16[2,128,128]{2,1,0:T(8,128)(2,1)S(1)}, bf16[2,128,128]{2,1,0:T(8,128)(2,1)S(1)}, u32[]{:S(2)}, u32[]{:S(2)}) collective-permute-start(bf16[2,128,128]{2,1,0:T(8,128)(2,1)S(1)} %pad_maximum_fusion), channel_id=1, source_target_pairs={{0,2},{2,4},{4,6},{6,8},{8,10},{10,12},{12,14},{1,3},{3,5},{5,7},{... | collective-permute-start | bytes 196616 | tf_op jit(solution)/shard_map/ppermute | solution.py:20
  6.0 0.8 copy.27
  6.8 0.1 eq.154
  6.9 0.9 collective-permute-done
  7.8 0.8 broadcast_select_fusion
  8.7 0.6 slice_bitcast_fusion
  9.3 7.7 %shard_map.118 = bf16[256,1024]{1,0:T(8,128)(2,1)} custom-call(f32[16]{0:T(128)} %sink_ref.1, bf16[256,1024]{1,0:T(8,128)(2,1)} %q_ref.1, bf16[128,128]{1,0:T(8,128)(2,1)} %get-tuple-element.20.pk_ref, bf16[256,128]{1,0:T(8,128)(2,1)} %k_ref.1, bf16[128,128]{1,0:T(8,128)(2,1)} %get-tuple-element.19.pv_ref, bf16[256,128]{1,0:T(8,128)(2,1)} %v_ref.1), custom_call_target="tpu_custom_call" | custom-call | flops 536870912 | bytes 1245184 | tf_op jit(solution)/shard_map/pallas_call | solution.py:123
  17.1 3.2 %fusion.68 = f32[256,1536]{1,0:T(8,128)} fusion(bf16[256,1024]{1,0:T(8,128)(2,1)} %shard_map.118, bf16[1024,1536]{1,0:T(8,128)(2,1)S(1)} %copy-done), kind=kOutput, calls=%fused_computation.135 | convolution fusion | flops 805306368 | bytes 5242880 | tf_op jit(solution)/shard_map/dot_general | solution.py:232
  20.4 2.3 %reduce-window.14 = s32[8,8,128]{2,1,0:T(8,128)S(1)} reduce-window(s32[8,8,128]{2,1,0:T(8,128)S(1)} %fusion.48, s32[]{:T(128)} %constant.67.clone.1), window={size=1x1x128 pad=0_0x0_0x127_0}, to_apply=%region_0.1 | reduce-window | flops 1040384 | bytes 65540 | tf_op jit(solution)/shard_map/reduce-window
  22.6 0.3 slice_reduce_fusion.1
  22.9 0.2 reduce-window.15
  23.2 0.1 sub.68
  23.4 0.8 copy.31
  24.1 0.8 copy.33
  24.9 0.1 copy.35
  25.0 1.5 add_select_fusion.1
  26.5 1.0 copy.36
  27.5 0.2 fusion.32
  27.8 2.4 %multiply_reduce_fusion.2 = (f32[256]{0:T(256)S(1)}, f32[256,1536]{1,0:T(8,128)S(1)}) fusion(f32[256,1536]{1,0:T(8,128)} %fusion.68, f32[256,1536]{1,0:T(8,128)} %collective-permute-done.1, bf16[256,1536]{1,0:T(8,128)(2,1)} %param.18), kind=kLoop, calls=%fused_computation.25 | loop fusion | flops 1965824 | bytes 5506048 | tf_op jit(solution)/shard_map/reduce_sum | solution.py:29
  30.2 1.1 copy-done.2
  31.3 0.2 multiply_convert_fusion
  31.5 1.5 convolution_convert_fusion.3
  33.1 0.8 constant_dynamic-slice_fusion.2
  33.8 4.3 %all-to-all-start = ((bf16[4,96,1536]{2,1,0:T(8,128)(2,1)}), bf16[4,96,1536]{2,1,0:T(8,128)(2,1)}, u32[]{:S(2)}, u32[]{:S(2)}) async-start(bf16[4,96,1536]{2,1,0:T(8,128)(2,1)} %bitcast.98), calls=%async_computation | async-start | bytes 2359296 | tf_op jit(solution)/shard_map/all_to_all | solution.py:251
  38.1 3.6 %collective-permute-start.2 = (s32[256,4]{1,0:T(8,128)S(1)}, s32[256,4]{1,0:T(8,128)S(1)}, u32[]{:S(2)}, u32[]{:S(2)}) collective-permute-start(s32[256,4]{1,0:T(8,128)S(1)} %copy.27), channel_id=1, source_target_pairs={{0,8},{8,0},{1,9},{9,1},{2,10},{10,2},{3,11},{11,3},{4,12},{12,4},... | collective-permute-start | bytes 12296 | tf_op jit(solution)/shard_map/ppermute | solution.py:152
  41.7 0.8 fusion.37
  42.6 12.1 %collective-permute-done.2 = s32[256,4]{1,0:T(8,128)S(1)} collective-permute-done((s32[256,4]{1,0:T(8,128)S(1)}, s32[256,4]{1,0:T(8,128)S(1)}, u32[]{:S(2)}, u32[]{:S(2)}) %collective-permute-start.2) | collective-permute-done | bytes 4128 | tf_op jit(solution)/shard_map/ppermute | solution.py:152
  54.8 2.3 %reduce-window.16 = s32[8,8,128]{2,1,0:T(8,128)S(1)} reduce-window(s32[8,8,128]{2,1,0:T(8,128)S(1)} %fusion.51, s32[]{:T(128)} %constant.67.clone.1), window={size=1x1x128 pad=0_0x0_0x127_0}, to_apply=%region_5.6 | reduce-window | flops 1040384 | bytes 65540 | tf_op jit(solution)/shard_map/reduce-window.2
  57.1 0.3 slice_reduce_fusion
  57.4 0.2 reduce-window.19
  57.5 3.4 %collective-permute-start.3 = (bf16[128,1536]{1,0:T(8,128)(2,1)}, bf16[128,1536]{1,0:T(8,128)(2,1)}, u32[]{:S(2)}, u32[]{:S(2)}) collective-permute-start(bf16[128,1536]{1,0:T(8,128)(2,1)} %constant_dynamic-slice_fusion.2), channel_id=1, source_target_pairs={{0,8},{8,0},{1,9},{9,1},{2,10},{10,2},{3,11},{11,3},{4,12},{12,4},... | collective-permute-start | bytes 1179656 | tf_op jit(solution)/shard_map/ppermute | solution.py:152
  61.1 0.1 reduce_sum.50
  61.3 1.4 fusion.41
  62.7 0.9 copy.39
  63.6 0.2 fusion.34
  63.8 15.1 %collective-permute-done.3 = bf16[128,1536]{1,0:T(8,128)(2,1)} collective-permute-done((bf16[128,1536]{1,0:T(8,128)(2,1)}, bf16[128,1536]{1,0:T(8,128)(2,1)}, u32[]{:S(2)}, u32[]{:S(2)}) %collective-permute-start.3) | collective-permute-done | bytes 393248 | tf_op jit(solution)/shard_map/ppermute | solution.py:152
  78.9 2.8 %convolution_convert_fusion.2 = bf16[512,1536]{1,0:T(8,128)(2,1)} fusion(bf16[128,512]{1,0:T(8,128)(2,1)S(1)} %fusion.34, bf16[128,1536]{1,0:T(8,128)(2,1)} %collective-permute-done.3), kind=kOutput, calls=%fused_computation.10 | convolution fusion | flops 202113024 | bytes 2097152 | tf_op jit(solution)/shard_map/dot_general | solution.py:194
  81.6 4.5 %all-to-all-start.1 = ((bf16[4,128,1536]{2,1,0:T(8,128)(2,1)}), bf16[4,128,1536]{2,1,0:T(8,128)(2,1)}, u32[]{:S(2)}, u32[]{:S(2)}) async-start(bf16[4,128,1536]{2,1,0:T(8,128)(2,1)} %bitcast.97), calls=%async_computation.1 | async-start | bytes 3145728 | tf_op jit(solution)/shard_map/all_to_all | solution.py:258
  86.2 2.4 %constant_dynamic-update-slice_fusion.1 = bf16[4,224,1536]{2,1,0:T(8,128)(2,1)} fusion(bf16[4,96,1536]{2,1,0:T(8,128)(2,1)} %all-to-all-done), kind=kLoop, calls=%fused_computation.96 | loop fusion | bytes 2359296
  88.5 16.6 %all-to-all-done.1 = bf16[4,128,1536]{2,1,0:T(8,128)(2,1)} async-done(((bf16[4,128,1536]{2,1,0:T(8,128)(2,1)}), bf16[4,128,1536]{2,1,0:T(8,128)(2,1)}, u32[]{:S(2)}, u32[]{:S(2)}) %all-to-all-start.1) | async-done | bytes 1572896 | tf_op jit(solution)/shard_map/all_to_all | solution.py:258
  105.1 2.8 %constant_dynamic-update-slice_fusion = bf16[4,224,1536]{2,1,0:T(8,128)(2,1)} fusion(bf16[4,224,1536]{2,1,0:T(8,128)(2,1)} %constant_dynamic-update-slice_fusion.1, bf16[4,128,1536]{2,1,0:T(8,128)(2,1)} %all-to-all-done.1), kind=kLoop, calls=%fused_computation.95 | loop fusion | bytes 3145728 | tf_op jit(solution)/shard_map/concatenate | solution.py:260
  108.0 7.3 %fusion.11 = f32[2,896,768]{2,1,0:T(8,128)S(1)} fusion(bf16[896,1536,1]{1,0,2:T(8,128)(2,1)} %bitcast.100, bf16[1,2,1536,768]{3,2,1,0:T(8,128)(2,1)} %param.20), kind=kOutput, calls=%fused_computation.20 | convolution fusion | flops 4227858432 | bytes 12976128 | tf_op jit(solution)/shard_map/rd,kdf->krf/dot_general | solution.py:56
  115.3 0.8 fusion.25
  116.1 4.4 %fusion.14 = f32[2,896,768]{2,1,0:T(8,128)S(1)} fusion(bf16[896,1536,1]{1,0,2:T(8,128)(2,1)S(1)} %bitcast.105, bf16[1,2,1536,768]{3,2,1,0:T(8,128)(2,1)S(1)} %bitcast.104), kind=kOutput, calls=%fused_computation.21 | convolution fusion | flops 4227858432 | bytes 12976128 | tf_op jit(solution)/shard_map/rd,kdf->krf/dot_general | solution.py:56
  120.5 2.4 %convolution_convert_fusion = bf16[896,1536]{1,0:T(8,128)(2,1)S(1)} fusion(bf16[1,768,1536]{2,1,0:T(8,128)(2,1)S(1)} %copy-done.6, f32[2,896,768]{2,1,0:T(8,128)S(1)} %fusion.14), kind=kOutput, calls=%fused_computation.7 | convolution fusion | flops 2120810496 | bytes 10616832 | tf_op jit(solution)/shard_map/dot_general | solution.py:139
  122.9 0.6 collective-permute-start.5
  123.5 2.3 %convolution_convert_fusion.1 = bf16[896,1536]{1,0:T(8,128)(2,1)S(1)} fusion(bf16[896,768]{1,0:T(8,128)(2,1)S(1)} %fusion.25, bf16[1,768,1536]{2,1,0:T(8,128)(2,1)S(1)} %copy-done.6), kind=kOutput, calls=%fused_computation.8 | convolution fusion | flops 2115305472 | bytes 6488064 | tf_op jit(solution)/shard_map/dot_general | solution.py:144
  125.8 2.4 %collective-permute-done.5 = bf16[4,224,1536]{2,1,0:T(8,128)(2,1)S(1)} collective-permute-done((bf16[4,224,1536]{2,1,0:T(8,128)(2,1)S(1)}, bf16[4,224,1536]{2,1,0:T(8,128)(2,1)S(1)}, u32[]{:S(2)}, u32[]{:S(2)}) %collective-permute-start.5) | collective-permute-done | bytes 2752544 | tf_op jit(solution)/shard_map/ppermute | solution.py:25
  128.2 0.8 fusion
  129.1 1.5 copy-done.1
  130.6 1.3 slice.65
  131.9 4.3 %all-to-all-start.2 = ((bf16[4,128,1536]{2,1,0:T(8,128)(2,1)}), bf16[4,128,1536]{2,1,0:T(8,128)(2,1)}, u32[]{:S(2)}, u32[]{:S(2)}) async-start(bf16[4,128,1536]{2,1,0:T(8,128)(2,1)} %slice.65), calls=%async_computation.2 | async-start | bytes 3145728 | tf_op jit(solution)/shard_map/all_to_all | solution.py:262
  136.2 3.3 %collective-permute-start.6 = (f32[256,4]{0,1:T(4,128)S(1)}, f32[256,4]{0,1:T(4,128)S(1)}, u32[]{:S(2)}, u32[]{:S(2)}) collective-permute-start(f32[256,4]{0,1:T(4,128)S(1)} %copy-done.8), channel_id=1, source_target_pairs={{0,8},{8,0},{1,9},{9,1},{2,10},{10,2},{3,11},{11,3},{4,12},{12,4},... | collective-permute-start | bytes 12296 | tf_op jit(solution)/shard_map/ppermute | solution.py:152
  139.5 14.7 %collective-permute-done.6 = f32[256,4]{0,1:T(4,128)S(1)} collective-permute-done((f32[256,4]{0,1:T(4,128)S(1)}, f32[256,4]{0,1:T(4,128)S(1)}, u32[]{:S(2)}, u32[]{:S(2)}) %collective-permute-start.6) | collective-permute-done | bytes 4128 | tf_op jit(solution)/shard_map/ppermute | solution.py:152
  154.2 2.4 %slice.64 = bf16[4,96,1536]{2,1,0:T(8,128)(2,1)} slice(bf16[4,224,1536]{2,1,0:T(8,128)(2,1)} %copy-done.1), slice={[0:4], [0:96], [0:1536]} | slice | bytes 2359296 | tf_op jit(solution)/shard_map/slice | solution.py:265
  156.6 3.3 %multiply_reduce_fusion.1 = bf16[128,1536]{1,0:T(8,128)(2,1)} fusion(f32[128,4]{0,1:T(4,128)S(1)} %constant_dynamic-slice_fusion.1, bf16[512,1536,1]{1,0,2:T(8,128)(2,1)} %bitcast.23, s32[128,4]{0,1:T(4,128)S(1)} %copy.39), kind=kOutput, calls=%fused_computation.9 | convolution fusion | flops 806944768 | bytes 1970176 | tf_op jit(solution)/shard_map/dot_general | solution.py:204
  159.9 7.5 %all-to-all-start.3 = ((bf16[4,96,1536]{2,1,0:T(8,128)(2,1)}), bf16[4,96,1536]{2,1,0:T(8,128)(2,1)}, u32[]{:S(2)}, u32[]{:S(2)}) async-start(bf16[4,96,1536]{2,1,0:T(8,128)(2,1)} %slice.64), calls=%async_computation.3 | async-start | bytes 2359296 | tf_op jit(solution)/shard_map/all_to_all | solution.py:268
  167.4 15.2 %all-to-all-done.3 = bf16[4,96,1536]{2,1,0:T(8,128)(2,1)} async-done(((bf16[4,96,1536]{2,1,0:T(8,128)(2,1)}), bf16[4,96,1536]{2,1,0:T(8,128)(2,1)}, u32[]{:S(2)}, u32[]{:S(2)}) %all-to-all-start.3) | async-done | bytes 1179680 | tf_op jit(solution)/shard_map/all_to_all | solution.py:268
  182.6 3.6 %multiply_reduce_fusion = f32[256,1536]{1,0:T(8,128)S(1)} fusion(bf16[384,1536,1]{1,0,2:T(8,128)(2,1)} %bitcast.25, f32[256,4]{0,1:T(4,128)S(1)} %copy-done.8, s32[256,4]{0,1:T(4,128)S(1)} %copy.36), kind=kOutput, calls=%fused_computation | convolution fusion | flops 1211105280 | bytes 2760704 | tf_op jit(solution)/shard_map/dot_general | solution.py:204
  186.4 20.8 %collective-permute-done.8 = bf16[128,1536]{1,0:T(8,128)(2,1)S(1)} collective-permute-done((bf16[128,1536]{1,0:T(8,128)(2,1)S(1)}, bf16[128,1536]{1,0:T(8,128)(2,1)S(1)}, u32[]{:S(2)}, u32[]{:S(2)}) %collective-permute-start.8) | collective-permute-done | bytes 393248 | tf_op jit(solution)/shard_map/ppermute | solution.py:152
  207.2 0.2 add_convert_fusion
  207.5 1.8 collective-permute-done.9
  209.4 2.2 %maximum_select_fusion = bf16[256,1536]{1,0:T(8,128)(2,1)} fusion(bf16[128,1536]{1,0:T(8,128)(2,1)} %collective-permute-done.9, bf16[128,1536]{1,0:T(8,128)(2,1)S(1)} %add_convert_fusion, pred[]{:T(512)S(6)} %eq.148), kind=kLoop, calls=%fused_computation.40 | loop fusion | flops 3538944 | bytes 1572865 | tf_op jit(solution)/shard_map/jit(_where)/select_n | solution.py:160
  (50 shorter events, 1.1 us)
Async XLA Ops:
  0.0 17.0 %copy-start = (bf16[1024,1536]{1,0:T(8,128)(2,1)S(1)}, bf16[1024,1536]{1,0:T(8,128)(2,1)}, u32[]{:S(2)}) copy-start(bf16[1024,1536]{1,0:T(8,128)(2,1)} %param.17) | copy-start | bytes 9437188
  0.9 6.9 %collective-permute-start = (bf16[2,128,128]{2,1,0:T(8,128)(2,1)S(1)}, bf16[2,128,128]{2,1,0:T(8,128)(2,1)S(1)}, u32[]{:S(2)}, u32[]{:S(2)}) collective-permute-start(bf16[2,128,128]{2,1,0:T(8,128)(2,1)S(1)} %pad_maximum_fusion), channel_id=1, source_target_pairs={{0,2},{2,4},{4,6},{6,8},{8,10},{10,12},{12,14},{1,3},{3,5},{5,7},{... | collective-permute-start | bytes 196616 | tf_op jit(solution)/shard_map/ppermute | solution.py:20
  17.0 6.3 %copy-start.4 = (s32[256,4]{0,1:T(4,128)S(1)}, s32[256,4]{0,1:T(4,128)}, u32[]{:S(2)}) copy-start(s32[256,4]{0,1:T(4,128)} %param.22) | copy-start | bytes 12292
  20.2 7.5 %collective-permute-start.1 = (f32[256,1536]{1,0:T(8,128)}, f32[256,1536]{1,0:T(8,128)}, u32[]{:S(2)}, u32[]{:S(2)}) collective-permute-start(f32[256,1536]{1,0:T(8,128)} %fusion.68), channel_id=1, source_target_pairs={{0,1},{1,0},{2,3},{3,2},{4,5},{5,4},{6,7},{7,6},{8,9},{9,8},{10,11... | collective-permute-start | bytes 4718600 | tf_op jit(solution)/shard_map/ppermute | solution.py:25
  27.7 3.6 %copy-start.5 = (f32[1536]{0:T(1024)S(1)}, f32[1536]{0:T(1024)}, u32[]{:S(2)}) copy-start(f32[1536]{0:T(1024)} %param.19) | copy-start | bytes 18436
  30.2 1.1 copy-start.2
  33.8 47.8 %all-to-all-start = ((bf16[4,96,1536]{2,1,0:T(8,128)(2,1)}), bf16[4,96,1536]{2,1,0:T(8,128)(2,1)}, u32[]{:S(2)}, u32[]{:S(2)}) async-start(bf16[4,96,1536]{2,1,0:T(8,128)(2,1)} %bitcast.98), calls=%async_computation | async-start | bytes 2359296 | tf_op jit(solution)/shard_map/all_to_all | solution.py:251
  38.1 16.6 %collective-permute-start.2 = (s32[256,4]{1,0:T(8,128)S(1)}, s32[256,4]{1,0:T(8,128)S(1)}, u32[]{:S(2)}, u32[]{:S(2)}) collective-permute-start(s32[256,4]{1,0:T(8,128)S(1)} %copy.27), channel_id=1, source_target_pairs={{0,8},{8,0},{1,9},{9,1},{2,10},{10,2},{3,11},{11,3},{4,12},{12,4},... | collective-permute-start | bytes 12296 | tf_op jit(solution)/shard_map/ppermute | solution.py:152
  57.5 21.3 %collective-permute-start.3 = (bf16[128,1536]{1,0:T(8,128)(2,1)}, bf16[128,1536]{1,0:T(8,128)(2,1)}, u32[]{:S(2)}, u32[]{:S(2)}) collective-permute-start(bf16[128,1536]{1,0:T(8,128)(2,1)} %constant_dynamic-slice_fusion.2), channel_id=1, source_target_pairs={{0,8},{8,0},{1,9},{9,1},{2,10},{10,2},{3,11},{11,3},{4,12},{12,4},... | collective-permute-start | bytes 1179656 | tf_op jit(solution)/shard_map/ppermute | solution.py:152
  81.6 23.5 %all-to-all-start.1 = ((bf16[4,128,1536]{2,1,0:T(8,128)(2,1)}), bf16[4,128,1536]{2,1,0:T(8,128)(2,1)}, u32[]{:S(2)}, u32[]{:S(2)}) async-start(bf16[4,128,1536]{2,1,0:T(8,128)(2,1)} %bitcast.97), calls=%async_computation.1 | async-start | bytes 3145728 | tf_op jit(solution)/shard_map/all_to_all | solution.py:258
  105.1 10.9 %slice-start = ((s8[4718592]{0:T(1024)(128)(4,1)}), s8[4194304]{0:T(1024)(128)(4,1)S(1)}, s32[]{:S(2)}) async-start(s8[4718592]{0:T(1024)(128)(4,1)} %bitcast.103), calls=%async_computation.4 | async-start | bytes 8388608
  108.0 8.1 %collective-permute-start.4 = (bf16[4,224,1536]{2,1,0:T(8,128)(2,1)}, bf16[4,224,1536]{2,1,0:T(8,128)(2,1)S(1)}, u32[]{:S(2)}, u32[]{:S(2)}) collective-permute-start(bf16[4,224,1536]{2,1,0:T(8,128)(2,1)} %constant_dynamic-update-slice_fusion), channel_id=1, source_target_pairs={{0,1},{1,0},{2,3},{3,2},{4,5},{5,4},{6,7},{7,6},{8,9},{9,8},{10,11... | collective-permute-start | bytes 8257544 | tf_op jit(solution)/shard_map/ppermute | solution.py:25
  108.0 8.1 %slice-start.1 = ((s8[4718592]{0:T(1024)(128)(4,1)}), s8[524288]{0:T(1024)(128)(4,1)S(1)}, s32[]{:S(2)}) async-start(s8[4718592]{0:T(1024)(128)(4,1)} %bitcast.103), calls=%async_computation.5 | async-start | bytes 1048576
  116.1 4.4 %copy-start.6 = (bf16[1,768,1536]{2,1,0:T(8,128)(2,1)S(1)}, bf16[1,768,1536]{2,1,0:T(8,128)(2,1)}, u32[]{:S(2)}) copy-start(bf16[1,768,1536]{2,1,0:T(8,128)(2,1)} %param.21) | copy-start | bytes 7077892
  122.9 5.3 %collective-permute-start.5 = (bf16[4,224,1536]{2,1,0:T(8,128)(2,1)S(1)}, bf16[4,224,1536]{2,1,0:T(8,128)(2,1)S(1)}, u32[]{:S(2)}, u32[]{:S(2)}) collective-permute-start(bf16[4,224,1536]{2,1,0:T(8,128)(2,1)S(1)} %bitcast.106), channel_id=1, source_target_pairs={{0,1},{1,0},{2,3},{3,2},{4,5},{5,4},{6,7},{7,6},{8,9},{9,8},{10,11... | collective-permute-start | bytes 8257544 | tf_op jit(solution)/shard_map/ppermute | solution.py:25
  129.0 1.6 copy-start.1
  130.6 5.6 %copy-start.8 = (f32[256,4]{0,1:T(4,128)S(1)}, f32[256,4]{0,1:T(4,128)}, u32[]{:S(2)}) copy-start(f32[256,4]{0,1:T(4,128)} %param.23) | copy-start | bytes 12292
  131.9 24.8 %all-to-all-start.2 = ((bf16[4,128,1536]{2,1,0:T(8,128)(2,1)}), bf16[4,128,1536]{2,1,0:T(8,128)(2,1)}, u32[]{:S(2)}, u32[]{:S(2)}) async-start(bf16[4,128,1536]{2,1,0:T(8,128)(2,1)} %slice.65), calls=%async_computation.2 | async-start | bytes 3145728 | tf_op jit(solution)/shard_map/all_to_all | solution.py:262
  136.2 18.0 %collective-permute-start.6 = (f32[256,4]{0,1:T(4,128)S(1)}, f32[256,4]{0,1:T(4,128)S(1)}, u32[]{:S(2)}, u32[]{:S(2)}) collective-permute-start(f32[256,4]{0,1:T(4,128)S(1)} %copy-done.8), channel_id=1, source_target_pairs={{0,8},{8,0},{1,9},{9,1},{2,10},{10,2},{3,11},{11,3},{4,12},{12,4},... | collective-permute-start | bytes 12296 | tf_op jit(solution)/shard_map/ppermute | solution.py:152
  159.9 22.7 %all-to-all-start.3 = ((bf16[4,96,1536]{2,1,0:T(8,128)(2,1)}), bf16[4,96,1536]{2,1,0:T(8,128)(2,1)}, u32[]{:S(2)}, u32[]{:S(2)}) async-start(bf16[4,96,1536]{2,1,0:T(8,128)(2,1)} %slice.64), calls=%async_computation.3 | async-start | bytes 2359296 | tf_op jit(solution)/shard_map/all_to_all | solution.py:268
  182.6 3.8 %copy-start.7 = (bf16[128,1536]{1,0:T(8,128)(2,1)S(1)}, bf16[128,1536]{1,0:T(8,128)(2,1)}, u32[]{:S(2)}) copy-start(bf16[128,1536]{1,0:T(8,128)(2,1)} %multiply_reduce_fusion.1) | copy-start | bytes 1179652
  182.6 24.6 %copy-start.3 = (f32[256,1536]{1,0:T(8,128)S(1)}, f32[256,1536]{1,0:T(8,128)}, u32[]{:S(2)}) copy-start(f32[256,1536]{1,0:T(8,128)} %copy-done.2) | copy-start | bytes 4718596
  186.3 20.9 %collective-permute-start.7 = (f32[128,1536]{1,0:T(8,128)S(1)}, f32[128,1536]{1,0:T(8,128)S(1)}, u32[]{:S(2)}, u32[]{:S(2)}) collective-permute-start(f32[128,1536]{1,0:T(8,128)S(1)} %constant_dynamic-slice_fusion), channel_id=1, source_target_pairs={{0,1},{1,0},{2,3},{3,2},{4,5},{5,4},{6,7},{7,6},{8,9},{9,8},{10,11... | collective-permute-start | bytes 2359304 | tf_op jit(solution)/shard_map/ppermute | solution.py:25
  186.4 20.8 %collective-permute-start.8 = (bf16[128,1536]{1,0:T(8,128)(2,1)S(1)}, bf16[128,1536]{1,0:T(8,128)(2,1)S(1)}, u32[]{:S(2)}, u32[]{:S(2)}) collective-permute-start(bf16[128,1536]{1,0:T(8,128)(2,1)S(1)} %copy-done.7), channel_id=1, source_target_pairs={{0,8},{8,0},{1,9},{9,1},{2,10},{10,2},{3,11},{11,3},{4,12},{12,4},... | collective-permute-start | bytes 1179656 | tf_op jit(solution)/shard_map/ppermute | solution.py:152
  207.4 1.9 collective-permute-start.9

commit v12 on v6

--- a/solution.py
+++ b/solution.py
@@ -59,7 +59,7 @@
     return ((up_val + 1.0) * gate_val * jax.nn.sigmoid(GLU_ALPHA * gate_val)).astype(jnp.bfloat16)
 
 
-def attention_kernel(sink_ref, q_ref, pk_ref, k_ref, pv_ref, v_ref, o_ref):
+def attention_kernel(sink_ref, q_ref, pk_ref, k_ref, pv_ref, v_ref, w_ref, o_ref, heads_ref):
     rows = q_ref.shape[0]
     prior = pk_ref.shape[0]
     span = 2 * WINDOW
@@ -105,28 +105,32 @@
                 probs = (weights_exp * (1.0 / denominator)).astype(jnp.bfloat16)
                 out = jnp.dot(probs, v_placed, preferred_element_type=jnp.float32)
                 total = out if total is None else total + out
-            o_ref[b * WINDOW : (b + 1) * WINDOW, j * pair_cols : (j + 1) * pair_cols] = total.astype(
-                o_ref.dtype
+            heads_ref[b * WINDOW : (b + 1) * WINDOW, j * pair_cols : (j + 1) * pair_cols] = total.astype(
+                heads_ref.dtype
             )
-
-
-def attend_kernel(queries, prior_keys, key_rows, prior_values, values, sink_logits):
+    o_ref[...] = jnp.dot(heads_ref[...], w_ref[...], preferred_element_type=jnp.float32)
+
+
+def attend_kernel(queries, prior_keys, key_rows, prior_values, values, sink_logits, out_weight):
     rows, cols = queries.shape
     heads = cols // HEAD_DIM
     span = 2 * WINDOW
+    width = out_weight.shape[1]
     cost = pl.CostEstimate(
-        flops=2 * 2 * rows * span * 2 * HEAD_DIM * heads,
+        flops=2 * 2 * rows * span * 2 * HEAD_DIM * heads + 2 * rows * cols * width,
         transcendentals=rows * span * heads,
-        bytes_accessed=2 * rows * cols * 2 + 2 * (rows + WINDOW) * key_rows.shape[1] * 2,
+        bytes_accessed=rows * cols * 2 + out_weight.size * 2 + rows * width * 4
+        + 2 * (rows + WINDOW) * key_rows.shape[1] * 2,
     )
     vmem = pl.BlockSpec(memory_space=pltpu.VMEM)
     return pl.pallas_call(
         attention_kernel,
-        out_shape=jax.ShapeDtypeStruct((rows, cols), jnp.bfloat16),
-        in_specs=[pl.BlockSpec(memory_space=pltpu.SMEM)] + [vmem] * 5,
+        out_shape=jax.ShapeDtypeStruct((rows, width), jnp.float32),
+        in_specs=[pl.BlockSpec(memory_space=pltpu.SMEM)] + [vmem] * 6,
         out_specs=vmem,
+        scratch_shapes=[pltpu.VMEM((rows, cols), jnp.bfloat16)],
         cost_estimate=cost,
-    )(sink_logits, queries, prior_keys, key_rows, prior_values, values)
+    )(sink_logits, queries, prior_keys, key_rows, prior_values, values, out_weight)
 
 
 def on_device(
@@ -148,8 +152,7 @@
     rim_rows = jnp.stack([key_rows[tok_rows - window_rows :], values[tok_rows - window_rows :]])
     received = shifted(rim_rows, "seq", 1)
     prior = jnp.where(lax.axis_index("seq") == 0, cached_rows, received)
-    pieces = attend_kernel(queries, prior[0], key_rows, prior[1], values, sink_logits)
-    partial_rows = jnp.dot(pieces, out_weight, preferred_element_type=jnp.float32)
+    partial_rows = attend_kernel(queries, prior[0], key_rows, prior[1], values, sink_logits, out_weight)
     mixed_rows = residual.astype(jnp.float32) + (partial_rows + swap_exp(partial_rows))
     normed = rms_normalize(mixed_rows, norm_gain)
 

time: 170 us -> 168 us (0.988)
  matrix products: 18.8 us -> 15.6 us
  Pallas kernels: 7.73 us -> 10 us
    dot_general x1 -> x0, matrix products: 3.19 us -> none  [on_device(): jnp.dot(pieces, out_weight, preferred_element_type=jnp.float32)]
    pallas_call x1, Pallas kernels: 7.73 us -> 10 us  [attend_kernel(): pl.pallas_call(attention_kernel, out_shape=jax.ShapeDtypeStruct((rows, wi...]
where the time goes in v12:
time: 168 us
  blocking collectives  118 us (70%)
  matrix products  15.6 us (9%)
  Pallas kernels  10 us (6%)
  other arithmetic  8.8 us (5%)
  waiting for transfers between devices  7.47 us (4%)
  starting transfers between devices  5.5 us (3%)
  local copies, waits for them, and re-layouts  2.58 us (2%)
    all_to_all x1, blocking collectives, on_device(): lax.all_to_all(outgoing, 'seq', split_axis=0, concat_axis=0, tiled=True)  60.1 us
    all_to_all x1, blocking collectives, on_device(): lax.all_to_all(result, 'seq', split_axis=0, concat_axis=0, tiled=True)  57.8 us
    pallas_call x1, Pallas kernels, attend_kernel(): pl.pallas_call(attention_kernel, out_shape=jax.ShapeDtypeStruct((rows, wi...  10 us
    dot_general x2, matrix products, expert_hidden(): jnp.einsum('rd,kdf->krf', rows, expert_in, preferred_element_type=jnp.flo...  7.62 us
    ppermute x4, waiting for transfers between devices, swap_exp(): return lax.ppermute(x, 'exp', [(i, (i + 1) % size) for i in range(size)])  5.59 us
    ppermute x1, starting transfers between devices, shifted(): return lax.ppermute(shard, axis, pairs)  4.87 us
  transfers between devices with their start and end apart: 5, of which 3 were waited for; matrix products, arithmetic and copies ran while one was open for 6% of the time, Pallas kernels for 0%

profile of v12, /device:TPU:0, one launch (start us, length us, event | category | flops | bytes accessed | tf_op | source)
XLA Modules:
  0.0 168.1 jit_solution(14672614603315598702)
XLA Ops:
  0.0 0.0 copy-start
  0.0 0.9 slice_bitcast_fusion.2
  0.9 4.9 %collective-permute-start = (bf16[2,128,128]{2,1,0:T(8,128)(2,1)S(1)}, bf16[2,128,128]{2,1,0:T(8,128)(2,1)S(1)}, u32[]{:S(2)}, u32[]{:S(2)}) collective-permute-start(bf16[2,128,128]{2,1,0:T(8,128)(2,1)S(1)} %pad_maximum_fusion), channel_id=1, source_target_pairs={{0,2},{2,4},{4,6},{6,8},{8,10},{10,12},{12,14},{1,3},{3,5},{5,7},{... | collective-permute-start | bytes 196616 | tf_op jit(solution)/shard_map/ppermute | solution.py:20
  5.8 1.9 %collective-permute-done = bf16[2,128,128]{2,1,0:T(8,128)(2,1)S(1)} collective-permute-done((bf16[2,128,128]{2,1,0:T(8,128)(2,1)S(1)}, bf16[2,128,128]{2,1,0:T(8,128)(2,1)S(1)}, u32[]{:S(2)}, u32[]{:S(2)}) %collective-permute-start) | collective-permute-done | bytes 65568 | tf_op jit(solution)/shard_map/ppermute | solution.py:20
  7.7 0.8 broadcast_select_fusion
  8.6 0.6 slice_bitcast_fusion
  9.2 0.0 copy-start.2
  9.2 0.0 copy-start.1
  9.2 10.0 %shard_map.118 = f32[256,1536]{1,0:T(8,128)} custom-call(f32[16]{0:T(128)} %sink_ref.1, bf16[256,1024]{1,0:T(8,128)(2,1)} %q_ref.1, bf16[128,128]{1,0:T(8,128)(2,1)} %get-tuple-element.12.pk_ref, bf16[256,128]{1,0:T(8,128)(2,1)} %k_ref.1, bf16[128,128]{1,0:T(8,128)(2,1)} %get-tuple-element.11.pv_ref, bf16[256,128]{1,0:T(8,128)(2,1)} %v_ref.1, ...), custom_call_target="tpu_custom_call" | custom-call | flops 1342177280 | bytes 5439488 | tf_op jit(solution)/shard_map/pallas_call | solution.py:126
  19.2 0.0 collective-permute-start.1
  19.2 0.0 copy-done.2
  19.2 0.1 copy.19
  19.4 0.1 eq.69
  19.5 0.1 eq.65
  19.6 2.3 %reduce-window.6 = s32[8,8,128]{2,1,0:T(8,128)S(1)} reduce-window(s32[8,8,128]{2,1,0:T(8,128)S(1)} %fusion.32, s32[]{:T(128)} %constant.13.clone.1), window={size=1x1x128 pad=0_0x0_0x127_0}, to_apply=%region_0.1 | reduce-window | flops 1040384 | bytes 65540 | tf_op jit(solution)/shard_map/reduce-window
  21.9 0.3 slice_reduce_fusion
  22.2 0.2 reduce-window.9
  22.3 0.1 add_bitcast_fusion
  22.4 0.1 sub.26
  22.6 0.1 copy.22
  22.8 0.1 copy.23
  22.8 0.4 fusion.22
  23.3 0.0 copy-start.3
  23.3 0.0 collective-permute-done.1
  23.3 0.0 copy-done.1
  23.3 0.0 slice-start
  23.4 2.4 %multiply_reduce_fusion.1 = (f32[256]{0:T(256)S(1)}, f32[256,1536]{1,0:T(8,128)S(1)}) fusion(f32[256,1536]{1,0:T(8,128)} %shard_map.118, f32[256,1536]{1,0:T(8,128)} %collective-permute-done.1, bf16[256,1536]{1,0:T(8,128)(2,1)S(1)} %copy-done.1), kind=kLoop, calls=%fused_computation.29 | loop fusion | flops 1965824 | bytes 5506048 | tf_op jit(solution)/shard_map/reduce_sum | solution.py:29
  25.7 0.0 copy-done.3
  25.7 0.0 slice-start.1
  25.8 0.9 convolution_convert_fusion.2
  26.6 60.1 %all_to_all.10 = bf16[8,96,1536]{2,1,0:T(8,128)(2,1)S(1)} all-to-all(bf16[8,96,1536]{2,1,0:T(8,128)(2,1)S(1)} %bitcast.67), channel_id=1, replica_groups=mesh['groups'=2,'seq'=8,'exp'=2] {'seq'}, dimensions={0} | all-to-all | bytes 4718592 | tf_op jit(solution)/shard_map/all_to_all | solution.py:181
  86.8 0.0 collective-permute-start.2
  86.8 0.0 slice-done
  86.8 0.0 slice-done.1
  86.8 3.8 %fusion.16 = f32[2,768,768]{2,1,0:T(8,128)S(1)} fusion(bf16[768,1536,1]{1,0,2:T(8,128)(2,1)S(1)} %bitcast.69, bf16[1,2,1536,768]{3,2,1,0:T(8,128)(2,1)S(1)} %bitcast.73), kind=kOutput, calls=%fused_computation.24 | convolution fusion | flops 3623878656 | bytes 11796480 | tf_op jit(solution)/shard_map/rd,kdf->krf/dot_general | solution.py:56
  90.6 0.7 fusion.27
  91.3 0.0 collective-permute-done.2
  91.3 3.8 %fusion.19 = f32[2,768,768]{2,1,0:T(8,128)S(1)} fusion(bf16[768,1536,1]{1,0,2:T(8,128)(2,1)S(1)} %bitcast.74, bf16[1,2,1536,768]{3,2,1,0:T(8,128)(2,1)S(1)} %bitcast.73), kind=kOutput, calls=%fused_computation.25 | convolution fusion | flops 3623878656 | bytes 11796480 | tf_op jit(solution)/shard_map/rd,kdf->krf/dot_general | solution.py:56
  95.1 0.0 copy-done
  95.1 2.1 %convolution_convert_fusion = bf16[768,1536]{1,0:T(8,128)(2,1)S(1)} fusion(bf16[1,768,1536]{2,1,0:T(8,128)(2,1)S(1)} %copy-done, f32[2,768,768]{2,1,0:T(8,128)S(1)} %fusion.19), kind=kOutput, calls=%fused_computation.7 | convolution fusion | flops 1817837568 | bytes 9437184 | tf_op jit(solution)/shard_map/dot_general | solution.py:187
  97.2 0.5 collective-permute-start.3
  97.8 2.0 %convolution_convert_fusion.1 = bf16[768,1536]{1,0:T(8,128)(2,1)S(1)} fusion(bf16[768,768]{1,0:T(8,128)(2,1)S(1)} %fusion.27, bf16[1,768,1536]{2,1,0:T(8,128)(2,1)S(1)} %copy-done), kind=kOutput, calls=%fused_computation.8 | convolution fusion | flops 1813118976 | bytes 5898240 | tf_op jit(solution)/shard_map/dot_general | solution.py:192
  99.7 2.2 %collective-permute-done.3 = bf16[8,96,1536]{2,1,0:T(8,128)(2,1)S(1)} collective-permute-done((bf16[8,96,1536]{2,1,0:T(8,128)(2,1)S(1)}, bf16[8,96,1536]{2,1,0:T(8,128)(2,1)S(1)}, u32[]{:S(2)}, u32[]{:S(2)}) %collective-permute-start.3) | collective-permute-done | bytes 2359328 | tf_op jit(solution)/shard_map/ppermute | solution.py:25
  101.9 0.7 fusion
  102.6 0.0 copy-start.4
  102.6 57.8 %all_to_all.11 = bf16[8,96,1536]{2,1,0:T(8,128)(2,1)S(1)} all-to-all(bf16[8,96,1536]{2,1,0:T(8,128)(2,1)S(1)} %fusion), channel_id=1, replica_groups=mesh['groups'=2,'seq'=8,'exp'=2] {'seq'}, dimensions={0} | all-to-all | bytes 4718592 | tf_op jit(solution)/shard_map/all_to_all | solution.py:197
  160.4 0.0 copy-done.4
  160.4 3.0 %multiply_reduce_fusion = f32[256,1536]{1,0:T(8,128)S(1)} fusion(bf16[768,1536,1]{1,0,2:T(8,128)(2,1)S(1)} %bitcast.70, f32[256,4]{0,1:T(4,128)S(1)} %copy-done.4, s32[256,4]{0,1:T(4,128)S(1)} %copy.23), kind=kOutput, calls=%fused_computation | convolution fusion | flops 2419458048 | bytes 3940352 | tf_op jit(solution)/shard_map/dot_general | solution.py:198
  163.4 0.1 collective-permute-start.4
  163.5 3.4 %collective-permute-done.4 = f32[256,1536]{1,0:T(8,128)S(1)} collective-permute-done((f32[256,1536]{1,0:T(8,128)S(1)}, f32[256,1536]{1,0:T(8,128)S(1)}, u32[]{:S(2)}, u32[]{:S(2)}) %collective-permute-start.4) | collective-permute-done | bytes 1572896 | tf_op jit(solution)/shard_map/ppermute | solution.py:25
  166.9 1.2 add_convert_fusion
  (8 shorter events, 0.1 us)
Async XLA Ops:
  0.0 95.1 %copy-start = (bf16[1,768,1536]{2,1,0:T(8,128)(2,1)S(1)}, bf16[1,768,1536]{2,1,0:T(8,128)(2,1)}, u32[]{:S(2)}) copy-start(bf16[1,768,1536]{2,1,0:T(8,128)(2,1)} %param.21) | copy-start | bytes 7077892
  0.9 6.8 %collective-permute-start = (bf16[2,128,128]{2,1,0:T(8,128)(2,1)S(1)}, bf16[2,128,128]{2,1,0:T(8,128)(2,1)S(1)}, u32[]{:S(2)}, u32[]{:S(2)}) collective-permute-start(bf16[2,128,128]{2,1,0:T(8,128)(2,1)S(1)} %pad_maximum_fusion), channel_id=1, source_target_pairs={{0,2},{2,4},{4,6},{6,8},{8,10},{10,12},{12,14},{1,3},{3,5},{5,7},{... | collective-permute-start | bytes 196616 | tf_op jit(solution)/shard_map/ppermute | solution.py:20
  9.2 10.0 %copy-start.2 = (s32[256,4]{0,1:T(4,128)S(1)}, s32[256,4]{0,1:T(4,128)}, u32[]{:S(2)}) copy-start(s32[256,4]{0,1:T(4,128)} %param.22) | copy-start | bytes 12292
  9.2 14.1 %copy-start.1 = (bf16[256,1536]{1,0:T(8,128)(2,1)S(1)}, bf16[256,1536]{1,0:T(8,128)(2,1)}, u32[]{:S(2)}) copy-start(bf16[256,1536]{1,0:T(8,128)(2,1)} %param.18) | copy-start | bytes 2359300
  19.2 4.1 %collective-permute-start.1 = (f32[256,1536]{1,0:T(8,128)}, f32[256,1536]{1,0:T(8,128)}, u32[]{:S(2)}, u32[]{:S(2)}) collective-permute-start(f32[256,1536]{1,0:T(8,128)} %shard_map.118), channel_id=1, source_target_pairs={{0,1},{1,0},{2,3},{3,2},{4,5},{5,4},{6,7},{7,6},{8,9},{9,8},{10,11... | collective-permute-start | bytes 4718600 | tf_op jit(solution)/shard_map/ppermute | solution.py:25
  23.3 2.4 %copy-start.3 = (f32[1536]{0:T(1024)S(1)}, f32[1536]{0:T(1024)}, u32[]{:S(2)}) copy-start(f32[1536]{0:T(1024)} %param.19) | copy-start | bytes 18436
  23.3 63.5 %slice-start = ((s8[4718592]{0:T(1024)(128)(4,1)}), s8[4194304]{0:T(1024)(128)(4,1)S(1)}, s32[]{:S(2)}) async-start(s8[4718592]{0:T(1024)(128)(4,1)} %bitcast.72), calls=%async_computation.2 | async-start | bytes 8388608
  25.7 61.1 %slice-start.1 = ((s8[4718592]{0:T(1024)(128)(4,1)}), s8[524288]{0:T(1024)(128)(4,1)S(1)}, s32[]{:S(2)}) async-start(s8[4718592]{0:T(1024)(128)(4,1)} %bitcast.72), calls=%async_computation.3 | async-start | bytes 1048576
  86.8 4.5 %collective-permute-start.2 = (bf16[8,96,1536]{2,1,0:T(8,128)(2,1)S(1)}, bf16[8,96,1536]{2,1,0:T(8,128)(2,1)S(1)}, u32[]{:S(2)}, u32[]{:S(2)}) collective-permute-start(bf16[8,96,1536]{2,1,0:T(8,128)(2,1)S(1)} %all_to_all.10), channel_id=1, source_target_pairs={{0,1},{1,0},{2,3},{3,2},{4,5},{5,4},{6,7},{7,6},{8,9},{9,8},{10,11... | collective-permute-start | bytes 7077896 | tf_op jit(solution)/shard_map/ppermute | solution.py:25
  97.2 4.7 %collective-permute-start.3 = (bf16[8,96,1536]{2,1,0:T(8,128)(2,1)S(1)}, bf16[8,96,1536]{2,1,0:T(8,128)(2,1)S(1)}, u32[]{:S(2)}, u32[]{:S(2)}) collective-permute-start(bf16[8,96,1536]{2,1,0:T(8,128)(2,1)S(1)} %bitcast.75), channel_id=1, source_target_pairs={{0,1},{1,0},{2,3},{3,2},{4,5},{5,4},{6,7},{7,6},{8,9},{9,8},{10,11... | collective-permute-start | bytes 7077896 | tf_op jit(solution)/shard_map/ppermute | solution.py:25
  102.6 57.8 %copy-start.4 = (f32[256,4]{0,1:T(4,128)S(1)}, f32[256,4]{0,1:T(4,128)}, u32[]{:S(2)}) copy-start(f32[256,4]{0,1:T(4,128)} %param.23) | copy-start | bytes 12292
  163.4 3.5 %collective-permute-start.4 = (f32[256,1536]{1,0:T(8,128)S(1)}, f32[256,1536]{1,0:T(8,128)S(1)}, u32[]{:S(2)}, u32[]{:S(2)}) collective-permute-start(f32[256,1536]{1,0:T(8,128)S(1)} %multiply_reduce_fusion), channel_id=1, source_target_pairs={{0,1},{1,0},{2,3},{3,2},{4,5},{5,4},{6,7},{7,6},{8,9},{9,8},{10,11... | collective-permute-start | bytes 4718600 | tf_op jit(solution)/shard_map/ppermute | solution.py:25

commit v13 on v3

--- a/solution.py
+++ b/solution.py
@@ -1,6 +1,8 @@
 import jax
 import jax.numpy as jnp
 from jax import lax
+from jax.experimental import pallas as pl
+from jax.experimental.pallas import tpu as pltpu
 from jax.sharding import PartitionSpec as P
 
 HEAD_DIM = 64
@@ -57,6 +59,107 @@
     return ((up_val + 1.0) * gate_val * jax.nn.sigmoid(GLU_ALPHA * gate_val)).astype(jnp.bfloat16)
 
 
+def attention_kernel(sink_ref, q_ref, k_ref, v_ref, w_ref, *rest):
+    o_ref, heads_ref = rest[-2], rest[-1]
+    span = k_ref.shape[0]
+    pair_cols = 2 * HEAD_DIM
+    pairs = q_ref.shape[1] // pair_cols
+    kv_count = k_ref.shape[1] // HEAD_DIM
+    per_kv = pairs // kv_count
+    q_pos = lax.broadcasted_iota(jnp.int32, (WINDOW, span), 0)
+    k_pos = lax.broadcasted_iota(jnp.int32, (WINDOW, span), 1)
+    allowed = (k_pos > q_pos) & (k_pos <= q_pos + WINDOW)
+    lane_half = lax.broadcasted_iota(jnp.int32, (span, pair_cols), 1) // HEAD_DIM
+    key_win = k_ref[...]
+    value_win = v_ref[...]
+    swapped_k = pltpu.roll(key_win, HEAD_DIM, 1)
+    swapped_v = pltpu.roll(value_win, HEAD_DIM, 1)
+    placed = {}
+    for kv in range(kv_count):
+        for a in range(2):
+            src_k = key_win if (kv % 2) == a else swapped_k
+            src_v = value_win if (kv % 2) == a else swapped_v
+            placed[kv, a] = (
+                jnp.where(lane_half == a, src_k, jnp.zeros_like(src_k)),
+                jnp.where(lane_half == a, src_v, jnp.zeros_like(src_v)),
+            )
+    for j in range(pairs):
+        kv = j // per_kv
+        q_pair = q_ref[:, j * pair_cols : (j + 1) * pair_cols]
+        total = None
+        for a in range(2):
+            k_placed, v_placed = placed[kv, a]
+            scores = lax.dot_general(
+                q_pair, k_placed, (((1,), (1,)), ((), ())), preferred_element_type=jnp.float32
+            ) * HEAD_DIM ** (-0.5)
+            scores = jnp.where(allowed, scores, -jnp.inf)
+            sink = sink_ref[2 * j + a]
+            largest = jnp.maximum(jnp.max(scores, axis=-1, keepdims=True), sink)
+            weights_exp = jnp.exp(scores - largest)
+            denominator = jnp.exp(sink - largest) + jnp.sum(weights_exp, axis=-1, keepdims=True)
+            probs = (weights_exp * (1.0 / denominator)).astype(jnp.bfloat16)
+            out = jnp.dot(probs, v_placed, preferred_element_type=jnp.float32)
+            total = out if total is None else total + out
+        heads_ref[:, j * pair_cols : (j + 1) * pair_cols] = total.astype(heads_ref.dtype)
+    o_ref[...] = jnp.dot(heads_ref[...], w_ref[...], preferred_element_type=jnp.float32)
+
+
+def attend_rows(block, queries, key_win, value_win, sink_logits, out_weight, into=None):
+    rows, cols = queries.shape
+    heads = cols // HEAD_DIM
+    span = key_win.shape[0]
+    width = out_weight.shape[1]
+    cost = pl.CostEstimate(
+        flops=2 * 2 * WINDOW * span * 2 * HEAD_DIM * heads + 2 * WINDOW * cols * width,
+        transcendentals=WINDOW * span * heads,
+        bytes_accessed=WINDOW * cols * 2 + out_weight.size * 2 + WINDOW * width * 4 + 2 * key_win.size * 2,
+    )
+    whole = lambda shape: pl.BlockSpec(shape, lambda i: (0, 0))
+    in_specs = [
+        pl.BlockSpec(memory_space=pltpu.SMEM),
+        pl.BlockSpec((WINDOW, cols), lambda i: (block, 0)),
+        whole(key_win.shape),
+        whole(value_win.shape),
+        whole(out_weight.shape),
+    ]
+    args = [sink_logits, queries, key_win, value_win, out_weight]
+    aliases = {}
+    if into is not None:
+        in_specs.append(pl.BlockSpec(memory_space=pl.ANY))
+        args.append(into)
+        aliases = {len(args) - 1: 0}
+    return pl.pallas_call(
+        attention_kernel,
+        out_shape=jax.ShapeDtypeStruct((rows, width), jnp.float32),
+        in_specs=in_specs,
+        out_specs=pl.BlockSpec((WINDOW, width), lambda i: (block, 0)),
+        grid=(1,),
+        scratch_shapes=[pltpu.VMEM((WINDOW, cols), jnp.bfloat16)],
+        input_output_aliases=aliases,
+        cost_estimate=cost,
+    )(*args)
+
+
+def attend_kernel(queries, prior_keys, key_rows, prior_values, values, sink_logits, out_weight):
+    rows = queries.shape[0]
+    blocks = rows // WINDOW
+    result = None
+    for block in range(blocks - 1, 0, -1):
+        first = (block - 1) * WINDOW
+        result = attend_rows(
+            block,
+            queries,
+            key_rows[first : first + 2 * WINDOW],
+            values[first : first + 2 * WINDOW],
+            sink_logits,
+            out_weight,
+            result,
+        )
+    key_win = jnp.concatenate([prior_keys, key_rows[:WINDOW]], axis=0)
+    value_win = jnp.concatenate([prior_values, values[:WINDOW]], axis=0)
+    return attend_rows(0, queries, key_win, value_win, sink_logits, out_weight, result)
+
+
 def on_device(
     queries,
     key_rows,
@@ -76,11 +179,7 @@
     rim_rows = jnp.stack([key_rows[tok_rows - window_rows :], values[tok_rows - window_rows :]])
     received = shifted(rim_rows, "seq", 1)
     prior = jnp.where(lax.axis_index("seq") == 0, cached_rows, received)
-    keys_all = jnp.concatenate([prior[0], key_rows], axis=0)
-    values_all = jnp.concatenate([prior[1], values], axis=0)
-    block_rows = min(tok_rows, 512)
-    pieces = attend_block(queries, keys_all, values_all, sink_logits, block_rows, window_rows)
-    partial_rows = jnp.dot(pieces, out_weight, preferred_element_type=jnp.float32)
+    partial_rows = attend_kernel(queries, prior[0], key_rows, prior[1], values, sink_logits, out_weight)
     mixed_rows = residual.astype(jnp.float32) + (partial_rows + swap_exp(partial_rows))
     normed = rms_normalize(mixed_rows, norm_gain)
 

time: 171 us -> 168 us (0.982)
  Pallas kernels: 0 us -> 12.8 us
  matrix products: 24.4 us -> 15.6 us
  local copies, waits for them, and re-layouts: 8.14 us -> 2.01 us
    pallas_call x0 -> x2, Pallas kernels: none -> 12.8 us  [attend_rows(): pl.pallas_call(attention_kernel, out_shape=jax.ShapeDtypeStruct((rows, wi...]
    dot_general x3 -> x0, matrix products: 8.84 us -> none  [the longest x1 4.57 us: attend_block(): jnp.einsum('hgqk,khd->qhgd', probs, value_block, preferred_element_type=j...]
    unnamed x20 -> x17, local copies, waits for them, and re-layouts: 5.39 us -> 0.18 us
  transfers between devices with their start and end apart: 5 -> 5, of which waited for: 2 -> 2; matrix products, arithmetic and copies ran while one was open for 9% -> 6% of each run, Pallas kernels for 0% -> 4%
where the time goes in v13:
time: 168 us
  blocking collectives  117 us (70%)
  matrix products  15.6 us (9%)
  Pallas kernels  12.8 us (8%)
  other arithmetic  9.22 us (5%)
  waiting for transfers between devices  5.59 us (3%)
  starting transfers between devices  5.51 us (3%)
  local copies, waits for them, and re-layouts  2.01 us (1%)
    all_to_all x1, blocking collectives, on_device(): lax.all_to_all(outgoing, 'seq', split_axis=0, concat_axis=0, tiled=True)  59.1 us
    all_to_all x1, blocking collectives, on_device(): lax.all_to_all(result, 'seq', split_axis=0, concat_axis=0, tiled=True)  57.8 us
    pallas_call x2, Pallas kernels, attend_rows(): pl.pallas_call(attention_kernel, out_shape=jax.ShapeDtypeStruct((rows, wi...  12.8 us
    dot_general x2, matrix products, expert_hidden(): jnp.einsum('rd,kdf->krf', rows, expert_in, preferred_element_type=jnp.flo...  7.62 us
    ppermute x4, waiting for transfers between devices, swap_exp(): return lax.ppermute(x, 'exp', [(i, (i + 1) % size) for i in range(size)])  5.59 us
    ppermute x1, starting transfers between devices, shifted(): return lax.ppermute(shard, axis, pairs)  4.87 us
  transfers between devices with their start and end apart: 5, of which 2 were waited for; matrix products, arithmetic and copies ran while one was open for 6% of the time, Pallas kernels for 4%

profile of v13, /device:TPU:0, one launch (start us, length us, event | category | flops | bytes accessed | tf_op | source)
XLA Modules:
  0.0 167.9 jit_solution(13177543076927739415)
XLA Ops:
  0.0 0.0 copy-start
  0.0 1.0 slice_bitcast_fusion.3
  1.0 4.9 %collective-permute-start = (bf16[2,128,128]{2,1,0:T(8,128)(2,1)S(1)}, bf16[2,128,128]{2,1,0:T(8,128)(2,1)S(1)}, u32[]{:S(2)}, u32[]{:S(2)}) collective-permute-start(bf16[2,128,128]{2,1,0:T(8,128)(2,1)S(1)} %pad_maximum_fusion), channel_id=1, source_target_pairs={{0,2},{2,4},{4,6},{6,8},{8,10},{10,12},{12,14},{1,3},{3,5},{5,7},{... | collective-permute-start | bytes 196616 | tf_op jit(solution)/shard_map/ppermute | solution.py:20
  5.9 0.0 copy-start.2
  5.9 6.4 %shard_map.118.rest_0_ = f32[256,1536]{1,0:T(8,128)} custom-call(f32[16]{0:T(128)} %sink_ref.3, bf16[256,1024]{1,0:T(8,128)(2,1)} %q_ref.3, bf16[256,128]{1,0:T(8,128)(2,1)} %k_ref.1, bf16[256,128]{1,0:T(8,128)(2,1)} %v_ref.1, bf16[1024,1536]{1,0:T(8,128)(2,1)} %w_ref.3), custom_call_target="tpu_custom_call" | custom-call | flops 671088640 | bytes 4325376 | tf_op jit(solution)/shard_map/pallas_call | solution.py:131
  12.3 0.0 collective-permute-done
  12.3 0.0 copy-done.2
  12.3 0.6 pad_maximum_fusion.2.v_ref
  13.0 0.6 pad_maximum_fusion.1.k_ref
  13.6 0.0 copy-start.3
  13.6 6.4 %shard_map.119 = f32[256,1536]{1,0:T(8,128)} custom-call(f32[16]{0:T(128)} %sink_ref.3, bf16[256,1024]{1,0:T(8,128)(2,1)} %q_ref.3, bf16[256,128]{1,0:T(8,128)(2,1)} %pad_maximum_fusion.1.k_ref, bf16[256,128]{1,0:T(8,128)(2,1)} %pad_maximum_fusion.2.v_ref, bf16[1024,1536]{1,0:T(8,128)(2,1)} %w_ref.3, ...), custom_call_target="tpu_custom_call", output_to_operand_aliasing={{}: (5, {})} | custom-call | flops 671088640 | bytes 4325376 | tf_op jit(solution)/shard_map/pallas_call | solution.py:131
  20.0 0.0 copy-start.1
  20.0 0.0 collective-permute-start.1
  20.0 0.0 copy-done.3
  20.0 0.1 copy.20
  20.1 0.1 eq.69
  20.2 0.1 eq.65
  20.4 2.3 %reduce-window.6 = s32[8,8,128]{2,1,0:T(8,128)S(1)} reduce-window(s32[8,8,128]{2,1,0:T(8,128)S(1)} %fusion.32, s32[]{:T(128)} %constant.13.clone.1), window={size=1x1x128 pad=0_0x0_0x127_0}, to_apply=%region_0.1 | reduce-window | flops 1040384 | bytes 65540 | tf_op jit(solution)/shard_map/reduce-window
  22.6 0.3 slice_reduce_fusion
  22.9 0.2 reduce-window.9
  23.1 0.1 add_bitcast_fusion
  23.2 0.1 sub.26
  23.4 0.1 copy.23
  23.5 0.1 copy.24
  23.6 0.4 fusion.22
  24.1 0.0 copy-start.4
  24.1 0.0 collective-permute-done.1
  24.1 0.0 copy-done.1
  24.1 0.0 slice-start
  24.1 2.4 %multiply_reduce_fusion.1 = (f32[256]{0:T(256)S(1)}, f32[256,1536]{1,0:T(8,128)S(1)}) fusion(f32[256,1536]{1,0:T(8,128)} %shard_map.119, f32[256,1536]{1,0:T(8,128)} %collective-permute-done.1, bf16[256,1536]{1,0:T(8,128)(2,1)S(1)} %copy-done.1), kind=kLoop, calls=%fused_computation.29 | loop fusion | flops 1965824 | bytes 5506048 | tf_op jit(solution)/shard_map/reduce_sum | solution.py:29
  26.5 0.0 copy-done.4
  26.5 0.0 slice-start.1
  26.5 0.9 convolution_convert_fusion.2
  27.4 59.1 %all_to_all.10 = bf16[8,96,1536]{2,1,0:T(8,128)(2,1)S(1)} all-to-all(bf16[8,96,1536]{2,1,0:T(8,128)(2,1)S(1)} %bitcast.67), channel_id=1, replica_groups=mesh['groups'=2,'seq'=8,'exp'=2] {'seq'}, dimensions={0} | all-to-all | bytes 4718592 | tf_op jit(solution)/shard_map/all_to_all | solution.py:208
  86.5 0.0 collective-permute-start.2
  86.5 0.0 slice-done
  86.5 0.0 slice-done.1
  86.6 3.8 %fusion.16 = f32[2,768,768]{2,1,0:T(8,128)S(1)} fusion(bf16[768,1536,1]{1,0,2:T(8,128)(2,1)S(1)} %bitcast.69, bf16[1,2,1536,768]{3,2,1,0:T(8,128)(2,1)S(1)} %bitcast.73), kind=kOutput, calls=%fused_computation.24 | convolution fusion | flops 3623878656 | bytes 11796480 | tf_op jit(solution)/shard_map/rd,kdf->krf/dot_general | solution.py:56
  90.4 0.7 fusion.27
  91.1 0.0 collective-permute-done.2
  91.1 3.8 %fusion.19 = f32[2,768,768]{2,1,0:T(8,128)S(1)} fusion(bf16[768,1536,1]{1,0,2:T(8,128)(2,1)S(1)} %bitcast.74, bf16[1,2,1536,768]{3,2,1,0:T(8,128)(2,1)S(1)} %bitcast.73), kind=kOutput, calls=%fused_computation.25 | convolution fusion | flops 3623878656 | bytes 11796480 | tf_op jit(solution)/shard_map/rd,kdf->krf/dot_general | solution.py:56
  94.9 0.0 copy-done
  94.9 2.1 %convolution_convert_fusion = bf16[768,1536]{1,0:T(8,128)(2,1)S(1)} fusion(bf16[1,768,1536]{2,1,0:T(8,128)(2,1)S(1)} %copy-done, f32[2,768,768]{2,1,0:T(8,128)S(1)} %fusion.19), kind=kOutput, calls=%fused_computation.7 | convolution fusion | flops 1817837568 | bytes 9437184 | tf_op jit(solution)/shard_map/dot_general | solution.py:214
  97.0 0.6 collective-permute-start.3
  97.5 2.0 %convolution_convert_fusion.1 = bf16[768,1536]{1,0:T(8,128)(2,1)S(1)} fusion(bf16[768,768]{1,0:T(8,128)(2,1)S(1)} %fusion.27, bf16[1,768,1536]{2,1,0:T(8,128)(2,1)S(1)} %copy-done), kind=kOutput, calls=%fused_computation.8 | convolution fusion | flops 1813118976 | bytes 5898240 | tf_op jit(solution)/shard_map/dot_general | solution.py:219
  99.5 2.2 %collective-permute-done.3 = bf16[8,96,1536]{2,1,0:T(8,128)(2,1)S(1)} collective-permute-done((bf16[8,96,1536]{2,1,0:T(8,128)(2,1)S(1)}, bf16[8,96,1536]{2,1,0:T(8,128)(2,1)S(1)}, u32[]{:S(2)}, u32[]{:S(2)}) %collective-permute-start.3) | collective-permute-done | bytes 2359328 | tf_op jit(solution)/shard_map/ppermute | solution.py:25
  101.7 0.7 fusion
  102.4 0.0 copy-start.5
  102.4 57.8 %all_to_all.11 = bf16[8,96,1536]{2,1,0:T(8,128)(2,1)S(1)} all-to-all(bf16[8,96,1536]{2,1,0:T(8,128)(2,1)S(1)} %fusion), channel_id=1, replica_groups=mesh['groups'=2,'seq'=8,'exp'=2] {'seq'}, dimensions={0} | all-to-all | bytes 4718592 | tf_op jit(solution)/shard_map/all_to_all | solution.py:224
  160.2 0.0 copy-done.5
  160.2 3.0 %multiply_reduce_fusion = f32[256,1536]{1,0:T(8,128)S(1)} fusion(bf16[768,1536,1]{1,0,2:T(8,128)(2,1)S(1)} %bitcast.70, f32[256,4]{0,1:T(4,128)S(1)} %copy-done.5, s32[256,4]{0,1:T(4,128)S(1)} %copy.24), kind=kOutput, calls=%fused_computation | convolution fusion | flops 2419458048 | bytes 3940352 | tf_op jit(solution)/shard_map/dot_general | solution.py:225
  163.2 0.1 collective-permute-start.4
  163.3 3.4 %collective-permute-done.4 = f32[256,1536]{1,0:T(8,128)S(1)} collective-permute-done((f32[256,1536]{1,0:T(8,128)S(1)}, f32[256,1536]{1,0:T(8,128)S(1)}, u32[]{:S(2)}, u32[]{:S(2)}) %collective-permute-start.4) | collective-permute-done | bytes 1572896 | tf_op jit(solution)/shard_map/ppermute | solution.py:25
  166.7 1.2 add_convert_fusion
  (10 shorter events, 0.1 us)
Async XLA Ops:
  0.0 94.9 %copy-start = (bf16[1,768,1536]{2,1,0:T(8,128)(2,1)S(1)}, bf16[1,768,1536]{2,1,0:T(8,128)(2,1)}, u32[]{:S(2)}) copy-start(bf16[1,768,1536]{2,1,0:T(8,128)(2,1)} %param.21) | copy-start | bytes 7077892
  1.0 11.3 %collective-permute-start = (bf16[2,128,128]{2,1,0:T(8,128)(2,1)S(1)}, bf16[2,128,128]{2,1,0:T(8,128)(2,1)S(1)}, u32[]{:S(2)}, u32[]{:S(2)}) collective-permute-start(bf16[2,128,128]{2,1,0:T(8,128)(2,1)S(1)} %pad_maximum_fusion), channel_id=1, source_target_pairs={{0,2},{2,4},{4,6},{6,8},{8,10},{10,12},{12,14},{1,3},{3,5},{5,7},{... | collective-permute-start | bytes 196616 | tf_op jit(solution)/shard_map/ppermute | solution.py:20
  5.9 6.4 %copy-start.2 = (bf16[2,128,128]{2,1,0:T(8,128)(2,1)S(1)}, bf16[2,128,128]{2,1,0:T(8,128)(2,1)}, u32[]{:S(2)}) copy-start(bf16[2,128,128]{2,1,0:T(8,128)(2,1)} %param.15) | copy-start | bytes 196612
  13.6 6.4 %copy-start.3 = (s32[256,4]{0,1:T(4,128)S(1)}, s32[256,4]{0,1:T(4,128)}, u32[]{:S(2)}) copy-start(s32[256,4]{0,1:T(4,128)} %param.22) | copy-start | bytes 12292
  20.0 4.1 %copy-start.1 = (bf16[256,1536]{1,0:T(8,128)(2,1)S(1)}, bf16[256,1536]{1,0:T(8,128)(2,1)}, u32[]{:S(2)}) copy-start(bf16[256,1536]{1,0:T(8,128)(2,1)} %param.18) | copy-start | bytes 2359300
  20.0 4.1 %collective-permute-start.1 = (f32[256,1536]{1,0:T(8,128)}, f32[256,1536]{1,0:T(8,128)}, u32[]{:S(2)}, u32[]{:S(2)}) collective-permute-start(f32[256,1536]{1,0:T(8,128)} %shard_map.119), channel_id=1, source_target_pairs={{0,1},{1,0},{2,3},{3,2},{4,5},{5,4},{6,7},{7,6},{8,9},{9,8},{10,11... | collective-permute-start | bytes 4718600 | tf_op jit(solution)/shard_map/ppermute | solution.py:25
  24.1 2.4 %copy-start.4 = (f32[1536]{0:T(1024)S(1)}, f32[1536]{0:T(1024)}, u32[]{:S(2)}) copy-start(f32[1536]{0:T(1024)} %param.19) | copy-start | bytes 18436
  24.1 62.5 %slice-start = ((s8[4718592]{0:T(1024)(128)(4,1)}), s8[4194304]{0:T(1024)(128)(4,1)S(1)}, s32[]{:S(2)}) async-start(s8[4718592]{0:T(1024)(128)(4,1)} %bitcast.72), calls=%async_computation.2 | async-start | bytes 8388608
  26.5 60.1 %slice-start.1 = ((s8[4718592]{0:T(1024)(128)(4,1)}), s8[524288]{0:T(1024)(128)(4,1)S(1)}, s32[]{:S(2)}) async-start(s8[4718592]{0:T(1024)(128)(4,1)} %bitcast.72), calls=%async_computation.3 | async-start | bytes 1048576
  86.5 4.5 %collective-permute-start.2 = (bf16[8,96,1536]{2,1,0:T(8,128)(2,1)S(1)}, bf16[8,96,1536]{2,1,0:T(8,128)(2,1)S(1)}, u32[]{:S(2)}, u32[]{:S(2)}) collective-permute-start(bf16[8,96,1536]{2,1,0:T(8,128)(2,1)S(1)} %all_to_all.10), channel_id=1, source_target_pairs={{0,1},{1,0},{2,3},{3,2},{4,5},{5,4},{6,7},{7,6},{8,9},{9,8},{10,11... | collective-permute-start | bytes 7077896 | tf_op jit(solution)/shard_map/ppermute | solution.py:25
  97.0 4.7 %collective-permute-start.3 = (bf16[8,96,1536]{2,1,0:T(8,128)(2,1)S(1)}, bf16[8,96,1536]{2,1,0:T(8,128)(2,1)S(1)}, u32[]{:S(2)}, u32[]{:S(2)}) collective-permute-start(bf16[8,96,1536]{2,1,0:T(8,128)(2,1)S(1)} %bitcast.75), channel_id=1, source_target_pairs={{0,1},{1,0},{2,3},{3,2},{4,5},{5,4},{6,7},{7,6},{8,9},{9,8},{10,11... | collective-permute-start | bytes 7077896 | tf_op jit(solution)/shard_map/ppermute | solution.py:25
  102.4 57.8 %copy-start.5 = (f32[256,4]{0,1:T(4,128)S(1)}, f32[256,4]{0,1:T(4,128)}, u32[]{:S(2)}) copy-start(f32[256,4]{0,1:T(4,128)} %param.23) | copy-start | bytes 12292
  163.2 3.5 %collective-permute-start.4 = (f32[256,1536]{1,0:T(8,128)S(1)}, f32[256,1536]{1,0:T(8,128)S(1)}, u32[]{:S(2)}, u32[]{:S(2)}) collective-permute-start(f32[256,1536]{1,0:T(8,128)S(1)} %multiply_reduce_fusion), channel_id=1, source_target_pairs={{0,1},{1,0},{2,3},{3,2},{4,5},{5,4},{6,7},{7,6},{8,9},{9,8},{10,11... | collective-permute-start | bytes 4718600 | tf_op jit(solution)/shard_map/ppermute | solution.py:25

commit v14 on v12

--- a/solution.py
+++ b/solution.py
@@ -8,6 +8,7 @@
 HEAD_DIM = 64
 WINDOW = 128
 TOP = 4
+SHIFT_LIMIT = 8
 
 
 GLU_ALPHA = 1.702
@@ -23,6 +24,19 @@
 def swap_exp(x):
     size = lax.axis_size("exp")
     return lax.ppermute(x, "exp", [(i, (i + 1) % size) for i in range(size)])
+
+
+def seq_all_to_all(blocks):
+    return lax.all_to_all(blocks, "seq", split_axis=0, concat_axis=0, tiled=True)
+
+
+def shift_exchange(blocks, sign):
+    size = lax.axis_size("seq")
+    out = [blocks[0]]
+    for step in range(1, size):
+        pairs = [(i, (i + sign * step) % size) for i in range(size)]
+        out.append(lax.ppermute(blocks[step], "seq", pairs))
+    return jnp.stack(out)
 
 
 def rms_normalize(mixed_rows, norm_gain):
@@ -169,7 +183,9 @@
     slot_rank = jnp.sum(expert_hits * (jnp.cumsum(expert_hits, axis=0) - 1), axis=1)
     local_rank = slot_rank - core * half
     mine = (local_rank >= 0) & (local_rank < half)
-    slot_id = jnp.where(mine, flat_experts * half + local_rank, -1)
+    by_shift = experts <= SHIFT_LIMIT
+    offset = (flat_experts - lax.axis_index("seq")) % experts if by_shift else flat_experts
+    slot_id = jnp.where(mine, offset * half + local_rank, -1)
     slot_iota = jnp.arange(slots, dtype=jnp.int32)
     pick = (slot_id[:, None] == slot_iota[None, :]).astype(jnp.bfloat16)
     select = jnp.max(pick.reshape(tok_rows, TOP, slots), axis=1).T
@@ -178,7 +194,7 @@
         .astype(jnp.bfloat16)
         .reshape(experts, half, width)
     )
-    slot_rows = lax.all_to_all(outgoing, "seq", split_axis=0, concat_axis=0, tiled=True)
+    slot_rows = shift_exchange(outgoing, 1) if by_shift else seq_all_to_all(outgoing)
     other_rows = swap_exp(slot_rows)
     own_hidden = expert_hidden(slot_rows.reshape(-1, width), expert_in[0])
     own_hidden, other_rows = lax.optimization_barrier((own_hidden, other_rows))
@@ -194,7 +210,7 @@
         .reshape(experts, half, width)
     )
     result = (own_part.astype(jnp.float32) + their_part.astype(jnp.float32)).astype(jnp.bfloat16)
-    returned = lax.all_to_all(result, "seq", split_axis=0, concat_axis=0, tiled=True)
+    returned = shift_exchange(result, -1) if by_shift else seq_all_to_all(result)
     picked = jnp.dot(pick, returned.reshape(slots, width), preferred_element_type=jnp.float32)
     weighted = jnp.sum(picked.reshape(tok_rows, TOP, width) * route_gates[:, :, None], axis=1)
     moe = weighted + swap_exp(weighted)

time: 168 us -> 162 us (0.964)
  blocking collectives: 118 us -> 0 us
  waiting for transfers between devices: 7.47 us -> 79.2 us
  starting transfers between devices: 5.5 us -> 44.9 us
    all_to_all x2 -> x0, blocking collectives: 118 us -> none  [the longest x1 60.1 us: on_device(): lax.all_to_all(outgoing, 'seq', split_axis=0, concat_axis=0, tiled=True)]
    ppermute x0 -> x14, waiting for transfers between devices: none -> 71.7 us  [shift_exchange(): out.append(lax.ppermute(blocks[step], 'seq', pairs))]
    ppermute x0 -> x14, starting transfers between devices: none -> 39.4 us  [shift_exchange(): out.append(lax.ppermute(blocks[step], 'seq', pairs))]
  transfers between devices with their start and end apart: 5 -> 19, of which waited for: 3 -> 11; matrix products, arithmetic and copies ran while one was open for 6% -> 7% of each run, Pallas kernels for 0% -> 0%
where the time goes in v14:
time: 162 us
  waiting for transfers between devices  79.2 us (49%)
  starting transfers between devices  44.9 us (28%)
  matrix products  15.6 us (10%)
  Pallas kernels  10 us (6%)
  other arithmetic  8.63 us (5%)
  local copies, waits for them, and re-layouts  3.14 us (2%)
    ppermute x14, waiting for transfers between devices, shift_exchange(): out.append(lax.ppermute(blocks[step], 'seq', pairs))  71.7 us
    ppermute x14, starting transfers between devices, shift_exchange(): out.append(lax.ppermute(blocks[step], 'seq', pairs))  39.4 us
    pallas_call x1, Pallas kernels, attend_kernel(): pl.pallas_call(attention_kernel, out_shape=jax.ShapeDtypeStruct((rows, wi...  10 us
    dot_general x2, matrix products, expert_hidden(): jnp.einsum('rd,kdf->krf', rows, expert_in, preferred_element_type=jnp.flo...  7.62 us
    ppermute x4, waiting for transfers between devices, swap_exp(): return lax.ppermute(x, 'exp', [(i, (i + 1) % size) for i in range(size)])  5.57 us
    ppermute x1, starting transfers between devices, shifted(): return lax.ppermute(shard, axis, pairs)  4.87 us
  transfers between devices with their start and end apart: 19, of which 11 were waited for; matrix products, arithmetic and copies ran while one was open for 7% of the time, Pallas kernels for 0%

profile of v14, /device:TPU:0, one launch (start us, length us, event | category | flops | bytes accessed | tf_op | source)
XLA Modules:
  0.0 161.9 jit_solution(17750914401055719954)
XLA Ops:
  0.0 0.9 slice_bitcast_fusion.10
  0.9 4.9 %collective-permute-start = (bf16[2,128,128]{2,1,0:T(8,128)(2,1)S(1)}, bf16[2,128,128]{2,1,0:T(8,128)(2,1)S(1)}, u32[]{:S(2)}, u32[]{:S(2)}) collective-permute-start(bf16[2,128,128]{2,1,0:T(8,128)(2,1)S(1)} %pad_maximum_fusion), channel_id=1, source_target_pairs={{0,2},{2,4},{4,6},{6,8},{8,10},{10,12},{12,14},{1,3},{3,5},{5,7},{... | collective-permute-start | bytes 196616 | tf_op jit(solution)/shard_map/ppermute | solution.py:21
  5.8 1.9 %collective-permute-done = bf16[2,128,128]{2,1,0:T(8,128)(2,1)S(1)} collective-permute-done((bf16[2,128,128]{2,1,0:T(8,128)(2,1)S(1)}, bf16[2,128,128]{2,1,0:T(8,128)(2,1)S(1)}, u32[]{:S(2)}, u32[]{:S(2)}) %collective-permute-start) | collective-permute-done | bytes 65568 | tf_op jit(solution)/shard_map/ppermute | solution.py:21
  7.7 0.8 broadcast_select_fusion
  8.6 0.6 slice_bitcast_fusion.8
  9.2 10.0 %shard_map.118 = f32[256,1536]{1,0:T(8,128)} custom-call(f32[16]{0:T(128)} %sink_ref.1, bf16[256,1024]{1,0:T(8,128)(2,1)} %q_ref.1, bf16[128,128]{1,0:T(8,128)(2,1)} %get-tuple-element.27.pk_ref, bf16[256,128]{1,0:T(8,128)(2,1)} %k_ref.1, bf16[128,128]{1,0:T(8,128)(2,1)} %get-tuple-element.26.pv_ref, bf16[256,128]{1,0:T(8,128)(2,1)} %v_ref.1, ...), custom_call_target="tpu_custom_call" | custom-call | flops 1342177280 | bytes 5439488 | tf_op jit(solution)/shard_map/pallas_call | solution.py:140
  19.2 0.0 collective-permute-start.1
  19.2 0.1 copy.33
  19.4 0.1 eq.71
  19.5 0.1 eq.67
  19.6 2.3 %reduce-window.6 = s32[8,8,128]{2,1,0:T(8,128)S(1)} reduce-window(s32[8,8,128]{2,1,0:T(8,128)S(1)} %fusion.33, s32[]{:T(128)} %constant.19.clone.1), window={size=1x1x128 pad=0_0x0_0x127_0}, to_apply=%region_0.1 | reduce-window | flops 1040384 | bytes 65540 | tf_op jit(solution)/shard_map/reduce-window
  21.9 0.3 slice_reduce_fusion
  22.2 0.2 reduce-window.9
  22.3 0.1 add_bitcast_fusion
  22.5 0.1 sub.36
  22.6 0.1 copy.35
  22.7 0.4 fusion.22
  23.2 0.0 copy-start.3
  23.2 0.0 collective-permute-done.1
  23.2 2.2 %multiply_reduce_fusion.1 = (f32[256]{0:T(256)S(1)}, f32[256,1536]{1,0:T(8,128)S(1)}) fusion(f32[256,1536]{1,0:T(8,128)} %shard_map.118, f32[256,1536]{1,0:T(8,128)} %collective-permute-done.1, bf16[256,1536]{1,0:T(8,128)(2,1)S(1)} %copy-done.1), kind=kLoop, calls=%fused_computation.29 | loop fusion | flops 1965824 | bytes 5506048 | tf_op jit(solution)/shard_map/reduce_sum | solution.py:43
  25.4 0.0 slice-start
  25.4 0.9 convolution_convert_fusion.2
  26.3 0.0 slice-start.1
  26.3 0.1 fusion.40
  26.5 1.6 collective-permute-start.2
  28.1 1.6 collective-permute-start.3
  29.7 3.4 %collective-permute-start.4 = (bf16[96,1536]{1,0:T(8,128)(2,1)S(1)}, bf16[96,1536]{1,0:T(8,128)(2,1)S(1)}, u32[]{:S(2)}, u32[]{:S(2)}) collective-permute-start(bf16[96,1536]{1,0:T(8,128)(2,1)S(1)} %get-tuple-element.23), channel_id=1, source_target_pairs={{0,6},{2,8},{4,10},{6,12},{8,14},{10,0},{12,2},{14,4},{1,7},{3,9},... | collective-permute-start | bytes 884744 | tf_op jit(solution)/shard_map/ppermute | solution.py:38
  33.1 1.2 collective-permute-start.5
  34.3 1.8 %collective-permute-start.6 = (bf16[96,1536]{1,0:T(8,128)(2,1)S(1)}, bf16[96,1536]{1,0:T(8,128)(2,1)S(1)}, u32[]{:S(2)}, u32[]{:S(2)}) collective-permute-start(bf16[96,1536]{1,0:T(8,128)(2,1)S(1)} %get-tuple-element.21), channel_id=1, source_target_pairs={{0,10},{2,12},{4,14},{6,0},{8,2},{10,4},{12,6},{14,8},{1,11},{3,13... | collective-permute-start | bytes 884744 | tf_op jit(solution)/shard_map/ppermute | solution.py:38
  36.1 3.2 %collective-permute-done.2 = bf16[96,1536]{1,0:T(8,128)(2,1)S(1)} collective-permute-done((bf16[96,1536]{1,0:T(8,128)(2,1)S(1)}, bf16[96,1536]{1,0:T(8,128)(2,1)S(1)}, u32[]{:S(2)}, u32[]{:S(2)}) %collective-permute-start.2) | collective-permute-done | bytes 294944 | tf_op jit(solution)/shard_map/ppermute | solution.py:38
  39.3 2.4 %collective-permute-start.7 = (bf16[96,1536]{1,0:T(8,128)(2,1)S(1)}, bf16[96,1536]{1,0:T(8,128)(2,1)S(1)}, u32[]{:S(2)}, u32[]{:S(2)}) collective-permute-start(bf16[96,1536]{1,0:T(8,128)(2,1)S(1)} %get-tuple-element.20), channel_id=1, source_target_pairs={{0,12},{2,14},{4,0},{6,2},{8,4},{10,6},{12,8},{14,10},{1,13},{3,15... | collective-permute-start | bytes 884744 | tf_op jit(solution)/shard_map/ppermute | solution.py:38
  41.8 0.0 collective-permute-done.3
  41.8 6.0 %collective-permute-start.8 = (bf16[96,1536]{1,0:T(8,128)(2,1)S(1)}, bf16[96,1536]{1,0:T(8,128)(2,1)S(1)}, u32[]{:S(2)}, u32[]{:S(2)}) collective-permute-start(bf16[96,1536]{1,0:T(8,128)(2,1)S(1)} %get-tuple-element.19), channel_id=1, source_target_pairs={{0,14},{2,0},{4,2},{6,4},{8,6},{10,8},{12,10},{14,12},{1,15},{3,1}... | collective-permute-start | bytes 884744 | tf_op jit(solution)/shard_map/ppermute | solution.py:38
  47.8 16.4 %collective-permute-done.4 = bf16[96,1536]{1,0:T(8,128)(2,1)S(1)} collective-permute-done((bf16[96,1536]{1,0:T(8,128)(2,1)S(1)}, bf16[96,1536]{1,0:T(8,128)(2,1)S(1)}, u32[]{:S(2)}, u32[]{:S(2)}) %collective-permute-start.4) | collective-permute-done | bytes 294944 | tf_op jit(solution)/shard_map/ppermute | solution.py:38
  64.2 0.3 collective-permute-done.5
  64.5 0.0 collective-permute-done.6
  64.6 0.0 collective-permute-done.7
  64.6 3.3 %collective-permute-done.8 = bf16[96,1536]{1,0:T(8,128)(2,1)S(1)} collective-permute-done((bf16[96,1536]{1,0:T(8,128)(2,1)S(1)}, bf16[96,1536]{1,0:T(8,128)(2,1)S(1)}, u32[]{:S(2)}, u32[]{:S(2)}) %collective-permute-start.8) | collective-permute-done | bytes 294944 | tf_op jit(solution)/shard_map/ppermute | solution.py:38
  68.0 0.1 collective-permute-start.9
  68.1 3.8 %fusion.16 = f32[2,768,768]{2,1,0:T(8,128)S(1)} fusion(bf16[768,1536,1]{1,0,2:T(8,128)(2,1)S(1)} %bitcast.114, bf16[1,2,1536,768]{3,2,1,0:T(8,128)(2,1)S(1)} %bitcast.117), kind=kOutput, calls=%fused_computation.24 | convolution fusion | flops 3623878656 | bytes 11796480 | tf_op jit(solution)/shard_map/rd,kdf->krf/dot_general | solution.py:70
  71.9 0.7 fusion.27
  72.6 0.0 collective-permute-done.9
  72.6 3.8 %fusion.19 = f32[2,768,768]{2,1,0:T(8,128)S(1)} fusion(bf16[768,1536,1]{1,0,2:T(8,128)(2,1)S(1)} %bitcast.118, bf16[1,2,1536,768]{3,2,1,0:T(8,128)(2,1)S(1)} %bitcast.117), kind=kOutput, calls=%fused_computation.25 | convolution fusion | flops 3623878656 | bytes 11796480 | tf_op jit(solution)/shard_map/rd,kdf->krf/dot_general | solution.py:70
  76.4 2.1 %convolution_convert_fusion = bf16[768,1536]{1,0:T(8,128)(2,1)S(1)} fusion(bf16[1,768,1536]{2,1,0:T(8,128)(2,1)S(1)} %copy-done, f32[2,768,768]{2,1,0:T(8,128)S(1)} %fusion.19), kind=kOutput, calls=%fused_computation.7 | convolution fusion | flops 1817837568 | bytes 9437184 | tf_op jit(solution)/shard_map/dot_general | solution.py:203
  78.5 0.5 collective-permute-start.10
  79.0 2.0 %convolution_convert_fusion.1 = bf16[768,1536]{1,0:T(8,128)(2,1)S(1)} fusion(bf16[768,768]{1,0:T(8,128)(2,1)S(1)} %fusion.27, bf16[1,768,1536]{2,1,0:T(8,128)(2,1)S(1)} %copy-done), kind=kOutput, calls=%fused_computation.8 | convolution fusion | flops 1813118976 | bytes 5898240 | tf_op jit(solution)/shard_map/dot_general | solution.py:208
  81.0 2.2 %collective-permute-done.10 = bf16[8,96,1536]{2,1,0:T(8,128)(2,1)S(1)} collective-permute-done((bf16[8,96,1536]{2,1,0:T(8,128)(2,1)S(1)}, bf16[8,96,1536]{2,1,0:T(8,128)(2,1)S(1)}, u32[]{:S(2)}, u32[]{:S(2)}) %collective-permute-start.10) | collective-permute-done | bytes 2359328 | tf_op jit(solution)/shard_map/ppermute | solution.py:26
  83.2 0.7 fusion
  83.9 0.2 slice_bitcast_fusion
  84.1 0.0 copy-start.4
  84.1 18.0 %collective-permute-start.11 = (bf16[96,1536]{1,0:T(8,128)(2,1)S(1)}, bf16[96,1536]{1,0:T(8,128)(2,1)S(1)}, u32[]{:S(2)}, u32[]{:S(2)}) collective-permute-start(bf16[96,1536]{1,0:T(8,128)(2,1)S(1)} %get-tuple-element.17), channel_id=1, source_target_pairs={{0,14},{2,0},{4,2},{6,4},{8,6},{10,8},{12,10},{14,12},{1,15},{3,1}... | collective-permute-start | bytes 884744 | tf_op jit(solution)/shard_map/ppermute | solution.py:38
  102.2 0.0 collective-permute-start.12
  102.2 0.4 collective-permute-start.13
  102.6 2.5 %collective-permute-start.14 = (bf16[96,1536]{1,0:T(8,128)(2,1)S(1)}, bf16[96,1536]{1,0:T(8,128)(2,1)S(1)}, u32[]{:S(2)}, u32[]{:S(2)}) collective-permute-start(bf16[96,1536]{1,0:T(8,128)(2,1)S(1)} %get-tuple-element.14), channel_id=1, source_target_pairs={{0,8},{2,10},{4,12},{6,14},{8,0},{10,2},{12,4},{14,6},{1,9},{3,11}... | collective-permute-start | bytes 884744 | tf_op jit(solution)/shard_map/ppermute | solution.py:38
  105.1 0.3 collective-permute-start.15
  105.5 4.1 %collective-permute-done.11 = bf16[96,1536]{1,0:T(8,128)(2,1)S(1)} collective-permute-done((bf16[96,1536]{1,0:T(8,128)(2,1)S(1)}, bf16[96,1536]{1,0:T(8,128)(2,1)S(1)}, u32[]{:S(2)}, u32[]{:S(2)}) %collective-permute-start.11) | collective-permute-done | bytes 294944 | tf_op jit(solution)/shard_map/ppermute | solution.py:38
  109.6 6.3 %collective-permute-done.12 = bf16[96,1536]{1,0:T(8,128)(2,1)S(1)} collective-permute-done((bf16[96,1536]{1,0:T(8,128)(2,1)S(1)}, bf16[96,1536]{1,0:T(8,128)(2,1)S(1)}, u32[]{:S(2)}, u32[]{:S(2)}) %collective-permute-start.12) | collective-permute-done | bytes 294944 | tf_op jit(solution)/shard_map/ppermute | solution.py:38
  115.9 6.3 %collective-permute-done.13 = bf16[96,1536]{1,0:T(8,128)(2,1)S(1)} collective-permute-done((bf16[96,1536]{1,0:T(8,128)(2,1)S(1)}, bf16[96,1536]{1,0:T(8,128)(2,1)S(1)}, u32[]{:S(2)}, u32[]{:S(2)}) %collective-permute-start.13) | collective-permute-done | bytes 294944 | tf_op jit(solution)/shard_map/ppermute | solution.py:38
  122.2 31.8 %collective-permute-done.14 = bf16[96,1536]{1,0:T(8,128)(2,1)S(1)} collective-permute-done((bf16[96,1536]{1,0:T(8,128)(2,1)S(1)}, bf16[96,1536]{1,0:T(8,128)(2,1)S(1)}, u32[]{:S(2)}, u32[]{:S(2)}) %collective-permute-start.14) | collective-permute-done | bytes 294944 | tf_op jit(solution)/shard_map/ppermute | solution.py:38
  154.0 0.0 collective-permute-done.15
  154.2 3.0 %multiply_reduce_fusion = f32[256,1536]{1,0:T(8,128)S(1)} fusion(bf16[768,1536,1]{1,0,2:T(8,128)(2,1)S(1)} %bitcast.113, f32[256,4]{0,1:T(4,128)S(1)} %copy-done.4, s32[256,4]{0,1:T(4,128)S(1)} %fusion.37), kind=kOutput, calls=%fused_computation | convolution fusion | flops 2419458048 | bytes 3940352 | tf_op jit(solution)/shard_map/dot_general | solution.py:214
  157.2 0.1 collective-permute-start.18
  157.3 3.4 %collective-permute-done.18 = f32[256,1536]{1,0:T(8,128)S(1)} collective-permute-done((f32[256,1536]{1,0:T(8,128)S(1)}, f32[256,1536]{1,0:T(8,128)S(1)}, u32[]{:S(2)}, u32[]{:S(2)}) %collective-permute-start.18) | collective-permute-done | bytes 1572896 | tf_op jit(solution)/shard_map/ppermute | solution.py:26
  160.7 1.2 add_convert_fusion
  (36 shorter events, 0.4 us)
Async XLA Ops:
  0.0 76.4 %copy-start = (bf16[1,768,1536]{2,1,0:T(8,128)(2,1)S(1)}, bf16[1,768,1536]{2,1,0:T(8,128)(2,1)}, u32[]{:S(2)}) copy-start(bf16[1,768,1536]{2,1,0:T(8,128)(2,1)} %param.21) | copy-start | bytes 7077892
  0.9 6.8 %collective-permute-start = (bf16[2,128,128]{2,1,0:T(8,128)(2,1)S(1)}, bf16[2,128,128]{2,1,0:T(8,128)(2,1)S(1)}, u32[]{:S(2)}, u32[]{:S(2)}) collective-permute-start(bf16[2,128,128]{2,1,0:T(8,128)(2,1)S(1)} %pad_maximum_fusion), channel_id=1, source_target_pairs={{0,2},{2,4},{4,6},{6,8},{8,10},{10,12},{12,14},{1,3},{3,5},{5,7},{... | collective-permute-start | bytes 196616 | tf_op jit(solution)/shard_map/ppermute | solution.py:21
  9.2 10.0 %copy-start.2 = (s32[256,4]{0,1:T(4,128)S(1)}, s32[256,4]{0,1:T(4,128)}, u32[]{:S(2)}) copy-start(s32[256,4]{0,1:T(4,128)} %param.22) | copy-start | bytes 12292
  9.2 14.0 %copy-start.1 = (bf16[256,1536]{1,0:T(8,128)(2,1)S(1)}, bf16[256,1536]{1,0:T(8,128)(2,1)}, u32[]{:S(2)}) copy-start(bf16[256,1536]{1,0:T(8,128)(2,1)} %param.18) | copy-start | bytes 2359300
  19.2 3.9 %collective-permute-start.1 = (f32[256,1536]{1,0:T(8,128)}, f32[256,1536]{1,0:T(8,128)}, u32[]{:S(2)}, u32[]{:S(2)}) collective-permute-start(f32[256,1536]{1,0:T(8,128)} %shard_map.118), channel_id=1, source_target_pairs={{0,1},{1,0},{2,3},{3,2},{4,5},{5,4},{6,7},{7,6},{8,9},{9,8},{10,11... | collective-permute-start | bytes 4718600 | tf_op jit(solution)/shard_map/ppermute | solution.py:26
  23.2 2.3 %copy-start.3 = (f32[1536]{0:T(1024)S(1)}, f32[1536]{0:T(1024)}, u32[]{:S(2)}) copy-start(f32[1536]{0:T(1024)} %param.19) | copy-start | bytes 18436
  25.4 42.6 %slice-start = ((s8[4718592]{0:T(1024)(128)(4,1)}), s8[4194304]{0:T(1024)(128)(4,1)S(1)}, s32[]{:S(2)}) async-start(s8[4718592]{0:T(1024)(128)(4,1)} %bitcast.116), calls=%async_computation | async-start | bytes 8388608
  26.3 41.7 %slice-start.1 = ((s8[4718592]{0:T(1024)(128)(4,1)}), s8[524288]{0:T(1024)(128)(4,1)S(1)}, s32[]{:S(2)}) async-start(s8[4718592]{0:T(1024)(128)(4,1)} %bitcast.116), calls=%async_computation.1 | async-start | bytes 1048576
  26.5 12.8 %collective-permute-start.2 = (bf16[96,1536]{1,0:T(8,128)(2,1)S(1)}, bf16[96,1536]{1,0:T(8,128)(2,1)S(1)}, u32[]{:S(2)}, u32[]{:S(2)}) collective-permute-start(bf16[96,1536]{1,0:T(8,128)(2,1)S(1)} %get-tuple-element.25), channel_id=1, source_target_pairs={{0,2},{2,4},{4,6},{6,8},{8,10},{10,12},{12,14},{14,0},{1,3},{3,5},... | collective-permute-start | bytes 884744 | tf_op jit(solution)/shard_map/ppermute | solution.py:38
  28.1 13.7 %collective-permute-start.3 = (bf16[96,1536]{1,0:T(8,128)(2,1)S(1)}, bf16[96,1536]{1,0:T(8,128)(2,1)S(1)}, u32[]{:S(2)}, u32[]{:S(2)}) collective-permute-start(bf16[96,1536]{1,0:T(8,128)(2,1)S(1)} %get-tuple-element.24), channel_id=1, source_target_pairs={{0,4},{2,6},{4,8},{6,10},{8,12},{10,14},{12,0},{14,2},{1,5},{3,7},... | collective-permute-start | bytes 884744 | tf_op jit(solution)/shard_map/ppermute | solution.py:38
  29.7 34.6 %collective-permute-start.4 = (bf16[96,1536]{1,0:T(8,128)(2,1)S(1)}, bf16[96,1536]{1,0:T(8,128)(2,1)S(1)}, u32[]{:S(2)}, u32[]{:S(2)}) collective-permute-start(bf16[96,1536]{1,0:T(8,128)(2,1)S(1)} %get-tuple-element.23), channel_id=1, source_target_pairs={{0,6},{2,8},{4,10},{6,12},{8,14},{10,0},{12,2},{14,4},{1,7},{3,9},... | collective-permute-start | bytes 884744 | tf_op jit(solution)/shard_map/ppermute | solution.py:38
  33.1 31.4 %collective-permute-start.5 = (bf16[96,1536]{1,0:T(8,128)(2,1)S(1)}, bf16[96,1536]{1,0:T(8,128)(2,1)S(1)}, u32[]{:S(2)}, u32[]{:S(2)}) collective-permute-start(bf16[96,1536]{1,0:T(8,128)(2,1)S(1)} %get-tuple-element.22), channel_id=1, source_target_pairs={{0,8},{2,10},{4,12},{6,14},{8,0},{10,2},{12,4},{14,6},{1,9},{3,11}... | collective-permute-start | bytes 884744 | tf_op jit(solution)/shard_map/ppermute | solution.py:38
  34.3 30.2 %collective-permute-start.6 = (bf16[96,1536]{1,0:T(8,128)(2,1)S(1)}, bf16[96,1536]{1,0:T(8,128)(2,1)S(1)}, u32[]{:S(2)}, u32[]{:S(2)}) collective-permute-start(bf16[96,1536]{1,0:T(8,128)(2,1)S(1)} %get-tuple-element.21), channel_id=1, source_target_pairs={{0,10},{2,12},{4,14},{6,0},{8,2},{10,4},{12,6},{14,8},{1,11},{3,13... | collective-permute-start | bytes 884744 | tf_op jit(solution)/shard_map/ppermute | solution.py:38
  39.3 25.2 %collective-permute-start.7 = (bf16[96,1536]{1,0:T(8,128)(2,1)S(1)}, bf16[96,1536]{1,0:T(8,128)(2,1)S(1)}, u32[]{:S(2)}, u32[]{:S(2)}) collective-permute-start(bf16[96,1536]{1,0:T(8,128)(2,1)S(1)} %get-tuple-element.20), channel_id=1, source_target_pairs={{0,12},{2,14},{4,0},{6,2},{8,4},{10,6},{12,8},{14,10},{1,13},{3,15... | collective-permute-start | bytes 884744 | tf_op jit(solution)/shard_map/ppermute | solution.py:38
  41.8 26.2 %collective-permute-start.8 = (bf16[96,1536]{1,0:T(8,128)(2,1)S(1)}, bf16[96,1536]{1,0:T(8,128)(2,1)S(1)}, u32[]{:S(2)}, u32[]{:S(2)}) collective-permute-start(bf16[96,1536]{1,0:T(8,128)(2,1)S(1)} %get-tuple-element.19), channel_id=1, source_target_pairs={{0,14},{2,0},{4,2},{6,4},{8,6},{10,8},{12,10},{14,12},{1,15},{3,1}... | collective-permute-start | bytes 884744 | tf_op jit(solution)/shard_map/ppermute | solution.py:38
  68.0 4.6 %collective-permute-start.9 = (bf16[8,96,1536]{2,1,0:T(8,128)(2,1)S(1)}, bf16[8,96,1536]{2,1,0:T(8,128)(2,1)S(1)}, u32[]{:S(2)}, u32[]{:S(2)}) collective-permute-start(bf16[8,96,1536]{2,1,0:T(8,128)(2,1)S(1)} %bitcast_dynamic-update-slice_fusion.7), channel_id=1, source_target_pairs={{0,1},{1,0},{2,3},{3,2},{4,5},{5,4},{6,7},{7,6},{8,9},{9,8},{10,11... | collective-permute-start | bytes 7077896 | tf_op jit(solution)/shard_map/ppermute | solution.py:26
  78.5 4.7 %collective-permute-start.10 = (bf16[8,96,1536]{2,1,0:T(8,128)(2,1)S(1)}, bf16[8,96,1536]{2,1,0:T(8,128)(2,1)S(1)}, u32[]{:S(2)}, u32[]{:S(2)}) collective-permute-start(bf16[8,96,1536]{2,1,0:T(8,128)(2,1)S(1)} %bitcast.119), channel_id=1, source_target_pairs={{0,1},{1,0},{2,3},{3,2},{4,5},{5,4},{6,7},{7,6},{8,9},{9,8},{10,11... | collective-permute-start | bytes 7077896 | tf_op jit(solution)/shard_map/ppermute | solution.py:26
  84.1 70.1 %copy-start.4 = (f32[256,4]{0,1:T(4,128)S(1)}, f32[256,4]{0,1:T(4,128)}, u32[]{:S(2)}) copy-start(f32[256,4]{0,1:T(4,128)} %param.23) | copy-start | bytes 12292
  84.1 25.5 %collective-permute-start.11 = (bf16[96,1536]{1,0:T(8,128)(2,1)S(1)}, bf16[96,1536]{1,0:T(8,128)(2,1)S(1)}, u32[]{:S(2)}, u32[]{:S(2)}) collective-permute-start(bf16[96,1536]{1,0:T(8,128)(2,1)S(1)} %get-tuple-element.17), channel_id=1, source_target_pairs={{0,14},{2,0},{4,2},{6,4},{8,6},{10,8},{12,10},{14,12},{1,15},{3,1}... | collective-permute-start | bytes 884744 | tf_op jit(solution)/shard_map/ppermute | solution.py:38
  102.2 13.8 %collective-permute-start.12 = (bf16[96,1536]{1,0:T(8,128)(2,1)S(1)}, bf16[96,1536]{1,0:T(8,128)(2,1)S(1)}, u32[]{:S(2)}, u32[]{:S(2)}) collective-permute-start(bf16[96,1536]{1,0:T(8,128)(2,1)S(1)} %get-tuple-element.16), channel_id=1, source_target_pairs={{0,12},{2,14},{4,0},{6,2},{8,4},{10,6},{12,8},{14,10},{1,13},{3,15... | collective-permute-start | bytes 884744 | tf_op jit(solution)/shard_map/ppermute | solution.py:38
  102.2 20.1 %collective-permute-start.13 = (bf16[96,1536]{1,0:T(8,128)(2,1)S(1)}, bf16[96,1536]{1,0:T(8,128)(2,1)S(1)}, u32[]{:S(2)}, u32[]{:S(2)}) collective-permute-start(bf16[96,1536]{1,0:T(8,128)(2,1)S(1)} %get-tuple-element.15), channel_id=1, source_target_pairs={{0,10},{2,12},{4,14},{6,0},{8,2},{10,4},{12,6},{14,8},{1,11},{3,13... | collective-permute-start | bytes 884744 | tf_op jit(solution)/shard_map/ppermute | solution.py:38
  102.6 51.4 %collective-permute-start.14 = (bf16[96,1536]{1,0:T(8,128)(2,1)S(1)}, bf16[96,1536]{1,0:T(8,128)(2,1)S(1)}, u32[]{:S(2)}, u32[]{:S(2)}) collective-permute-start(bf16[96,1536]{1,0:T(8,128)(2,1)S(1)} %get-tuple-element.14), channel_id=1, source_target_pairs={{0,8},{2,10},{4,12},{6,14},{8,0},{10,2},{12,4},{14,6},{1,9},{3,11}... | collective-permute-start | bytes 884744 | tf_op jit(solution)/shard_map/ppermute | solution.py:38
  105.1 48.9 %collective-permute-start.15 = (bf16[96,1536]{1,0:T(8,128)(2,1)S(1)}, bf16[96,1536]{1,0:T(8,128)(2,1)S(1)}, u32[]{:S(2)}, u32[]{:S(2)}) collective-permute-start(bf16[96,1536]{1,0:T(8,128)(2,1)S(1)} %get-tuple-element.13), channel_id=1, source_target_pairs={{0,6},{2,8},{4,10},{6,12},{8,14},{10,0},{12,2},{14,4},{1,7},{3,9},... | collective-permute-start | bytes 884744 | tf_op jit(solution)/shard_map/ppermute | solution.py:38
  109.6 44.5 %collective-permute-start.16 = (bf16[96,1536]{1,0:T(8,128)(2,1)S(1)}, bf16[96,1536]{1,0:T(8,128)(2,1)S(1)}, u32[]{:S(2)}, u32[]{:S(2)}) collective-permute-start(bf16[96,1536]{1,0:T(8,128)(2,1)S(1)} %get-tuple-element.12), channel_id=1, source_target_pairs={{0,4},{2,6},{4,8},{6,10},{8,12},{10,14},{12,0},{14,2},{1,5},{3,7},... | collective-permute-start | bytes 884744 | tf_op jit(solution)/shard_map/ppermute | solution.py:38
  115.9 38.2 %collective-permute-start.17 = (bf16[96,1536]{1,0:T(8,128)(2,1)S(1)}, bf16[96,1536]{1,0:T(8,128)(2,1)S(1)}, u32[]{:S(2)}, u32[]{:S(2)}) collective-permute-start(bf16[96,1536]{1,0:T(8,128)(2,1)S(1)} %get-tuple-element.11), channel_id=1, source_target_pairs={{0,2},{2,4},{4,6},{6,8},{8,10},{10,12},{12,14},{14,0},{1,3},{3,5},... | collective-permute-start | bytes 884744 | tf_op jit(solution)/shard_map/ppermute | solution.py:38
  157.2 3.5 %collective-permute-start.18 = (f32[256,1536]{1,0:T(8,128)S(1)}, f32[256,1536]{1,0:T(8,128)S(1)}, u32[]{:S(2)}, u32[]{:S(2)}) collective-permute-start(f32[256,1536]{1,0:T(8,128)S(1)} %multiply_reduce_fusion), channel_id=1, source_target_pairs={{0,1},{1,0},{2,3},{3,2},{4,5},{5,4},{6,7},{7,6},{8,9},{9,8},{10,11... | collective-permute-start | bytes 4718600 | tf_op jit(solution)/shard_map/ppermute | solution.py:26

commit v15 on v14

--- a/solution.py
+++ b/solution.py
@@ -32,11 +32,12 @@
 
 def shift_exchange(blocks, sign):
     size = lax.axis_size("seq")
-    out = [blocks[0]]
-    for step in range(1, size):
+    out = {0: blocks[0]}
+    steps = range(1, size) if sign > 0 else range(size - 1, 0, -1)
+    for step in steps:
         pairs = [(i, (i + sign * step) % size) for i in range(size)]
-        out.append(lax.ppermute(blocks[step], "seq", pairs))
-    return jnp.stack(out)
+        out[step] = lax.ppermute(blocks[step], "seq", pairs)
+    return jnp.stack([out[step] for step in range(size)])
 
 
 def rms_normalize(mixed_rows, norm_gain):

time: 162 us -> 162 us (level)
  no operation moved by 1% of the time
where the time goes in v15:
time: 162 us
  waiting for transfers between devices  79.2 us (49%)
  starting transfers between devices  44.9 us (28%)
  matrix products  15.6 us (10%)
  Pallas kernels  10 us (6%)
  other arithmetic  8.63 us (5%)
  local copies, waits for them, and re-layouts  3.14 us (2%)
    ppermute x14, waiting for transfers between devices, shift_exchange(): out[step] = lax.ppermute(blocks[step], 'seq', pairs)  71.7 us
    ppermute x14, starting transfers between devices, shift_exchange(): out[step] = lax.ppermute(blocks[step], 'seq', pairs)  39.4 us
    pallas_call x1, Pallas kernels, attend_kernel(): pl.pallas_call(attention_kernel, out_shape=jax.ShapeDtypeStruct((rows, wi...  10 us
    dot_general x2, matrix products, expert_hidden(): jnp.einsum('rd,kdf->krf', rows, expert_in, preferred_element_type=jnp.flo...  7.62 us
    ppermute x4, waiting for transfers between devices, swap_exp(): return lax.ppermute(x, 'exp', [(i, (i + 1) % size) for i in range(size)])  5.57 us
    ppermute x1, starting transfers between devices, shifted(): return lax.ppermute(shard, axis, pairs)  4.87 us
  transfers between devices with their start and end apart: 19, of which 11 were waited for; matrix products, arithmetic and copies ran while one was open for 7% of the time, Pallas kernels for 0%

profile of v15, /device:TPU:0, one launch (start us, length us, event | category | flops | bytes accessed | tf_op | source)
XLA Modules:
  0.0 161.9 jit_solution(17750914401055719954)
XLA Ops:
  0.0 0.9 slice_bitcast_fusion.10
  0.9 4.9 %collective-permute-start = (bf16[2,128,128]{2,1,0:T(8,128)(2,1)S(1)}, bf16[2,128,128]{2,1,0:T(8,128)(2,1)S(1)}, u32[]{:S(2)}, u32[]{:S(2)}) collective-permute-start(bf16[2,128,128]{2,1,0:T(8,128)(2,1)S(1)} %pad_maximum_fusion), channel_id=1, source_target_pairs={{0,2},{2,4},{4,6},{6,8},{8,10},{10,12},{12,14},{1,3},{3,5},{5,7},{... | collective-permute-start | bytes 196616 | tf_op jit(solution)/shard_map/ppermute | solution.py:21
  5.8 1.9 %collective-permute-done = bf16[2,128,128]{2,1,0:T(8,128)(2,1)S(1)} collective-permute-done((bf16[2,128,128]{2,1,0:T(8,128)(2,1)S(1)}, bf16[2,128,128]{2,1,0:T(8,128)(2,1)S(1)}, u32[]{:S(2)}, u32[]{:S(2)}) %collective-permute-start) | collective-permute-done | bytes 65568 | tf_op jit(solution)/shard_map/ppermute | solution.py:21
  7.7 0.8 broadcast_select_fusion
  8.6 0.6 slice_bitcast_fusion.8
  9.2 10.0 %shard_map.118 = f32[256,1536]{1,0:T(8,128)} custom-call(f32[16]{0:T(128)} %sink_ref.1, bf16[256,1024]{1,0:T(8,128)(2,1)} %q_ref.1, bf16[128,128]{1,0:T(8,128)(2,1)} %get-tuple-element.27.pk_ref, bf16[256,128]{1,0:T(8,128)(2,1)} %k_ref.1, bf16[128,128]{1,0:T(8,128)(2,1)} %get-tuple-element.26.pv_ref, bf16[256,128]{1,0:T(8,128)(2,1)} %v_ref.1, ...), custom_call_target="tpu_custom_call" | custom-call | flops 1342177280 | bytes 5439488 | tf_op jit(solution)/shard_map/pallas_call | solution.py:141
  19.2 0.0 collective-permute-start.1
  19.2 0.1 copy.33
  19.4 0.1 eq.71
  19.5 0.1 eq.67
  19.6 2.3 %reduce-window.6 = s32[8,8,128]{2,1,0:T(8,128)S(1)} reduce-window(s32[8,8,128]{2,1,0:T(8,128)S(1)} %fusion.33, s32[]{:T(128)} %constant.19.clone.1), window={size=1x1x128 pad=0_0x0_0x127_0}, to_apply=%region_0.1 | reduce-window | flops 1040384 | bytes 65540 | tf_op jit(solution)/shard_map/reduce-window
  21.9 0.3 slice_reduce_fusion
  22.2 0.2 reduce-window.9
  22.3 0.1 add_bitcast_fusion
  22.5 0.1 sub.36
  22.6 0.1 copy.35
  22.7 0.4 fusion.22
  23.2 0.0 copy-start.3
  23.2 0.0 collective-permute-done.1
  23.2 2.2 %multiply_reduce_fusion.1 = (f32[256]{0:T(256)S(1)}, f32[256,1536]{1,0:T(8,128)S(1)}) fusion(f32[256,1536]{1,0:T(8,128)} %shard_map.118, f32[256,1536]{1,0:T(8,128)} %collective-permute-done.1, bf16[256,1536]{1,0:T(8,128)(2,1)S(1)} %copy-done.1), kind=kLoop, calls=%fused_computation.29 | loop fusion | flops 1965824 | bytes 5506048 | tf_op jit(solution)/shard_map/reduce_sum | solution.py:44
  25.4 0.0 slice-start
  25.4 0.9 convolution_convert_fusion.2
  26.3 0.0 slice-start.1
  26.3 0.1 fusion.40
  26.5 1.6 collective-permute-start.2
  28.1 1.6 collective-permute-start.3
  29.7 3.4 %collective-permute-start.4 = (bf16[96,1536]{1,0:T(8,128)(2,1)S(1)}, bf16[96,1536]{1,0:T(8,128)(2,1)S(1)}, u32[]{:S(2)}, u32[]{:S(2)}) collective-permute-start(bf16[96,1536]{1,0:T(8,128)(2,1)S(1)} %get-tuple-element.23), channel_id=1, source_target_pairs={{0,6},{2,8},{4,10},{6,12},{8,14},{10,0},{12,2},{14,4},{1,7},{3,9},... | collective-permute-start | bytes 884744 | tf_op jit(solution)/shard_map/ppermute | solution.py:39
  33.1 1.2 collective-permute-start.5
  34.3 1.8 %collective-permute-start.6 = (bf16[96,1536]{1,0:T(8,128)(2,1)S(1)}, bf16[96,1536]{1,0:T(8,128)(2,1)S(1)}, u32[]{:S(2)}, u32[]{:S(2)}) collective-permute-start(bf16[96,1536]{1,0:T(8,128)(2,1)S(1)} %get-tuple-element.21), channel_id=1, source_target_pairs={{0,10},{2,12},{4,14},{6,0},{8,2},{10,4},{12,6},{14,8},{1,11},{3,13... | collective-permute-start | bytes 884744 | tf_op jit(solution)/shard_map/ppermute | solution.py:39
  36.1 3.2 %collective-permute-done.2 = bf16[96,1536]{1,0:T(8,128)(2,1)S(1)} collective-permute-done((bf16[96,1536]{1,0:T(8,128)(2,1)S(1)}, bf16[96,1536]{1,0:T(8,128)(2,1)S(1)}, u32[]{:S(2)}, u32[]{:S(2)}) %collective-permute-start.2) | collective-permute-done | bytes 294944 | tf_op jit(solution)/shard_map/ppermute | solution.py:39
  39.3 2.4 %collective-permute-start.7 = (bf16[96,1536]{1,0:T(8,128)(2,1)S(1)}, bf16[96,1536]{1,0:T(8,128)(2,1)S(1)}, u32[]{:S(2)}, u32[]{:S(2)}) collective-permute-start(bf16[96,1536]{1,0:T(8,128)(2,1)S(1)} %get-tuple-element.20), channel_id=1, source_target_pairs={{0,12},{2,14},{4,0},{6,2},{8,4},{10,6},{12,8},{14,10},{1,13},{3,15... | collective-permute-start | bytes 884744 | tf_op jit(solution)/shard_map/ppermute | solution.py:39
  41.8 0.0 collective-permute-done.3
  41.8 6.0 %collective-permute-start.8 = (bf16[96,1536]{1,0:T(8,128)(2,1)S(1)}, bf16[96,1536]{1,0:T(8,128)(2,1)S(1)}, u32[]{:S(2)}, u32[]{:S(2)}) collective-permute-start(bf16[96,1536]{1,0:T(8,128)(2,1)S(1)} %get-tuple-element.19), channel_id=1, source_target_pairs={{0,14},{2,0},{4,2},{6,4},{8,6},{10,8},{12,10},{14,12},{1,15},{3,1}... | collective-permute-start | bytes 884744 | tf_op jit(solution)/shard_map/ppermute | solution.py:39
  47.8 16.4 %collective-permute-done.4 = bf16[96,1536]{1,0:T(8,128)(2,1)S(1)} collective-permute-done((bf16[96,1536]{1,0:T(8,128)(2,1)S(1)}, bf16[96,1536]{1,0:T(8,128)(2,1)S(1)}, u32[]{:S(2)}, u32[]{:S(2)}) %collective-permute-start.4) | collective-permute-done | bytes 294944 | tf_op jit(solution)/shard_map/ppermute | solution.py:39
  64.2 0.3 collective-permute-done.5
  64.5 0.0 collective-permute-done.6
  64.6 0.0 collective-permute-done.7
  64.6 3.3 %collective-permute-done.8 = bf16[96,1536]{1,0:T(8,128)(2,1)S(1)} collective-permute-done((bf16[96,1536]{1,0:T(8,128)(2,1)S(1)}, bf16[96,1536]{1,0:T(8,128)(2,1)S(1)}, u32[]{:S(2)}, u32[]{:S(2)}) %collective-permute-start.8) | collective-permute-done | bytes 294944 | tf_op jit(solution)/shard_map/ppermute | solution.py:39
  68.0 0.1 collective-permute-start.9
  68.1 3.8 %fusion.16 = f32[2,768,768]{2,1,0:T(8,128)S(1)} fusion(bf16[768,1536,1]{1,0,2:T(8,128)(2,1)S(1)} %bitcast.114, bf16[1,2,1536,768]{3,2,1,0:T(8,128)(2,1)S(1)} %bitcast.117), kind=kOutput, calls=%fused_computation.24 | convolution fusion | flops 3623878656 | bytes 11796480 | tf_op jit(solution)/shard_map/rd,kdf->krf/dot_general | solution.py:71
  71.9 0.7 fusion.27
  72.6 0.0 collective-permute-done.9
  72.6 3.8 %fusion.19 = f32[2,768,768]{2,1,0:T(8,128)S(1)} fusion(bf16[768,1536,1]{1,0,2:T(8,128)(2,1)S(1)} %bitcast.118, bf16[1,2,1536,768]{3,2,1,0:T(8,128)(2,1)S(1)} %bitcast.117), kind=kOutput, calls=%fused_computation.25 | convolution fusion | flops 3623878656 | bytes 11796480 | tf_op jit(solution)/shard_map/rd,kdf->krf/dot_general | solution.py:71
  76.4 2.1 %convolution_convert_fusion = bf16[768,1536]{1,0:T(8,128)(2,1)S(1)} fusion(bf16[1,768,1536]{2,1,0:T(8,128)(2,1)S(1)} %copy-done, f32[2,768,768]{2,1,0:T(8,128)S(1)} %fusion.19), kind=kOutput, calls=%fused_computation.7 | convolution fusion | flops 1817837568 | bytes 9437184 | tf_op jit(solution)/shard_map/dot_general | solution.py:204
  78.5 0.5 collective-permute-start.10
  79.0 2.0 %convolution_convert_fusion.1 = bf16[768,1536]{1,0:T(8,128)(2,1)S(1)} fusion(bf16[768,768]{1,0:T(8,128)(2,1)S(1)} %fusion.27, bf16[1,768,1536]{2,1,0:T(8,128)(2,1)S(1)} %copy-done), kind=kOutput, calls=%fused_computation.8 | convolution fusion | flops 1813118976 | bytes 5898240 | tf_op jit(solution)/shard_map/dot_general | solution.py:209
  81.0 2.2 %collective-permute-done.10 = bf16[8,96,1536]{2,1,0:T(8,128)(2,1)S(1)} collective-permute-done((bf16[8,96,1536]{2,1,0:T(8,128)(2,1)S(1)}, bf16[8,96,1536]{2,1,0:T(8,128)(2,1)S(1)}, u32[]{:S(2)}, u32[]{:S(2)}) %collective-permute-start.10) | collective-permute-done | bytes 2359328 | tf_op jit(solution)/shard_map/ppermute | solution.py:26
  83.2 0.7 fusion
  83.9 0.2 slice_bitcast_fusion
  84.1 0.0 copy-start.4
  84.1 18.0 %collective-permute-start.11 = (bf16[96,1536]{1,0:T(8,128)(2,1)S(1)}, bf16[96,1536]{1,0:T(8,128)(2,1)S(1)}, u32[]{:S(2)}, u32[]{:S(2)}) collective-permute-start(bf16[96,1536]{1,0:T(8,128)(2,1)S(1)} %get-tuple-element.17), channel_id=1, source_target_pairs={{0,14},{2,0},{4,2},{6,4},{8,6},{10,8},{12,10},{14,12},{1,15},{3,1}... | collective-permute-start | bytes 884744 | tf_op jit(solution)/shard_map/ppermute | solution.py:39
  102.2 0.0 collective-permute-start.12
  102.2 0.4 collective-permute-start.13
  102.6 2.5 %collective-permute-start.14 = (bf16[96,1536]{1,0:T(8,128)(2,1)S(1)}, bf16[96,1536]{1,0:T(8,128)(2,1)S(1)}, u32[]{:S(2)}, u32[]{:S(2)}) collective-permute-start(bf16[96,1536]{1,0:T(8,128)(2,1)S(1)} %get-tuple-element.14), channel_id=1, source_target_pairs={{0,8},{2,10},{4,12},{6,14},{8,0},{10,2},{12,4},{14,6},{1,9},{3,11}... | collective-permute-start | bytes 884744 | tf_op jit(solution)/shard_map/ppermute | solution.py:39
  105.1 0.3 collective-permute-start.15
  105.5 4.1 %collective-permute-done.11 = bf16[96,1536]{1,0:T(8,128)(2,1)S(1)} collective-permute-done((bf16[96,1536]{1,0:T(8,128)(2,1)S(1)}, bf16[96,1536]{1,0:T(8,128)(2,1)S(1)}, u32[]{:S(2)}, u32[]{:S(2)}) %collective-permute-start.11) | collective-permute-done | bytes 294944 | tf_op jit(solution)/shard_map/ppermute | solution.py:39
  109.6 6.3 %collective-permute-done.12 = bf16[96,1536]{1,0:T(8,128)(2,1)S(1)} collective-permute-done((bf16[96,1536]{1,0:T(8,128)(2,1)S(1)}, bf16[96,1536]{1,0:T(8,128)(2,1)S(1)}, u32[]{:S(2)}, u32[]{:S(2)}) %collective-permute-start.12) | collective-permute-done | bytes 294944 | tf_op jit(solution)/shard_map/ppermute | solution.py:39
  115.9 6.3 %collective-permute-done.13 = bf16[96,1536]{1,0:T(8,128)(2,1)S(1)} collective-permute-done((bf16[96,1536]{1,0:T(8,128)(2,1)S(1)}, bf16[96,1536]{1,0:T(8,128)(2,1)S(1)}, u32[]{:S(2)}, u32[]{:S(2)}) %collective-permute-start.13) | collective-permute-done | bytes 294944 | tf_op jit(solution)/shard_map/ppermute | solution.py:39
  122.2 31.8 %collective-permute-done.14 = bf16[96,1536]{1,0:T(8,128)(2,1)S(1)} collective-permute-done((bf16[96,1536]{1,0:T(8,128)(2,1)S(1)}, bf16[96,1536]{1,0:T(8,128)(2,1)S(1)}, u32[]{:S(2)}, u32[]{:S(2)}) %collective-permute-start.14) | collective-permute-done | bytes 294944 | tf_op jit(solution)/shard_map/ppermute | solution.py:39
  154.0 0.0 collective-permute-done.15
  154.2 3.0 %multiply_reduce_fusion = f32[256,1536]{1,0:T(8,128)S(1)} fusion(bf16[768,1536,1]{1,0,2:T(8,128)(2,1)S(1)} %bitcast.113, f32[256,4]{0,1:T(4,128)S(1)} %copy-done.4, s32[256,4]{0,1:T(4,128)S(1)} %fusion.37), kind=kOutput, calls=%fused_computation | convolution fusion | flops 2419458048 | bytes 3940352 | tf_op jit(solution)/shard_map/dot_general | solution.py:215
  157.2 0.1 collective-permute-start.18
  157.3 3.4 %collective-permute-done.18 = f32[256,1536]{1,0:T(8,128)S(1)} collective-permute-done((f32[256,1536]{1,0:T(8,128)S(1)}, f32[256,1536]{1,0:T(8,128)S(1)}, u32[]{:S(2)}, u32[]{:S(2)}) %collective-permute-start.18) | collective-permute-done | bytes 1572896 | tf_op jit(solution)/shard_map/ppermute | solution.py:26
  160.7 1.2 add_convert_fusion
  (36 shorter events, 0.4 us)
Async XLA Ops:
  0.0 76.4 %copy-start = (bf16[1,768,1536]{2,1,0:T(8,128)(2,1)S(1)}, bf16[1,768,1536]{2,1,0:T(8,128)(2,1)}, u32[]{:S(2)}) copy-start(bf16[1,768,1536]{2,1,0:T(8,128)(2,1)} %param.21) | copy-start | bytes 7077892
  0.9 6.8 %collective-permute-start = (bf16[2,128,128]{2,1,0:T(8,128)(2,1)S(1)}, bf16[2,128,128]{2,1,0:T(8,128)(2,1)S(1)}, u32[]{:S(2)}, u32[]{:S(2)}) collective-permute-start(bf16[2,128,128]{2,1,0:T(8,128)(2,1)S(1)} %pad_maximum_fusion), channel_id=1, source_target_pairs={{0,2},{2,4},{4,6},{6,8},{8,10},{10,12},{12,14},{1,3},{3,5},{5,7},{... | collective-permute-start | bytes 196616 | tf_op jit(solution)/shard_map/ppermute | solution.py:21
  9.2 10.0 %copy-start.2 = (s32[256,4]{0,1:T(4,128)S(1)}, s32[256,4]{0,1:T(4,128)}, u32[]{:S(2)}) copy-start(s32[256,4]{0,1:T(4,128)} %param.22) | copy-start | bytes 12292
  9.2 14.0 %copy-start.1 = (bf16[256,1536]{1,0:T(8,128)(2,1)S(1)}, bf16[256,1536]{1,0:T(8,128)(2,1)}, u32[]{:S(2)}) copy-start(bf16[256,1536]{1,0:T(8,128)(2,1)} %param.18) | copy-start | bytes 2359300
  19.2 3.9 %collective-permute-start.1 = (f32[256,1536]{1,0:T(8,128)}, f32[256,1536]{1,0:T(8,128)}, u32[]{:S(2)}, u32[]{:S(2)}) collective-permute-start(f32[256,1536]{1,0:T(8,128)} %shard_map.118), channel_id=1, source_target_pairs={{0,1},{1,0},{2,3},{3,2},{4,5},{5,4},{6,7},{7,6},{8,9},{9,8},{10,11... | collective-permute-start | bytes 4718600 | tf_op jit(solution)/shard_map/ppermute | solution.py:26
  23.2 2.3 %copy-start.3 = (f32[1536]{0:T(1024)S(1)}, f32[1536]{0:T(1024)}, u32[]{:S(2)}) copy-start(f32[1536]{0:T(1024)} %param.19) | copy-start | bytes 18436
  25.4 42.6 %slice-start = ((s8[4718592]{0:T(1024)(128)(4,1)}), s8[4194304]{0:T(1024)(128)(4,1)S(1)}, s32[]{:S(2)}) async-start(s8[4718592]{0:T(1024)(128)(4,1)} %bitcast.116), calls=%async_computation | async-start | bytes 8388608
  26.3 41.7 %slice-start.1 = ((s8[4718592]{0:T(1024)(128)(4,1)}), s8[524288]{0:T(1024)(128)(4,1)S(1)}, s32[]{:S(2)}) async-start(s8[4718592]{0:T(1024)(128)(4,1)} %bitcast.116), calls=%async_computation.1 | async-start | bytes 1048576
  26.5 12.8 %collective-permute-start.2 = (bf16[96,1536]{1,0:T(8,128)(2,1)S(1)}, bf16[96,1536]{1,0:T(8,128)(2,1)S(1)}, u32[]{:S(2)}, u32[]{:S(2)}) collective-permute-start(bf16[96,1536]{1,0:T(8,128)(2,1)S(1)} %get-tuple-element.25), channel_id=1, source_target_pairs={{0,2},{2,4},{4,6},{6,8},{8,10},{10,12},{12,14},{14,0},{1,3},{3,5},... | collective-permute-start | bytes 884744 | tf_op jit(solution)/shard_map/ppermute | solution.py:39
  28.1 13.7 %collective-permute-start.3 = (bf16[96,1536]{1,0:T(8,128)(2,1)S(1)}, bf16[96,1536]{1,0:T(8,128)(2,1)S(1)}, u32[]{:S(2)}, u32[]{:S(2)}) collective-permute-start(bf16[96,1536]{1,0:T(8,128)(2,1)S(1)} %get-tuple-element.24), channel_id=1, source_target_pairs={{0,4},{2,6},{4,8},{6,10},{8,12},{10,14},{12,0},{14,2},{1,5},{3,7},... | collective-permute-start | bytes 884744 | tf_op jit(solution)/shard_map/ppermute | solution.py:39
  29.7 34.6 %collective-permute-start.4 = (bf16[96,1536]{1,0:T(8,128)(2,1)S(1)}, bf16[96,1536]{1,0:T(8,128)(2,1)S(1)}, u32[]{:S(2)}, u32[]{:S(2)}) collective-permute-start(bf16[96,1536]{1,0:T(8,128)(2,1)S(1)} %get-tuple-element.23), channel_id=1, source_target_pairs={{0,6},{2,8},{4,10},{6,12},{8,14},{10,0},{12,2},{14,4},{1,7},{3,9},... | collective-permute-start | bytes 884744 | tf_op jit(solution)/shard_map/ppermute | solution.py:39
  33.1 31.4 %collective-permute-start.5 = (bf16[96,1536]{1,0:T(8,128)(2,1)S(1)}, bf16[96,1536]{1,0:T(8,128)(2,1)S(1)}, u32[]{:S(2)}, u32[]{:S(2)}) collective-permute-start(bf16[96,1536]{1,0:T(8,128)(2,1)S(1)} %get-tuple-element.22), channel_id=1, source_target_pairs={{0,8},{2,10},{4,12},{6,14},{8,0},{10,2},{12,4},{14,6},{1,9},{3,11}... | collective-permute-start | bytes 884744 | tf_op jit(solution)/shard_map/ppermute | solution.py:39
  34.3 30.2 %collective-permute-start.6 = (bf16[96,1536]{1,0:T(8,128)(2,1)S(1)}, bf16[96,1536]{1,0:T(8,128)(2,1)S(1)}, u32[]{:S(2)}, u32[]{:S(2)}) collective-permute-start(bf16[96,1536]{1,0:T(8,128)(2,1)S(1)} %get-tuple-element.21), channel_id=1, source_target_pairs={{0,10},{2,12},{4,14},{6,0},{8,2},{10,4},{12,6},{14,8},{1,11},{3,13... | collective-permute-start | bytes 884744 | tf_op jit(solution)/shard_map/ppermute | solution.py:39
  39.3 25.2 %collective-permute-start.7 = (bf16[96,1536]{1,0:T(8,128)(2,1)S(1)}, bf16[96,1536]{1,0:T(8,128)(2,1)S(1)}, u32[]{:S(2)}, u32[]{:S(2)}) collective-permute-start(bf16[96,1536]{1,0:T(8,128)(2,1)S(1)} %get-tuple-element.20), channel_id=1, source_target_pairs={{0,12},{2,14},{4,0},{6,2},{8,4},{10,6},{12,8},{14,10},{1,13},{3,15... | collective-permute-start | bytes 884744 | tf_op jit(solution)/shard_map/ppermute | solution.py:39
  41.8 26.2 %collective-permute-start.8 = (bf16[96,1536]{1,0:T(8,128)(2,1)S(1)}, bf16[96,1536]{1,0:T(8,128)(2,1)S(1)}, u32[]{:S(2)}, u32[]{:S(2)}) collective-permute-start(bf16[96,1536]{1,0:T(8,128)(2,1)S(1)} %get-tuple-element.19), channel_id=1, source_target_pairs={{0,14},{2,0},{4,2},{6,4},{8,6},{10,8},{12,10},{14,12},{1,15},{3,1}... | collective-permute-start | bytes 884744 | tf_op jit(solution)/shard_map/ppermute | solution.py:39
  68.0 4.6 %collective-permute-start.9 = (bf16[8,96,1536]{2,1,0:T(8,128)(2,1)S(1)}, bf16[8,96,1536]{2,1,0:T(8,128)(2,1)S(1)}, u32[]{:S(2)}, u32[]{:S(2)}) collective-permute-start(bf16[8,96,1536]{2,1,0:T(8,128)(2,1)S(1)} %bitcast_dynamic-update-slice_fusion.7), channel_id=1, source_target_pairs={{0,1},{1,0},{2,3},{3,2},{4,5},{5,4},{6,7},{7,6},{8,9},{9,8},{10,11... | collective-permute-start | bytes 7077896 | tf_op jit(solution)/shard_map/ppermute | solution.py:26
  78.5 4.7 %collective-permute-start.10 = (bf16[8,96,1536]{2,1,0:T(8,128)(2,1)S(1)}, bf16[8,96,1536]{2,1,0:T(8,128)(2,1)S(1)}, u32[]{:S(2)}, u32[]{:S(2)}) collective-permute-start(bf16[8,96,1536]{2,1,0:T(8,128)(2,1)S(1)} %bitcast.119), channel_id=1, source_target_pairs={{0,1},{1,0},{2,3},{3,2},{4,5},{5,4},{6,7},{7,6},{8,9},{9,8},{10,11... | collective-permute-start | bytes 7077896 | tf_op jit(solution)/shard_map/ppermute | solution.py:26
  84.1 70.1 %copy-start.4 = (f32[256,4]{0,1:T(4,128)S(1)}, f32[256,4]{0,1:T(4,128)}, u32[]{:S(2)}) copy-start(f32[256,4]{0,1:T(4,128)} %param.23) | copy-start | bytes 12292
  84.1 25.5 %collective-permute-start.11 = (bf16[96,1536]{1,0:T(8,128)(2,1)S(1)}, bf16[96,1536]{1,0:T(8,128)(2,1)S(1)}, u32[]{:S(2)}, u32[]{:S(2)}) collective-permute-start(bf16[96,1536]{1,0:T(8,128)(2,1)S(1)} %get-tuple-element.17), channel_id=1, source_target_pairs={{0,14},{2,0},{4,2},{6,4},{8,6},{10,8},{12,10},{14,12},{1,15},{3,1}... | collective-permute-start | bytes 884744 | tf_op jit(solution)/shard_map/ppermute | solution.py:39
  102.2 13.8 %collective-permute-start.12 = (bf16[96,1536]{1,0:T(8,128)(2,1)S(1)}, bf16[96,1536]{1,0:T(8,128)(2,1)S(1)}, u32[]{:S(2)}, u32[]{:S(2)}) collective-permute-start(bf16[96,1536]{1,0:T(8,128)(2,1)S(1)} %get-tuple-element.16), channel_id=1, source_target_pairs={{0,12},{2,14},{4,0},{6,2},{8,4},{10,6},{12,8},{14,10},{1,13},{3,15... | collective-permute-start | bytes 884744 | tf_op jit(solution)/shard_map/ppermute | solution.py:39
  102.2 20.1 %collective-permute-start.13 = (bf16[96,1536]{1,0:T(8,128)(2,1)S(1)}, bf16[96,1536]{1,0:T(8,128)(2,1)S(1)}, u32[]{:S(2)}, u32[]{:S(2)}) collective-permute-start(bf16[96,1536]{1,0:T(8,128)(2,1)S(1)} %get-tuple-element.15), channel_id=1, source_target_pairs={{0,10},{2,12},{4,14},{6,0},{8,2},{10,4},{12,6},{14,8},{1,11},{3,13... | collective-permute-start | bytes 884744 | tf_op jit(solution)/shard_map/ppermute | solution.py:39
  102.6 51.4 %collective-permute-start.14 = (bf16[96,1536]{1,0:T(8,128)(2,1)S(1)}, bf16[96,1536]{1,0:T(8,128)(2,1)S(1)}, u32[]{:S(2)}, u32[]{:S(2)}) collective-permute-start(bf16[96,1536]{1,0:T(8,128)(2,1)S(1)} %get-tuple-element.14), channel_id=1, source_target_pairs={{0,8},{2,10},{4,12},{6,14},{8,0},{10,2},{12,4},{14,6},{1,9},{3,11}... | collective-permute-start | bytes 884744 | tf_op jit(solution)/shard_map/ppermute | solution.py:39
  105.1 48.9 %collective-permute-start.15 = (bf16[96,1536]{1,0:T(8,128)(2,1)S(1)}, bf16[96,1536]{1,0:T(8,128)(2,1)S(1)}, u32[]{:S(2)}, u32[]{:S(2)}) collective-permute-start(bf16[96,1536]{1,0:T(8,128)(2,1)S(1)} %get-tuple-element.13), channel_id=1, source_target_pairs={{0,6},{2,8},{4,10},{6,12},{8,14},{10,0},{12,2},{14,4},{1,7},{3,9},... | collective-permute-start | bytes 884744 | tf_op jit(solution)/shard_map/ppermute | solution.py:39
  109.6 44.5 %collective-permute-start.16 = (bf16[96,1536]{1,0:T(8,128)(2,1)S(1)}, bf16[96,1536]{1,0:T(8,128)(2,1)S(1)}, u32[]{:S(2)}, u32[]{:S(2)}) collective-permute-start(bf16[96,1536]{1,0:T(8,128)(2,1)S(1)} %get-tuple-element.12), channel_id=1, source_target_pairs={{0,4},{2,6},{4,8},{6,10},{8,12},{10,14},{12,0},{14,2},{1,5},{3,7},... | collective-permute-start | bytes 884744 | tf_op jit(solution)/shard_map/ppermute | solution.py:39
  115.9 38.2 %collective-permute-start.17 = (bf16[96,1536]{1,0:T(8,128)(2,1)S(1)}, bf16[96,1536]{1,0:T(8,128)(2,1)S(1)}, u32[]{:S(2)}, u32[]{:S(2)}) collective-permute-start(bf16[96,1536]{1,0:T(8,128)(2,1)S(1)} %get-tuple-element.11), channel_id=1, source_target_pairs={{0,2},{2,4},{4,6},{6,8},{8,10},{10,12},{12,14},{14,0},{1,3},{3,5},... | collective-permute-start | bytes 884744 | tf_op jit(solution)/shard_map/ppermute | solution.py:39
  157.2 3.5 %collective-permute-start.18 = (f32[256,1536]{1,0:T(8,128)S(1)}, f32[256,1536]{1,0:T(8,128)S(1)}, u32[]{:S(2)}, u32[]{:S(2)}) collective-permute-start(f32[256,1536]{1,0:T(8,128)S(1)} %multiply_reduce_fusion), channel_id=1, source_target_pairs={{0,1},{1,0},{2,3},{3,2},{4,5},{5,4},{6,7},{7,6},{8,9},{9,8},{10,11... | collective-permute-start | bytes 4718600 | tf_op jit(solution)/shard_map/ppermute | solution.py:26

commit v16 on v14

--- a/solution.py
+++ b/solution.py
@@ -213,7 +213,8 @@
     returned = shift_exchange(result, -1) if by_shift else seq_all_to_all(result)
     picked = jnp.dot(pick, returned.reshape(slots, width), preferred_element_type=jnp.float32)
     weighted = jnp.sum(picked.reshape(tok_rows, TOP, width) * route_gates[:, :, None], axis=1)
-    moe = weighted + swap_exp(weighted)
+    rounded = weighted.astype(jnp.bfloat16)
+    moe = rounded.astype(jnp.float32) + swap_exp(rounded).astype(jnp.float32)
     return (mixed_rows + moe).astype(jnp.bfloat16)
 
 

time: 162 us -> 161 us (level)
  no operation moved by 1% of the time
where the time goes in v16:
time: 161 us
  waiting for transfers between devices  78.1 us (49%)
  starting transfers between devices  44.9 us (28%)
  matrix products  15.6 us (10%)
  Pallas kernels  10 us (6%)
  other arithmetic  8.63 us (5%)
  local copies, waits for them, and re-layouts  3.14 us (2%)
    ppermute x14, waiting for transfers between devices, shift_exchange(): out.append(lax.ppermute(blocks[step], 'seq', pairs))  71.7 us
    ppermute x14, starting transfers between devices, shift_exchange(): out.append(lax.ppermute(blocks[step], 'seq', pairs))  39.4 us
    pallas_call x1, Pallas kernels, attend_kernel(): pl.pallas_call(attention_kernel, out_shape=jax.ShapeDtypeStruct((rows, wi...  10 us
    dot_general x2, matrix products, expert_hidden(): jnp.einsum('rd,kdf->krf', rows, expert_in, preferred_element_type=jnp.flo...  7.62 us
    ppermute x1, starting transfers between devices, shifted(): return lax.ppermute(shard, axis, pairs)  4.87 us
    ppermute x4, waiting for transfers between devices, swap_exp(): return lax.ppermute(x, 'exp', [(i, (i + 1) % size) for i in range(size)])  4.44 us
  transfers between devices with their start and end apart: 19, of which 11 were waited for; matrix products, arithmetic and copies ran while one was open for 7% of the time, Pallas kernels for 0%

profile of v16, /device:TPU:0, one launch (start us, length us, event | category | flops | bytes accessed | tf_op | source)
XLA Modules:
  0.0 160.8 jit_solution(8763127292856600856)
XLA Ops:
  0.0 0.9 slice_bitcast_fusion.10
  0.9 4.9 %collective-permute-start = (bf16[2,128,128]{2,1,0:T(8,128)(2,1)S(1)}, bf16[2,128,128]{2,1,0:T(8,128)(2,1)S(1)}, u32[]{:S(2)}, u32[]{:S(2)}) collective-permute-start(bf16[2,128,128]{2,1,0:T(8,128)(2,1)S(1)} %pad_maximum_fusion), channel_id=1, source_target_pairs={{0,2},{2,4},{4,6},{6,8},{8,10},{10,12},{12,14},{1,3},{3,5},{5,7},{... | collective-permute-start | bytes 196616 | tf_op jit(solution)/shard_map/ppermute | solution.py:21
  5.8 1.9 %collective-permute-done = bf16[2,128,128]{2,1,0:T(8,128)(2,1)S(1)} collective-permute-done((bf16[2,128,128]{2,1,0:T(8,128)(2,1)S(1)}, bf16[2,128,128]{2,1,0:T(8,128)(2,1)S(1)}, u32[]{:S(2)}, u32[]{:S(2)}) %collective-permute-start) | collective-permute-done | bytes 65568 | tf_op jit(solution)/shard_map/ppermute | solution.py:21
  7.7 0.8 broadcast_select_fusion
  8.6 0.6 slice_bitcast_fusion.8
  9.2 10.0 %shard_map.118 = f32[256,1536]{1,0:T(8,128)} custom-call(f32[16]{0:T(128)} %sink_ref.1, bf16[256,1024]{1,0:T(8,128)(2,1)} %q_ref.1, bf16[128,128]{1,0:T(8,128)(2,1)} %get-tuple-element.27.pk_ref, bf16[256,128]{1,0:T(8,128)(2,1)} %k_ref.1, bf16[128,128]{1,0:T(8,128)(2,1)} %get-tuple-element.26.pv_ref, bf16[256,128]{1,0:T(8,128)(2,1)} %v_ref.1, ...), custom_call_target="tpu_custom_call" | custom-call | flops 1342177280 | bytes 5439488 | tf_op jit(solution)/shard_map/pallas_call | solution.py:140
  19.2 0.0 collective-permute-start.1
  19.2 0.1 copy.33
  19.4 0.1 eq.71
  19.5 0.1 eq.67
  19.6 2.3 %reduce-window.6 = s32[8,8,128]{2,1,0:T(8,128)S(1)} reduce-window(s32[8,8,128]{2,1,0:T(8,128)S(1)} %fusion.33, s32[]{:T(128)} %constant.19.clone.1), window={size=1x1x128 pad=0_0x0_0x127_0}, to_apply=%region_0.1 | reduce-window | flops 1040384 | bytes 65540 | tf_op jit(solution)/shard_map/reduce-window
  21.9 0.3 slice_reduce_fusion
  22.2 0.2 reduce-window.9
  22.3 0.1 add_bitcast_fusion
  22.5 0.1 sub.36
  22.6 0.1 copy.35
  22.7 0.4 fusion.22
  23.2 0.0 copy-start.3
  23.2 0.0 collective-permute-done.1
  23.2 2.2 %multiply_reduce_fusion.1 = (f32[256]{0:T(256)S(1)}, f32[256,1536]{1,0:T(8,128)S(1)}) fusion(f32[256,1536]{1,0:T(8,128)} %shard_map.118, f32[256,1536]{1,0:T(8,128)} %collective-permute-done.1, bf16[256,1536]{1,0:T(8,128)(2,1)S(1)} %copy-done.1), kind=kLoop, calls=%fused_computation.29 | loop fusion | flops 1965824 | bytes 5506048 | tf_op jit(solution)/shard_map/reduce_sum | solution.py:43
  25.4 0.0 slice-start
  25.4 0.9 convolution_convert_fusion.2
  26.3 0.0 slice-start.1
  26.3 0.1 fusion.40
  26.5 1.6 collective-permute-start.2
  28.1 1.6 collective-permute-start.3
  29.7 3.4 %collective-permute-start.4 = (bf16[96,1536]{1,0:T(8,128)(2,1)S(1)}, bf16[96,1536]{1,0:T(8,128)(2,1)S(1)}, u32[]{:S(2)}, u32[]{:S(2)}) collective-permute-start(bf16[96,1536]{1,0:T(8,128)(2,1)S(1)} %get-tuple-element.23), channel_id=1, source_target_pairs={{0,6},{2,8},{4,10},{6,12},{8,14},{10,0},{12,2},{14,4},{1,7},{3,9},... | collective-permute-start | bytes 884744 | tf_op jit(solution)/shard_map/ppermute | solution.py:38
  33.1 1.2 collective-permute-start.5
  34.3 1.8 %collective-permute-start.6 = (bf16[96,1536]{1,0:T(8,128)(2,1)S(1)}, bf16[96,1536]{1,0:T(8,128)(2,1)S(1)}, u32[]{:S(2)}, u32[]{:S(2)}) collective-permute-start(bf16[96,1536]{1,0:T(8,128)(2,1)S(1)} %get-tuple-element.21), channel_id=1, source_target_pairs={{0,10},{2,12},{4,14},{6,0},{8,2},{10,4},{12,6},{14,8},{1,11},{3,13... | collective-permute-start | bytes 884744 | tf_op jit(solution)/shard_map/ppermute | solution.py:38
  36.1 3.2 %collective-permute-done.2 = bf16[96,1536]{1,0:T(8,128)(2,1)S(1)} collective-permute-done((bf16[96,1536]{1,0:T(8,128)(2,1)S(1)}, bf16[96,1536]{1,0:T(8,128)(2,1)S(1)}, u32[]{:S(2)}, u32[]{:S(2)}) %collective-permute-start.2) | collective-permute-done | bytes 294944 | tf_op jit(solution)/shard_map/ppermute | solution.py:38
  39.3 2.4 %collective-permute-start.7 = (bf16[96,1536]{1,0:T(8,128)(2,1)S(1)}, bf16[96,1536]{1,0:T(8,128)(2,1)S(1)}, u32[]{:S(2)}, u32[]{:S(2)}) collective-permute-start(bf16[96,1536]{1,0:T(8,128)(2,1)S(1)} %get-tuple-element.20), channel_id=1, source_target_pairs={{0,12},{2,14},{4,0},{6,2},{8,4},{10,6},{12,8},{14,10},{1,13},{3,15... | collective-permute-start | bytes 884744 | tf_op jit(solution)/shard_map/ppermute | solution.py:38
  41.8 0.0 collective-permute-done.3
  41.8 6.0 %collective-permute-start.8 = (bf16[96,1536]{1,0:T(8,128)(2,1)S(1)}, bf16[96,1536]{1,0:T(8,128)(2,1)S(1)}, u32[]{:S(2)}, u32[]{:S(2)}) collective-permute-start(bf16[96,1536]{1,0:T(8,128)(2,1)S(1)} %get-tuple-element.19), channel_id=1, source_target_pairs={{0,14},{2,0},{4,2},{6,4},{8,6},{10,8},{12,10},{14,12},{1,15},{3,1}... | collective-permute-start | bytes 884744 | tf_op jit(solution)/shard_map/ppermute | solution.py:38
  47.8 16.4 %collective-permute-done.4 = bf16[96,1536]{1,0:T(8,128)(2,1)S(1)} collective-permute-done((bf16[96,1536]{1,0:T(8,128)(2,1)S(1)}, bf16[96,1536]{1,0:T(8,128)(2,1)S(1)}, u32[]{:S(2)}, u32[]{:S(2)}) %collective-permute-start.4) | collective-permute-done | bytes 294944 | tf_op jit(solution)/shard_map/ppermute | solution.py:38
  64.2 0.3 collective-permute-done.5
  64.5 0.0 collective-permute-done.6
  64.6 0.0 collective-permute-done.7
  64.6 3.3 %collective-permute-done.8 = bf16[96,1536]{1,0:T(8,128)(2,1)S(1)} collective-permute-done((bf16[96,1536]{1,0:T(8,128)(2,1)S(1)}, bf16[96,1536]{1,0:T(8,128)(2,1)S(1)}, u32[]{:S(2)}, u32[]{:S(2)}) %collective-permute-start.8) | collective-permute-done | bytes 294944 | tf_op jit(solution)/shard_map/ppermute | solution.py:38
  68.0 0.1 collective-permute-start.9
  68.1 3.8 %fusion.16 = f32[2,768,768]{2,1,0:T(8,128)S(1)} fusion(bf16[768,1536,1]{1,0,2:T(8,128)(2,1)S(1)} %bitcast.114, bf16[1,2,1536,768]{3,2,1,0:T(8,128)(2,1)S(1)} %bitcast.117), kind=kOutput, calls=%fused_computation.24 | convolution fusion | flops 3623878656 | bytes 11796480 | tf_op jit(solution)/shard_map/rd,kdf->krf/dot_general | solution.py:70
  71.9 0.7 fusion.27
  72.6 3.8 %fusion.19 = f32[2,768,768]{2,1,0:T(8,128)S(1)} fusion(bf16[768,1536,1]{1,0,2:T(8,128)(2,1)S(1)} %bitcast.118, bf16[1,2,1536,768]{3,2,1,0:T(8,128)(2,1)S(1)} %bitcast.117), kind=kOutput, calls=%fused_computation.25 | convolution fusion | flops 3623878656 | bytes 11796480 | tf_op jit(solution)/shard_map/rd,kdf->krf/dot_general | solution.py:70
  76.4 2.1 %convolution_convert_fusion = bf16[768,1536]{1,0:T(8,128)(2,1)S(1)} fusion(bf16[1,768,1536]{2,1,0:T(8,128)(2,1)S(1)} %copy-done, f32[2,768,768]{2,1,0:T(8,128)S(1)} %fusion.19), kind=kOutput, calls=%fused_computation.7 | convolution fusion | flops 1817837568 | bytes 9437184 | tf_op jit(solution)/shard_map/dot_general | solution.py:203
  78.5 0.5 collective-permute-start.10
  79.0 2.0 %convolution_convert_fusion.1 = bf16[768,1536]{1,0:T(8,128)(2,1)S(1)} fusion(bf16[768,768]{1,0:T(8,128)(2,1)S(1)} %fusion.27, bf16[1,768,1536]{2,1,0:T(8,128)(2,1)S(1)} %copy-done), kind=kOutput, calls=%fused_computation.8 | convolution fusion | flops 1813118976 | bytes 5898240 | tf_op jit(solution)/shard_map/dot_general | solution.py:208
  81.0 2.2 %collective-permute-done.10 = bf16[8,96,1536]{2,1,0:T(8,128)(2,1)S(1)} collective-permute-done((bf16[8,96,1536]{2,1,0:T(8,128)(2,1)S(1)}, bf16[8,96,1536]{2,1,0:T(8,128)(2,1)S(1)}, u32[]{:S(2)}, u32[]{:S(2)}) %collective-permute-start.10) | collective-permute-done | bytes 2359328 | tf_op jit(solution)/shard_map/ppermute | solution.py:26
  83.2 0.7 fusion
  83.9 0.2 slice_bitcast_fusion
  84.1 0.0 copy-start.4
  84.1 18.0 %collective-permute-start.11 = (bf16[96,1536]{1,0:T(8,128)(2,1)S(1)}, bf16[96,1536]{1,0:T(8,128)(2,1)S(1)}, u32[]{:S(2)}, u32[]{:S(2)}) collective-permute-start(bf16[96,1536]{1,0:T(8,128)(2,1)S(1)} %get-tuple-element.17), channel_id=1, source_target_pairs={{0,14},{2,0},{4,2},{6,4},{8,6},{10,8},{12,10},{14,12},{1,15},{3,1}... | collective-permute-start | bytes 884744 | tf_op jit(solution)/shard_map/ppermute | solution.py:38
  102.2 0.4 collective-permute-start.13
  102.6 2.5 %collective-permute-start.14 = (bf16[96,1536]{1,0:T(8,128)(2,1)S(1)}, bf16[96,1536]{1,0:T(8,128)(2,1)S(1)}, u32[]{:S(2)}, u32[]{:S(2)}) collective-permute-start(bf16[96,1536]{1,0:T(8,128)(2,1)S(1)} %get-tuple-element.14), channel_id=1, source_target_pairs={{0,8},{2,10},{4,12},{6,14},{8,0},{10,2},{12,4},{14,6},{1,9},{3,11}... | collective-permute-start | bytes 884744 | tf_op jit(solution)/shard_map/ppermute | solution.py:38
  105.1 0.3 collective-permute-start.15
  105.5 4.1 %collective-permute-done.11 = bf16[96,1536]{1,0:T(8,128)(2,1)S(1)} collective-permute-done((bf16[96,1536]{1,0:T(8,128)(2,1)S(1)}, bf16[96,1536]{1,0:T(8,128)(2,1)S(1)}, u32[]{:S(2)}, u32[]{:S(2)}) %collective-permute-start.11) | collective-permute-done | bytes 294944 | tf_op jit(solution)/shard_map/ppermute | solution.py:38
  109.6 6.3 %collective-permute-done.12 = bf16[96,1536]{1,0:T(8,128)(2,1)S(1)} collective-permute-done((bf16[96,1536]{1,0:T(8,128)(2,1)S(1)}, bf16[96,1536]{1,0:T(8,128)(2,1)S(1)}, u32[]{:S(2)}, u32[]{:S(2)}) %collective-permute-start.12) | collective-permute-done | bytes 294944 | tf_op jit(solution)/shard_map/ppermute | solution.py:38
  115.9 6.3 %collective-permute-done.13 = bf16[96,1536]{1,0:T(8,128)(2,1)S(1)} collective-permute-done((bf16[96,1536]{1,0:T(8,128)(2,1)S(1)}, bf16[96,1536]{1,0:T(8,128)(2,1)S(1)}, u32[]{:S(2)}, u32[]{:S(2)}) %collective-permute-start.13) | collective-permute-done | bytes 294944 | tf_op jit(solution)/shard_map/ppermute | solution.py:38
  122.2 31.8 %collective-permute-done.14 = bf16[96,1536]{1,0:T(8,128)(2,1)S(1)} collective-permute-done((bf16[96,1536]{1,0:T(8,128)(2,1)S(1)}, bf16[96,1536]{1,0:T(8,128)(2,1)S(1)}, u32[]{:S(2)}, u32[]{:S(2)}) %collective-permute-start.14) | collective-permute-done | bytes 294944 | tf_op jit(solution)/shard_map/ppermute | solution.py:38
  154.0 0.0 collective-permute-done.15
  154.1 0.0 collective-permute-done.16
  154.1 0.0 collective-permute-done.17
  154.2 3.1 %multiply_reduce_fusion = bf16[256,1536]{1,0:T(8,128)(2,1)S(1)} fusion(bf16[768,1536,1]{1,0,2:T(8,128)(2,1)S(1)} %bitcast.113, f32[256,4]{0,1:T(4,128)S(1)} %copy-done.4, s32[256,4]{0,1:T(4,128)S(1)} %fusion.37), kind=kOutput, calls=%fused_computation | convolution fusion | flops 2419458048 | bytes 3153920 | tf_op jit(solution)/shard_map/dot_general | solution.py:214
  157.3 0.1 collective-permute-start.18
  157.4 2.3 %collective-permute-done.18 = bf16[256,1536]{1,0:T(8,128)(2,1)S(1)} collective-permute-done((bf16[256,1536]{1,0:T(8,128)(2,1)S(1)}, bf16[256,1536]{1,0:T(8,128)(2,1)S(1)}, u32[]{:S(2)}, u32[]{:S(2)}) %collective-permute-start.18) | collective-permute-done | bytes 786464 | tf_op jit(solution)/shard_map/ppermute | solution.py:26
  159.6 1.2 add_convert_fusion
  (36 shorter events, 0.4 us)
Async XLA Ops:
  0.0 76.4 %copy-start = (bf16[1,768,1536]{2,1,0:T(8,128)(2,1)S(1)}, bf16[1,768,1536]{2,1,0:T(8,128)(2,1)}, u32[]{:S(2)}) copy-start(bf16[1,768,1536]{2,1,0:T(8,128)(2,1)} %param.21) | copy-start | bytes 7077892
  0.9 6.8 %collective-permute-start = (bf16[2,128,128]{2,1,0:T(8,128)(2,1)S(1)}, bf16[2,128,128]{2,1,0:T(8,128)(2,1)S(1)}, u32[]{:S(2)}, u32[]{:S(2)}) collective-permute-start(bf16[2,128,128]{2,1,0:T(8,128)(2,1)S(1)} %pad_maximum_fusion), channel_id=1, source_target_pairs={{0,2},{2,4},{4,6},{6,8},{8,10},{10,12},{12,14},{1,3},{3,5},{5,7},{... | collective-permute-start | bytes 196616 | tf_op jit(solution)/shard_map/ppermute | solution.py:21
  9.2 10.0 %copy-start.2 = (s32[256,4]{0,1:T(4,128)S(1)}, s32[256,4]{0,1:T(4,128)}, u32[]{:S(2)}) copy-start(s32[256,4]{0,1:T(4,128)} %param.22) | copy-start | bytes 12292
  9.2 14.0 %copy-start.1 = (bf16[256,1536]{1,0:T(8,128)(2,1)S(1)}, bf16[256,1536]{1,0:T(8,128)(2,1)}, u32[]{:S(2)}) copy-start(bf16[256,1536]{1,0:T(8,128)(2,1)} %param.18) | copy-start | bytes 2359300
  19.2 3.9 %collective-permute-start.1 = (f32[256,1536]{1,0:T(8,128)}, f32[256,1536]{1,0:T(8,128)}, u32[]{:S(2)}, u32[]{:S(2)}) collective-permute-start(f32[256,1536]{1,0:T(8,128)} %shard_map.118), channel_id=1, source_target_pairs={{0,1},{1,0},{2,3},{3,2},{4,5},{5,4},{6,7},{7,6},{8,9},{9,8},{10,11... | collective-permute-start | bytes 4718600 | tf_op jit(solution)/shard_map/ppermute | solution.py:26
  23.2 2.3 %copy-start.3 = (f32[1536]{0:T(1024)S(1)}, f32[1536]{0:T(1024)}, u32[]{:S(2)}) copy-start(f32[1536]{0:T(1024)} %param.19) | copy-start | bytes 18436
  25.4 42.6 %slice-start = ((s8[4718592]{0:T(1024)(128)(4,1)}), s8[4194304]{0:T(1024)(128)(4,1)S(1)}, s32[]{:S(2)}) async-start(s8[4718592]{0:T(1024)(128)(4,1)} %bitcast.116), calls=%async_computation | async-start | bytes 8388608
  26.3 41.7 %slice-start.1 = ((s8[4718592]{0:T(1024)(128)(4,1)}), s8[524288]{0:T(1024)(128)(4,1)S(1)}, s32[]{:S(2)}) async-start(s8[4718592]{0:T(1024)(128)(4,1)} %bitcast.116), calls=%async_computation.1 | async-start | bytes 1048576
  26.5 12.8 %collective-permute-start.2 = (bf16[96,1536]{1,0:T(8,128)(2,1)S(1)}, bf16[96,1536]{1,0:T(8,128)(2,1)S(1)}, u32[]{:S(2)}, u32[]{:S(2)}) collective-permute-start(bf16[96,1536]{1,0:T(8,128)(2,1)S(1)} %get-tuple-element.25), channel_id=1, source_target_pairs={{0,2},{2,4},{4,6},{6,8},{8,10},{10,12},{12,14},{14,0},{1,3},{3,5},... | collective-permute-start | bytes 884744 | tf_op jit(solution)/shard_map/ppermute | solution.py:38
  28.1 13.7 %collective-permute-start.3 = (bf16[96,1536]{1,0:T(8,128)(2,1)S(1)}, bf16[96,1536]{1,0:T(8,128)(2,1)S(1)}, u32[]{:S(2)}, u32[]{:S(2)}) collective-permute-start(bf16[96,1536]{1,0:T(8,128)(2,1)S(1)} %get-tuple-element.24), channel_id=1, source_target_pairs={{0,4},{2,6},{4,8},{6,10},{8,12},{10,14},{12,0},{14,2},{1,5},{3,7},... | collective-permute-start | bytes 884744 | tf_op jit(solution)/shard_map/ppermute | solution.py:38
  29.7 34.6 %collective-permute-start.4 = (bf16[96,1536]{1,0:T(8,128)(2,1)S(1)}, bf16[96,1536]{1,0:T(8,128)(2,1)S(1)}, u32[]{:S(2)}, u32[]{:S(2)}) collective-permute-start(bf16[96,1536]{1,0:T(8,128)(2,1)S(1)} %get-tuple-element.23), channel_id=1, source_target_pairs={{0,6},{2,8},{4,10},{6,12},{8,14},{10,0},{12,2},{14,4},{1,7},{3,9},... | collective-permute-start | bytes 884744 | tf_op jit(solution)/shard_map/ppermute | solution.py:38
  33.1 31.4 %collective-permute-start.5 = (bf16[96,1536]{1,0:T(8,128)(2,1)S(1)}, bf16[96,1536]{1,0:T(8,128)(2,1)S(1)}, u32[]{:S(2)}, u32[]{:S(2)}) collective-permute-start(bf16[96,1536]{1,0:T(8,128)(2,1)S(1)} %get-tuple-element.22), channel_id=1, source_target_pairs={{0,8},{2,10},{4,12},{6,14},{8,0},{10,2},{12,4},{14,6},{1,9},{3,11}... | collective-permute-start | bytes 884744 | tf_op jit(solution)/shard_map/ppermute | solution.py:38
  34.3 30.2 %collective-permute-start.6 = (bf16[96,1536]{1,0:T(8,128)(2,1)S(1)}, bf16[96,1536]{1,0:T(8,128)(2,1)S(1)}, u32[]{:S(2)}, u32[]{:S(2)}) collective-permute-start(bf16[96,1536]{1,0:T(8,128)(2,1)S(1)} %get-tuple-element.21), channel_id=1, source_target_pairs={{0,10},{2,12},{4,14},{6,0},{8,2},{10,4},{12,6},{14,8},{1,11},{3,13... | collective-permute-start | bytes 884744 | tf_op jit(solution)/shard_map/ppermute | solution.py:38
  39.3 25.2 %collective-permute-start.7 = (bf16[96,1536]{1,0:T(8,128)(2,1)S(1)}, bf16[96,1536]{1,0:T(8,128)(2,1)S(1)}, u32[]{:S(2)}, u32[]{:S(2)}) collective-permute-start(bf16[96,1536]{1,0:T(8,128)(2,1)S(1)} %get-tuple-element.20), channel_id=1, source_target_pairs={{0,12},{2,14},{4,0},{6,2},{8,4},{10,6},{12,8},{14,10},{1,13},{3,15... | collective-permute-start | bytes 884744 | tf_op jit(solution)/shard_map/ppermute | solution.py:38
  41.8 26.2 %collective-permute-start.8 = (bf16[96,1536]{1,0:T(8,128)(2,1)S(1)}, bf16[96,1536]{1,0:T(8,128)(2,1)S(1)}, u32[]{:S(2)}, u32[]{:S(2)}) collective-permute-start(bf16[96,1536]{1,0:T(8,128)(2,1)S(1)} %get-tuple-element.19), channel_id=1, source_target_pairs={{0,14},{2,0},{4,2},{6,4},{8,6},{10,8},{12,10},{14,12},{1,15},{3,1}... | collective-permute-start | bytes 884744 | tf_op jit(solution)/shard_map/ppermute | solution.py:38
  68.0 4.6 %collective-permute-start.9 = (bf16[8,96,1536]{2,1,0:T(8,128)(2,1)S(1)}, bf16[8,96,1536]{2,1,0:T(8,128)(2,1)S(1)}, u32[]{:S(2)}, u32[]{:S(2)}) collective-permute-start(bf16[8,96,1536]{2,1,0:T(8,128)(2,1)S(1)} %bitcast_dynamic-update-slice_fusion.7), channel_id=1, source_target_pairs={{0,1},{1,0},{2,3},{3,2},{4,5},{5,4},{6,7},{7,6},{8,9},{9,8},{10,11... | collective-permute-start | bytes 7077896 | tf_op jit(solution)/shard_map/ppermute | solution.py:26
  78.5 4.7 %collective-permute-start.10 = (bf16[8,96,1536]{2,1,0:T(8,128)(2,1)S(1)}, bf16[8,96,1536]{2,1,0:T(8,128)(2,1)S(1)}, u32[]{:S(2)}, u32[]{:S(2)}) collective-permute-start(bf16[8,96,1536]{2,1,0:T(8,128)(2,1)S(1)} %bitcast.119), channel_id=1, source_target_pairs={{0,1},{1,0},{2,3},{3,2},{4,5},{5,4},{6,7},{7,6},{8,9},{9,8},{10,11... | collective-permute-start | bytes 7077896 | tf_op jit(solution)/shard_map/ppermute | solution.py:26
  84.1 70.1 %copy-start.4 = (f32[256,4]{0,1:T(4,128)S(1)}, f32[256,4]{0,1:T(4,128)}, u32[]{:S(2)}) copy-start(f32[256,4]{0,1:T(4,128)} %param.23) | copy-start | bytes 12292
  84.1 25.5 %collective-permute-start.11 = (bf16[96,1536]{1,0:T(8,128)(2,1)S(1)}, bf16[96,1536]{1,0:T(8,128)(2,1)S(1)}, u32[]{:S(2)}, u32[]{:S(2)}) collective-permute-start(bf16[96,1536]{1,0:T(8,128)(2,1)S(1)} %get-tuple-element.17), channel_id=1, source_target_pairs={{0,14},{2,0},{4,2},{6,4},{8,6},{10,8},{12,10},{14,12},{1,15},{3,1}... | collective-permute-start | bytes 884744 | tf_op jit(solution)/shard_map/ppermute | solution.py:38
  102.2 13.8 %collective-permute-start.12 = (bf16[96,1536]{1,0:T(8,128)(2,1)S(1)}, bf16[96,1536]{1,0:T(8,128)(2,1)S(1)}, u32[]{:S(2)}, u32[]{:S(2)}) collective-permute-start(bf16[96,1536]{1,0:T(8,128)(2,1)S(1)} %get-tuple-element.16), channel_id=1, source_target_pairs={{0,12},{2,14},{4,0},{6,2},{8,4},{10,6},{12,8},{14,10},{1,13},{3,15... | collective-permute-start | bytes 884744 | tf_op jit(solution)/shard_map/ppermute | solution.py:38
  102.2 20.1 %collective-permute-start.13 = (bf16[96,1536]{1,0:T(8,128)(2,1)S(1)}, bf16[96,1536]{1,0:T(8,128)(2,1)S(1)}, u32[]{:S(2)}, u32[]{:S(2)}) collective-permute-start(bf16[96,1536]{1,0:T(8,128)(2,1)S(1)} %get-tuple-element.15), channel_id=1, source_target_pairs={{0,10},{2,12},{4,14},{6,0},{8,2},{10,4},{12,6},{14,8},{1,11},{3,13... | collective-permute-start | bytes 884744 | tf_op jit(solution)/shard_map/ppermute | solution.py:38
  102.6 51.4 %collective-permute-start.14 = (bf16[96,1536]{1,0:T(8,128)(2,1)S(1)}, bf16[96,1536]{1,0:T(8,128)(2,1)S(1)}, u32[]{:S(2)}, u32[]{:S(2)}) collective-permute-start(bf16[96,1536]{1,0:T(8,128)(2,1)S(1)} %get-tuple-element.14), channel_id=1, source_target_pairs={{0,8},{2,10},{4,12},{6,14},{8,0},{10,2},{12,4},{14,6},{1,9},{3,11}... | collective-permute-start | bytes 884744 | tf_op jit(solution)/shard_map/ppermute | solution.py:38
  105.1 48.9 %collective-permute-start.15 = (bf16[96,1536]{1,0:T(8,128)(2,1)S(1)}, bf16[96,1536]{1,0:T(8,128)(2,1)S(1)}, u32[]{:S(2)}, u32[]{:S(2)}) collective-permute-start(bf16[96,1536]{1,0:T(8,128)(2,1)S(1)} %get-tuple-element.13), channel_id=1, source_target_pairs={{0,6},{2,8},{4,10},{6,12},{8,14},{10,0},{12,2},{14,4},{1,7},{3,9},... | collective-permute-start | bytes 884744 | tf_op jit(solution)/shard_map/ppermute | solution.py:38
  109.6 44.5 %collective-permute-start.16 = (bf16[96,1536]{1,0:T(8,128)(2,1)S(1)}, bf16[96,1536]{1,0:T(8,128)(2,1)S(1)}, u32[]{:S(2)}, u32[]{:S(2)}) collective-permute-start(bf16[96,1536]{1,0:T(8,128)(2,1)S(1)} %get-tuple-element.12), channel_id=1, source_target_pairs={{0,4},{2,6},{4,8},{6,10},{8,12},{10,14},{12,0},{14,2},{1,5},{3,7},... | collective-permute-start | bytes 884744 | tf_op jit(solution)/shard_map/ppermute | solution.py:38
  115.9 38.2 %collective-permute-start.17 = (bf16[96,1536]{1,0:T(8,128)(2,1)S(1)}, bf16[96,1536]{1,0:T(8,128)(2,1)S(1)}, u32[]{:S(2)}, u32[]{:S(2)}) collective-permute-start(bf16[96,1536]{1,0:T(8,128)(2,1)S(1)} %get-tuple-element.11), channel_id=1, source_target_pairs={{0,2},{2,4},{4,6},{6,8},{8,10},{10,12},{12,14},{14,0},{1,3},{3,5},... | collective-permute-start | bytes 884744 | tf_op jit(solution)/shard_map/ppermute | solution.py:38
  157.3 2.4 %collective-permute-start.18 = (bf16[256,1536]{1,0:T(8,128)(2,1)S(1)}, bf16[256,1536]{1,0:T(8,128)(2,1)S(1)}, u32[]{:S(2)}, u32[]{:S(2)}) collective-permute-start(bf16[256,1536]{1,0:T(8,128)(2,1)S(1)} %multiply_reduce_fusion), channel_id=1, source_target_pairs={{0,1},{1,0},{2,3},{3,2},{4,5},{5,4},{6,7},{7,6},{8,9},{9,8},{10,11... | collective-permute-start | bytes 2359304 | tf_op jit(solution)/shard_map/ppermute | solution.py:26

commit v17 on v16

--- a/solution.py
+++ b/solution.py
@@ -73,16 +73,19 @@
     return ((up_val + 1.0) * gate_val * jax.nn.sigmoid(GLU_ALPHA * gate_val)).astype(jnp.bfloat16)
 
 
-def attention_kernel(sink_ref, q_ref, pk_ref, k_ref, pv_ref, v_ref, w_ref, o_ref, heads_ref):
+def attention_kernel(sink_ref, first_ref, q_ref, cached_ref, recv_ref, k_ref, v_ref, w_ref, o_ref, heads_ref):
     rows = q_ref.shape[0]
-    prior = pk_ref.shape[0]
+    prior = cached_ref.shape[1]
     span = 2 * WINDOW
     pair_cols = 2 * HEAD_DIM
     pairs = q_ref.shape[1] // pair_cols
     kv_count = k_ref.shape[1] // HEAD_DIM
     per_kv = pairs // kv_count
-    keys_all = jnp.concatenate([pk_ref[...], k_ref[...]], axis=0)
-    values_all = jnp.concatenate([pv_ref[...], v_ref[...]], axis=0)
+    first = first_ref[0] == 1
+    prior_keys = jnp.where(first, cached_ref[0], recv_ref[0])
+    prior_values = jnp.where(first, cached_ref[1], recv_ref[1])
+    keys_all = jnp.concatenate([prior_keys, k_ref[...]], axis=0)
+    values_all = jnp.concatenate([prior_values, v_ref[...]], axis=0)
     q_pos = lax.broadcasted_iota(jnp.int32, (WINDOW, span), 0)
     k_pos = lax.broadcasted_iota(jnp.int32, (WINDOW, span), 1)
     allowed = (k_pos > q_pos) & (k_pos <= q_pos + WINDOW)
@@ -125,7 +128,7 @@
     o_ref[...] = jnp.dot(heads_ref[...], w_ref[...], preferred_element_type=jnp.float32)
 
 
-def attend_kernel(queries, prior_keys, key_rows, prior_values, values, sink_logits, out_weight):
+def attend_kernel(queries, first_block, cached_rows, received, key_rows, values, sink_logits, out_weight):
     rows, cols = queries.shape
     heads = cols // HEAD_DIM
     span = 2 * WINDOW
@@ -140,11 +143,11 @@
     return pl.pallas_call(
         attention_kernel,
         out_shape=jax.ShapeDtypeStruct((rows, width), jnp.float32),
-        in_specs=[pl.BlockSpec(memory_space=pltpu.SMEM)] + [vmem] * 6,
+        in_specs=[pl.BlockSpec(memory_space=pltpu.SMEM)] * 2 + [vmem] * 6,
         out_specs=vmem,
         scratch_shapes=[pltpu.VMEM((rows, cols), jnp.bfloat16)],
         cost_estimate=cost,
-    )(sink_logits, queries, prior_keys, key_rows, prior_values, values, out_weight)
+    )(sink_logits, first_block, queries, cached_rows, received, key_rows, values, out_weight)
 
 
 def on_device(
@@ -165,8 +168,10 @@
     window_rows = WINDOW
     rim_rows = jnp.stack([key_rows[tok_rows - window_rows :], values[tok_rows - window_rows :]])
     received = shifted(rim_rows, "seq", 1)
-    prior = jnp.where(lax.axis_index("seq") == 0, cached_rows, received)
-    partial_rows = attend_kernel(queries, prior[0], key_rows, prior[1], values, sink_logits, out_weight)
+    first_block = (lax.axis_index("seq") == 0).astype(jnp.int32).reshape(1)
+    partial_rows = attend_kernel(
+        queries, first_block, cached_rows, received, key_rows, values, sink_logits, out_weight
+    )
     mixed_rows = residual.astype(jnp.float32) + (partial_rows + swap_exp(partial_rows))
     normed = rms_normalize(mixed_rows, norm_gain)
 

time: 161 us -> 161 us (level)
  no operation moved by 1% of the time
where the time goes in v17:
time: 161 us
  waiting for transfers between devices  77.9 us (48%)
  starting transfers between devices  45.9 us (29%)
  matrix products  15.6 us (10%)
  Pallas kernels  10.1 us (6%)
  other arithmetic  7.78 us (5%)
  local copies, waits for them, and re-layouts  3.14 us (2%)
    ppermute x14, waiting for transfers between devices, shift_exchange(): out.append(lax.ppermute(blocks[step], 'seq', pairs))  71.6 us
    ppermute x14, starting transfers between devices, shift_exchange(): out.append(lax.ppermute(blocks[step], 'seq', pairs))  40.3 us
    pallas_call x1, Pallas kernels, attend_kernel(): pl.pallas_call(attention_kernel, out_shape=jax.ShapeDtypeStruct((rows, wi...  10.1 us
    dot_general x2, matrix products, expert_hidden(): jnp.einsum('rd,kdf->krf', rows, expert_in, preferred_element_type=jnp.flo...  7.62 us
    ppermute x1, starting transfers between devices, shifted(): return lax.ppermute(shard, axis, pairs)  4.87 us
    ppermute x4, waiting for transfers between devices, swap_exp(): return lax.ppermute(x, 'exp', [(i, (i + 1) % size) for i in range(size)])  4.44 us
  transfers between devices with their start and end apart: 19, of which 11 were waited for; matrix products, arithmetic and copies ran while one was open for 7% of the time, Pallas kernels for 0%

profile of v17, /device:TPU:0, one launch (start us, length us, event | category | flops | bytes accessed | tf_op | source)
XLA Modules:
  0.0 160.9 jit_solution(2776560428806699023)
XLA Ops:
  0.0 0.9 slice_bitcast_fusion.8
  0.9 4.9 %collective-permute-start = (bf16[2,128,128]{2,1,0:T(8,128)(2,1)S(1)}, bf16[2,128,128]{2,1,0:T(8,128)(2,1)S(1)}, u32[]{:S(2)}, u32[]{:S(2)}) collective-permute-start(bf16[2,128,128]{2,1,0:T(8,128)(2,1)S(1)} %pad_maximum_fusion), channel_id=1, source_target_pairs={{0,2},{2,4},{4,6},{6,8},{8,10},{10,12},{12,14},{1,3},{3,5},{5,7},{... | collective-permute-start | bytes 196616 | tf_op jit(solution)/shard_map/ppermute | solution.py:21
  5.8 1.9 %collective-permute-done.recv_ref = bf16[2,128,128]{2,1,0:T(8,128)(2,1)S(1)} collective-permute-done((bf16[2,128,128]{2,1,0:T(8,128)(2,1)S(1)}, bf16[2,128,128]{2,1,0:T(8,128)(2,1)S(1)}, u32[]{:S(2)}, u32[]{:S(2)}) %collective-permute-start) | collective-permute-done | bytes 65568 | tf_op jit(solution)/shard_map/ppermute | solution.py:21
  7.7 0.6 copy-done.2
  8.3 10.1 %shard_map.118 = f32[256,1536]{1,0:T(8,128)} custom-call(f32[16]{0:T(128)} %sink_ref.1, s32[1]{0:T(128)} %bitcast.first_ref, bf16[256,1024]{1,0:T(8,128)(2,1)} %q_ref.1, bf16[2,128,128]{2,1,0:T(8,128)(2,1)} %cached_ref.1, bf16[2,128,128]{2,1,0:T(8,128)(2,1)} %copy-done.2, bf16[256,128]{1,0:T(8,128)(2,1)} %k_ref.1, bf16[256,128]{1,0:T(8,128)(2,1)} %v_ref.1, ...), custom_call_target="tpu_custom_call" | custom-call | flops 1342177280 | bytes 5439488 | tf_op jit(solution)/shard_map/pallas_call | solution.py:143
  18.4 0.0 collective-permute-start.1
  18.5 0.1 copy.33
  18.6 0.1 eq.71
  18.7 0.1 eq.67
  18.8 2.3 %reduce-window.6 = s32[8,8,128]{2,1,0:T(8,128)S(1)} reduce-window(s32[8,8,128]{2,1,0:T(8,128)S(1)} %fusion.33, s32[]{:T(128)} %constant.19.clone.1), window={size=1x1x128 pad=0_0x0_0x127_0}, to_apply=%region_0.0 | reduce-window | flops 1040384 | bytes 65540 | tf_op jit(solution)/shard_map/reduce-window
  21.1 0.3 slice_reduce_fusion
  21.4 0.2 reduce-window.9
  21.6 0.1 add_bitcast_fusion
  21.7 0.1 sub.36
  21.8 0.1 copy.35
  21.9 0.4 fusion.22
  22.4 0.0 copy-start.4
  22.4 0.0 collective-permute-done.1
  22.4 2.2 %multiply_reduce_fusion.1 = (f32[256]{0:T(256)S(1)}, f32[256,1536]{1,0:T(8,128)S(1)}) fusion(f32[256,1536]{1,0:T(8,128)} %shard_map.118, f32[256,1536]{1,0:T(8,128)} %collective-permute-done.1, bf16[256,1536]{1,0:T(8,128)(2,1)S(1)} %copy-done.1), kind=kLoop, calls=%fused_computation.29 | loop fusion | flops 1965824 | bytes 5506048 | tf_op jit(solution)/shard_map/reduce_sum | solution.py:43
  24.6 0.0 slice-start
  24.7 0.9 convolution_convert_fusion.2
  25.6 0.0 slice-start.1
  25.6 0.1 fusion.40
  25.7 2.4 %collective-permute-start.2 = (bf16[96,1536]{1,0:T(8,128)(2,1)S(1)}, bf16[96,1536]{1,0:T(8,128)(2,1)S(1)}, u32[]{:S(2)}, u32[]{:S(2)}) collective-permute-start(bf16[96,1536]{1,0:T(8,128)(2,1)S(1)} %get-tuple-element.25), channel_id=1, source_target_pairs={{0,2},{2,4},{4,6},{6,8},{8,10},{10,12},{12,14},{14,0},{1,3},{3,5},... | collective-permute-start | bytes 884744 | tf_op jit(solution)/shard_map/ppermute | solution.py:38
  28.1 1.6 collective-permute-start.3
  29.7 3.4 %collective-permute-start.4 = (bf16[96,1536]{1,0:T(8,128)(2,1)S(1)}, bf16[96,1536]{1,0:T(8,128)(2,1)S(1)}, u32[]{:S(2)}, u32[]{:S(2)}) collective-permute-start(bf16[96,1536]{1,0:T(8,128)(2,1)S(1)} %get-tuple-element.23), channel_id=1, source_target_pairs={{0,6},{2,8},{4,10},{6,12},{8,14},{10,0},{12,2},{14,4},{1,7},{3,9},... | collective-permute-start | bytes 884744 | tf_op jit(solution)/shard_map/ppermute | solution.py:38
  33.1 1.2 collective-permute-start.5
  34.4 1.7 %collective-permute-start.6 = (bf16[96,1536]{1,0:T(8,128)(2,1)S(1)}, bf16[96,1536]{1,0:T(8,128)(2,1)S(1)}, u32[]{:S(2)}, u32[]{:S(2)}) collective-permute-start(bf16[96,1536]{1,0:T(8,128)(2,1)S(1)} %get-tuple-element.21), channel_id=1, source_target_pairs={{0,10},{2,12},{4,14},{6,0},{8,2},{10,4},{12,6},{14,8},{1,11},{3,13... | collective-permute-start | bytes 884744 | tf_op jit(solution)/shard_map/ppermute | solution.py:38
  36.1 3.1 %collective-permute-done.2 = bf16[96,1536]{1,0:T(8,128)(2,1)S(1)} collective-permute-done((bf16[96,1536]{1,0:T(8,128)(2,1)S(1)}, bf16[96,1536]{1,0:T(8,128)(2,1)S(1)}, u32[]{:S(2)}, u32[]{:S(2)}) %collective-permute-start.2) | collective-permute-done | bytes 294944 | tf_op jit(solution)/shard_map/ppermute | solution.py:38
  39.2 2.6 %collective-permute-start.7 = (bf16[96,1536]{1,0:T(8,128)(2,1)S(1)}, bf16[96,1536]{1,0:T(8,128)(2,1)S(1)}, u32[]{:S(2)}, u32[]{:S(2)}) collective-permute-start(bf16[96,1536]{1,0:T(8,128)(2,1)S(1)} %get-tuple-element.20), channel_id=1, source_target_pairs={{0,12},{2,14},{4,0},{6,2},{8,4},{10,6},{12,8},{14,10},{1,13},{3,15... | collective-permute-start | bytes 884744 | tf_op jit(solution)/shard_map/ppermute | solution.py:38
  41.8 0.0 collective-permute-done.3
  41.8 6.0 %collective-permute-start.8 = (bf16[96,1536]{1,0:T(8,128)(2,1)S(1)}, bf16[96,1536]{1,0:T(8,128)(2,1)S(1)}, u32[]{:S(2)}, u32[]{:S(2)}) collective-permute-start(bf16[96,1536]{1,0:T(8,128)(2,1)S(1)} %get-tuple-element.19), channel_id=1, source_target_pairs={{0,14},{2,0},{4,2},{6,4},{8,6},{10,8},{12,10},{14,12},{1,15},{3,1}... | collective-permute-start | bytes 884744 | tf_op jit(solution)/shard_map/ppermute | solution.py:38
  47.9 16.3 %collective-permute-done.4 = bf16[96,1536]{1,0:T(8,128)(2,1)S(1)} collective-permute-done((bf16[96,1536]{1,0:T(8,128)(2,1)S(1)}, bf16[96,1536]{1,0:T(8,128)(2,1)S(1)}, u32[]{:S(2)}, u32[]{:S(2)}) %collective-permute-start.4) | collective-permute-done | bytes 294944 | tf_op jit(solution)/shard_map/ppermute | solution.py:38
  64.3 0.3 collective-permute-done.5
  64.6 0.0 collective-permute-done.6
  64.6 0.0 collective-permute-done.7
  64.6 3.4 %collective-permute-done.8 = bf16[96,1536]{1,0:T(8,128)(2,1)S(1)} collective-permute-done((bf16[96,1536]{1,0:T(8,128)(2,1)S(1)}, bf16[96,1536]{1,0:T(8,128)(2,1)S(1)}, u32[]{:S(2)}, u32[]{:S(2)}) %collective-permute-start.8) | collective-permute-done | bytes 294944 | tf_op jit(solution)/shard_map/ppermute | solution.py:38
  68.0 0.1 collective-permute-start.9
  68.1 3.8 %fusion.16 = f32[2,768,768]{2,1,0:T(8,128)S(1)} fusion(bf16[768,1536,1]{1,0,2:T(8,128)(2,1)S(1)} %bitcast.111, bf16[1,2,1536,768]{3,2,1,0:T(8,128)(2,1)S(1)} %bitcast.114), kind=kOutput, calls=%fused_computation.24 | convolution fusion | flops 3623878656 | bytes 11796480 | tf_op jit(solution)/shard_map/rd,kdf->krf/dot_general | solution.py:70
  71.9 0.7 fusion.27
  72.6 0.0 collective-permute-done.9
  72.6 3.8 %fusion.19 = f32[2,768,768]{2,1,0:T(8,128)S(1)} fusion(bf16[768,1536,1]{1,0,2:T(8,128)(2,1)S(1)} %bitcast.115, bf16[1,2,1536,768]{3,2,1,0:T(8,128)(2,1)S(1)} %bitcast.114), kind=kOutput, calls=%fused_computation.25 | convolution fusion | flops 3623878656 | bytes 11796480 | tf_op jit(solution)/shard_map/rd,kdf->krf/dot_general | solution.py:70
  76.5 2.1 %convolution_convert_fusion = bf16[768,1536]{1,0:T(8,128)(2,1)S(1)} fusion(bf16[1,768,1536]{2,1,0:T(8,128)(2,1)S(1)} %copy-done, f32[2,768,768]{2,1,0:T(8,128)S(1)} %fusion.19), kind=kOutput, calls=%fused_computation.7 | convolution fusion | flops 1817837568 | bytes 9437184 | tf_op jit(solution)/shard_map/dot_general | solution.py:208
  78.5 0.5 collective-permute-start.10
  79.1 2.0 %convolution_convert_fusion.1 = bf16[768,1536]{1,0:T(8,128)(2,1)S(1)} fusion(bf16[768,768]{1,0:T(8,128)(2,1)S(1)} %fusion.27, bf16[1,768,1536]{2,1,0:T(8,128)(2,1)S(1)} %copy-done), kind=kOutput, calls=%fused_computation.8 | convolution fusion | flops 1813118976 | bytes 5898240 | tf_op jit(solution)/shard_map/dot_general | solution.py:213
  81.1 2.2 %collective-permute-done.10 = bf16[8,96,1536]{2,1,0:T(8,128)(2,1)S(1)} collective-permute-done((bf16[8,96,1536]{2,1,0:T(8,128)(2,1)S(1)}, bf16[8,96,1536]{2,1,0:T(8,128)(2,1)S(1)}, u32[]{:S(2)}, u32[]{:S(2)}) %collective-permute-start.10) | collective-permute-done | bytes 2359328 | tf_op jit(solution)/shard_map/ppermute | solution.py:26
  83.2 0.7 fusion
  83.9 0.2 slice_bitcast_fusion
  84.1 0.0 copy-start.5
  84.2 18.0 %collective-permute-start.11 = (bf16[96,1536]{1,0:T(8,128)(2,1)S(1)}, bf16[96,1536]{1,0:T(8,128)(2,1)S(1)}, u32[]{:S(2)}, u32[]{:S(2)}) collective-permute-start(bf16[96,1536]{1,0:T(8,128)(2,1)S(1)} %get-tuple-element.17), channel_id=1, source_target_pairs={{0,14},{2,0},{4,2},{6,4},{8,6},{10,8},{12,10},{14,12},{1,15},{3,1}... | collective-permute-start | bytes 884744 | tf_op jit(solution)/shard_map/ppermute | solution.py:38
  102.2 0.0 collective-permute-start.12
  102.2 0.4 collective-permute-start.13
  102.6 2.6 %collective-permute-start.14 = (bf16[96,1536]{1,0:T(8,128)(2,1)S(1)}, bf16[96,1536]{1,0:T(8,128)(2,1)S(1)}, u32[]{:S(2)}, u32[]{:S(2)}) collective-permute-start(bf16[96,1536]{1,0:T(8,128)(2,1)S(1)} %get-tuple-element.14), channel_id=1, source_target_pairs={{0,8},{2,10},{4,12},{6,14},{8,0},{10,2},{12,4},{14,6},{1,9},{3,11}... | collective-permute-start | bytes 884744 | tf_op jit(solution)/shard_map/ppermute | solution.py:38
  105.2 0.3 collective-permute-start.15
  105.5 4.1 %collective-permute-done.11 = bf16[96,1536]{1,0:T(8,128)(2,1)S(1)} collective-permute-done((bf16[96,1536]{1,0:T(8,128)(2,1)S(1)}, bf16[96,1536]{1,0:T(8,128)(2,1)S(1)}, u32[]{:S(2)}, u32[]{:S(2)}) %collective-permute-start.11) | collective-permute-done | bytes 294944 | tf_op jit(solution)/shard_map/ppermute | solution.py:38
  109.6 0.0 collective-permute-start.16
  109.7 6.3 %collective-permute-done.12 = bf16[96,1536]{1,0:T(8,128)(2,1)S(1)} collective-permute-done((bf16[96,1536]{1,0:T(8,128)(2,1)S(1)}, bf16[96,1536]{1,0:T(8,128)(2,1)S(1)}, u32[]{:S(2)}, u32[]{:S(2)}) %collective-permute-start.12) | collective-permute-done | bytes 294944 | tf_op jit(solution)/shard_map/ppermute | solution.py:38
  116.0 6.3 %collective-permute-done.13 = bf16[96,1536]{1,0:T(8,128)(2,1)S(1)} collective-permute-done((bf16[96,1536]{1,0:T(8,128)(2,1)S(1)}, bf16[96,1536]{1,0:T(8,128)(2,1)S(1)}, u32[]{:S(2)}, u32[]{:S(2)}) %collective-permute-start.13) | collective-permute-done | bytes 294944 | tf_op jit(solution)/shard_map/ppermute | solution.py:38
  122.3 31.8 %collective-permute-done.14 = bf16[96,1536]{1,0:T(8,128)(2,1)S(1)} collective-permute-done((bf16[96,1536]{1,0:T(8,128)(2,1)S(1)}, bf16[96,1536]{1,0:T(8,128)(2,1)S(1)}, u32[]{:S(2)}, u32[]{:S(2)}) %collective-permute-start.14) | collective-permute-done | bytes 294944 | tf_op jit(solution)/shard_map/ppermute | solution.py:38
  154.1 0.0 collective-permute-done.15
  154.2 3.1 %multiply_reduce_fusion = bf16[256,1536]{1,0:T(8,128)(2,1)S(1)} fusion(bf16[768,1536,1]{1,0,2:T(8,128)(2,1)S(1)} %bitcast.110, f32[256,4]{0,1:T(4,128)S(1)} %copy-done.5, s32[256,4]{0,1:T(4,128)S(1)} %fusion.37), kind=kOutput, calls=%fused_computation | convolution fusion | flops 2419458048 | bytes 3153920 | tf_op jit(solution)/shard_map/dot_general | solution.py:219
  157.3 0.1 collective-permute-start.18
  157.4 2.3 %collective-permute-done.18 = bf16[256,1536]{1,0:T(8,128)(2,1)S(1)} collective-permute-done((bf16[256,1536]{1,0:T(8,128)(2,1)S(1)}, bf16[256,1536]{1,0:T(8,128)(2,1)S(1)}, u32[]{:S(2)}, u32[]{:S(2)}) %collective-permute-start.18) | collective-permute-done | bytes 786464 | tf_op jit(solution)/shard_map/ppermute | solution.py:26
  159.7 1.2 add_convert_fusion
  (36 shorter events, 0.4 us)
Async XLA Ops:
  0.0 76.4 %copy-start = (bf16[1,768,1536]{2,1,0:T(8,128)(2,1)S(1)}, bf16[1,768,1536]{2,1,0:T(8,128)(2,1)}, u32[]{:S(2)}) copy-start(bf16[1,768,1536]{2,1,0:T(8,128)(2,1)} %param.21) | copy-start | bytes 7077892
  0.9 6.8 %collective-permute-start = (bf16[2,128,128]{2,1,0:T(8,128)(2,1)S(1)}, bf16[2,128,128]{2,1,0:T(8,128)(2,1)S(1)}, u32[]{:S(2)}, u32[]{:S(2)}) collective-permute-start(bf16[2,128,128]{2,1,0:T(8,128)(2,1)S(1)} %pad_maximum_fusion), channel_id=1, source_target_pairs={{0,2},{2,4},{4,6},{6,8},{8,10},{10,12},{12,14},{1,3},{3,5},{5,7},{... | collective-permute-start | bytes 196616 | tf_op jit(solution)/shard_map/ppermute | solution.py:21
  7.7 0.6 copy-start.2
  8.3 10.1 %copy-start.3 = (s32[256,4]{0,1:T(4,128)S(1)}, s32[256,4]{0,1:T(4,128)}, u32[]{:S(2)}) copy-start(s32[256,4]{0,1:T(4,128)} %param.22) | copy-start | bytes 12292
  8.3 14.1 %copy-start.1 = (bf16[256,1536]{1,0:T(8,128)(2,1)S(1)}, bf16[256,1536]{1,0:T(8,128)(2,1)}, u32[]{:S(2)}) copy-start(bf16[256,1536]{1,0:T(8,128)(2,1)} %param.18) | copy-start | bytes 2359300
  18.4 3.9 %collective-permute-start.1 = (f32[256,1536]{1,0:T(8,128)}, f32[256,1536]{1,0:T(8,128)}, u32[]{:S(2)}, u32[]{:S(2)}) collective-permute-start(f32[256,1536]{1,0:T(8,128)} %shard_map.118), channel_id=1, source_target_pairs={{0,1},{1,0},{2,3},{3,2},{4,5},{5,4},{6,7},{7,6},{8,9},{9,8},{10,11... | collective-permute-start | bytes 4718600 | tf_op jit(solution)/shard_map/ppermute | solution.py:26
  22.4 2.3 %copy-start.4 = (f32[1536]{0:T(1024)S(1)}, f32[1536]{0:T(1024)}, u32[]{:S(2)}) copy-start(f32[1536]{0:T(1024)} %param.19) | copy-start | bytes 18436
  24.6 43.5 %slice-start = ((s8[4718592]{0:T(1024)(128)(4,1)}), s8[4194304]{0:T(1024)(128)(4,1)S(1)}, s32[]{:S(2)}) async-start(s8[4718592]{0:T(1024)(128)(4,1)} %bitcast.113), calls=%async_computation | async-start | bytes 8388608
  25.6 42.6 %slice-start.1 = ((s8[4718592]{0:T(1024)(128)(4,1)}), s8[524288]{0:T(1024)(128)(4,1)S(1)}, s32[]{:S(2)}) async-start(s8[4718592]{0:T(1024)(128)(4,1)} %bitcast.113), calls=%async_computation.1 | async-start | bytes 1048576
  25.7 13.5 %collective-permute-start.2 = (bf16[96,1536]{1,0:T(8,128)(2,1)S(1)}, bf16[96,1536]{1,0:T(8,128)(2,1)S(1)}, u32[]{:S(2)}, u32[]{:S(2)}) collective-permute-start(bf16[96,1536]{1,0:T(8,128)(2,1)S(1)} %get-tuple-element.25), channel_id=1, source_target_pairs={{0,2},{2,4},{4,6},{6,8},{8,10},{10,12},{12,14},{14,0},{1,3},{3,5},... | collective-permute-start | bytes 884744 | tf_op jit(solution)/shard_map/ppermute | solution.py:38
  28.1 13.7 %collective-permute-start.3 = (bf16[96,1536]{1,0:T(8,128)(2,1)S(1)}, bf16[96,1536]{1,0:T(8,128)(2,1)S(1)}, u32[]{:S(2)}, u32[]{:S(2)}) collective-permute-start(bf16[96,1536]{1,0:T(8,128)(2,1)S(1)} %get-tuple-element.24), channel_id=1, source_target_pairs={{0,4},{2,6},{4,8},{6,10},{8,12},{10,14},{12,0},{14,2},{1,5},{3,7},... | collective-permute-start | bytes 884744 | tf_op jit(solution)/shard_map/ppermute | solution.py:38
  29.7 34.6 %collective-permute-start.4 = (bf16[96,1536]{1,0:T(8,128)(2,1)S(1)}, bf16[96,1536]{1,0:T(8,128)(2,1)S(1)}, u32[]{:S(2)}, u32[]{:S(2)}) collective-permute-start(bf16[96,1536]{1,0:T(8,128)(2,1)S(1)} %get-tuple-element.23), channel_id=1, source_target_pairs={{0,6},{2,8},{4,10},{6,12},{8,14},{10,0},{12,2},{14,4},{1,7},{3,9},... | collective-permute-start | bytes 884744 | tf_op jit(solution)/shard_map/ppermute | solution.py:38
  33.1 31.4 %collective-permute-start.5 = (bf16[96,1536]{1,0:T(8,128)(2,1)S(1)}, bf16[96,1536]{1,0:T(8,128)(2,1)S(1)}, u32[]{:S(2)}, u32[]{:S(2)}) collective-permute-start(bf16[96,1536]{1,0:T(8,128)(2,1)S(1)} %get-tuple-element.22), channel_id=1, source_target_pairs={{0,8},{2,10},{4,12},{6,14},{8,0},{10,2},{12,4},{14,6},{1,9},{3,11}... | collective-permute-start | bytes 884744 | tf_op jit(solution)/shard_map/ppermute | solution.py:38
  34.4 30.2 %collective-permute-start.6 = (bf16[96,1536]{1,0:T(8,128)(2,1)S(1)}, bf16[96,1536]{1,0:T(8,128)(2,1)S(1)}, u32[]{:S(2)}, u32[]{:S(2)}) collective-permute-start(bf16[96,1536]{1,0:T(8,128)(2,1)S(1)} %get-tuple-element.21), channel_id=1, source_target_pairs={{0,10},{2,12},{4,14},{6,0},{8,2},{10,4},{12,6},{14,8},{1,11},{3,13... | collective-permute-start | bytes 884744 | tf_op jit(solution)/shard_map/ppermute | solution.py:38
  39.2 25.4 %collective-permute-start.7 = (bf16[96,1536]{1,0:T(8,128)(2,1)S(1)}, bf16[96,1536]{1,0:T(8,128)(2,1)S(1)}, u32[]{:S(2)}, u32[]{:S(2)}) collective-permute-start(bf16[96,1536]{1,0:T(8,128)(2,1)S(1)} %get-tuple-element.20), channel_id=1, source_target_pairs={{0,12},{2,14},{4,0},{6,2},{8,4},{10,6},{12,8},{14,10},{1,13},{3,15... | collective-permute-start | bytes 884744 | tf_op jit(solution)/shard_map/ppermute | solution.py:38
  41.8 26.2 %collective-permute-start.8 = (bf16[96,1536]{1,0:T(8,128)(2,1)S(1)}, bf16[96,1536]{1,0:T(8,128)(2,1)S(1)}, u32[]{:S(2)}, u32[]{:S(2)}) collective-permute-start(bf16[96,1536]{1,0:T(8,128)(2,1)S(1)} %get-tuple-element.19), channel_id=1, source_target_pairs={{0,14},{2,0},{4,2},{6,4},{8,6},{10,8},{12,10},{14,12},{1,15},{3,1}... | collective-permute-start | bytes 884744 | tf_op jit(solution)/shard_map/ppermute | solution.py:38
  68.0 4.6 %collective-permute-start.9 = (bf16[8,96,1536]{2,1,0:T(8,128)(2,1)S(1)}, bf16[8,96,1536]{2,1,0:T(8,128)(2,1)S(1)}, u32[]{:S(2)}, u32[]{:S(2)}) collective-permute-start(bf16[8,96,1536]{2,1,0:T(8,128)(2,1)S(1)} %bitcast_dynamic-update-slice_fusion.7), channel_id=1, source_target_pairs={{0,1},{1,0},{2,3},{3,2},{4,5},{5,4},{6,7},{7,6},{8,9},{9,8},{10,11... | collective-permute-start | bytes 7077896 | tf_op jit(solution)/shard_map/ppermute | solution.py:26
  78.5 4.7 %collective-permute-start.10 = (bf16[8,96,1536]{2,1,0:T(8,128)(2,1)S(1)}, bf16[8,96,1536]{2,1,0:T(8,128)(2,1)S(1)}, u32[]{:S(2)}, u32[]{:S(2)}) collective-permute-start(bf16[8,96,1536]{2,1,0:T(8,128)(2,1)S(1)} %bitcast.116), channel_id=1, source_target_pairs={{0,1},{1,0},{2,3},{3,2},{4,5},{5,4},{6,7},{7,6},{8,9},{9,8},{10,11... | collective-permute-start | bytes 7077896 | tf_op jit(solution)/shard_map/ppermute | solution.py:26
  84.1 70.1 %copy-start.5 = (f32[256,4]{0,1:T(4,128)S(1)}, f32[256,4]{0,1:T(4,128)}, u32[]{:S(2)}) copy-start(f32[256,4]{0,1:T(4,128)} %param.23) | copy-start | bytes 12292
  84.2 25.5 %collective-permute-start.11 = (bf16[96,1536]{1,0:T(8,128)(2,1)S(1)}, bf16[96,1536]{1,0:T(8,128)(2,1)S(1)}, u32[]{:S(2)}, u32[]{:S(2)}) collective-permute-start(bf16[96,1536]{1,0:T(8,128)(2,1)S(1)} %get-tuple-element.17), channel_id=1, source_target_pairs={{0,14},{2,0},{4,2},{6,4},{8,6},{10,8},{12,10},{14,12},{1,15},{3,1}... | collective-permute-start | bytes 884744 | tf_op jit(solution)/shard_map/ppermute | solution.py:38
  102.2 13.8 %collective-permute-start.12 = (bf16[96,1536]{1,0:T(8,128)(2,1)S(1)}, bf16[96,1536]{1,0:T(8,128)(2,1)S(1)}, u32[]{:S(2)}, u32[]{:S(2)}) collective-permute-start(bf16[96,1536]{1,0:T(8,128)(2,1)S(1)} %get-tuple-element.16), channel_id=1, source_target_pairs={{0,12},{2,14},{4,0},{6,2},{8,4},{10,6},{12,8},{14,10},{1,13},{3,15... | collective-permute-start | bytes 884744 | tf_op jit(solution)/shard_map/ppermute | solution.py:38
  102.2 20.1 %collective-permute-start.13 = (bf16[96,1536]{1,0:T(8,128)(2,1)S(1)}, bf16[96,1536]{1,0:T(8,128)(2,1)S(1)}, u32[]{:S(2)}, u32[]{:S(2)}) collective-permute-start(bf16[96,1536]{1,0:T(8,128)(2,1)S(1)} %get-tuple-element.15), channel_id=1, source_target_pairs={{0,10},{2,12},{4,14},{6,0},{8,2},{10,4},{12,6},{14,8},{1,11},{3,13... | collective-permute-start | bytes 884744 | tf_op jit(solution)/shard_map/ppermute | solution.py:38
  102.6 51.4 %collective-permute-start.14 = (bf16[96,1536]{1,0:T(8,128)(2,1)S(1)}, bf16[96,1536]{1,0:T(8,128)(2,1)S(1)}, u32[]{:S(2)}, u32[]{:S(2)}) collective-permute-start(bf16[96,1536]{1,0:T(8,128)(2,1)S(1)} %get-tuple-element.14), channel_id=1, source_target_pairs={{0,8},{2,10},{4,12},{6,14},{8,0},{10,2},{12,4},{14,6},{1,9},{3,11}... | collective-permute-start | bytes 884744 | tf_op jit(solution)/shard_map/ppermute | solution.py:38
  105.2 48.9 %collective-permute-start.15 = (bf16[96,1536]{1,0:T(8,128)(2,1)S(1)}, bf16[96,1536]{1,0:T(8,128)(2,1)S(1)}, u32[]{:S(2)}, u32[]{:S(2)}) collective-permute-start(bf16[96,1536]{1,0:T(8,128)(2,1)S(1)} %get-tuple-element.13), channel_id=1, source_target_pairs={{0,6},{2,8},{4,10},{6,12},{8,14},{10,0},{12,2},{14,4},{1,7},{3,9},... | collective-permute-start | bytes 884744 | tf_op jit(solution)/shard_map/ppermute | solution.py:38
  109.6 44.5 %collective-permute-start.16 = (bf16[96,1536]{1,0:T(8,128)(2,1)S(1)}, bf16[96,1536]{1,0:T(8,128)(2,1)S(1)}, u32[]{:S(2)}, u32[]{:S(2)}) collective-permute-start(bf16[96,1536]{1,0:T(8,128)(2,1)S(1)} %get-tuple-element.12), channel_id=1, source_target_pairs={{0,4},{2,6},{4,8},{6,10},{8,12},{10,14},{12,0},{14,2},{1,5},{3,7},... | collective-permute-start | bytes 884744 | tf_op jit(solution)/shard_map/ppermute | solution.py:38
  115.9 38.2 %collective-permute-start.17 = (bf16[96,1536]{1,0:T(8,128)(2,1)S(1)}, bf16[96,1536]{1,0:T(8,128)(2,1)S(1)}, u32[]{:S(2)}, u32[]{:S(2)}) collective-permute-start(bf16[96,1536]{1,0:T(8,128)(2,1)S(1)} %get-tuple-element.11), channel_id=1, source_target_pairs={{0,2},{2,4},{4,6},{6,8},{8,10},{10,12},{12,14},{14,0},{1,3},{3,5},... | collective-permute-start | bytes 884744 | tf_op jit(solution)/shard_map/ppermute | solution.py:38
  157.3 2.4 %collective-permute-start.18 = (bf16[256,1536]{1,0:T(8,128)(2,1)S(1)}, bf16[256,1536]{1,0:T(8,128)(2,1)S(1)}, u32[]{:S(2)}, u32[]{:S(2)}) collective-permute-start(bf16[256,1536]{1,0:T(8,128)(2,1)S(1)} %multiply_reduce_fusion), channel_id=1, source_target_pairs={{0,1},{1,0},{2,3},{3,2},{4,5},{5,4},{6,7},{7,6},{8,9},{9,8},{10,11... | collective-permute-start | bytes 2359304 | tf_op jit(solution)/shard_map/ppermute | solution.py:26

commit v18 on v17

--- a/solution.py
+++ b/solution.py
@@ -28,6 +28,17 @@
 
 def seq_all_to_all(blocks):
     return lax.all_to_all(blocks, "seq", split_axis=0, concat_axis=0, tiled=True)
+
+
+def return_exchange(blocks):
+    size = lax.axis_size("seq")
+    me = lax.axis_index("seq")
+    out = [lax.dynamic_index_in_dim(blocks, me, 0, keepdims=False)]
+    for step in range(1, size):
+        pairs = [(i, (i - step) % size) for i in range(size)]
+        source = lax.dynamic_index_in_dim(blocks, (me - step) % size, 0, keepdims=False)
+        out.append(lax.ppermute(source, "seq", pairs))
+    return jnp.stack(out)
 
 
 def shift_exchange(blocks, sign):
@@ -190,16 +201,18 @@
     mine = (local_rank >= 0) & (local_rank < half)
     by_shift = experts <= SHIFT_LIMIT
     offset = (flat_experts - lax.axis_index("seq")) % experts if by_shift else flat_experts
-    slot_id = jnp.where(mine, offset * half + local_rank, -1)
+    slot_id = jnp.where(mine, flat_experts * half + local_rank, -1)
+    back_id = jnp.where(mine, offset * half + local_rank, -1)
     slot_iota = jnp.arange(slots, dtype=jnp.int32)
     pick = (slot_id[:, None] == slot_iota[None, :]).astype(jnp.bfloat16)
+    back_pick = (back_id[:, None] == slot_iota[None, :]).astype(jnp.bfloat16)
     select = jnp.max(pick.reshape(tok_rows, TOP, slots), axis=1).T
     outgoing = (
         jnp.dot(select, normed, preferred_element_type=jnp.float32)
         .astype(jnp.bfloat16)
         .reshape(experts, half, width)
     )
-    slot_rows = shift_exchange(outgoing, 1) if by_shift else seq_all_to_all(outgoing)
+    slot_rows = seq_all_to_all(outgoing)
     other_rows = swap_exp(slot_rows)
     own_hidden = expert_hidden(slot_rows.reshape(-1, width), expert_in[0])
     own_hidden, other_rows = lax.optimization_barrier((own_hidden, other_rows))
@@ -215,8 +228,8 @@
         .reshape(experts, half, width)
     )
     result = (own_part.astype(jnp.float32) + their_part.astype(jnp.float32)).astype(jnp.bfloat16)
-    returned = shift_exchange(result, -1) if by_shift else seq_all_to_all(result)
-    picked = jnp.dot(pick, returned.reshape(slots, width), preferred_element_type=jnp.float32)
+    returned = return_exchange(result) if by_shift else seq_all_to_all(result)
+    picked = jnp.dot(back_pick, returned.reshape(slots, width), preferred_element_type=jnp.float32)
     weighted = jnp.sum(picked.reshape(tok_rows, TOP, width) * route_gates[:, :, None], axis=1)
     rounded = weighted.astype(jnp.bfloat16)
     moe = rounded.astype(jnp.float32) + swap_exp(rounded).astype(jnp.float32)

time: 161 us -> 168 us (1.043)
  blocking collectives: 0 us -> 60.9 us
  starting transfers between devices: 45.9 us -> 13.4 us
  waiting for transfers between devices: 77.9 us -> 53.9 us
  other arithmetic: 7.78 us -> 9.59 us
    all_to_all x0 -> x1, blocking collectives: none -> 60.9 us  [seq_all_to_all(): lax.all_to_all(blocks, 'seq', split_axis=0, concat_axis=0, tiled=True)]
    ppermute x14 -> x7, starting transfers between devices: 40.3 us -> 7.97 us  [return_exchange(): out.append(lax.ppermute(source, 'seq', pairs))]
    ppermute x14 -> x7, waiting for transfers between devices: 71.6 us -> 47.2 us  [return_exchange(): out.append(lax.ppermute(source, 'seq', pairs))]
  transfers between devices with their start and end apart: 19 -> 12, of which waited for: 11 -> 8; matrix products, arithmetic and copies ran while one was open for 7% -> 6% of each run, Pallas kernels for 0% -> 0%
where the time goes in v18:
time: 168 us
  blocking collectives  60.9 us (36%)
  waiting for transfers between devices  53.9 us (32%)
  matrix products  17.1 us (10%)
  starting transfers between devices  13.4 us (8%)
  Pallas kernels  10.1 us (6%)
  other arithmetic  9.59 us (6%)
  local copies, waits for them, and re-layouts  2.86 us (2%)
    all_to_all x1, blocking collectives, seq_all_to_all(): lax.all_to_all(blocks, 'seq', split_axis=0, concat_axis=0, tiled=True)  60.9 us
    ppermute x7, waiting for transfers between devices, return_exchange(): out.append(lax.ppermute(source, 'seq', pairs))  47.2 us
    pallas_call x1, Pallas kernels, attend_kernel(): pl.pallas_call(attention_kernel, out_shape=jax.ShapeDtypeStruct((rows, wi...  10.1 us
    ppermute x7, starting transfers between devices, return_exchange(): out.append(lax.ppermute(source, 'seq', pairs))  7.97 us
    dot_general x2, matrix products, expert_hidden(): jnp.einsum('rd,kdf->krf', rows, expert_in, preferred_element_type=jnp.flo...  7.62 us
    ppermute x1, starting transfers between devices, shifted(): return lax.ppermute(shard, axis, pairs)  4.87 us
    ppermute x4, waiting for transfers between devices, swap_exp(): return lax.ppermute(x, 'exp', [(i, (i + 1) % size) for i in range(size)])  4.8 us
    dot_general x1, matrix products, on_device(): jnp.dot(other_hidden, expert_out[0], preferred_element_type=jnp.float32)  3.49 us
  transfers between devices with their start and end apart: 12, of which 8 were waited for; matrix products, arithmetic and copies ran while one was open for 6% of the time, Pallas kernels for 0%

profile of v18, /device:TPU:0, one launch (start us, length us, event | category | flops | bytes accessed | tf_op | source)
XLA Modules:
  0.0 168.2 jit_solution(18407967580976081003)
XLA Ops:
  0.0 0.0 copy-start
  0.0 0.9 slice_bitcast_fusion
  0.9 4.9 %collective-permute-start = (bf16[2,128,128]{2,1,0:T(8,128)(2,1)S(1)}, bf16[2,128,128]{2,1,0:T(8,128)(2,1)S(1)}, u32[]{:S(2)}, u32[]{:S(2)}) collective-permute-start(bf16[2,128,128]{2,1,0:T(8,128)(2,1)S(1)} %pad_maximum_fusion), channel_id=1, source_target_pairs={{0,2},{2,4},{4,6},{6,8},{8,10},{10,12},{12,14},{1,3},{3,5},{5,7},{... | collective-permute-start | bytes 196616 | tf_op jit(solution)/shard_map/ppermute | solution.py:21
  5.8 1.9 %collective-permute-done.recv_ref = bf16[2,128,128]{2,1,0:T(8,128)(2,1)S(1)} collective-permute-done((bf16[2,128,128]{2,1,0:T(8,128)(2,1)S(1)}, bf16[2,128,128]{2,1,0:T(8,128)(2,1)S(1)}, u32[]{:S(2)}, u32[]{:S(2)}) %collective-permute-start) | collective-permute-done | bytes 65568 | tf_op jit(solution)/shard_map/ppermute | solution.py:21
  7.7 0.6 copy-done.4
  8.3 10.1 %shard_map.118 = f32[256,1536]{1,0:T(8,128)} custom-call(f32[16]{0:T(128)} %sink_ref.1, s32[1]{0:T(128)} %bitcast.first_ref, bf16[256,1024]{1,0:T(8,128)(2,1)} %q_ref.1, bf16[2,128,128]{2,1,0:T(8,128)(2,1)} %cached_ref.1, bf16[2,128,128]{2,1,0:T(8,128)(2,1)} %copy-done.4, bf16[256,128]{1,0:T(8,128)(2,1)} %k_ref.1, bf16[256,128]{1,0:T(8,128)(2,1)} %v_ref.1, ...), custom_call_target="tpu_custom_call" | custom-call | flops 1342177280 | bytes 5439488 | tf_op jit(solution)/shard_map/pallas_call | solution.py:154
  18.4 0.0 collective-permute-start.1
  18.4 0.0 copy-done.5
  18.4 0.1 copy.37
  18.6 0.1 eq.86
  18.7 0.1 eq.82
  18.8 2.3 %reduce-window.6 = s32[8,8,128]{2,1,0:T(8,128)S(1)} reduce-window(s32[8,8,128]{2,1,0:T(8,128)S(1)} %fusion.32, s32[]{:T(128)} %constant.100.clone.1), window={size=1x1x128 pad=0_0x0_0x127_0}, to_apply=%region_0.0 | reduce-window | flops 1040384 | bytes 65540 | tf_op jit(solution)/shard_map/reduce-window
  21.1 0.3 slice_reduce_fusion
  21.4 0.2 reduce-window.9
  21.5 0.1 add_bitcast_fusion
  21.7 0.1 sub.60
  21.8 0.1 copy.39
  21.9 0.4 fusion.22
  22.4 0.0 copy-start.6
  22.4 0.0 collective-permute-done.1
  22.4 0.0 copy-done.3
  22.4 0.0 slice-start
  22.4 2.4 %multiply_reduce_fusion.1 = (f32[256]{0:T(256)S(1)}, f32[256,1536]{1,0:T(8,128)S(1)}) fusion(f32[256,1536]{1,0:T(8,128)} %shard_map.118, f32[256,1536]{1,0:T(8,128)} %collective-permute-done.1, bf16[256,1536]{1,0:T(8,128)(2,1)S(1)} %copy-done.3), kind=kLoop, calls=%fused_computation.29 | loop fusion | flops 1965824 | bytes 5506048 | tf_op jit(solution)/shard_map/reduce_sum | solution.py:54
  24.8 0.0 copy-done.6
  24.8 0.0 slice-start.1
  24.8 0.9 convolution_convert_fusion.2
  25.7 60.9 %all_to_all.5 = bf16[8,96,1536]{2,1,0:T(8,128)(2,1)S(1)} all-to-all(bf16[8,96,1536]{2,1,0:T(8,128)(2,1)S(1)} %bitcast.92), channel_id=1, replica_groups=mesh['groups'=2,'seq'=8,'exp'=2] {'seq'}, dimensions={0} | all-to-all | bytes 4718592 | tf_op jit(solution)/shard_map/all_to_all | solution.py:30
  86.7 0.0 copy-done.1
  86.7 0.0 collective-permute-start.2
  86.7 0.0 slice-done
  86.7 0.0 slice-done.1
  86.7 3.8 %fusion.16 = f32[2,768,768]{2,1,0:T(8,128)S(1)} fusion(bf16[768,1536,1]{1,0,2:T(8,128)(2,1)S(1)} %bitcast.94, bf16[1,2,1536,768]{3,2,1,0:T(8,128)(2,1)S(1)} %bitcast.98), kind=kOutput, calls=%fused_computation.24 | convolution fusion | flops 3623878656 | bytes 11796480 | tf_op jit(solution)/shard_map/rd,kdf->krf/dot_general | solution.py:81
  90.5 0.7 fusion.27
  91.2 0.0 collective-permute-done.2
  91.2 3.8 %fusion.19 = f32[2,768,768]{2,1,0:T(8,128)S(1)} fusion(bf16[768,1536,1]{1,0,2:T(8,128)(2,1)S(1)} %bitcast.99, bf16[1,2,1536,768]{3,2,1,0:T(8,128)(2,1)S(1)} %bitcast.98), kind=kOutput, calls=%fused_computation.25 | convolution fusion | flops 3623878656 | bytes 11796480 | tf_op jit(solution)/shard_map/rd,kdf->krf/dot_general | solution.py:81
  95.0 0.0 copy-done
  95.0 3.5 %convolution_convert_fusion = bf16[768,1536]{1,0:T(8,128)(2,1)} fusion(bf16[1,768,1536]{2,1,0:T(8,128)(2,1)S(1)} %copy-done, f32[2,768,768]{2,1,0:T(8,128)S(1)} %fusion.19), kind=kOutput, calls=%fused_computation.7 | convolution fusion | flops 1817837568 | bytes 9437184 | tf_op jit(solution)/shard_map/dot_general | solution.py:221
  98.5 0.5 collective-permute-start.3
  99.0 2.0 %convolution_convert_fusion.1 = bf16[768,1536]{1,0:T(8,128)(2,1)S(1)} fusion(bf16[768,768]{1,0:T(8,128)(2,1)S(1)} %fusion.27, bf16[1,768,1536]{2,1,0:T(8,128)(2,1)S(1)} %copy-done), kind=kOutput, calls=%fused_computation.8 | convolution fusion | flops 1813118976 | bytes 5898240 | tf_op jit(solution)/shard_map/dot_general | solution.py:226
  101.0 2.5 %collective-permute-done.3 = bf16[8,96,1536]{2,1,0:T(8,128)(2,1)} collective-permute-done((bf16[8,96,1536]{2,1,0:T(8,128)(2,1)}, bf16[8,96,1536]{2,1,0:T(8,128)(2,1)}, u32[]{:S(2)}, u32[]{:S(2)}) %collective-permute-start.3) | collective-permute-done | bytes 2359328 | tf_op jit(solution)/shard_map/ppermute | solution.py:26
  103.5 2.3 %fusion = bf16[8,96,1536]{2,1,0:T(8,128)(2,1)S(1)} fusion(bf16[8,96,1536]{2,1,0:T(8,128)(2,1)S(1)} %bitcast.93, bf16[8,96,1536]{2,1,0:T(8,128)(2,1)} %collective-permute-done.3), kind=kLoop, calls=%fused_computation.2 | loop fusion | flops 4718592 | bytes 7077888 | tf_op jit(solution)/shard_map/convert_element_type | solution.py:230
  105.8 0.3 dynamic-slice_bitcast_fusion
  106.1 0.0 copy-start.7
  106.1 2.4 %collective-permute-start.4 = (bf16[96,1536]{1,0:T(8,128)(2,1)S(1)}, bf16[96,1536]{1,0:T(8,128)(2,1)S(1)}, u32[]{:S(2)}, u32[]{:S(2)}) collective-permute-start(bf16[96,1536]{1,0:T(8,128)(2,1)S(1)} %get-tuple-element.17), channel_id=1, source_target_pairs={{0,14},{2,0},{4,2},{6,4},{8,6},{10,8},{12,10},{14,12},{1,15},{3,1}... | collective-permute-start | bytes 884744 | tf_op jit(solution)/shard_map/ppermute | solution.py:40
  108.5 0.0 collective-permute-start.5
  108.5 1.7 collective-permute-start.6
  110.2 1.5 collective-permute-start.7
  111.7 1.7 %collective-permute-start.8 = (bf16[96,1536]{1,0:T(8,128)(2,1)S(1)}, bf16[96,1536]{1,0:T(8,128)(2,1)S(1)}, u32[]{:S(2)}, u32[]{:S(2)}) collective-permute-start(bf16[96,1536]{1,0:T(8,128)(2,1)S(1)} %get-tuple-element.13), channel_id=1, source_target_pairs={{0,6},{2,8},{4,10},{6,12},{8,14},{10,0},{12,2},{14,4},{1,7},{3,9},... | collective-permute-start | bytes 884744 | tf_op jit(solution)/shard_map/ppermute | solution.py:40
  113.5 2.5 %collective-permute-done.4 = bf16[96,1536]{1,0:T(8,128)(2,1)S(1)} collective-permute-done((bf16[96,1536]{1,0:T(8,128)(2,1)S(1)}, bf16[96,1536]{1,0:T(8,128)(2,1)S(1)}, u32[]{:S(2)}, u32[]{:S(2)}) %collective-permute-start.4) | collective-permute-done | bytes 294944 | tf_op jit(solution)/shard_map/ppermute | solution.py:40
  116.0 0.6 collective-permute-start.9
  116.6 6.3 %collective-permute-done.5 = bf16[96,1536]{1,0:T(8,128)(2,1)S(1)} collective-permute-done((bf16[96,1536]{1,0:T(8,128)(2,1)S(1)}, bf16[96,1536]{1,0:T(8,128)(2,1)S(1)}, u32[]{:S(2)}, u32[]{:S(2)}) %collective-permute-start.5) | collective-permute-done | bytes 294944 | tf_op jit(solution)/shard_map/ppermute | solution.py:40
  122.8 0.0 collective-permute-start.10
  122.9 5.8 %collective-permute-done.6 = bf16[96,1536]{1,0:T(8,128)(2,1)S(1)} collective-permute-done((bf16[96,1536]{1,0:T(8,128)(2,1)S(1)}, bf16[96,1536]{1,0:T(8,128)(2,1)S(1)}, u32[]{:S(2)}, u32[]{:S(2)}) %collective-permute-start.6) | collective-permute-done | bytes 294944 | tf_op jit(solution)/shard_map/ppermute | solution.py:40
  128.7 31.2 %collective-permute-done.7 = bf16[96,1536]{1,0:T(8,128)(2,1)S(1)} collective-permute-done((bf16[96,1536]{1,0:T(8,128)(2,1)S(1)}, bf16[96,1536]{1,0:T(8,128)(2,1)S(1)}, u32[]{:S(2)}, u32[]{:S(2)}) %collective-permute-start.7) | collective-permute-done | bytes 294944 | tf_op jit(solution)/shard_map/ppermute | solution.py:40
  159.9 1.5 collective-permute-done.8
  161.4 0.0 collective-permute-done.9
  161.5 0.0 collective-permute-done.10
  161.5 0.0 copy-done.7
  161.5 0.0 copy-start.2
  161.5 3.1 %multiply_reduce_fusion = bf16[256,1536]{1,0:T(8,128)(2,1)S(1)} fusion(bf16[768,1536,1]{1,0,2:T(8,128)(2,1)S(1)} %bitcast.95, f32[256,4]{0,1:T(4,128)S(1)} %copy-done.7, s32[256,4]{0,1:T(4,128)S(1)} %get-tuple-element.19), kind=kOutput, calls=%fused_computation | convolution fusion | flops 2419458048 | bytes 3153920 | tf_op jit(solution)/shard_map/dot_general | solution.py:232
  164.6 0.1 collective-permute-start.11
  164.7 2.3 %collective-permute-done.11 = bf16[256,1536]{1,0:T(8,128)(2,1)S(1)} collective-permute-done((bf16[256,1536]{1,0:T(8,128)(2,1)S(1)}, bf16[256,1536]{1,0:T(8,128)(2,1)S(1)}, u32[]{:S(2)}, u32[]{:S(2)}) %collective-permute-start.11) | collective-permute-done | bytes 786464 | tf_op jit(solution)/shard_map/ppermute | solution.py:26
  167.0 0.0 copy-done.2
  167.0 1.2 add_convert_fusion
  (18 shorter events, 0.2 us)
Async XLA Ops:
  0.0 95.0 %copy-start = (bf16[1,768,1536]{2,1,0:T(8,128)(2,1)S(1)}, bf16[1,768,1536]{2,1,0:T(8,128)(2,1)}, u32[]{:S(2)}) copy-start(bf16[1,768,1536]{2,1,0:T(8,128)(2,1)} %param.21) | copy-start | bytes 7077892
  0.9 6.8 %collective-permute-start = (bf16[2,128,128]{2,1,0:T(8,128)(2,1)S(1)}, bf16[2,128,128]{2,1,0:T(8,128)(2,1)S(1)}, u32[]{:S(2)}, u32[]{:S(2)}) collective-permute-start(bf16[2,128,128]{2,1,0:T(8,128)(2,1)S(1)} %pad_maximum_fusion), channel_id=1, source_target_pairs={{0,2},{2,4},{4,6},{6,8},{8,10},{10,12},{12,14},{1,3},{3,5},{5,7},{... | collective-permute-start | bytes 196616 | tf_op jit(solution)/shard_map/ppermute | solution.py:21
  7.7 0.6 copy-start.4
  8.3 10.1 %copy-start.5 = (s32[256,4]{0,1:T(4,128)S(1)}, s32[256,4]{0,1:T(4,128)}, u32[]{:S(2)}) copy-start(s32[256,4]{0,1:T(4,128)} %param.22) | copy-start | bytes 12292
  8.3 14.0 %copy-start.3 = (bf16[256,1536]{1,0:T(8,128)(2,1)S(1)}, bf16[256,1536]{1,0:T(8,128)(2,1)}, u32[]{:S(2)}) copy-start(bf16[256,1536]{1,0:T(8,128)(2,1)} %param.18) | copy-start | bytes 2359300
  18.4 3.9 %collective-permute-start.1 = (f32[256,1536]{1,0:T(8,128)}, f32[256,1536]{1,0:T(8,128)}, u32[]{:S(2)}, u32[]{:S(2)}) collective-permute-start(f32[256,1536]{1,0:T(8,128)} %shard_map.118), channel_id=1, source_target_pairs={{0,1},{1,0},{2,3},{3,2},{4,5},{5,4},{6,7},{7,6},{8,9},{9,8},{10,11... | collective-permute-start | bytes 4718600 | tf_op jit(solution)/shard_map/ppermute | solution.py:26
  22.4 2.4 %copy-start.6 = (f32[1536]{0:T(1024)S(1)}, f32[1536]{0:T(1024)}, u32[]{:S(2)}) copy-start(f32[1536]{0:T(1024)} %param.19) | copy-start | bytes 18436
  22.4 64.3 %slice-start = ((s8[4718592]{0:T(1024)(128)(4,1)}), s8[4194304]{0:T(1024)(128)(4,1)S(1)}, s32[]{:S(2)}) async-start(s8[4718592]{0:T(1024)(128)(4,1)} %bitcast.97), calls=%async_computation.1 | async-start | bytes 8388608
  24.8 61.9 %copy-start.1 = (f32[256,1536]{1,0:T(8,128)}, f32[256,1536]{1,0:T(8,128)S(1)}, u32[]{:S(2)}) copy-start(f32[256,1536]{1,0:T(8,128)S(1)} %get-tuple-element.10) | copy-start | bytes 4718596
  24.8 61.9 %slice-start.1 = ((s8[4718592]{0:T(1024)(128)(4,1)}), s8[524288]{0:T(1024)(128)(4,1)S(1)}, s32[]{:S(2)}) async-start(s8[4718592]{0:T(1024)(128)(4,1)} %bitcast.97), calls=%async_computation.2 | async-start | bytes 1048576
  86.7 4.5 %collective-permute-start.2 = (bf16[8,96,1536]{2,1,0:T(8,128)(2,1)S(1)}, bf16[8,96,1536]{2,1,0:T(8,128)(2,1)S(1)}, u32[]{:S(2)}, u32[]{:S(2)}) collective-permute-start(bf16[8,96,1536]{2,1,0:T(8,128)(2,1)S(1)} %all_to_all.5), channel_id=1, source_target_pairs={{0,1},{1,0},{2,3},{3,2},{4,5},{5,4},{6,7},{7,6},{8,9},{9,8},{10,11... | collective-permute-start | bytes 7077896 | tf_op jit(solution)/shard_map/ppermute | solution.py:26
  98.5 5.0 %collective-permute-start.3 = (bf16[8,96,1536]{2,1,0:T(8,128)(2,1)}, bf16[8,96,1536]{2,1,0:T(8,128)(2,1)}, u32[]{:S(2)}, u32[]{:S(2)}) collective-permute-start(bf16[8,96,1536]{2,1,0:T(8,128)(2,1)} %bitcast.17), channel_id=1, source_target_pairs={{0,1},{1,0},{2,3},{3,2},{4,5},{5,4},{6,7},{7,6},{8,9},{9,8},{10,11... | collective-permute-start | bytes 7077896 | tf_op jit(solution)/shard_map/ppermute | solution.py:26
  106.1 55.4 %copy-start.7 = (f32[256,4]{0,1:T(4,128)S(1)}, f32[256,4]{0,1:T(4,128)}, u32[]{:S(2)}) copy-start(f32[256,4]{0,1:T(4,128)} %param.23) | copy-start | bytes 12292
  106.1 9.9 %collective-permute-start.4 = (bf16[96,1536]{1,0:T(8,128)(2,1)S(1)}, bf16[96,1536]{1,0:T(8,128)(2,1)S(1)}, u32[]{:S(2)}, u32[]{:S(2)}) collective-permute-start(bf16[96,1536]{1,0:T(8,128)(2,1)S(1)} %get-tuple-element.17), channel_id=1, source_target_pairs={{0,14},{2,0},{4,2},{6,4},{8,6},{10,8},{12,10},{14,12},{1,15},{3,1}... | collective-permute-start | bytes 884744 | tf_op jit(solution)/shard_map/ppermute | solution.py:40
  108.5 14.3 %collective-permute-start.5 = (bf16[96,1536]{1,0:T(8,128)(2,1)S(1)}, bf16[96,1536]{1,0:T(8,128)(2,1)S(1)}, u32[]{:S(2)}, u32[]{:S(2)}) collective-permute-start(bf16[96,1536]{1,0:T(8,128)(2,1)S(1)} %get-tuple-element.16), channel_id=1, source_target_pairs={{0,12},{2,14},{4,0},{6,2},{8,4},{10,6},{12,8},{14,10},{1,13},{3,15... | collective-permute-start | bytes 884744 | tf_op jit(solution)/shard_map/ppermute | solution.py:40
  108.5 20.1 %collective-permute-start.6 = (bf16[96,1536]{1,0:T(8,128)(2,1)S(1)}, bf16[96,1536]{1,0:T(8,128)(2,1)S(1)}, u32[]{:S(2)}, u32[]{:S(2)}) collective-permute-start(bf16[96,1536]{1,0:T(8,128)(2,1)S(1)} %get-tuple-element.15), channel_id=1, source_target_pairs={{0,10},{2,12},{4,14},{6,0},{8,2},{10,4},{12,6},{14,8},{1,11},{3,13... | collective-permute-start | bytes 884744 | tf_op jit(solution)/shard_map/ppermute | solution.py:40
  110.2 49.7 %collective-permute-start.7 = (bf16[96,1536]{1,0:T(8,128)(2,1)S(1)}, bf16[96,1536]{1,0:T(8,128)(2,1)S(1)}, u32[]{:S(2)}, u32[]{:S(2)}) collective-permute-start(bf16[96,1536]{1,0:T(8,128)(2,1)S(1)} %get-tuple-element.14), channel_id=1, source_target_pairs={{0,8},{2,10},{4,12},{6,14},{8,0},{10,2},{12,4},{14,6},{1,9},{3,11}... | collective-permute-start | bytes 884744 | tf_op jit(solution)/shard_map/ppermute | solution.py:40
  111.7 49.7 %collective-permute-start.8 = (bf16[96,1536]{1,0:T(8,128)(2,1)S(1)}, bf16[96,1536]{1,0:T(8,128)(2,1)S(1)}, u32[]{:S(2)}, u32[]{:S(2)}) collective-permute-start(bf16[96,1536]{1,0:T(8,128)(2,1)S(1)} %get-tuple-element.13), channel_id=1, source_target_pairs={{0,6},{2,8},{4,10},{6,12},{8,14},{10,0},{12,2},{14,4},{1,7},{3,9},... | collective-permute-start | bytes 884744 | tf_op jit(solution)/shard_map/ppermute | solution.py:40
  116.0 45.5 %collective-permute-start.9 = (bf16[96,1536]{1,0:T(8,128)(2,1)S(1)}, bf16[96,1536]{1,0:T(8,128)(2,1)S(1)}, u32[]{:S(2)}, u32[]{:S(2)}) collective-permute-start(bf16[96,1536]{1,0:T(8,128)(2,1)S(1)} %get-tuple-element.12), channel_id=1, source_target_pairs={{0,4},{2,6},{4,8},{6,10},{8,12},{10,14},{12,0},{14,2},{1,5},{3,7},... | collective-permute-start | bytes 884744 | tf_op jit(solution)/shard_map/ppermute | solution.py:40
  122.8 38.6 %collective-permute-start.10 = (bf16[96,1536]{1,0:T(8,128)(2,1)S(1)}, bf16[96,1536]{1,0:T(8,128)(2,1)S(1)}, u32[]{:S(2)}, u32[]{:S(2)}) collective-permute-start(bf16[96,1536]{1,0:T(8,128)(2,1)S(1)} %get-tuple-element.11), channel_id=1, source_target_pairs={{0,2},{2,4},{4,6},{6,8},{8,10},{10,12},{12,14},{14,0},{1,3},{3,5},... | collective-permute-start | bytes 884744 | tf_op jit(solution)/shard_map/ppermute | solution.py:40
  161.5 5.5 %copy-start.2 = (f32[256,1536]{1,0:T(8,128)S(1)}, f32[256,1536]{1,0:T(8,128)}, u32[]{:S(2)}) copy-start(f32[256,1536]{1,0:T(8,128)} %copy-done.1) | copy-start | bytes 4718596
  164.6 2.4 %collective-permute-start.11 = (bf16[256,1536]{1,0:T(8,128)(2,1)S(1)}, bf16[256,1536]{1,0:T(8,128)(2,1)S(1)}, u32[]{:S(2)}, u32[]{:S(2)}) collective-permute-start(bf16[256,1536]{1,0:T(8,128)(2,1)S(1)} %multiply_reduce_fusion), channel_id=1, source_target_pairs={{0,1},{1,0},{2,3},{3,2},{4,5},{5,4},{6,7},{7,6},{8,9},{9,8},{10,11... | collective-permute-start | bytes 2359304 | tf_op jit(solution)/shard_map/ppermute | solution.py:26

commit v19 on v17

--- a/solution.py
+++ b/solution.py
@@ -216,8 +216,15 @@
     )
     result = (own_part.astype(jnp.float32) + their_part.astype(jnp.float32)).astype(jnp.bfloat16)
     returned = shift_exchange(result, -1) if by_shift else seq_all_to_all(result)
-    picked = jnp.dot(pick, returned.reshape(slots, width), preferred_element_type=jnp.float32)
-    weighted = jnp.sum(picked.reshape(tok_rows, TOP, width) * route_gates[:, :, None], axis=1)
+    gate_table = jnp.sum(
+        pick.reshape(tok_rows, TOP, slots).astype(jnp.float32) * route_gates[:, :, None], axis=1
+    )
+    gate_high = gate_table.astype(jnp.bfloat16)
+    gate_low = (gate_table - gate_high.astype(jnp.float32)).astype(jnp.bfloat16)
+    flat_returned = returned.reshape(slots, width)
+    weighted = jnp.dot(gate_high, flat_returned, preferred_element_type=jnp.float32) + jnp.dot(
+        gate_low, flat_returned, preferred_element_type=jnp.float32
+    )
     rounded = weighted.astype(jnp.bfloat16)
     moe = rounded.astype(jnp.float32) + swap_exp(rounded).astype(jnp.float32)
     return (mixed_rows + moe).astype(jnp.bfloat16)

time: 161 us -> 160 us (level)
  transfers between devices with their start and end apart: 19 -> 19, of which waited for: 11 -> 12; matrix products, arithmetic and copies ran while one was open for 7% -> 7% of each run, Pallas kernels for 0% -> 0%
where the time goes in v19:
time: 160 us
  waiting for transfers between devices  78.2 us (49%)
  starting transfers between devices  46 us (29%)
  matrix products  14.2 us (9%)
  Pallas kernels  10.1 us (6%)
  other arithmetic  8.28 us (5%)
  local copies, waits for them, and re-layouts  3.14 us (2%)
    ppermute x14, waiting for transfers between devices, shift_exchange(): out.append(lax.ppermute(blocks[step], 'seq', pairs))  71.8 us
    ppermute x14, starting transfers between devices, shift_exchange(): out.append(lax.ppermute(blocks[step], 'seq', pairs))  40.4 us
    pallas_call x1, Pallas kernels, attend_kernel(): pl.pallas_call(attention_kernel, out_shape=jax.ShapeDtypeStruct((rows, wi...  10.1 us
    dot_general x2, matrix products, expert_hidden(): jnp.einsum('rd,kdf->krf', rows, expert_in, preferred_element_type=jnp.flo...  7.62 us
    ppermute x1, starting transfers between devices, shifted(): return lax.ppermute(shard, axis, pairs)  4.87 us
    ppermute x4, waiting for transfers between devices, swap_exp(): return lax.ppermute(x, 'exp', [(i, (i + 1) % size) for i in range(size)])  4.44 us
  transfers between devices with their start and end apart: 19, of which 12 were waited for; matrix products, arithmetic and copies ran while one was open for 7% of the time, Pallas kernels for 0%

profile of v19, /device:TPU:0, one launch (start us, length us, event | category | flops | bytes accessed | tf_op | source)
XLA Modules:
  0.0 160.2 jit_solution(17569351201046041614)
XLA Ops:
  0.0 0.9 slice_bitcast_fusion.8
  0.9 4.9 %collective-permute-start = (bf16[2,128,128]{2,1,0:T(8,128)(2,1)S(1)}, bf16[2,128,128]{2,1,0:T(8,128)(2,1)S(1)}, u32[]{:S(2)}, u32[]{:S(2)}) collective-permute-start(bf16[2,128,128]{2,1,0:T(8,128)(2,1)S(1)} %pad_maximum_fusion), channel_id=1, source_target_pairs={{0,2},{2,4},{4,6},{6,8},{8,10},{10,12},{12,14},{1,3},{3,5},{5,7},{... | collective-permute-start | bytes 196616 | tf_op jit(solution)/shard_map/ppermute | solution.py:21
  5.8 1.9 %collective-permute-done.recv_ref = bf16[2,128,128]{2,1,0:T(8,128)(2,1)S(1)} collective-permute-done((bf16[2,128,128]{2,1,0:T(8,128)(2,1)S(1)}, bf16[2,128,128]{2,1,0:T(8,128)(2,1)S(1)}, u32[]{:S(2)}, u32[]{:S(2)}) %collective-permute-start) | collective-permute-done | bytes 65568 | tf_op jit(solution)/shard_map/ppermute | solution.py:21
  7.7 0.6 copy-done.2
  8.3 10.1 %shard_map.118 = f32[256,1536]{1,0:T(8,128)} custom-call(f32[16]{0:T(128)} %sink_ref.1, s32[1]{0:T(128)} %bitcast.first_ref, bf16[256,1024]{1,0:T(8,128)(2,1)} %q_ref.1, bf16[2,128,128]{2,1,0:T(8,128)(2,1)} %cached_ref.1, bf16[2,128,128]{2,1,0:T(8,128)(2,1)} %copy-done.2, bf16[256,128]{1,0:T(8,128)(2,1)} %k_ref.1, bf16[256,128]{1,0:T(8,128)(2,1)} %v_ref.1, ...), custom_call_target="tpu_custom_call" | custom-call | flops 1342177280 | bytes 5439488 | tf_op jit(solution)/shard_map/pallas_call | solution.py:143
  18.4 0.0 collective-permute-start.1
  18.5 0.1 copy.33
  18.6 0.1 eq.49
  18.7 0.1 eq.45
  18.8 2.3 %reduce-window.6 = s32[8,8,128]{2,1,0:T(8,128)S(1)} reduce-window(s32[8,8,128]{2,1,0:T(8,128)S(1)} %fusion.34, s32[]{:T(128)} %constant.19.clone.1), window={size=1x1x128 pad=0_0x0_0x127_0}, to_apply=%region_0.0 | reduce-window | flops 1040384 | bytes 65540 | tf_op jit(solution)/shard_map/reduce-window
  21.1 0.3 slice_reduce_fusion
  21.4 0.2 reduce-window.9
  21.6 0.1 add_bitcast_fusion
  21.7 0.1 sub.39
  21.8 0.1 copy.35
  21.9 0.4 fusion.21
  22.4 0.0 copy-start.4
  22.4 2.2 %multiply_reduce_fusion.1 = (f32[256]{0:T(256)S(1)}, f32[256,1536]{1,0:T(8,128)S(1)}) fusion(f32[256,1536]{1,0:T(8,128)} %shard_map.118, f32[256,1536]{1,0:T(8,128)} %collective-permute-done.1, bf16[256,1536]{1,0:T(8,128)(2,1)S(1)} %copy-done.1), kind=kLoop, calls=%fused_computation.29 | loop fusion | flops 1965824 | bytes 5506048 | tf_op jit(solution)/shard_map/reduce_sum | solution.py:43
  24.6 0.0 slice-start
  24.7 0.9 convolution_convert_fusion.2
  25.6 0.0 slice-start.1
  25.6 0.1 fusion.41
  25.7 2.4 %collective-permute-start.2 = (bf16[96,1536]{1,0:T(8,128)(2,1)S(1)}, bf16[96,1536]{1,0:T(8,128)(2,1)S(1)}, u32[]{:S(2)}, u32[]{:S(2)}) collective-permute-start(bf16[96,1536]{1,0:T(8,128)(2,1)S(1)} %get-tuple-element.25), channel_id=1, source_target_pairs={{0,2},{2,4},{4,6},{6,8},{8,10},{10,12},{12,14},{14,0},{1,3},{3,5},... | collective-permute-start | bytes 884744 | tf_op jit(solution)/shard_map/ppermute | solution.py:38
  28.1 1.6 collective-permute-start.3
  29.7 3.4 %collective-permute-start.4 = (bf16[96,1536]{1,0:T(8,128)(2,1)S(1)}, bf16[96,1536]{1,0:T(8,128)(2,1)S(1)}, u32[]{:S(2)}, u32[]{:S(2)}) collective-permute-start(bf16[96,1536]{1,0:T(8,128)(2,1)S(1)} %get-tuple-element.23), channel_id=1, source_target_pairs={{0,6},{2,8},{4,10},{6,12},{8,14},{10,0},{12,2},{14,4},{1,7},{3,9},... | collective-permute-start | bytes 884744 | tf_op jit(solution)/shard_map/ppermute | solution.py:38
  33.1 1.2 collective-permute-start.5
  34.4 1.7 %collective-permute-start.6 = (bf16[96,1536]{1,0:T(8,128)(2,1)S(1)}, bf16[96,1536]{1,0:T(8,128)(2,1)S(1)}, u32[]{:S(2)}, u32[]{:S(2)}) collective-permute-start(bf16[96,1536]{1,0:T(8,128)(2,1)S(1)} %get-tuple-element.21), channel_id=1, source_target_pairs={{0,10},{2,12},{4,14},{6,0},{8,2},{10,4},{12,6},{14,8},{1,11},{3,13... | collective-permute-start | bytes 884744 | tf_op jit(solution)/shard_map/ppermute | solution.py:38
  36.1 3.1 %collective-permute-done.2 = bf16[96,1536]{1,0:T(8,128)(2,1)S(1)} collective-permute-done((bf16[96,1536]{1,0:T(8,128)(2,1)S(1)}, bf16[96,1536]{1,0:T(8,128)(2,1)S(1)}, u32[]{:S(2)}, u32[]{:S(2)}) %collective-permute-start.2) | collective-permute-done | bytes 294944 | tf_op jit(solution)/shard_map/ppermute | solution.py:38
  39.2 2.6 %collective-permute-start.7 = (bf16[96,1536]{1,0:T(8,128)(2,1)S(1)}, bf16[96,1536]{1,0:T(8,128)(2,1)S(1)}, u32[]{:S(2)}, u32[]{:S(2)}) collective-permute-start(bf16[96,1536]{1,0:T(8,128)(2,1)S(1)} %get-tuple-element.20), channel_id=1, source_target_pairs={{0,12},{2,14},{4,0},{6,2},{8,4},{10,6},{12,8},{14,10},{1,13},{3,15... | collective-permute-start | bytes 884744 | tf_op jit(solution)/shard_map/ppermute | solution.py:38
  41.8 0.0 collective-permute-done.3
  41.8 6.0 %collective-permute-start.8 = (bf16[96,1536]{1,0:T(8,128)(2,1)S(1)}, bf16[96,1536]{1,0:T(8,128)(2,1)S(1)}, u32[]{:S(2)}, u32[]{:S(2)}) collective-permute-start(bf16[96,1536]{1,0:T(8,128)(2,1)S(1)} %get-tuple-element.19), channel_id=1, source_target_pairs={{0,14},{2,0},{4,2},{6,4},{8,6},{10,8},{12,10},{14,12},{1,15},{3,1}... | collective-permute-start | bytes 884744 | tf_op jit(solution)/shard_map/ppermute | solution.py:38
  47.9 16.4 %collective-permute-done.4 = bf16[96,1536]{1,0:T(8,128)(2,1)S(1)} collective-permute-done((bf16[96,1536]{1,0:T(8,128)(2,1)S(1)}, bf16[96,1536]{1,0:T(8,128)(2,1)S(1)}, u32[]{:S(2)}, u32[]{:S(2)}) %collective-permute-start.4) | collective-permute-done | bytes 294944 | tf_op jit(solution)/shard_map/ppermute | solution.py:38
  64.3 0.3 collective-permute-done.5
  64.6 3.4 %collective-permute-done.8 = bf16[96,1536]{1,0:T(8,128)(2,1)S(1)} collective-permute-done((bf16[96,1536]{1,0:T(8,128)(2,1)S(1)}, bf16[96,1536]{1,0:T(8,128)(2,1)S(1)}, u32[]{:S(2)}, u32[]{:S(2)}) %collective-permute-start.8) | collective-permute-done | bytes 294944 | tf_op jit(solution)/shard_map/ppermute | solution.py:38
  68.0 0.1 collective-permute-start.9
  68.1 3.8 %fusion.15 = f32[2,768,768]{2,1,0:T(8,128)S(1)} fusion(bf16[768,1536,1]{1,0,2:T(8,128)(2,1)S(1)} %bitcast.108, bf16[1,2,1536,768]{3,2,1,0:T(8,128)(2,1)S(1)} %bitcast.111), kind=kOutput, calls=%fused_computation.24 | convolution fusion | flops 3623878656 | bytes 11796480 | tf_op jit(solution)/shard_map/rd,kdf->krf/dot_general | solution.py:70
  71.9 0.7 fusion.25
  72.6 0.0 collective-permute-done.9
  72.6 3.8 %fusion.18 = f32[2,768,768]{2,1,0:T(8,128)S(1)} fusion(bf16[768,1536,1]{1,0,2:T(8,128)(2,1)S(1)} %bitcast.112, bf16[1,2,1536,768]{3,2,1,0:T(8,128)(2,1)S(1)} %bitcast.111), kind=kOutput, calls=%fused_computation.25 | convolution fusion | flops 3623878656 | bytes 11796480 | tf_op jit(solution)/shard_map/rd,kdf->krf/dot_general | solution.py:70
  76.5 2.1 %convolution_convert_fusion = bf16[768,1536]{1,0:T(8,128)(2,1)S(1)} fusion(bf16[1,768,1536]{2,1,0:T(8,128)(2,1)S(1)} %copy-done, f32[2,768,768]{2,1,0:T(8,128)S(1)} %fusion.18), kind=kOutput, calls=%fused_computation.6 | convolution fusion | flops 1817837568 | bytes 9437184 | tf_op jit(solution)/shard_map/dot_general | solution.py:208
  78.5 0.5 collective-permute-start.10
  79.1 2.0 %convolution_convert_fusion.1 = bf16[768,1536]{1,0:T(8,128)(2,1)S(1)} fusion(bf16[768,768]{1,0:T(8,128)(2,1)S(1)} %fusion.25, bf16[1,768,1536]{2,1,0:T(8,128)(2,1)S(1)} %copy-done), kind=kOutput, calls=%fused_computation.7 | convolution fusion | flops 1813118976 | bytes 5898240 | tf_op jit(solution)/shard_map/dot_general | solution.py:213
  81.1 2.2 %collective-permute-done.10 = bf16[8,96,1536]{2,1,0:T(8,128)(2,1)S(1)} collective-permute-done((bf16[8,96,1536]{2,1,0:T(8,128)(2,1)S(1)}, bf16[8,96,1536]{2,1,0:T(8,128)(2,1)S(1)}, u32[]{:S(2)}, u32[]{:S(2)}) %collective-permute-start.10) | collective-permute-done | bytes 2359328 | tf_op jit(solution)/shard_map/ppermute | solution.py:26
  83.2 0.7 fusion
  83.9 0.0 copy-start.5
  83.9 0.2 slice_bitcast_fusion
  84.2 18.0 %collective-permute-start.11 = (bf16[96,1536]{1,0:T(8,128)(2,1)S(1)}, bf16[96,1536]{1,0:T(8,128)(2,1)S(1)}, u32[]{:S(2)}, u32[]{:S(2)}) collective-permute-start(bf16[96,1536]{1,0:T(8,128)(2,1)S(1)} %get-tuple-element.17), channel_id=1, source_target_pairs={{0,14},{2,0},{4,2},{6,4},{8,6},{10,8},{12,10},{14,12},{1,15},{3,1}... | collective-permute-start | bytes 884744 | tf_op jit(solution)/shard_map/ppermute | solution.py:38
  102.2 0.5 multiply_reduce_fusion
  102.7 0.1 collective-permute-start.12
  102.8 0.7 collective-permute-start.13
  103.5 2.6 %collective-permute-start.14 = (bf16[96,1536]{1,0:T(8,128)(2,1)S(1)}, bf16[96,1536]{1,0:T(8,128)(2,1)S(1)}, u32[]{:S(2)}, u32[]{:S(2)}) collective-permute-start(bf16[96,1536]{1,0:T(8,128)(2,1)S(1)} %get-tuple-element.14), channel_id=1, source_target_pairs={{0,8},{2,10},{4,12},{6,14},{8,0},{10,2},{12,4},{14,6},{1,9},{3,11}... | collective-permute-start | bytes 884744 | tf_op jit(solution)/shard_map/ppermute | solution.py:38
  106.1 0.1 collective-permute-start.15
  106.1 3.5 %collective-permute-done.11 = bf16[96,1536]{1,0:T(8,128)(2,1)S(1)} collective-permute-done((bf16[96,1536]{1,0:T(8,128)(2,1)S(1)}, bf16[96,1536]{1,0:T(8,128)(2,1)S(1)}, u32[]{:S(2)}, u32[]{:S(2)}) %collective-permute-start.11) | collective-permute-done | bytes 294944 | tf_op jit(solution)/shard_map/ppermute | solution.py:38
  109.7 6.3 %collective-permute-done.12 = bf16[96,1536]{1,0:T(8,128)(2,1)S(1)} collective-permute-done((bf16[96,1536]{1,0:T(8,128)(2,1)S(1)}, bf16[96,1536]{1,0:T(8,128)(2,1)S(1)}, u32[]{:S(2)}, u32[]{:S(2)}) %collective-permute-start.12) | collective-permute-done | bytes 294944 | tf_op jit(solution)/shard_map/ppermute | solution.py:38
  116.0 6.3 %collective-permute-done.13 = bf16[96,1536]{1,0:T(8,128)(2,1)S(1)} collective-permute-done((bf16[96,1536]{1,0:T(8,128)(2,1)S(1)}, bf16[96,1536]{1,0:T(8,128)(2,1)S(1)}, u32[]{:S(2)}, u32[]{:S(2)}) %collective-permute-start.13) | collective-permute-done | bytes 294944 | tf_op jit(solution)/shard_map/ppermute | solution.py:38
  122.3 31.8 %collective-permute-done.14 = bf16[96,1536]{1,0:T(8,128)(2,1)S(1)} collective-permute-done((bf16[96,1536]{1,0:T(8,128)(2,1)S(1)}, bf16[96,1536]{1,0:T(8,128)(2,1)S(1)}, u32[]{:S(2)}, u32[]{:S(2)}) %collective-permute-start.14) | collective-permute-done | bytes 294944 | tf_op jit(solution)/shard_map/ppermute | solution.py:38
  154.1 0.9 collective-permute-done.15
  155.0 0.0 collective-permute-done.16
  155.1 0.0 collective-permute-done.17
  155.1 0.8 fusion.28
  155.9 0.8 fusion.6
  156.7 0.1 collective-permute-start.18
  156.8 2.3 %collective-permute-done.18 = bf16[256,1536]{1,0:T(8,128)(2,1)S(1)} collective-permute-done((bf16[256,1536]{1,0:T(8,128)(2,1)S(1)}, bf16[256,1536]{1,0:T(8,128)(2,1)S(1)}, u32[]{:S(2)}, u32[]{:S(2)}) %collective-permute-start.18) | collective-permute-done | bytes 786464 | tf_op jit(solution)/shard_map/ppermute | solution.py:26
  159.1 1.2 add_convert_fusion
  (38 shorter events, 0.4 us)
Async XLA Ops:
  0.0 76.4 %copy-start = (bf16[1,768,1536]{2,1,0:T(8,128)(2,1)S(1)}, bf16[1,768,1536]{2,1,0:T(8,128)(2,1)}, u32[]{:S(2)}) copy-start(bf16[1,768,1536]{2,1,0:T(8,128)(2,1)} %param.21) | copy-start | bytes 7077892
  0.9 6.8 %collective-permute-start = (bf16[2,128,128]{2,1,0:T(8,128)(2,1)S(1)}, bf16[2,128,128]{2,1,0:T(8,128)(2,1)S(1)}, u32[]{:S(2)}, u32[]{:S(2)}) collective-permute-start(bf16[2,128,128]{2,1,0:T(8,128)(2,1)S(1)} %pad_maximum_fusion), channel_id=1, source_target_pairs={{0,2},{2,4},{4,6},{6,8},{8,10},{10,12},{12,14},{1,3},{3,5},{5,7},{... | collective-permute-start | bytes 196616 | tf_op jit(solution)/shard_map/ppermute | solution.py:21
  7.7 0.6 copy-start.2
  8.3 10.1 %copy-start.3 = (s32[256,4]{0,1:T(4,128)S(1)}, s32[256,4]{0,1:T(4,128)}, u32[]{:S(2)}) copy-start(s32[256,4]{0,1:T(4,128)} %param.22) | copy-start | bytes 12292
  8.3 14.1 %copy-start.1 = (bf16[256,1536]{1,0:T(8,128)(2,1)S(1)}, bf16[256,1536]{1,0:T(8,128)(2,1)}, u32[]{:S(2)}) copy-start(bf16[256,1536]{1,0:T(8,128)(2,1)} %param.18) | copy-start | bytes 2359300
  18.4 3.9 %collective-permute-start.1 = (f32[256,1536]{1,0:T(8,128)}, f32[256,1536]{1,0:T(8,128)}, u32[]{:S(2)}, u32[]{:S(2)}) collective-permute-start(f32[256,1536]{1,0:T(8,128)} %shard_map.118), channel_id=1, source_target_pairs={{0,1},{1,0},{2,3},{3,2},{4,5},{5,4},{6,7},{7,6},{8,9},{9,8},{10,11... | collective-permute-start | bytes 4718600 | tf_op jit(solution)/shard_map/ppermute | solution.py:26
  22.4 2.3 %copy-start.4 = (f32[1536]{0:T(1024)S(1)}, f32[1536]{0:T(1024)}, u32[]{:S(2)}) copy-start(f32[1536]{0:T(1024)} %param.19) | copy-start | bytes 18436
  24.6 43.5 %slice-start = ((s8[4718592]{0:T(1024)(128)(4,1)}), s8[4194304]{0:T(1024)(128)(4,1)S(1)}, s32[]{:S(2)}) async-start(s8[4718592]{0:T(1024)(128)(4,1)} %bitcast.110), calls=%async_computation | async-start | bytes 8388608
  25.6 42.6 %slice-start.1 = ((s8[4718592]{0:T(1024)(128)(4,1)}), s8[524288]{0:T(1024)(128)(4,1)S(1)}, s32[]{:S(2)}) async-start(s8[4718592]{0:T(1024)(128)(4,1)} %bitcast.110), calls=%async_computation.1 | async-start | bytes 1048576
  25.7 13.5 %collective-permute-start.2 = (bf16[96,1536]{1,0:T(8,128)(2,1)S(1)}, bf16[96,1536]{1,0:T(8,128)(2,1)S(1)}, u32[]{:S(2)}, u32[]{:S(2)}) collective-permute-start(bf16[96,1536]{1,0:T(8,128)(2,1)S(1)} %get-tuple-element.25), channel_id=1, source_target_pairs={{0,2},{2,4},{4,6},{6,8},{8,10},{10,12},{12,14},{14,0},{1,3},{3,5},... | collective-permute-start | bytes 884744 | tf_op jit(solution)/shard_map/ppermute | solution.py:38
  28.1 13.7 %collective-permute-start.3 = (bf16[96,1536]{1,0:T(8,128)(2,1)S(1)}, bf16[96,1536]{1,0:T(8,128)(2,1)S(1)}, u32[]{:S(2)}, u32[]{:S(2)}) collective-permute-start(bf16[96,1536]{1,0:T(8,128)(2,1)S(1)} %get-tuple-element.24), channel_id=1, source_target_pairs={{0,4},{2,6},{4,8},{6,10},{8,12},{10,14},{12,0},{14,2},{1,5},{3,7},... | collective-permute-start | bytes 884744 | tf_op jit(solution)/shard_map/ppermute | solution.py:38
  29.7 34.6 %collective-permute-start.4 = (bf16[96,1536]{1,0:T(8,128)(2,1)S(1)}, bf16[96,1536]{1,0:T(8,128)(2,1)S(1)}, u32[]{:S(2)}, u32[]{:S(2)}) collective-permute-start(bf16[96,1536]{1,0:T(8,128)(2,1)S(1)} %get-tuple-element.23), channel_id=1, source_target_pairs={{0,6},{2,8},{4,10},{6,12},{8,14},{10,0},{12,2},{14,4},{1,7},{3,9},... | collective-permute-start | bytes 884744 | tf_op jit(solution)/shard_map/ppermute | solution.py:38
  33.1 31.4 %collective-permute-start.5 = (bf16[96,1536]{1,0:T(8,128)(2,1)S(1)}, bf16[96,1536]{1,0:T(8,128)(2,1)S(1)}, u32[]{:S(2)}, u32[]{:S(2)}) collective-permute-start(bf16[96,1536]{1,0:T(8,128)(2,1)S(1)} %get-tuple-element.22), channel_id=1, source_target_pairs={{0,8},{2,10},{4,12},{6,14},{8,0},{10,2},{12,4},{14,6},{1,9},{3,11}... | collective-permute-start | bytes 884744 | tf_op jit(solution)/shard_map/ppermute | solution.py:38
  34.4 30.2 %collective-permute-start.6 = (bf16[96,1536]{1,0:T(8,128)(2,1)S(1)}, bf16[96,1536]{1,0:T(8,128)(2,1)S(1)}, u32[]{:S(2)}, u32[]{:S(2)}) collective-permute-start(bf16[96,1536]{1,0:T(8,128)(2,1)S(1)} %get-tuple-element.21), channel_id=1, source_target_pairs={{0,10},{2,12},{4,14},{6,0},{8,2},{10,4},{12,6},{14,8},{1,11},{3,13... | collective-permute-start | bytes 884744 | tf_op jit(solution)/shard_map/ppermute | solution.py:38
  39.2 25.4 %collective-permute-start.7 = (bf16[96,1536]{1,0:T(8,128)(2,1)S(1)}, bf16[96,1536]{1,0:T(8,128)(2,1)S(1)}, u32[]{:S(2)}, u32[]{:S(2)}) collective-permute-start(bf16[96,1536]{1,0:T(8,128)(2,1)S(1)} %get-tuple-element.20), channel_id=1, source_target_pairs={{0,12},{2,14},{4,0},{6,2},{8,4},{10,6},{12,8},{14,10},{1,13},{3,15... | collective-permute-start | bytes 884744 | tf_op jit(solution)/shard_map/ppermute | solution.py:38
  41.8 26.2 %collective-permute-start.8 = (bf16[96,1536]{1,0:T(8,128)(2,1)S(1)}, bf16[96,1536]{1,0:T(8,128)(2,1)S(1)}, u32[]{:S(2)}, u32[]{:S(2)}) collective-permute-start(bf16[96,1536]{1,0:T(8,128)(2,1)S(1)} %get-tuple-element.19), channel_id=1, source_target_pairs={{0,14},{2,0},{4,2},{6,4},{8,6},{10,8},{12,10},{14,12},{1,15},{3,1}... | collective-permute-start | bytes 884744 | tf_op jit(solution)/shard_map/ppermute | solution.py:38
  68.0 4.6 %collective-permute-start.9 = (bf16[8,96,1536]{2,1,0:T(8,128)(2,1)S(1)}, bf16[8,96,1536]{2,1,0:T(8,128)(2,1)S(1)}, u32[]{:S(2)}, u32[]{:S(2)}) collective-permute-start(bf16[8,96,1536]{2,1,0:T(8,128)(2,1)S(1)} %bitcast_dynamic-update-slice_fusion.7), channel_id=1, source_target_pairs={{0,1},{1,0},{2,3},{3,2},{4,5},{5,4},{6,7},{7,6},{8,9},{9,8},{10,11... | collective-permute-start | bytes 7077896 | tf_op jit(solution)/shard_map/ppermute | solution.py:26
  78.5 4.7 %collective-permute-start.10 = (bf16[8,96,1536]{2,1,0:T(8,128)(2,1)S(1)}, bf16[8,96,1536]{2,1,0:T(8,128)(2,1)S(1)}, u32[]{:S(2)}, u32[]{:S(2)}) collective-permute-start(bf16[8,96,1536]{2,1,0:T(8,128)(2,1)S(1)} %bitcast.113), channel_id=1, source_target_pairs={{0,1},{1,0},{2,3},{3,2},{4,5},{5,4},{6,7},{7,6},{8,9},{9,8},{10,11... | collective-permute-start | bytes 7077896 | tf_op jit(solution)/shard_map/ppermute | solution.py:26
  83.9 18.3 %copy-start.5 = (f32[256,4]{0,1:T(4,128)S(1)}, f32[256,4]{0,1:T(4,128)}, u32[]{:S(2)}) copy-start(f32[256,4]{0,1:T(4,128)} %param.23) | copy-start | bytes 12292
  84.2 25.5 %collective-permute-start.11 = (bf16[96,1536]{1,0:T(8,128)(2,1)S(1)}, bf16[96,1536]{1,0:T(8,128)(2,1)S(1)}, u32[]{:S(2)}, u32[]{:S(2)}) collective-permute-start(bf16[96,1536]{1,0:T(8,128)(2,1)S(1)} %get-tuple-element.17), channel_id=1, source_target_pairs={{0,14},{2,0},{4,2},{6,4},{8,6},{10,8},{12,10},{14,12},{1,15},{3,1}... | collective-permute-start | bytes 884744 | tf_op jit(solution)/shard_map/ppermute | solution.py:38
  102.7 13.2 %collective-permute-start.12 = (bf16[96,1536]{1,0:T(8,128)(2,1)S(1)}, bf16[96,1536]{1,0:T(8,128)(2,1)S(1)}, u32[]{:S(2)}, u32[]{:S(2)}) collective-permute-start(bf16[96,1536]{1,0:T(8,128)(2,1)S(1)} %get-tuple-element.16), channel_id=1, source_target_pairs={{0,12},{2,14},{4,0},{6,2},{8,4},{10,6},{12,8},{14,10},{1,13},{3,15... | collective-permute-start | bytes 884744 | tf_op jit(solution)/shard_map/ppermute | solution.py:38
  102.8 19.5 %collective-permute-start.13 = (bf16[96,1536]{1,0:T(8,128)(2,1)S(1)}, bf16[96,1536]{1,0:T(8,128)(2,1)S(1)}, u32[]{:S(2)}, u32[]{:S(2)}) collective-permute-start(bf16[96,1536]{1,0:T(8,128)(2,1)S(1)} %get-tuple-element.15), channel_id=1, source_target_pairs={{0,10},{2,12},{4,14},{6,0},{8,2},{10,4},{12,6},{14,8},{1,11},{3,13... | collective-permute-start | bytes 884744 | tf_op jit(solution)/shard_map/ppermute | solution.py:38
  103.5 50.5 %collective-permute-start.14 = (bf16[96,1536]{1,0:T(8,128)(2,1)S(1)}, bf16[96,1536]{1,0:T(8,128)(2,1)S(1)}, u32[]{:S(2)}, u32[]{:S(2)}) collective-permute-start(bf16[96,1536]{1,0:T(8,128)(2,1)S(1)} %get-tuple-element.14), channel_id=1, source_target_pairs={{0,8},{2,10},{4,12},{6,14},{8,0},{10,2},{12,4},{14,6},{1,9},{3,11}... | collective-permute-start | bytes 884744 | tf_op jit(solution)/shard_map/ppermute | solution.py:38
  106.1 48.9 %collective-permute-start.15 = (bf16[96,1536]{1,0:T(8,128)(2,1)S(1)}, bf16[96,1536]{1,0:T(8,128)(2,1)S(1)}, u32[]{:S(2)}, u32[]{:S(2)}) collective-permute-start(bf16[96,1536]{1,0:T(8,128)(2,1)S(1)} %get-tuple-element.13), channel_id=1, source_target_pairs={{0,6},{2,8},{4,10},{6,12},{8,14},{10,0},{12,2},{14,4},{1,7},{3,9},... | collective-permute-start | bytes 884744 | tf_op jit(solution)/shard_map/ppermute | solution.py:38
  109.6 45.4 %collective-permute-start.16 = (bf16[96,1536]{1,0:T(8,128)(2,1)S(1)}, bf16[96,1536]{1,0:T(8,128)(2,1)S(1)}, u32[]{:S(2)}, u32[]{:S(2)}) collective-permute-start(bf16[96,1536]{1,0:T(8,128)(2,1)S(1)} %get-tuple-element.12), channel_id=1, source_target_pairs={{0,4},{2,6},{4,8},{6,10},{8,12},{10,14},{12,0},{14,2},{1,5},{3,7},... | collective-permute-start | bytes 884744 | tf_op jit(solution)/shard_map/ppermute | solution.py:38
  116.0 39.1 %collective-permute-start.17 = (bf16[96,1536]{1,0:T(8,128)(2,1)S(1)}, bf16[96,1536]{1,0:T(8,128)(2,1)S(1)}, u32[]{:S(2)}, u32[]{:S(2)}) collective-permute-start(bf16[96,1536]{1,0:T(8,128)(2,1)S(1)} %get-tuple-element.11), channel_id=1, source_target_pairs={{0,2},{2,4},{4,6},{6,8},{8,10},{10,12},{12,14},{14,0},{1,3},{3,5},... | collective-permute-start | bytes 884744 | tf_op jit(solution)/shard_map/ppermute | solution.py:38
  156.7 2.4 %collective-permute-start.18 = (bf16[256,1536]{1,0:T(8,128)(2,1)S(1)}, bf16[256,1536]{1,0:T(8,128)(2,1)S(1)}, u32[]{:S(2)}, u32[]{:S(2)}) collective-permute-start(bf16[256,1536]{1,0:T(8,128)(2,1)S(1)} %fusion.6), channel_id=1, source_target_pairs={{0,1},{1,0},{2,3},{3,2},{4,5},{5,4},{6,7},{7,6},{8,9},{9,8},{10,11... | collective-permute-start | bytes 2359304 | tf_op jit(solution)/shard_map/ppermute | solution.py:26

commit v20 on v19

--- a/solution.py
+++ b/solution.py
@@ -107,13 +107,15 @@
                 )
         for j in range(pairs):
             kv = j // per_kv
-            q_pair = q_ref[b * WINDOW : (b + 1) * WINDOW, j * pair_cols : (j + 1) * pair_cols]
+            q_pair = q_ref[b * WINDOW : (b + 1) * WINDOW, j * pair_cols : (j + 1) * pair_cols] * HEAD_DIM ** (
+                -0.5
+            )
             total = None
             for a in range(2):
                 k_placed, v_placed = placed[kv, a]
                 scores = lax.dot_general(
                     q_pair, k_placed, (((1,), (1,)), ((), ())), preferred_element_type=jnp.float32
-                ) * HEAD_DIM ** (-0.5)
+                )
                 scores = jnp.where(allowed, scores, -jnp.inf)
                 sink = sink_ref[2 * j + a]
                 largest = jnp.maximum(jnp.max(scores, axis=-1, keepdims=True), sink)

time: 160 us -> 160 us (level)
  no operation moved by 1% of the time
where the time goes in v20:
time: 160 us
  waiting for transfers between devices  78.1 us (49%)
  starting transfers between devices  46 us (29%)
  matrix products  14.2 us (9%)
  Pallas kernels  10.1 us (6%)
  other arithmetic  8.28 us (5%)
  local copies, waits for them, and re-layouts  3.14 us (2%)
    ppermute x14, waiting for transfers between devices, shift_exchange(): out.append(lax.ppermute(blocks[step], 'seq', pairs))  71.8 us
    ppermute x14, starting transfers between devices, shift_exchange(): out.append(lax.ppermute(blocks[step], 'seq', pairs))  40.5 us
    pallas_call x1, Pallas kernels, attend_kernel(): pl.pallas_call(attention_kernel, out_shape=jax.ShapeDtypeStruct((rows, wi...  10.1 us
    dot_general x2, matrix products, expert_hidden(): jnp.einsum('rd,kdf->krf', rows, expert_in, preferred_element_type=jnp.flo...  7.62 us
    ppermute x1, starting transfers between devices, shifted(): return lax.ppermute(shard, axis, pairs)  4.87 us
    ppermute x4, waiting for transfers between devices, swap_exp(): return lax.ppermute(x, 'exp', [(i, (i + 1) % size) for i in range(size)])  4.44 us
  transfers between devices with their start and end apart: 19, of which 12 were waited for; matrix products, arithmetic and copies ran while one was open for 7% of the time, Pallas kernels for 0%

profile of v20, /device:TPU:0, one launch (start us, length us, event | category | flops | bytes accessed | tf_op | source)
XLA Modules:
  0.0 160.3 jit_solution(12852208573998077511)
XLA Ops:
  0.0 0.9 slice_bitcast_fusion.8
  0.9 4.9 %collective-permute-start = (bf16[2,128,128]{2,1,0:T(8,128)(2,1)S(1)}, bf16[2,128,128]{2,1,0:T(8,128)(2,1)S(1)}, u32[]{:S(2)}, u32[]{:S(2)}) collective-permute-start(bf16[2,128,128]{2,1,0:T(8,128)(2,1)S(1)} %pad_maximum_fusion), channel_id=1, source_target_pairs={{0,2},{2,4},{4,6},{6,8},{8,10},{10,12},{12,14},{1,3},{3,5},{5,7},{... | collective-permute-start | bytes 196616 | tf_op jit(solution)/shard_map/ppermute | solution.py:21
  5.8 1.9 %collective-permute-done.recv_ref = bf16[2,128,128]{2,1,0:T(8,128)(2,1)S(1)} collective-permute-done((bf16[2,128,128]{2,1,0:T(8,128)(2,1)S(1)}, bf16[2,128,128]{2,1,0:T(8,128)(2,1)S(1)}, u32[]{:S(2)}, u32[]{:S(2)}) %collective-permute-start) | collective-permute-done | bytes 65568 | tf_op jit(solution)/shard_map/ppermute | solution.py:21
  7.7 0.6 copy-done.2
  8.3 10.1 %shard_map.118 = f32[256,1536]{1,0:T(8,128)} custom-call(f32[16]{0:T(128)} %sink_ref.1, s32[1]{0:T(128)} %bitcast.first_ref, bf16[256,1024]{1,0:T(8,128)(2,1)} %q_ref.1, bf16[2,128,128]{2,1,0:T(8,128)(2,1)} %cached_ref.1, bf16[2,128,128]{2,1,0:T(8,128)(2,1)} %copy-done.2, bf16[256,128]{1,0:T(8,128)(2,1)} %k_ref.1, bf16[256,128]{1,0:T(8,128)(2,1)} %v_ref.1, ...), custom_call_target="tpu_custom_call" | custom-call | flops 1342177280 | bytes 5439488 | tf_op jit(solution)/shard_map/pallas_call | solution.py:145
  18.4 0.0 collective-permute-start.1
  18.5 0.1 copy.33
  18.6 0.1 eq.49
  18.7 0.1 eq.45
  18.9 2.3 %reduce-window.6 = s32[8,8,128]{2,1,0:T(8,128)S(1)} reduce-window(s32[8,8,128]{2,1,0:T(8,128)S(1)} %fusion.34, s32[]{:T(128)} %constant.19.clone.1), window={size=1x1x128 pad=0_0x0_0x127_0}, to_apply=%region_0.0 | reduce-window | flops 1040384 | bytes 65540 | tf_op jit(solution)/shard_map/reduce-window
  21.1 0.3 slice_reduce_fusion
  21.4 0.2 reduce-window.9
  21.6 0.1 add_bitcast_fusion
  21.7 0.1 sub.39
  21.8 0.1 copy.35
  21.9 0.4 fusion.21
  22.4 0.0 copy-start.4
  22.4 0.0 collective-permute-done.1
  22.4 2.2 %multiply_reduce_fusion.1 = (f32[256]{0:T(256)S(1)}, f32[256,1536]{1,0:T(8,128)S(1)}) fusion(f32[256,1536]{1,0:T(8,128)} %shard_map.118, f32[256,1536]{1,0:T(8,128)} %collective-permute-done.1, bf16[256,1536]{1,0:T(8,128)(2,1)S(1)} %copy-done.1), kind=kLoop, calls=%fused_computation.29 | loop fusion | flops 1965824 | bytes 5506048 | tf_op jit(solution)/shard_map/reduce_sum | solution.py:43
  24.6 0.0 slice-start
  24.7 0.9 convolution_convert_fusion.2
  25.6 0.0 slice-start.1
  25.6 0.1 fusion.41
  25.7 2.4 %collective-permute-start.2 = (bf16[96,1536]{1,0:T(8,128)(2,1)S(1)}, bf16[96,1536]{1,0:T(8,128)(2,1)S(1)}, u32[]{:S(2)}, u32[]{:S(2)}) collective-permute-start(bf16[96,1536]{1,0:T(8,128)(2,1)S(1)} %get-tuple-element.25), channel_id=1, source_target_pairs={{0,2},{2,4},{4,6},{6,8},{8,10},{10,12},{12,14},{14,0},{1,3},{3,5},... | collective-permute-start | bytes 884744 | tf_op jit(solution)/shard_map/ppermute | solution.py:38
  28.1 1.6 collective-permute-start.3
  29.7 3.4 %collective-permute-start.4 = (bf16[96,1536]{1,0:T(8,128)(2,1)S(1)}, bf16[96,1536]{1,0:T(8,128)(2,1)S(1)}, u32[]{:S(2)}, u32[]{:S(2)}) collective-permute-start(bf16[96,1536]{1,0:T(8,128)(2,1)S(1)} %get-tuple-element.23), channel_id=1, source_target_pairs={{0,6},{2,8},{4,10},{6,12},{8,14},{10,0},{12,2},{14,4},{1,7},{3,9},... | collective-permute-start | bytes 884744 | tf_op jit(solution)/shard_map/ppermute | solution.py:38
  33.1 1.2 collective-permute-start.5
  34.4 1.7 %collective-permute-start.6 = (bf16[96,1536]{1,0:T(8,128)(2,1)S(1)}, bf16[96,1536]{1,0:T(8,128)(2,1)S(1)}, u32[]{:S(2)}, u32[]{:S(2)}) collective-permute-start(bf16[96,1536]{1,0:T(8,128)(2,1)S(1)} %get-tuple-element.21), channel_id=1, source_target_pairs={{0,10},{2,12},{4,14},{6,0},{8,2},{10,4},{12,6},{14,8},{1,11},{3,13... | collective-permute-start | bytes 884744 | tf_op jit(solution)/shard_map/ppermute | solution.py:38
  36.1 3.1 %collective-permute-done.2 = bf16[96,1536]{1,0:T(8,128)(2,1)S(1)} collective-permute-done((bf16[96,1536]{1,0:T(8,128)(2,1)S(1)}, bf16[96,1536]{1,0:T(8,128)(2,1)S(1)}, u32[]{:S(2)}, u32[]{:S(2)}) %collective-permute-start.2) | collective-permute-done | bytes 294944 | tf_op jit(solution)/shard_map/ppermute | solution.py:38
  39.2 2.6 %collective-permute-start.7 = (bf16[96,1536]{1,0:T(8,128)(2,1)S(1)}, bf16[96,1536]{1,0:T(8,128)(2,1)S(1)}, u32[]{:S(2)}, u32[]{:S(2)}) collective-permute-start(bf16[96,1536]{1,0:T(8,128)(2,1)S(1)} %get-tuple-element.20), channel_id=1, source_target_pairs={{0,12},{2,14},{4,0},{6,2},{8,4},{10,6},{12,8},{14,10},{1,13},{3,15... | collective-permute-start | bytes 884744 | tf_op jit(solution)/shard_map/ppermute | solution.py:38
  41.8 6.0 %collective-permute-start.8 = (bf16[96,1536]{1,0:T(8,128)(2,1)S(1)}, bf16[96,1536]{1,0:T(8,128)(2,1)S(1)}, u32[]{:S(2)}, u32[]{:S(2)}) collective-permute-start(bf16[96,1536]{1,0:T(8,128)(2,1)S(1)} %get-tuple-element.19), channel_id=1, source_target_pairs={{0,14},{2,0},{4,2},{6,4},{8,6},{10,8},{12,10},{14,12},{1,15},{3,1}... | collective-permute-start | bytes 884744 | tf_op jit(solution)/shard_map/ppermute | solution.py:38
  47.9 16.3 %collective-permute-done.4 = bf16[96,1536]{1,0:T(8,128)(2,1)S(1)} collective-permute-done((bf16[96,1536]{1,0:T(8,128)(2,1)S(1)}, bf16[96,1536]{1,0:T(8,128)(2,1)S(1)}, u32[]{:S(2)}, u32[]{:S(2)}) %collective-permute-start.4) | collective-permute-done | bytes 294944 | tf_op jit(solution)/shard_map/ppermute | solution.py:38
  64.3 0.3 collective-permute-done.5
  64.6 0.0 collective-permute-done.6
  64.6 0.0 collective-permute-done.7
  64.6 3.4 %collective-permute-done.8 = bf16[96,1536]{1,0:T(8,128)(2,1)S(1)} collective-permute-done((bf16[96,1536]{1,0:T(8,128)(2,1)S(1)}, bf16[96,1536]{1,0:T(8,128)(2,1)S(1)}, u32[]{:S(2)}, u32[]{:S(2)}) %collective-permute-start.8) | collective-permute-done | bytes 294944 | tf_op jit(solution)/shard_map/ppermute | solution.py:38
  68.0 0.1 collective-permute-start.9
  68.1 3.8 %fusion.15 = f32[2,768,768]{2,1,0:T(8,128)S(1)} fusion(bf16[768,1536,1]{1,0,2:T(8,128)(2,1)S(1)} %bitcast.108, bf16[1,2,1536,768]{3,2,1,0:T(8,128)(2,1)S(1)} %bitcast.111), kind=kOutput, calls=%fused_computation.24 | convolution fusion | flops 3623878656 | bytes 11796480 | tf_op jit(solution)/shard_map/rd,kdf->krf/dot_general | solution.py:70
  71.9 0.7 fusion.25
  72.6 0.0 collective-permute-done.9
  72.6 3.8 %fusion.18 = f32[2,768,768]{2,1,0:T(8,128)S(1)} fusion(bf16[768,1536,1]{1,0,2:T(8,128)(2,1)S(1)} %bitcast.112, bf16[1,2,1536,768]{3,2,1,0:T(8,128)(2,1)S(1)} %bitcast.111), kind=kOutput, calls=%fused_computation.25 | convolution fusion | flops 3623878656 | bytes 11796480 | tf_op jit(solution)/shard_map/rd,kdf->krf/dot_general | solution.py:70
  76.5 2.1 %convolution_convert_fusion = bf16[768,1536]{1,0:T(8,128)(2,1)S(1)} fusion(bf16[1,768,1536]{2,1,0:T(8,128)(2,1)S(1)} %copy-done, f32[2,768,768]{2,1,0:T(8,128)S(1)} %fusion.18), kind=kOutput, calls=%fused_computation.6 | convolution fusion | flops 1817837568 | bytes 9437184 | tf_op jit(solution)/shard_map/dot_general | solution.py:210
  78.5 0.5 collective-permute-start.10
  79.1 2.0 %convolution_convert_fusion.1 = bf16[768,1536]{1,0:T(8,128)(2,1)S(1)} fusion(bf16[768,768]{1,0:T(8,128)(2,1)S(1)} %fusion.25, bf16[1,768,1536]{2,1,0:T(8,128)(2,1)S(1)} %copy-done), kind=kOutput, calls=%fused_computation.7 | convolution fusion | flops 1813118976 | bytes 5898240 | tf_op jit(solution)/shard_map/dot_general | solution.py:215
  81.1 2.2 %collective-permute-done.10 = bf16[8,96,1536]{2,1,0:T(8,128)(2,1)S(1)} collective-permute-done((bf16[8,96,1536]{2,1,0:T(8,128)(2,1)S(1)}, bf16[8,96,1536]{2,1,0:T(8,128)(2,1)S(1)}, u32[]{:S(2)}, u32[]{:S(2)}) %collective-permute-start.10) | collective-permute-done | bytes 2359328 | tf_op jit(solution)/shard_map/ppermute | solution.py:26
  83.2 0.7 fusion
  83.9 0.0 copy-start.5
  83.9 0.2 slice_bitcast_fusion
  84.2 18.0 %collective-permute-start.11 = (bf16[96,1536]{1,0:T(8,128)(2,1)S(1)}, bf16[96,1536]{1,0:T(8,128)(2,1)S(1)}, u32[]{:S(2)}, u32[]{:S(2)}) collective-permute-start(bf16[96,1536]{1,0:T(8,128)(2,1)S(1)} %get-tuple-element.17), channel_id=1, source_target_pairs={{0,14},{2,0},{4,2},{6,4},{8,6},{10,8},{12,10},{14,12},{1,15},{3,1}... | collective-permute-start | bytes 884744 | tf_op jit(solution)/shard_map/ppermute | solution.py:38
  102.2 0.5 multiply_reduce_fusion
  102.7 0.1 collective-permute-start.12
  102.8 0.7 collective-permute-start.13
  103.5 2.6 %collective-permute-start.14 = (bf16[96,1536]{1,0:T(8,128)(2,1)S(1)}, bf16[96,1536]{1,0:T(8,128)(2,1)S(1)}, u32[]{:S(2)}, u32[]{:S(2)}) collective-permute-start(bf16[96,1536]{1,0:T(8,128)(2,1)S(1)} %get-tuple-element.14), channel_id=1, source_target_pairs={{0,8},{2,10},{4,12},{6,14},{8,0},{10,2},{12,4},{14,6},{1,9},{3,11}... | collective-permute-start | bytes 884744 | tf_op jit(solution)/shard_map/ppermute | solution.py:38
  106.1 0.0 collective-permute-start.15
  106.1 3.5 %collective-permute-done.11 = bf16[96,1536]{1,0:T(8,128)(2,1)S(1)} collective-permute-done((bf16[96,1536]{1,0:T(8,128)(2,1)S(1)}, bf16[96,1536]{1,0:T(8,128)(2,1)S(1)}, u32[]{:S(2)}, u32[]{:S(2)}) %collective-permute-start.11) | collective-permute-done | bytes 294944 | tf_op jit(solution)/shard_map/ppermute | solution.py:38
  109.7 6.3 %collective-permute-done.12 = bf16[96,1536]{1,0:T(8,128)(2,1)S(1)} collective-permute-done((bf16[96,1536]{1,0:T(8,128)(2,1)S(1)}, bf16[96,1536]{1,0:T(8,128)(2,1)S(1)}, u32[]{:S(2)}, u32[]{:S(2)}) %collective-permute-start.12) | collective-permute-done | bytes 294944 | tf_op jit(solution)/shard_map/ppermute | solution.py:38
  116.0 6.3 %collective-permute-done.13 = bf16[96,1536]{1,0:T(8,128)(2,1)S(1)} collective-permute-done((bf16[96,1536]{1,0:T(8,128)(2,1)S(1)}, bf16[96,1536]{1,0:T(8,128)(2,1)S(1)}, u32[]{:S(2)}, u32[]{:S(2)}) %collective-permute-start.13) | collective-permute-done | bytes 294944 | tf_op jit(solution)/shard_map/ppermute | solution.py:38
  122.3 31.7 %collective-permute-done.14 = bf16[96,1536]{1,0:T(8,128)(2,1)S(1)} collective-permute-done((bf16[96,1536]{1,0:T(8,128)(2,1)S(1)}, bf16[96,1536]{1,0:T(8,128)(2,1)S(1)}, u32[]{:S(2)}, u32[]{:S(2)}) %collective-permute-start.14) | collective-permute-done | bytes 294944 | tf_op jit(solution)/shard_map/ppermute | solution.py:38
  154.1 0.9 collective-permute-done.15
  155.1 0.8 fusion.28
  155.9 0.8 fusion.6
  156.7 0.1 collective-permute-start.18
  156.8 2.3 %collective-permute-done.18 = bf16[256,1536]{1,0:T(8,128)(2,1)S(1)} collective-permute-done((bf16[256,1536]{1,0:T(8,128)(2,1)S(1)}, bf16[256,1536]{1,0:T(8,128)(2,1)S(1)}, u32[]{:S(2)}, u32[]{:S(2)}) %collective-permute-start.18) | collective-permute-done | bytes 786464 | tf_op jit(solution)/shard_map/ppermute | solution.py:26
  159.1 1.2 add_convert_fusion
  (38 shorter events, 0.4 us)
Async XLA Ops:
  0.0 76.4 %copy-start = (bf16[1,768,1536]{2,1,0:T(8,128)(2,1)S(1)}, bf16[1,768,1536]{2,1,0:T(8,128)(2,1)}, u32[]{:S(2)}) copy-start(bf16[1,768,1536]{2,1,0:T(8,128)(2,1)} %param.21) | copy-start | bytes 7077892
  0.9 6.8 %collective-permute-start = (bf16[2,128,128]{2,1,0:T(8,128)(2,1)S(1)}, bf16[2,128,128]{2,1,0:T(8,128)(2,1)S(1)}, u32[]{:S(2)}, u32[]{:S(2)}) collective-permute-start(bf16[2,128,128]{2,1,0:T(8,128)(2,1)S(1)} %pad_maximum_fusion), channel_id=1, source_target_pairs={{0,2},{2,4},{4,6},{6,8},{8,10},{10,12},{12,14},{1,3},{3,5},{5,7},{... | collective-permute-start | bytes 196616 | tf_op jit(solution)/shard_map/ppermute | solution.py:21
  7.7 0.6 copy-start.2
  8.3 10.1 %copy-start.3 = (s32[256,4]{0,1:T(4,128)S(1)}, s32[256,4]{0,1:T(4,128)}, u32[]{:S(2)}) copy-start(s32[256,4]{0,1:T(4,128)} %param.22) | copy-start | bytes 12292
  8.3 14.1 %copy-start.1 = (bf16[256,1536]{1,0:T(8,128)(2,1)S(1)}, bf16[256,1536]{1,0:T(8,128)(2,1)}, u32[]{:S(2)}) copy-start(bf16[256,1536]{1,0:T(8,128)(2,1)} %param.18) | copy-start | bytes 2359300
  18.4 3.9 %collective-permute-start.1 = (f32[256,1536]{1,0:T(8,128)}, f32[256,1536]{1,0:T(8,128)}, u32[]{:S(2)}, u32[]{:S(2)}) collective-permute-start(f32[256,1536]{1,0:T(8,128)} %shard_map.118), channel_id=1, source_target_pairs={{0,1},{1,0},{2,3},{3,2},{4,5},{5,4},{6,7},{7,6},{8,9},{9,8},{10,11... | collective-permute-start | bytes 4718600 | tf_op jit(solution)/shard_map/ppermute | solution.py:26
  22.4 2.3 %copy-start.4 = (f32[1536]{0:T(1024)S(1)}, f32[1536]{0:T(1024)}, u32[]{:S(2)}) copy-start(f32[1536]{0:T(1024)} %param.19) | copy-start | bytes 18436
  24.6 43.5 %slice-start = ((s8[4718592]{0:T(1024)(128)(4,1)}), s8[4194304]{0:T(1024)(128)(4,1)S(1)}, s32[]{:S(2)}) async-start(s8[4718592]{0:T(1024)(128)(4,1)} %bitcast.110), calls=%async_computation | async-start | bytes 8388608
  25.6 42.6 %slice-start.1 = ((s8[4718592]{0:T(1024)(128)(4,1)}), s8[524288]{0:T(1024)(128)(4,1)S(1)}, s32[]{:S(2)}) async-start(s8[4718592]{0:T(1024)(128)(4,1)} %bitcast.110), calls=%async_computation.1 | async-start | bytes 1048576
  25.7 13.5 %collective-permute-start.2 = (bf16[96,1536]{1,0:T(8,128)(2,1)S(1)}, bf16[96,1536]{1,0:T(8,128)(2,1)S(1)}, u32[]{:S(2)}, u32[]{:S(2)}) collective-permute-start(bf16[96,1536]{1,0:T(8,128)(2,1)S(1)} %get-tuple-element.25), channel_id=1, source_target_pairs={{0,2},{2,4},{4,6},{6,8},{8,10},{10,12},{12,14},{14,0},{1,3},{3,5},... | collective-permute-start | bytes 884744 | tf_op jit(solution)/shard_map/ppermute | solution.py:38
  28.1 13.7 %collective-permute-start.3 = (bf16[96,1536]{1,0:T(8,128)(2,1)S(1)}, bf16[96,1536]{1,0:T(8,128)(2,1)S(1)}, u32[]{:S(2)}, u32[]{:S(2)}) collective-permute-start(bf16[96,1536]{1,0:T(8,128)(2,1)S(1)} %get-tuple-element.24), channel_id=1, source_target_pairs={{0,4},{2,6},{4,8},{6,10},{8,12},{10,14},{12,0},{14,2},{1,5},{3,7},... | collective-permute-start | bytes 884744 | tf_op jit(solution)/shard_map/ppermute | solution.py:38
  29.7 34.6 %collective-permute-start.4 = (bf16[96,1536]{1,0:T(8,128)(2,1)S(1)}, bf16[96,1536]{1,0:T(8,128)(2,1)S(1)}, u32[]{:S(2)}, u32[]{:S(2)}) collective-permute-start(bf16[96,1536]{1,0:T(8,128)(2,1)S(1)} %get-tuple-element.23), channel_id=1, source_target_pairs={{0,6},{2,8},{4,10},{6,12},{8,14},{10,0},{12,2},{14,4},{1,7},{3,9},... | collective-permute-start | bytes 884744 | tf_op jit(solution)/shard_map/ppermute | solution.py:38
  33.1 31.4 %collective-permute-start.5 = (bf16[96,1536]{1,0:T(8,128)(2,1)S(1)}, bf16[96,1536]{1,0:T(8,128)(2,1)S(1)}, u32[]{:S(2)}, u32[]{:S(2)}) collective-permute-start(bf16[96,1536]{1,0:T(8,128)(2,1)S(1)} %get-tuple-element.22), channel_id=1, source_target_pairs={{0,8},{2,10},{4,12},{6,14},{8,0},{10,2},{12,4},{14,6},{1,9},{3,11}... | collective-permute-start | bytes 884744 | tf_op jit(solution)/shard_map/ppermute | solution.py:38
  34.4 30.2 %collective-permute-start.6 = (bf16[96,1536]{1,0:T(8,128)(2,1)S(1)}, bf16[96,1536]{1,0:T(8,128)(2,1)S(1)}, u32[]{:S(2)}, u32[]{:S(2)}) collective-permute-start(bf16[96,1536]{1,0:T(8,128)(2,1)S(1)} %get-tuple-element.21), channel_id=1, source_target_pairs={{0,10},{2,12},{4,14},{6,0},{8,2},{10,4},{12,6},{14,8},{1,11},{3,13... | collective-permute-start | bytes 884744 | tf_op jit(solution)/shard_map/ppermute | solution.py:38
  39.2 25.4 %collective-permute-start.7 = (bf16[96,1536]{1,0:T(8,128)(2,1)S(1)}, bf16[96,1536]{1,0:T(8,128)(2,1)S(1)}, u32[]{:S(2)}, u32[]{:S(2)}) collective-permute-start(bf16[96,1536]{1,0:T(8,128)(2,1)S(1)} %get-tuple-element.20), channel_id=1, source_target_pairs={{0,12},{2,14},{4,0},{6,2},{8,4},{10,6},{12,8},{14,10},{1,13},{3,15... | collective-permute-start | bytes 884744 | tf_op jit(solution)/shard_map/ppermute | solution.py:38
  41.8 26.1 %collective-permute-start.8 = (bf16[96,1536]{1,0:T(8,128)(2,1)S(1)}, bf16[96,1536]{1,0:T(8,128)(2,1)S(1)}, u32[]{:S(2)}, u32[]{:S(2)}) collective-permute-start(bf16[96,1536]{1,0:T(8,128)(2,1)S(1)} %get-tuple-element.19), channel_id=1, source_target_pairs={{0,14},{2,0},{4,2},{6,4},{8,6},{10,8},{12,10},{14,12},{1,15},{3,1}... | collective-permute-start | bytes 884744 | tf_op jit(solution)/shard_map/ppermute | solution.py:38
  68.0 4.6 %collective-permute-start.9 = (bf16[8,96,1536]{2,1,0:T(8,128)(2,1)S(1)}, bf16[8,96,1536]{2,1,0:T(8,128)(2,1)S(1)}, u32[]{:S(2)}, u32[]{:S(2)}) collective-permute-start(bf16[8,96,1536]{2,1,0:T(8,128)(2,1)S(1)} %bitcast_dynamic-update-slice_fusion.7), channel_id=1, source_target_pairs={{0,1},{1,0},{2,3},{3,2},{4,5},{5,4},{6,7},{7,6},{8,9},{9,8},{10,11... | collective-permute-start | bytes 7077896 | tf_op jit(solution)/shard_map/ppermute | solution.py:26
  78.5 4.7 %collective-permute-start.10 = (bf16[8,96,1536]{2,1,0:T(8,128)(2,1)S(1)}, bf16[8,96,1536]{2,1,0:T(8,128)(2,1)S(1)}, u32[]{:S(2)}, u32[]{:S(2)}) collective-permute-start(bf16[8,96,1536]{2,1,0:T(8,128)(2,1)S(1)} %bitcast.113), channel_id=1, source_target_pairs={{0,1},{1,0},{2,3},{3,2},{4,5},{5,4},{6,7},{7,6},{8,9},{9,8},{10,11... | collective-permute-start | bytes 7077896 | tf_op jit(solution)/shard_map/ppermute | solution.py:26
  83.9 18.3 %copy-start.5 = (f32[256,4]{0,1:T(4,128)S(1)}, f32[256,4]{0,1:T(4,128)}, u32[]{:S(2)}) copy-start(f32[256,4]{0,1:T(4,128)} %param.23) | copy-start | bytes 12292
  84.2 25.5 %collective-permute-start.11 = (bf16[96,1536]{1,0:T(8,128)(2,1)S(1)}, bf16[96,1536]{1,0:T(8,128)(2,1)S(1)}, u32[]{:S(2)}, u32[]{:S(2)}) collective-permute-start(bf16[96,1536]{1,0:T(8,128)(2,1)S(1)} %get-tuple-element.17), channel_id=1, source_target_pairs={{0,14},{2,0},{4,2},{6,4},{8,6},{10,8},{12,10},{14,12},{1,15},{3,1}... | collective-permute-start | bytes 884744 | tf_op jit(solution)/shard_map/ppermute | solution.py:38
  102.7 13.2 %collective-permute-start.12 = (bf16[96,1536]{1,0:T(8,128)(2,1)S(1)}, bf16[96,1536]{1,0:T(8,128)(2,1)S(1)}, u32[]{:S(2)}, u32[]{:S(2)}) collective-permute-start(bf16[96,1536]{1,0:T(8,128)(2,1)S(1)} %get-tuple-element.16), channel_id=1, source_target_pairs={{0,12},{2,14},{4,0},{6,2},{8,4},{10,6},{12,8},{14,10},{1,13},{3,15... | collective-permute-start | bytes 884744 | tf_op jit(solution)/shard_map/ppermute | solution.py:38
  102.8 19.5 %collective-permute-start.13 = (bf16[96,1536]{1,0:T(8,128)(2,1)S(1)}, bf16[96,1536]{1,0:T(8,128)(2,1)S(1)}, u32[]{:S(2)}, u32[]{:S(2)}) collective-permute-start(bf16[96,1536]{1,0:T(8,128)(2,1)S(1)} %get-tuple-element.15), channel_id=1, source_target_pairs={{0,10},{2,12},{4,14},{6,0},{8,2},{10,4},{12,6},{14,8},{1,11},{3,13... | collective-permute-start | bytes 884744 | tf_op jit(solution)/shard_map/ppermute | solution.py:38
  103.5 50.5 %collective-permute-start.14 = (bf16[96,1536]{1,0:T(8,128)(2,1)S(1)}, bf16[96,1536]{1,0:T(8,128)(2,1)S(1)}, u32[]{:S(2)}, u32[]{:S(2)}) collective-permute-start(bf16[96,1536]{1,0:T(8,128)(2,1)S(1)} %get-tuple-element.14), channel_id=1, source_target_pairs={{0,8},{2,10},{4,12},{6,14},{8,0},{10,2},{12,4},{14,6},{1,9},{3,11}... | collective-permute-start | bytes 884744 | tf_op jit(solution)/shard_map/ppermute | solution.py:38
  106.1 48.9 %collective-permute-start.15 = (bf16[96,1536]{1,0:T(8,128)(2,1)S(1)}, bf16[96,1536]{1,0:T(8,128)(2,1)S(1)}, u32[]{:S(2)}, u32[]{:S(2)}) collective-permute-start(bf16[96,1536]{1,0:T(8,128)(2,1)S(1)} %get-tuple-element.13), channel_id=1, source_target_pairs={{0,6},{2,8},{4,10},{6,12},{8,14},{10,0},{12,2},{14,4},{1,7},{3,9},... | collective-permute-start | bytes 884744 | tf_op jit(solution)/shard_map/ppermute | solution.py:38
  109.6 45.4 %collective-permute-start.16 = (bf16[96,1536]{1,0:T(8,128)(2,1)S(1)}, bf16[96,1536]{1,0:T(8,128)(2,1)S(1)}, u32[]{:S(2)}, u32[]{:S(2)}) collective-permute-start(bf16[96,1536]{1,0:T(8,128)(2,1)S(1)} %get-tuple-element.12), channel_id=1, source_target_pairs={{0,4},{2,6},{4,8},{6,10},{8,12},{10,14},{12,0},{14,2},{1,5},{3,7},... | collective-permute-start | bytes 884744 | tf_op jit(solution)/shard_map/ppermute | solution.py:38
  116.0 39.1 %collective-permute-start.17 = (bf16[96,1536]{1,0:T(8,128)(2,1)S(1)}, bf16[96,1536]{1,0:T(8,128)(2,1)S(1)}, u32[]{:S(2)}, u32[]{:S(2)}) collective-permute-start(bf16[96,1536]{1,0:T(8,128)(2,1)S(1)} %get-tuple-element.11), channel_id=1, source_target_pairs={{0,2},{2,4},{4,6},{6,8},{8,10},{10,12},{12,14},{14,0},{1,3},{3,5},... | collective-permute-start | bytes 884744 | tf_op jit(solution)/shard_map/ppermute | solution.py:38
  156.7 2.4 %collective-permute-start.18 = (bf16[256,1536]{1,0:T(8,128)(2,1)S(1)}, bf16[256,1536]{1,0:T(8,128)(2,1)S(1)}, u32[]{:S(2)}, u32[]{:S(2)}) collective-permute-start(bf16[256,1536]{1,0:T(8,128)(2,1)S(1)} %fusion.6), channel_id=1, source_target_pairs={{0,1},{1,0},{2,3},{3,2},{4,5},{5,4},{6,7},{7,6},{8,9},{9,8},{10,11... | collective-permute-start | bytes 2359304 | tf_op jit(solution)/shard_map/ppermute | solution.py:26

commit v21 on v20

--- a/solution.py
+++ b/solution.py
@@ -73,7 +73,9 @@
     return ((up_val + 1.0) * gate_val * jax.nn.sigmoid(GLU_ALPHA * gate_val)).astype(jnp.bfloat16)
 
 
-def attention_kernel(sink_ref, first_ref, q_ref, cached_ref, recv_ref, k_ref, v_ref, w_ref, o_ref, heads_ref):
+def attention_kernel(
+    sink_ref, first_ref, q_ref, cached_ref, recv_k_ref, recv_v_ref, k_ref, v_ref, w_ref, o_ref, heads_ref
+):
     rows = q_ref.shape[0]
     prior = cached_ref.shape[1]
     span = 2 * WINDOW
@@ -82,8 +84,8 @@
     kv_count = k_ref.shape[1] // HEAD_DIM
     per_kv = pairs // kv_count
     first = first_ref[0] == 1
-    prior_keys = jnp.where(first, cached_ref[0], recv_ref[0])
-    prior_values = jnp.where(first, cached_ref[1], recv_ref[1])
+    prior_keys = jnp.where(first, cached_ref[0], recv_k_ref[...])
+    prior_values = jnp.where(first, cached_ref[1], recv_v_ref[...])
     keys_all = jnp.concatenate([prior_keys, k_ref[...]], axis=0)
     values_all = jnp.concatenate([prior_values, v_ref[...]], axis=0)
     q_pos = lax.broadcasted_iota(jnp.int32, (WINDOW, span), 0)
@@ -145,11 +147,11 @@
     return pl.pallas_call(
         attention_kernel,
         out_shape=jax.ShapeDtypeStruct((rows, width), jnp.float32),
-        in_specs=[pl.BlockSpec(memory_space=pltpu.SMEM)] * 2 + [vmem] * 6,
+        in_specs=[pl.BlockSpec(memory_space=pltpu.SMEM)] * 2 + [vmem] * 7,
         out_specs=vmem,
         scratch_shapes=[pltpu.VMEM((rows, cols), jnp.bfloat16)],
         cost_estimate=cost,
-    )(sink_logits, first_block, queries, cached_rows, received, key_rows, values, out_weight)
+    )(sink_logits, first_block, queries, cached_rows, *received, key_rows, values, out_weight)
 
 
 def on_device(
@@ -168,8 +170,7 @@
 ):
     tok_rows = queries.shape[0]
     window_rows = WINDOW
-    rim_rows = jnp.stack([key_rows[tok_rows - window_rows :], values[tok_rows - window_rows :]])
-    received = shifted(rim_rows, "seq", 1)
+    received = [shifted(rows[tok_rows - window_rows :], "seq", 1) for rows in (key_rows, values)]
     first_block = (lax.axis_index("seq") == 0).astype(jnp.int32).reshape(1)
     partial_rows = attend_kernel(
         queries, first_block, cached_rows, received, key_rows, values, sink_logits, out_weight

time: 160 us -> 164 us (1.025)
  starting transfers between devices: 46 us -> 49.5 us
    ppermute x1 -> x2, starting transfers between devices: 4.87 us -> 8.28 us  [shifted(): return lax.ppermute(shard, axis, pairs)]
    slice x1 -> x3, local copies, waits for them, and re-layouts: 0.28 us -> 1.95 us  [the longest x2 1.67 us: on_device(): rows[tok_rows - window_rows:]]
  transfers between devices with their start and end apart: 19 -> 20, of which waited for: 12 -> 12; matrix products, arithmetic and copies ran while one was open for 7% -> 7% of each run, Pallas kernels for 0% -> 0%
where the time goes in v21:
time: 164 us
  waiting for transfers between devices  77.7 us (47%)
  starting transfers between devices  49.5 us (30%)
  matrix products  14.1 us (9%)
  Pallas kernels  10.1 us (6%)
  other arithmetic  8.28 us (5%)
  local copies, waits for them, and re-layouts  3.86 us (2%)
    ppermute x14, waiting for transfers between devices, shift_exchange(): out.append(lax.ppermute(blocks[step], 'seq', pairs))  71.7 us
    ppermute x14, starting transfers between devices, shift_exchange(): out.append(lax.ppermute(blocks[step], 'seq', pairs))  40.5 us
    pallas_call x1, Pallas kernels, attend_kernel(): pl.pallas_call(attention_kernel, out_shape=jax.ShapeDtypeStruct((rows, wi...  10.1 us
    ppermute x2, starting transfers between devices, shifted(): return lax.ppermute(shard, axis, pairs)  8.28 us
    dot_general x2, matrix products, expert_hidden(): jnp.einsum('rd,kdf->krf', rows, expert_in, preferred_element_type=jnp.flo...  7.62 us
    ppermute x4, waiting for transfers between devices, swap_exp(): return lax.ppermute(x, 'exp', [(i, (i + 1) % size) for i in range(size)])  4.45 us
  transfers between devices with their start and end apart: 20, of which 12 were waited for; matrix products, arithmetic and copies ran while one was open for 7% of the time, Pallas kernels for 0%

profile of v21, /device:TPU:0, one launch (start us, length us, event | category | flops | bytes accessed | tf_op | source)
XLA Modules:
  0.0 164.0 jit_solution(4243611847998107028)
XLA Ops:
  0.0 0.9 slice.82
  0.9 4.9 %collective-permute-start = (bf16[128,128]{1,0:T(8,128)(2,1)S(1)}, bf16[128,128]{1,0:T(8,128)(2,1)S(1)}, u32[]{:S(2)}, u32[]{:S(2)}) collective-permute-start(bf16[128,128]{1,0:T(8,128)(2,1)S(1)} %slice.82), channel_id=1, source_target_pairs={{0,2},{2,4},{4,6},{6,8},{8,10},{10,12},{12,14},{1,3},{3,5},{5,7},{... | collective-permute-start | bytes 98312 | tf_op jit(solution)/shard_map/ppermute | solution.py:21
  5.8 0.8 slice.83
  6.5 3.4 %collective-permute-start.1 = (bf16[128,128]{1,0:T(8,128)(2,1)S(1)}, bf16[128,128]{1,0:T(8,128)(2,1)S(1)}, u32[]{:S(2)}, u32[]{:S(2)}) collective-permute-start(bf16[128,128]{1,0:T(8,128)(2,1)S(1)} %slice.83), channel_id=1, source_target_pairs={{0,2},{2,4},{4,6},{6,8},{8,10},{10,12},{12,14},{1,3},{3,5},{5,7},{... | collective-permute-start | bytes 98312 | tf_op jit(solution)/shard_map/ppermute | solution.py:21
  10.0 0.0 collective-permute-done.recv_k_ref
  10.0 0.0 copy-start.2
  10.0 1.5 collective-permute-done.1.recv_v_ref
  11.6 0.6 copy-done.3
  12.2 10.1 %shard_map.118 = f32[256,1536]{1,0:T(8,128)} custom-call(f32[16]{0:T(128)} %sink_ref.1, s32[1]{0:T(128)} %bitcast.first_ref, bf16[256,1024]{1,0:T(8,128)(2,1)} %q_ref.1, bf16[2,128,128]{2,1,0:T(8,128)(2,1)} %cached_ref.1, bf16[128,128]{1,0:T(8,128)(2,1)} %copy-done.2, bf16[128,128]{1,0:T(8,128)(2,1)} %copy-done.3, bf16[256,128]{1,0:T(8,128)(2,1)} %k_ref.1, ...), custom_call_target="tpu_custom_call" | custom-call | flops 1342177280 | bytes 5439488 | tf_op jit(solution)/shard_map/pallas_call | solution.py:147
  22.3 0.0 collective-permute-start.2
  22.3 0.1 copy.33
  22.4 0.1 eq.49
  22.5 0.1 eq.45
  22.7 2.3 %reduce-window.6 = s32[8,8,128]{2,1,0:T(8,128)S(1)} reduce-window(s32[8,8,128]{2,1,0:T(8,128)S(1)} %fusion.34, s32[]{:T(128)} %constant.19.clone.1), window={size=1x1x128 pad=0_0x0_0x127_0}, to_apply=%region_0.0 | reduce-window | flops 1040384 | bytes 65540 | tf_op jit(solution)/shard_map/reduce-window
  24.9 0.3 slice_reduce_fusion
  25.2 0.2 reduce-window.9
  25.4 0.1 add_bitcast_fusion
  25.5 0.1 sub.39
  25.7 0.1 copy.35
  25.8 0.4 fusion.21
  26.2 0.0 copy-start.5
  26.2 2.2 %multiply_reduce_fusion.1 = (f32[256]{0:T(256)S(1)}, f32[256,1536]{1,0:T(8,128)S(1)}) fusion(f32[256,1536]{1,0:T(8,128)} %shard_map.118, f32[256,1536]{1,0:T(8,128)} %collective-permute-done.2, bf16[256,1536]{1,0:T(8,128)(2,1)S(1)} %copy-done.1), kind=kLoop, calls=%fused_computation.29 | loop fusion | flops 1965824 | bytes 5506048 | tf_op jit(solution)/shard_map/reduce_sum | solution.py:43
  28.5 0.0 slice-start
  28.5 0.9 convolution_convert_fusion.2
  29.4 0.0 slice-start.1
  29.4 0.1 fusion.41
  29.5 2.4 %collective-permute-start.3 = (bf16[96,1536]{1,0:T(8,128)(2,1)S(1)}, bf16[96,1536]{1,0:T(8,128)(2,1)S(1)}, u32[]{:S(2)}, u32[]{:S(2)}) collective-permute-start(bf16[96,1536]{1,0:T(8,128)(2,1)S(1)} %get-tuple-element.25), channel_id=1, source_target_pairs={{0,2},{2,4},{4,6},{6,8},{8,10},{10,12},{12,14},{14,0},{1,3},{3,5},... | collective-permute-start | bytes 884744 | tf_op jit(solution)/shard_map/ppermute | solution.py:38
  31.9 1.6 collective-permute-start.4
  33.5 3.4 %collective-permute-start.5 = (bf16[96,1536]{1,0:T(8,128)(2,1)S(1)}, bf16[96,1536]{1,0:T(8,128)(2,1)S(1)}, u32[]{:S(2)}, u32[]{:S(2)}) collective-permute-start(bf16[96,1536]{1,0:T(8,128)(2,1)S(1)} %get-tuple-element.23), channel_id=1, source_target_pairs={{0,6},{2,8},{4,10},{6,12},{8,14},{10,0},{12,2},{14,4},{1,7},{3,9},... | collective-permute-start | bytes 884744 | tf_op jit(solution)/shard_map/ppermute | solution.py:38
  36.9 1.2 collective-permute-start.6
  38.1 1.2 collective-permute-start.7
  39.4 2.9 %collective-permute-done.3 = bf16[96,1536]{1,0:T(8,128)(2,1)S(1)} collective-permute-done((bf16[96,1536]{1,0:T(8,128)(2,1)S(1)}, bf16[96,1536]{1,0:T(8,128)(2,1)S(1)}, u32[]{:S(2)}, u32[]{:S(2)}) %collective-permute-start.3) | collective-permute-done | bytes 294944 | tf_op jit(solution)/shard_map/ppermute | solution.py:38
  42.3 3.3 %collective-permute-start.8 = (bf16[96,1536]{1,0:T(8,128)(2,1)S(1)}, bf16[96,1536]{1,0:T(8,128)(2,1)S(1)}, u32[]{:S(2)}, u32[]{:S(2)}) collective-permute-start(bf16[96,1536]{1,0:T(8,128)(2,1)S(1)} %get-tuple-element.20), channel_id=1, source_target_pairs={{0,12},{2,14},{4,0},{6,2},{8,4},{10,6},{12,8},{14,10},{1,13},{3,15... | collective-permute-start | bytes 884744 | tf_op jit(solution)/shard_map/ppermute | solution.py:38
  45.6 0.0 collective-permute-done.4
  45.6 6.0 %collective-permute-start.9 = (bf16[96,1536]{1,0:T(8,128)(2,1)S(1)}, bf16[96,1536]{1,0:T(8,128)(2,1)S(1)}, u32[]{:S(2)}, u32[]{:S(2)}) collective-permute-start(bf16[96,1536]{1,0:T(8,128)(2,1)S(1)} %get-tuple-element.19), channel_id=1, source_target_pairs={{0,14},{2,0},{4,2},{6,4},{8,6},{10,8},{12,10},{14,12},{1,15},{3,1}... | collective-permute-start | bytes 884744 | tf_op jit(solution)/shard_map/ppermute | solution.py:38
  51.7 15.5 %collective-permute-done.5 = bf16[96,1536]{1,0:T(8,128)(2,1)S(1)} collective-permute-done((bf16[96,1536]{1,0:T(8,128)(2,1)S(1)}, bf16[96,1536]{1,0:T(8,128)(2,1)S(1)}, u32[]{:S(2)}, u32[]{:S(2)}) %collective-permute-start.5) | collective-permute-done | bytes 294944 | tf_op jit(solution)/shard_map/ppermute | solution.py:38
  67.1 1.1 collective-permute-done.6
  68.3 3.4 %collective-permute-done.9 = bf16[96,1536]{1,0:T(8,128)(2,1)S(1)} collective-permute-done((bf16[96,1536]{1,0:T(8,128)(2,1)S(1)}, bf16[96,1536]{1,0:T(8,128)(2,1)S(1)}, u32[]{:S(2)}, u32[]{:S(2)}) %collective-permute-start.9) | collective-permute-done | bytes 294944 | tf_op jit(solution)/shard_map/ppermute | solution.py:38
  71.8 0.1 collective-permute-start.10
  71.9 3.8 %fusion.15 = f32[2,768,768]{2,1,0:T(8,128)S(1)} fusion(bf16[768,1536,1]{1,0,2:T(8,128)(2,1)S(1)} %bitcast.104, bf16[1,2,1536,768]{3,2,1,0:T(8,128)(2,1)S(1)} %bitcast.107), kind=kOutput, calls=%fused_computation.24 | convolution fusion | flops 3623878656 | bytes 11796480 | tf_op jit(solution)/shard_map/rd,kdf->krf/dot_general | solution.py:70
  75.7 0.7 fusion.25
  76.4 3.8 %fusion.18 = f32[2,768,768]{2,1,0:T(8,128)S(1)} fusion(bf16[768,1536,1]{1,0,2:T(8,128)(2,1)S(1)} %bitcast.108, bf16[1,2,1536,768]{3,2,1,0:T(8,128)(2,1)S(1)} %bitcast.107), kind=kOutput, calls=%fused_computation.25 | convolution fusion | flops 3623878656 | bytes 11796480 | tf_op jit(solution)/shard_map/rd,kdf->krf/dot_general | solution.py:70
  80.2 2.1 %convolution_convert_fusion = bf16[768,1536]{1,0:T(8,128)(2,1)S(1)} fusion(bf16[1,768,1536]{2,1,0:T(8,128)(2,1)S(1)} %copy-done, f32[2,768,768]{2,1,0:T(8,128)S(1)} %fusion.18), kind=kOutput, calls=%fused_computation.6 | convolution fusion | flops 1817837568 | bytes 9437184 | tf_op jit(solution)/shard_map/dot_general | solution.py:211
  82.3 0.5 collective-permute-start.11
  82.8 2.0 %convolution_convert_fusion.1 = bf16[768,1536]{1,0:T(8,128)(2,1)S(1)} fusion(bf16[768,768]{1,0:T(8,128)(2,1)S(1)} %fusion.25, bf16[1,768,1536]{2,1,0:T(8,128)(2,1)S(1)} %copy-done), kind=kOutput, calls=%fused_computation.7 | convolution fusion | flops 1813118976 | bytes 5898240 | tf_op jit(solution)/shard_map/dot_general | solution.py:216
  84.8 2.2 %collective-permute-done.11 = bf16[8,96,1536]{2,1,0:T(8,128)(2,1)S(1)} collective-permute-done((bf16[8,96,1536]{2,1,0:T(8,128)(2,1)S(1)}, bf16[8,96,1536]{2,1,0:T(8,128)(2,1)S(1)}, u32[]{:S(2)}, u32[]{:S(2)}) %collective-permute-start.11) | collective-permute-done | bytes 2359328 | tf_op jit(solution)/shard_map/ppermute | solution.py:26
  87.0 0.7 fusion
  87.7 0.0 copy-start.6
  87.7 0.2 slice_bitcast_fusion
  87.9 18.0 %collective-permute-start.12 = (bf16[96,1536]{1,0:T(8,128)(2,1)S(1)}, bf16[96,1536]{1,0:T(8,128)(2,1)S(1)}, u32[]{:S(2)}, u32[]{:S(2)}) collective-permute-start(bf16[96,1536]{1,0:T(8,128)(2,1)S(1)} %get-tuple-element.17), channel_id=1, source_target_pairs={{0,14},{2,0},{4,2},{6,4},{8,6},{10,8},{12,10},{14,12},{1,15},{3,1}... | collective-permute-start | bytes 884744 | tf_op jit(solution)/shard_map/ppermute | solution.py:38
  106.0 0.5 multiply_reduce_fusion
  106.5 0.1 collective-permute-start.13
  106.6 0.7 collective-permute-start.14
  107.2 2.6 %collective-permute-start.15 = (bf16[96,1536]{1,0:T(8,128)(2,1)S(1)}, bf16[96,1536]{1,0:T(8,128)(2,1)S(1)}, u32[]{:S(2)}, u32[]{:S(2)}) collective-permute-start(bf16[96,1536]{1,0:T(8,128)(2,1)S(1)} %get-tuple-element.14), channel_id=1, source_target_pairs={{0,8},{2,10},{4,12},{6,14},{8,0},{10,2},{12,4},{14,6},{1,9},{3,11}... | collective-permute-start | bytes 884744 | tf_op jit(solution)/shard_map/ppermute | solution.py:38
  109.9 3.6 %collective-permute-done.12 = bf16[96,1536]{1,0:T(8,128)(2,1)S(1)} collective-permute-done((bf16[96,1536]{1,0:T(8,128)(2,1)S(1)}, bf16[96,1536]{1,0:T(8,128)(2,1)S(1)}, u32[]{:S(2)}, u32[]{:S(2)}) %collective-permute-start.12) | collective-permute-done | bytes 294944 | tf_op jit(solution)/shard_map/ppermute | solution.py:38
  113.4 6.3 %collective-permute-done.13 = bf16[96,1536]{1,0:T(8,128)(2,1)S(1)} collective-permute-done((bf16[96,1536]{1,0:T(8,128)(2,1)S(1)}, bf16[96,1536]{1,0:T(8,128)(2,1)S(1)}, u32[]{:S(2)}, u32[]{:S(2)}) %collective-permute-start.13) | collective-permute-done | bytes 294944 | tf_op jit(solution)/shard_map/ppermute | solution.py:38
  119.8 6.3 %collective-permute-done.14 = bf16[96,1536]{1,0:T(8,128)(2,1)S(1)} collective-permute-done((bf16[96,1536]{1,0:T(8,128)(2,1)S(1)}, bf16[96,1536]{1,0:T(8,128)(2,1)S(1)}, u32[]{:S(2)}, u32[]{:S(2)}) %collective-permute-start.14) | collective-permute-done | bytes 294944 | tf_op jit(solution)/shard_map/ppermute | solution.py:38
  126.1 31.7 %collective-permute-done.15 = bf16[96,1536]{1,0:T(8,128)(2,1)S(1)} collective-permute-done((bf16[96,1536]{1,0:T(8,128)(2,1)S(1)}, bf16[96,1536]{1,0:T(8,128)(2,1)S(1)}, u32[]{:S(2)}, u32[]{:S(2)}) %collective-permute-start.15) | collective-permute-done | bytes 294944 | tf_op jit(solution)/shard_map/ppermute | solution.py:38
  157.8 0.9 collective-permute-done.16
  158.8 0.8 fusion.28
  159.6 0.8 fusion.6
  160.4 0.1 collective-permute-start.19
  160.5 2.3 %collective-permute-done.19 = bf16[256,1536]{1,0:T(8,128)(2,1)S(1)} collective-permute-done((bf16[256,1536]{1,0:T(8,128)(2,1)S(1)}, bf16[256,1536]{1,0:T(8,128)(2,1)S(1)}, u32[]{:S(2)}, u32[]{:S(2)}) %collective-permute-start.19) | collective-permute-done | bytes 786464 | tf_op jit(solution)/shard_map/ppermute | solution.py:26
  162.8 1.2 add_convert_fusion
  (42 shorter events, 0.4 us)
Async XLA Ops:
  0.0 80.2 %copy-start = (bf16[1,768,1536]{2,1,0:T(8,128)(2,1)S(1)}, bf16[1,768,1536]{2,1,0:T(8,128)(2,1)}, u32[]{:S(2)}) copy-start(bf16[1,768,1536]{2,1,0:T(8,128)(2,1)} %param.21) | copy-start | bytes 7077892
  0.9 9.1 %collective-permute-start = (bf16[128,128]{1,0:T(8,128)(2,1)S(1)}, bf16[128,128]{1,0:T(8,128)(2,1)S(1)}, u32[]{:S(2)}, u32[]{:S(2)}) collective-permute-start(bf16[128,128]{1,0:T(8,128)(2,1)S(1)} %slice.82), channel_id=1, source_target_pairs={{0,2},{2,4},{4,6},{6,8},{8,10},{10,12},{12,14},{1,3},{3,5},{5,7},{... | collective-permute-start | bytes 98312 | tf_op jit(solution)/shard_map/ppermute | solution.py:21
  6.5 5.0 %collective-permute-start.1 = (bf16[128,128]{1,0:T(8,128)(2,1)S(1)}, bf16[128,128]{1,0:T(8,128)(2,1)S(1)}, u32[]{:S(2)}, u32[]{:S(2)}) collective-permute-start(bf16[128,128]{1,0:T(8,128)(2,1)S(1)} %slice.83), channel_id=1, source_target_pairs={{0,2},{2,4},{4,6},{6,8},{8,10},{10,12},{12,14},{1,3},{3,5},{5,7},{... | collective-permute-start | bytes 98312 | tf_op jit(solution)/shard_map/ppermute | solution.py:21
  10.0 1.6 copy-start.2
  11.5 0.6 copy-start.3
  12.2 10.1 %copy-start.4 = (s32[256,4]{0,1:T(4,128)S(1)}, s32[256,4]{0,1:T(4,128)}, u32[]{:S(2)}) copy-start(s32[256,4]{0,1:T(4,128)} %param.22) | copy-start | bytes 12292
  12.2 14.1 %copy-start.1 = (bf16[256,1536]{1,0:T(8,128)(2,1)S(1)}, bf16[256,1536]{1,0:T(8,128)(2,1)}, u32[]{:S(2)}) copy-start(bf16[256,1536]{1,0:T(8,128)(2,1)} %param.18) | copy-start | bytes 2359300
  22.3 3.9 %collective-permute-start.2 = (f32[256,1536]{1,0:T(8,128)}, f32[256,1536]{1,0:T(8,128)}, u32[]{:S(2)}, u32[]{:S(2)}) collective-permute-start(f32[256,1536]{1,0:T(8,128)} %shard_map.118), channel_id=1, source_target_pairs={{0,1},{1,0},{2,3},{3,2},{4,5},{5,4},{6,7},{7,6},{8,9},{9,8},{10,11... | collective-permute-start | bytes 4718600 | tf_op jit(solution)/shard_map/ppermute | solution.py:26
  26.2 2.3 %copy-start.5 = (f32[1536]{0:T(1024)S(1)}, f32[1536]{0:T(1024)}, u32[]{:S(2)}) copy-start(f32[1536]{0:T(1024)} %param.19) | copy-start | bytes 18436
  28.5 43.4 %slice-start = ((s8[4718592]{0:T(1024)(128)(4,1)}), s8[4194304]{0:T(1024)(128)(4,1)S(1)}, s32[]{:S(2)}) async-start(s8[4718592]{0:T(1024)(128)(4,1)} %bitcast.106), calls=%async_computation | async-start | bytes 8388608
  29.4 42.5 %slice-start.1 = ((s8[4718592]{0:T(1024)(128)(4,1)}), s8[524288]{0:T(1024)(128)(4,1)S(1)}, s32[]{:S(2)}) async-start(s8[4718592]{0:T(1024)(128)(4,1)} %bitcast.106), calls=%async_computation.1 | async-start | bytes 1048576
  29.5 12.8 %collective-permute-start.3 = (bf16[96,1536]{1,0:T(8,128)(2,1)S(1)}, bf16[96,1536]{1,0:T(8,128)(2,1)S(1)}, u32[]{:S(2)}, u32[]{:S(2)}) collective-permute-start(bf16[96,1536]{1,0:T(8,128)(2,1)S(1)} %get-tuple-element.25), channel_id=1, source_target_pairs={{0,2},{2,4},{4,6},{6,8},{8,10},{10,12},{12,14},{14,0},{1,3},{3,5},... | collective-permute-start | bytes 884744 | tf_op jit(solution)/shard_map/ppermute | solution.py:38
  31.9 13.7 %collective-permute-start.4 = (bf16[96,1536]{1,0:T(8,128)(2,1)S(1)}, bf16[96,1536]{1,0:T(8,128)(2,1)S(1)}, u32[]{:S(2)}, u32[]{:S(2)}) collective-permute-start(bf16[96,1536]{1,0:T(8,128)(2,1)S(1)} %get-tuple-element.24), channel_id=1, source_target_pairs={{0,4},{2,6},{4,8},{6,10},{8,12},{10,14},{12,0},{14,2},{1,5},{3,7},... | collective-permute-start | bytes 884744 | tf_op jit(solution)/shard_map/ppermute | solution.py:38
  33.5 33.7 %collective-permute-start.5 = (bf16[96,1536]{1,0:T(8,128)(2,1)S(1)}, bf16[96,1536]{1,0:T(8,128)(2,1)S(1)}, u32[]{:S(2)}, u32[]{:S(2)}) collective-permute-start(bf16[96,1536]{1,0:T(8,128)(2,1)S(1)} %get-tuple-element.23), channel_id=1, source_target_pairs={{0,6},{2,8},{4,10},{6,12},{8,14},{10,0},{12,2},{14,4},{1,7},{3,9},... | collective-permute-start | bytes 884744 | tf_op jit(solution)/shard_map/ppermute | solution.py:38
  36.9 31.3 %collective-permute-start.6 = (bf16[96,1536]{1,0:T(8,128)(2,1)S(1)}, bf16[96,1536]{1,0:T(8,128)(2,1)S(1)}, u32[]{:S(2)}, u32[]{:S(2)}) collective-permute-start(bf16[96,1536]{1,0:T(8,128)(2,1)S(1)} %get-tuple-element.22), channel_id=1, source_target_pairs={{0,8},{2,10},{4,12},{6,14},{8,0},{10,2},{12,4},{14,6},{1,9},{3,11}... | collective-permute-start | bytes 884744 | tf_op jit(solution)/shard_map/ppermute | solution.py:38
  38.1 30.1 %collective-permute-start.7 = (bf16[96,1536]{1,0:T(8,128)(2,1)S(1)}, bf16[96,1536]{1,0:T(8,128)(2,1)S(1)}, u32[]{:S(2)}, u32[]{:S(2)}) collective-permute-start(bf16[96,1536]{1,0:T(8,128)(2,1)S(1)} %get-tuple-element.21), channel_id=1, source_target_pairs={{0,10},{2,12},{4,14},{6,0},{8,2},{10,4},{12,6},{14,8},{1,11},{3,13... | collective-permute-start | bytes 884744 | tf_op jit(solution)/shard_map/ppermute | solution.py:38
  42.3 26.0 %collective-permute-start.8 = (bf16[96,1536]{1,0:T(8,128)(2,1)S(1)}, bf16[96,1536]{1,0:T(8,128)(2,1)S(1)}, u32[]{:S(2)}, u32[]{:S(2)}) collective-permute-start(bf16[96,1536]{1,0:T(8,128)(2,1)S(1)} %get-tuple-element.20), channel_id=1, source_target_pairs={{0,12},{2,14},{4,0},{6,2},{8,4},{10,6},{12,8},{14,10},{1,13},{3,15... | collective-permute-start | bytes 884744 | tf_op jit(solution)/shard_map/ppermute | solution.py:38
  45.6 26.1 %collective-permute-start.9 = (bf16[96,1536]{1,0:T(8,128)(2,1)S(1)}, bf16[96,1536]{1,0:T(8,128)(2,1)S(1)}, u32[]{:S(2)}, u32[]{:S(2)}) collective-permute-start(bf16[96,1536]{1,0:T(8,128)(2,1)S(1)} %get-tuple-element.19), channel_id=1, source_target_pairs={{0,14},{2,0},{4,2},{6,4},{8,6},{10,8},{12,10},{14,12},{1,15},{3,1}... | collective-permute-start | bytes 884744 | tf_op jit(solution)/shard_map/ppermute | solution.py:38
  71.8 4.6 %collective-permute-start.10 = (bf16[8,96,1536]{2,1,0:T(8,128)(2,1)S(1)}, bf16[8,96,1536]{2,1,0:T(8,128)(2,1)S(1)}, u32[]{:S(2)}, u32[]{:S(2)}) collective-permute-start(bf16[8,96,1536]{2,1,0:T(8,128)(2,1)S(1)} %bitcast_dynamic-update-slice_fusion.7), channel_id=1, source_target_pairs={{0,1},{1,0},{2,3},{3,2},{4,5},{5,4},{6,7},{7,6},{8,9},{9,8},{10,11... | collective-permute-start | bytes 7077896 | tf_op jit(solution)/shard_map/ppermute | solution.py:26
  82.3 4.7 %collective-permute-start.11 = (bf16[8,96,1536]{2,1,0:T(8,128)(2,1)S(1)}, bf16[8,96,1536]{2,1,0:T(8,128)(2,1)S(1)}, u32[]{:S(2)}, u32[]{:S(2)}) collective-permute-start(bf16[8,96,1536]{2,1,0:T(8,128)(2,1)S(1)} %bitcast.109), channel_id=1, source_target_pairs={{0,1},{1,0},{2,3},{3,2},{4,5},{5,4},{6,7},{7,6},{8,9},{9,8},{10,11... | collective-permute-start | bytes 7077896 | tf_op jit(solution)/shard_map/ppermute | solution.py:26
  87.7 18.3 %copy-start.6 = (f32[256,4]{0,1:T(4,128)S(1)}, f32[256,4]{0,1:T(4,128)}, u32[]{:S(2)}) copy-start(f32[256,4]{0,1:T(4,128)} %param.23) | copy-start | bytes 12292
  87.9 25.5 %collective-permute-start.12 = (bf16[96,1536]{1,0:T(8,128)(2,1)S(1)}, bf16[96,1536]{1,0:T(8,128)(2,1)S(1)}, u32[]{:S(2)}, u32[]{:S(2)}) collective-permute-start(bf16[96,1536]{1,0:T(8,128)(2,1)S(1)} %get-tuple-element.17), channel_id=1, source_target_pairs={{0,14},{2,0},{4,2},{6,4},{8,6},{10,8},{12,10},{14,12},{1,15},{3,1}... | collective-permute-start | bytes 884744 | tf_op jit(solution)/shard_map/ppermute | solution.py:38
  106.5 13.2 %collective-permute-start.13 = (bf16[96,1536]{1,0:T(8,128)(2,1)S(1)}, bf16[96,1536]{1,0:T(8,128)(2,1)S(1)}, u32[]{:S(2)}, u32[]{:S(2)}) collective-permute-start(bf16[96,1536]{1,0:T(8,128)(2,1)S(1)} %get-tuple-element.16), channel_id=1, source_target_pairs={{0,12},{2,14},{4,0},{6,2},{8,4},{10,6},{12,8},{14,10},{1,13},{3,15... | collective-permute-start | bytes 884744 | tf_op jit(solution)/shard_map/ppermute | solution.py:38
  106.6 19.5 %collective-permute-start.14 = (bf16[96,1536]{1,0:T(8,128)(2,1)S(1)}, bf16[96,1536]{1,0:T(8,128)(2,1)S(1)}, u32[]{:S(2)}, u32[]{:S(2)}) collective-permute-start(bf16[96,1536]{1,0:T(8,128)(2,1)S(1)} %get-tuple-element.15), channel_id=1, source_target_pairs={{0,10},{2,12},{4,14},{6,0},{8,2},{10,4},{12,6},{14,8},{1,11},{3,13... | collective-permute-start | bytes 884744 | tf_op jit(solution)/shard_map/ppermute | solution.py:38
  107.2 50.5 %collective-permute-start.15 = (bf16[96,1536]{1,0:T(8,128)(2,1)S(1)}, bf16[96,1536]{1,0:T(8,128)(2,1)S(1)}, u32[]{:S(2)}, u32[]{:S(2)}) collective-permute-start(bf16[96,1536]{1,0:T(8,128)(2,1)S(1)} %get-tuple-element.14), channel_id=1, source_target_pairs={{0,8},{2,10},{4,12},{6,14},{8,0},{10,2},{12,4},{14,6},{1,9},{3,11}... | collective-permute-start | bytes 884744 | tf_op jit(solution)/shard_map/ppermute | solution.py:38
  109.9 48.9 %collective-permute-start.16 = (bf16[96,1536]{1,0:T(8,128)(2,1)S(1)}, bf16[96,1536]{1,0:T(8,128)(2,1)S(1)}, u32[]{:S(2)}, u32[]{:S(2)}) collective-permute-start(bf16[96,1536]{1,0:T(8,128)(2,1)S(1)} %get-tuple-element.13), channel_id=1, source_target_pairs={{0,6},{2,8},{4,10},{6,12},{8,14},{10,0},{12,2},{14,4},{1,7},{3,9},... | collective-permute-start | bytes 884744 | tf_op jit(solution)/shard_map/ppermute | solution.py:38
  113.4 45.3 %collective-permute-start.17 = (bf16[96,1536]{1,0:T(8,128)(2,1)S(1)}, bf16[96,1536]{1,0:T(8,128)(2,1)S(1)}, u32[]{:S(2)}, u32[]{:S(2)}) collective-permute-start(bf16[96,1536]{1,0:T(8,128)(2,1)S(1)} %get-tuple-element.12), channel_id=1, source_target_pairs={{0,4},{2,6},{4,8},{6,10},{8,12},{10,14},{12,0},{14,2},{1,5},{3,7},... | collective-permute-start | bytes 884744 | tf_op jit(solution)/shard_map/ppermute | solution.py:38
  119.7 39.1 %collective-permute-start.18 = (bf16[96,1536]{1,0:T(8,128)(2,1)S(1)}, bf16[96,1536]{1,0:T(8,128)(2,1)S(1)}, u32[]{:S(2)}, u32[]{:S(2)}) collective-permute-start(bf16[96,1536]{1,0:T(8,128)(2,1)S(1)} %get-tuple-element.11), channel_id=1, source_target_pairs={{0,2},{2,4},{4,6},{6,8},{8,10},{10,12},{12,14},{14,0},{1,3},{3,5},... | collective-permute-start | bytes 884744 | tf_op jit(solution)/shard_map/ppermute | solution.py:38
  160.4 2.4 %collective-permute-start.19 = (bf16[256,1536]{1,0:T(8,128)(2,1)S(1)}, bf16[256,1536]{1,0:T(8,128)(2,1)S(1)}, u32[]{:S(2)}, u32[]{:S(2)}) collective-permute-start(bf16[256,1536]{1,0:T(8,128)(2,1)S(1)} %fusion.6), channel_id=1, source_target_pairs={{0,1},{1,0},{2,3},{3,2},{4,5},{5,4},{6,7},{7,6},{8,9},{9,8},{10,11... | collective-permute-start | bytes 2359304 | tf_op jit(solution)/shard_map/ppermute | solution.py:26
